TPU v7x, 256 devices: a whole 4x4x8 slice. The times are simulated.
256 devices in a mesh: guide: 2 (over x_hi), req: 128 (over x_lo, y, z, core).
Axes of the slice: x: 4 (x_hi: 2, x_lo: 2; x = x_hi * 2 + x_lo), y: 4, z: 8, core: 2. Of those that a mesh axis runs over, the one named last changes fastest.
Arguments:
- hidden_in: bfloat16 [2, 3072, 2048], P('guide', 'req'), may hold values from -24 to 24
- attn_gain: float32 [2048], replicated, may hold values from 0.25 to 1.75
- w_qkv: bfloat16 [2048, 1920], P('guide'), may hold values from -0.125 to 0.125
- w_out: bfloat16 [1280, 2048], P('guide'), may hold values from -0.3125 to 0.3125
- final_gain: float32 [2048], replicated, may hold values from 0.25 to 1.75
- w_vocab: bfloat16 [2048, 32000], P(None, 'req'), may hold values from -0.125 to 0.125
- kv_pool: bfloat16 [2, 5888, 64, 640], P('guide', 'req'), may hold values from -1400 to 1400
- cache_len: int32 [2, 3072], P('guide'), may hold values from 1 to 512, as said below
- page_table: int32 [2, 3072, 8], P('guide'), may hold values from 0 to 45, as said below
- migrations: int32 [2, 128, 3], P('guide'), may hold values from 0 to 3071, as said below
Outputs:
- guided: float32 [3072, 32000], P('guide', 'req')
Inputs may be any that keep to these rules, and one draw needn't show every extreme that they name: `cache_len`: cached tokens of a request of group 0 number at most 512, of group 1 at most 256; both bounds are reached in each group. `page_table`: row i lists request i's pages in order as numbers within the pool of its owner (old owner if listed, else req index i // 24); entries past its last page are 0; pages of different requests on one device differ. `migrations`: 128 rows per group, distinct requests; the new owner is request // 24; the old owner differs from it by 1 to 2 modulo 128; at most one row per pair of owners; a listed request has at most 2 pages; in each group some new owner receives, from each of its 4 nearest old owners, a request of 2 pages.
All inputs are finite; a program needn't handle non-finite values.
Results may differ from a plain program's by a relative error of at most 0.011.
The roundings to bfloat16 on the way count: a program that leaves them out, or rounds other values in their place, can miss the bound.
Values may be sent and summed in bfloat16 or wider, within the bound.
No kernel may reach another device: no remote copies, remote signals or barrier semaphores. Data moves between devices by JAX's collectives and lax.ppermute only.
A program may use at most 128 MiB of HBM per device.

v0:
```python
import math

import jax
import jax.numpy as jnp
from jax import lax
from jax.sharding import PartitionSpec as P

QH = 20
KVH = 5
HD = 64
MAXP = 8
MIGP = 2
HOP = 2


epsilon = 1e-06
guidance = 3.0


def from_partner(block, axis, bit):
    count = lax.axis_size(axis)
    route = []
    for low in range(count):
        high = low | 1 << bit
        if high != low and high < count:
            route += [(low, high), (high, low)]
    return lax.ppermute(block, axis, route)


def shifted(value, axis, steps):
    count = lax.axis_size(axis)
    pairs = [(source, (source + steps) % count) for source in range(count)]
    return lax.ppermute(value, axis, pairs)


def rms_scale(values, gain):
    return values * lax.rsqrt(jnp.mean(values * values, axis=-1, keepdims=True) + epsilon) * gain


def masked_scores(queries, page_rows, lengths):
    count = page_rows.shape[0]
    span = page_rows.shape[1]
    half_width = page_rows.shape[2] // 2
    key_rows = page_rows[:, :, :half_width].reshape(count, span, KVH, HD)
    value_rows = page_rows[:, :, half_width:].reshape(count, span, KVH, HD)
    scores = jnp.einsum(
        "rkgd,rskd->rkgs", queries, key_rows, preferred_element_type=jnp.float32
    ) * (1.0 / math.sqrt(HD))
    living = jnp.arange(span, dtype=jnp.int32)[None, :] < lengths[:, None]
    scores = jnp.where(living[:, None, None, :], scores, -jnp.inf)
    return (scores, value_rows)


def attend_all(queries, page_rows, lengths, own_score, value_new):
    scores, value_rows = masked_scores(queries, page_rows, lengths)
    highest = jnp.maximum(jnp.max(scores, axis=-1), own_score)
    weights = jnp.exp(scores - highest[..., None])
    own_weight = jnp.exp(own_score - highest)
    denominator = jnp.sum(weights, axis=-1) + own_weight
    weighted = jnp.einsum(
        "rkgs,rskd->rkgd",
        weights.astype(jnp.bfloat16),
        value_rows,
        preferred_element_type=jnp.float32,
    )
    own_rounded = own_weight.astype(jnp.bfloat16).astype(jnp.float32)
    weighted = weighted + own_rounded[..., None] * value_new.astype(jnp.float32)[:, :, None, :]
    return (highest, denominator, weighted)


def gather_pages(pool, tables):
    picked = pool[tables]
    return picked.reshape(tables.shape[0], tables.shape[1] * pool.shape[1], pool.shape[2])


def body(
    hidden_in,
    attn_gain,
    w_qkv,
    w_out,
    final_gain,
    w_vocab,
    kv_pool,
    cache_len,
    page_table,
    migrations,
):
    device = lax.axis_index("req")
    devices = lax.axis_size("req")
    side = lax.axis_index("guide")
    local_rows = hidden_in.shape[1]
    group = QH // KVH
    query_width = QH * HD
    key_width = KVH * HD
    scaling = 1.0 / math.sqrt(HD)
    slots = 2 * HOP
    offsets = [number - HOP if number < HOP else number - HOP + 1 for number in range(slots)]
    states_in = hidden_in[0].astype(jnp.float32)
    normed = rms_scale(states_in, attn_gain).astype(jnp.bfloat16)
    partner_normed = from_partner(normed, "guide", 0)
    both_normed = jnp.where(
        side == 0, jnp.stack([normed, partner_normed]), jnp.stack([partner_normed, normed])
    )
    inner_half = w_qkv.shape[0]
    normed_part = lax.dynamic_slice_in_dim(both_normed, side * inner_half, inner_half, 2)
    selected = normed_part
    joined = lax.psum_scatter(
        jnp.einsum("grd,df->grf", selected, w_qkv, preferred_element_type=jnp.float32),
        "guide",
        scatter_dimension=0,
        tiled=True,
    )[0].astype(jnp.bfloat16)
    queries = joined[:, :query_width].reshape(local_rows, KVH, group, HD)
    new_keys = joined[:, query_width : query_width + key_width].reshape(local_rows, KVH, HD)
    new_values = joined[:, query_width + key_width :].reshape(local_rows, KVH, HD)
    own_score = (
        jnp.einsum("rkgd,rkd->rkg", queries, new_keys, preferred_element_type=jnp.float32) * scaling
    )
    tables = page_table[0]
    lengths_all = cache_len[0]
    listing = migrations[0]
    pool = kv_pool[0]
    pool_pages = pool.shape[0]
    first_row = device * local_rows
    own_table = lax.dynamic_slice_in_dim(tables, first_row, local_rows, 0)
    own_lengths = lax.dynamic_slice_in_dim(lengths_all, first_row, local_rows, 0)
    global_ids = first_row + jnp.arange(local_rows, dtype=jnp.int32)
    matches = listing[None, :, 0] == global_ids[:, None]
    is_moved = jnp.any(matches, axis=1)
    old_owner = jnp.sum(jnp.where(matches, listing[None, :, 1], 0), axis=1)
    distance = jnp.remainder(device - old_owner, devices)
    slot_of = jnp.where(distance <= HOP, HOP + distance - 1, HOP - (devices - distance))
    arrivals = []
    for number in range(slots):
        offset = offsets[number]
        holding = (listing[:, 1] == device) & (
            listing[:, 2] == jnp.remainder(device + offset, devices)
        )
        held_request = listing[jnp.argmax(holding), 0]
        pages_sent = pool[tables[held_request, :MIGP]]
        arrivals.append(shifted(pages_sent, "req", offset))
    extended = jnp.concatenate([pool] + arrivals, axis=0)
    page_column = jnp.minimum(jnp.arange(MAXP, dtype=jnp.int32), MIGP - 1)
    moved_pages = pool_pages + slot_of[:, None] * MIGP + page_column[None, :]
    used_table = jnp.where(is_moved[:, None], moved_pages, own_table)
    tops, sums, accs = attend_all(
        queries, gather_pages(extended, used_table), own_lengths, own_score, new_values
    )
    attended = (accs / sums[..., None]).reshape(local_rows, query_width).astype(jnp.bfloat16)
    partner_attended = from_partner(attended, "guide", 0)
    both_attended = jnp.where(
        side == 0, jnp.stack([attended, partner_attended]), jnp.stack([partner_attended, attended])
    )
    head_half = w_out.shape[0]
    attended_part = lax.dynamic_slice_in_dim(both_attended, side * head_half, head_half, 2)
    selected = attended_part
    state_after = (
        states_in
        + lax.psum_scatter(
            jnp.einsum("grc,cd->grd", selected, w_out, preferred_element_type=jnp.float32).astype(
                jnp.bfloat16
            ),
            "guide",
            scatter_dimension=0,
            tiled=True,
        ).astype(jnp.float32)[0]
    )
    final = rms_scale(state_after, final_gain).astype(jnp.bfloat16)
    logits = jnp.dot(
        lax.all_gather(final, "req", axis=0, tiled=True),
        w_vocab,
        preferred_element_type=jnp.float32,
    )
    halves = logits.reshape(2, logits.shape[0] // 2, logits.shape[1])
    paired = lax.all_to_all(
        halves.astype(jnp.bfloat16), "guide", split_axis=0, concat_axis=0, tiled=True
    ).astype(halves.dtype)
    return paired[1] + guidance * (paired[0] - paired[1])


def solution(mesh):
    in_specs = (
        P("guide", "req", None),
        P(),
        P("guide", None),
        P("guide", None),
        P(),
        P(None, "req"),
        P("guide", "req", None, None),
        P("guide", None),
        P("guide", None, None),
        P("guide", None, None),
    )
    out_specs = P("guide", "req")
    return jax.shard_map(body, mesh=mesh, in_specs=in_specs, out_specs=out_specs, check_vma=False)
```

profile of v0, /device:TPU:1, one launch (start us, length us, event | category | flops | bytes accessed | tf_op | source)
XLA Modules:
  0.0 424.0 jit_solution(11976493014555277146)
XLA Ops:
  17.8 1.5 constant_dynamic-slice_fusion.8
  27.9 2.6 gather_fusion
  30.6 9.8 %collective-permute-start.1 = (bf16[2,64,640]{2,1,0:T(8,128)(2,1)S(1)}, bf16[2,64,640]{2,1,0:T(8,128)(2,1)S(1)}, u32[]{:S(2)}, u32[]{:S(2)}) collective-permute-start(bf16[2,64,640]{2,1,0:T(8,128)(2,1)S(1)} %gather_fusion), channel_id=1, source_target_pairs={{0,126},{1,127},{2,0},{3,1},{4,2},{5,3},{6,4},{7,5},{8,6},{9,7},{1... | collective-permute-start | bytes 491528 | tf_op jit(solution)/shard_map/ppermute | solution.py:33
  40.4 2.7 gather_fusion.1
  44.1 3.3 gather_fusion.2
  48.2 3.3 gather_fusion.3
  52.5 1.6 fusion.22
  54.1 2.5 collective-permute-start
  56.7 4.2 %constant_dynamic-update-slice_fusion.4 = bf16[54,64,640]{2,1,0:T(8,128)(2,1)} fusion(bf16[1,46,64,640]{3,2,1,0:T(8,128)(2,1)} %param.16), kind=kLoop, calls=%fused_computation.70 | loop fusion | bytes 7536640
  63.2 3.7 fusion
  68.5 1.6 constant_dynamic-update-slice_fusion.1
  70.2 1.6 constant_dynamic-update-slice_fusion
  71.7 11.2 %gather_fusion.4 = bf16[192,64,640]{2,1,0:T(8,128)(2,1)} fusion(bf16[54,64,640]{2,1,0:T(8,128)(2,1)} %constant_dynamic-update-slice_fusion, s32[1024]{0:T(1024)S(1)} %pad_clamp_fusion), kind=kCustom, calls=%fused_computation.4 | custom fusion | bytes 31458048 | tf_op jit(solution)/shard_map/gather | solution.py:72
  82.9 16.8 %fusion.64 = (bf16[24,512,320]{2,1,0:T(8,128)(2,1)}, bf16[24,512,320]{2,1,0:T(8,128)(2,1)}) fusion(bf16[24,512,640]{2,1,0:T(8,128)(2,1)} %bitcast.139), kind=kLoop, calls=%fused_computation.128 | loop fusion | bytes 31457280 | tf_op jit(solution)/shard_map/slice | solution.py:44
  99.8 11.6 %copy.27 = bf16[24,512,320]{1,2,0:T(8,128)(2,1)} copy(bf16[24,512,320]{2,1,0:T(8,128)(2,1)} %get-tuple-element.17) | data formatting | bytes 15728640
  111.3 11.5 %copy.28 = bf16[24,512,320]{1,2,0:T(8,128)(2,1)} copy(bf16[24,512,320]{2,1,0:T(8,128)(2,1)} %get-tuple-element.18) | data formatting | bytes 15728640
  124.4 4.5 %fusion.65 = (f32[24,5,4]{2,1,0:T(8,128)S(1)}, f32[24,5,4,512]{3,2,1,0:T(4,128)S(1)}) fusion(bf16[24,5,4,64]{3,2,1,0:T(4,128)(2,1)S(1)} %reshape.351, bf16[24,512,5,64]{1,3,2,0:T(8,128)(2,1)} %bitcast.140, pred[24,512]{1,0:T(8,128)(4,1)S(1)} %iota_compare_fusion), kind=kOutput, calls=%fused_computation.129 | convolution fusion | flops 32194080 | bytes 8923008 | tf_op jit(solution)/shard_map/rkgd,rskd->rkgs/dot_general | solution.py:46
  130.5 5.8 %fusion.12 = bf16[24,5,4,64]{3,2,1,0:T(4,128)(2,1)S(1)} fusion(bf16[24,512,5,64]{1,3,2,0:T(8,128)(2,1)} %bitcast.141, f32[24,5,4,512]{3,2,1,0:T(4,128)} %copy-done.1, f32[24,5,4]{2,1,0:T(8,128)S(1)} %fusion.31, f32[24,5,4]{2,1,0:T(8,128)S(1)} %get-tuple-element.20, f32[24,5,64]{2,1,0:T(8,128)S(1)} %reshape.357, f32[24,5,4]{2,1,0:T(8,128)S(1)} %get-tuple-element.19), kind=kOutput, calls=%fused_computation.20 | convolution fusion | flops 32071680 | bytes 8945280 | tf_op jit(solution)/shard_map/rkgs,rskd->rkgd/dot_general | solution.py:60
  137.2 4.0 collective-permute-done.5
  142.7 14.7 %reduce-scatter.5.cloned.1.call-done = bf16[1,24,2048]{2,1,0:T(8,128)(2,1)} async-done(((bf16[2,24,2048]{2,1,0:T(8,128)(2,1)}), bf16[1,24,2048]{2,1,0:T(8,128)(2,1)}) %reduce-scatter.5.cloned.1.call-update) | async-done | bytes 98320 | tf_op jit(solution)/shard_map/reduce_scatter | solution.py:159
  158.4 1.6 multiply_convert_fusion
  160.1 224.3 %all-gather.2.cloned.1.call-done = bf16[3072,2048]{1,0:T(8,128)(2,1)} async-done(((bf16[24,2048]{1,0:T(8,128)(2,1)}), bf16[3072,2048]{1,0:T(8,128)(2,1)}) %all-gather.2.cloned.1.call-update) | async-done | bytes 12582928 | tf_op jit(solution)/shard_map/all_gather | solution.py:170
  384.4 8.2 %convolution_convert_fusion = bf16[3072,250]{1,0:T(8,128)(2,1)S(1)} fusion(bf16[3072,2048]{1,0:T(8,128)(2,1)} %all-gather.2.cloned.1.call-done, bf16[2048,250]{1,0:T(8,128)(2,1)} %param.15), kind=kOutput, calls=%fused_computation.7 | convolution fusion | flops 3146496000 | bytes 15142912 | tf_op jit(solution)/shard_map/dot_general | solution.py:169
  392.6 23.2 %all_to_all.5 = bf16[2,1536,250]{2,1,0:T(8,128)(2,1)S(1)} all-to-all(bf16[2,1536,250]{2,1,0:T(8,128)(2,1)S(1)} %bitcast.146), channel_id=1, replica_groups=mesh['guide'=2,'req'=128] {'guide'}, dimensions={0} | all-to-all | bytes 3072000 | tf_op jit(solution)/shard_map/all_to_all | solution.py:175
  (72 shorter events, 19.6 us)
Async XLA Ops:
  6.5 134.6 %copy-start = (bf16[640,2048]{1,0:T(8,128)(2,1)S(1)}, bf16[640,2048]{1,0:T(8,128)(2,1)}, u32[]{:S(2)}) copy-start(bf16[640,2048]{1,0:T(8,128)(2,1)} %param.13) | copy-start | bytes 7864324
  6.5 116.3 %reduce-scatter.7.cloned.1.call-start = ((), (), s32[]{:S(2)}) async-start(), calls=%async_computation.5 | async-start | bytes 552960
  30.6 36.6 %collective-permute-start.1 = (bf16[2,64,640]{2,1,0:T(8,128)(2,1)S(1)}, bf16[2,64,640]{2,1,0:T(8,128)(2,1)S(1)}, u32[]{:S(2)}, u32[]{:S(2)}) collective-permute-start(bf16[2,64,640]{2,1,0:T(8,128)(2,1)S(1)} %gather_fusion), channel_id=1, source_target_pairs={{0,126},{1,127},{2,0},{3,1},{4,2},{5,3},{6,4},{7,5},{8,6},{9,7},{1... | collective-permute-start | bytes 491528 | tf_op jit(solution)/shard_map/ppermute | solution.py:33
  40.4 20.6 %copy-start.2 = (bf16[1,24,2048]{2,1,0:T(8,128)(2,1)S(1)}, bf16[1,24,2048]{2,1,0:T(8,128)(2,1)}, u32[]{:S(2)}) copy-start(bf16[1,24,2048]{2,1,0:T(8,128)(2,1)} %param.10) | copy-start | bytes 294916
  40.4 20.6 %copy-start.3 = (f32[2048]{0:T(1024)S(1)}, f32[2048]{0:T(1024)}, u32[]{:S(2)}) copy-start(f32[2048]{0:T(1024)} %param.11) | copy-start | bytes 24580
  43.0 24.8 %collective-permute-start.2 = (bf16[2,64,640]{2,1,0:T(8,128)(2,1)S(1)}, bf16[2,64,640]{2,1,0:T(8,128)(2,1)S(1)}, u32[]{:S(2)}, u32[]{:S(2)}) collective-permute-start(bf16[2,64,640]{2,1,0:T(8,128)(2,1)S(1)} %gather_fusion.1), channel_id=1, source_target_pairs={{0,127},{1,0},{2,1},{3,2},{4,3},{5,4},{6,5},{7,6},{8,7},{9,8},{10,... | collective-permute-start | bytes 491528 | tf_op jit(solution)/shard_map/ppermute | solution.py:33
  47.4 21.2 %collective-permute-start.3 = (bf16[2,64,640]{2,1,0:T(8,128)(2,1)}, bf16[2,64,640]{2,1,0:T(8,128)(2,1)}, u32[]{:S(2)}, u32[]{:S(2)}) collective-permute-start(bf16[2,64,640]{2,1,0:T(8,128)(2,1)} %gather_fusion.2), channel_id=1, source_target_pairs={{0,1},{1,2},{2,3},{3,4},{4,5},{5,6},{6,7},{7,8},{8,9},{9,10},{10,1... | collective-permute-start | bytes 491528 | tf_op jit(solution)/shard_map/ppermute | solution.py:33
  51.5 18.7 %collective-permute-start.4 = (bf16[2,64,640]{2,1,0:T(8,128)(2,1)}, bf16[2,64,640]{2,1,0:T(8,128)(2,1)}, u32[]{:S(2)}, u32[]{:S(2)}) collective-permute-start(bf16[2,64,640]{2,1,0:T(8,128)(2,1)} %gather_fusion.3), channel_id=1, source_target_pairs={{0,2},{1,3},{2,4},{3,5},{4,6},{5,7},{6,8},{7,9},{8,10},{9,11},{10,... | collective-permute-start | bytes 491528 | tf_op jit(solution)/shard_map/ppermute | solution.py:33
  54.1 9.1 %collective-permute-start = (bf16[24,2048]{1,0:T(8,128)(2,1)}, bf16[24,2048]{1,0:T(8,128)(2,1)}, u32[]{:S(2)}, u32[]{:S(2)}) collective-permute-start(bf16[24,2048]{1,0:T(8,128)(2,1)} %fusion.22), channel_id=1, source_target_pairs={{0,128},{128,0},{1,129},{129,1},{2,130},{130,2},{3,131},{131,3},{4... | collective-permute-start | bytes 294920 | tf_op jit(solution)/shard_map/ppermute | solution.py:27
  66.9 90.5 %reduce-scatter.5.cloned.1.call-start = ((), (), s32[]{:S(2)}) async-start(), calls=%async_computation.3 | async-start | bytes 294912 | tf_op jit(solution)/shard_map/reduce_scatter | solution.py:159
  128.8 0.9 copy-start.1
  136.3 22.1 %copy-start.4 = (f32[2048]{0:T(1024)S(1)}, f32[2048]{0:T(1024)}, u32[]{:S(2)}) copy-start(f32[2048]{0:T(1024)} %param.14) | copy-start | bytes 24580
  136.5 4.7 %collective-permute-start.5 = (bf16[24,1280]{1,0:T(8,128)(2,1)S(1)}, bf16[24,1280]{1,0:T(8,128)(2,1)S(1)}, u32[]{:S(2)}, u32[]{:S(2)}) collective-permute-start(bf16[24,1280]{1,0:T(8,128)(2,1)S(1)} %convert_element_type.86), channel_id=1, source_target_pairs={{0,128},{128,0},{1,129},{129,1},{2,130},{130,2},{3,131},{131,3},{4... | collective-permute-start | bytes 184328 | tf_op jit(solution)/shard_map/ppermute | solution.py:27
  142.4 242.0 %all-gather.2.cloned.1.call-start = ((), (), s32[]{:S(2)}) async-start(), calls=%async_computation.4 | async-start | bytes 12681216 | tf_op jit(solution)/shard_map/all_gather | solution.py:170
Sparse Core Ops, SparseCore 0:
  67.0 15.8 reduce-scatter.6
  142.5 14.8 reduce-scatter.4
  160.2 224.1 all-gather.1
where the time goes:
time: 427 us; the launch traced here: 424 us
  waiting for transfers between devices  243 us (57%)
  local copies, waits for them, and re-layouts  77.6 us (18%)
  between operations  28.5 us (7%)
  matrix products  23.7 us (6%)
  blocking collectives  23.2 us (5%)
  starting transfers between devices  15.2 us (4%)
  other arithmetic  12.8 us (3%)
    all_gather x1, waiting for transfers between devices, body(): lax.all_gather(final, 'req', axis=0, tiled=True)  224 us
    unnamed x17, local copies, waits for them, and re-layouts  32.1 us
    all_to_all x1, blocking collectives, body(): lax.all_to_all(halves.astype(jnp.bfloat16), 'guide', split_axis=0, concat...  23.2 us
    slice x1, local copies, waits for them, and re-layouts, masked_scores(): key_rows = page_rows[:, :, :half_width].reshape(count, span, KVH, HD)  16.8 us
    reduce_scatter x1, waiting for transfers between devices, body(): lax.psum_scatter(jnp.einsum('grc,cd->grd', selected, w_out, preferred_ele...  14.7 us
    gather x4, local copies, waits for them, and re-layouts, body(): pages_sent = pool[tables[held_request, :MIGP]]  11.9 us
    ppermute x4, starting transfers between devices, shifted(): return lax.ppermute(value, axis, pairs)  11.6 us
    gather x1, local copies, waits for them, and re-layouts, gather_pages(): picked = pool[tables]  11.2 us
  transfers between devices with their start and end apart: 9, of which 3 were waited for; matrix products, arithmetic and copies ran while one was open for 18% of the time, Pallas kernels for 0%

commit v1 on v0

--- a/solution.py
+++ b/solution.py
@@ -166,16 +166,23 @@
         ).astype(jnp.float32)[0]
     )
     final = rms_scale(state_after, final_gain).astype(jnp.bfloat16)
-    logits = jnp.dot(
-        lax.all_gather(final, "req", axis=0, tiled=True),
-        w_vocab,
-        preferred_element_type=jnp.float32,
-    )
-    halves = logits.reshape(2, logits.shape[0] // 2, logits.shape[1])
-    paired = lax.all_to_all(
-        halves.astype(jnp.bfloat16), "guide", split_axis=0, concat_axis=0, tiled=True
-    ).astype(halves.dtype)
-    return paired[1] + guidance * (paired[0] - paired[1])
+    partner_final = from_partner(final, "guide", 0)
+    cond = jnp.where(side == 0, final, partner_final).astype(jnp.float32)
+    uncond = jnp.where(side == 0, partner_final, final).astype(jnp.float32)
+    combined = (uncond + guidance * (cond - uncond)).astype(jnp.bfloat16)
+    half_devices = devices // 2
+    half_rows = local_rows // 2
+    upper = device // half_devices
+    kept = lax.dynamic_slice_in_dim(combined, upper * half_rows, half_rows, 0)
+    sent = lax.dynamic_slice_in_dim(combined, (1 - upper) * half_rows, half_rows, 0)
+    swapped = shifted(sent, "req", half_devices)
+    mine = jnp.where(upper == side, kept, swapped)
+    gathered = lax.all_gather(mine, "req", axis=0, tiled=False)
+    gathered = gathered.reshape(2, half_devices, half_rows, gathered.shape[-1])
+    logits = jnp.einsum(
+        "xjkd,dv->jxkv", gathered, w_vocab, preferred_element_type=jnp.float32
+    )
+    return logits.reshape(half_devices * local_rows, logits.shape[-1])
 
 
 def solution(mesh):

time: 427 us -> 414 us (0.970)
  blocking collectives: 23.2 us -> 0 us
  waiting for transfers between devices: 243 us -> 248 us
  local copies, waits for them, and re-layouts: 77.6 us -> 82.4 us
    all_to_all x1 -> x0, blocking collectives: 23.2 us -> none  [body(): lax.all_to_all(halves.astype(jnp.bfloat16), 'guide', split_axis=0, concat...]
    ppermute x2 -> x3, waiting for transfers between devices: 3.99 us -> 8.85 us  [from_partner(): return lax.ppermute(block, axis, route)]
    ppermute x4 -> x5, starting transfers between devices: 11.6 us -> 12.3 us  [shifted(): return lax.ppermute(value, axis, pairs)]
  transfers between devices with their start and end apart: 9 -> 11, of which waited for: 3 -> 5; matrix products, arithmetic and copies ran while one was open for 18% -> 19% of each run, Pallas kernels for 0% -> 0%
where the time goes in v1:
time: 414 us; the launch traced here: 413 us
  waiting for transfers between devices  248 us (60%)
  local copies, waits for them, and re-layouts  82.4 us (20%)
  between operations  28.5 us (7%)
  matrix products  26.4 us (6%)
  starting transfers between devices  15.7 us (4%)
  other arithmetic  11.2 us (3%)
    all_gather x1, waiting for transfers between devices, body(): gathered = lax.all_gather(mine, 'req', axis=0, tiled=False)  222 us
    unnamed x17, local copies, waits for them, and re-layouts  32.1 us
    slice x1, local copies, waits for them, and re-layouts, masked_scores(): key_rows = page_rows[:, :, :half_width].reshape(count, span, KVH, HD)  16.8 us
    reduce_scatter x1, waiting for transfers between devices, body(): lax.psum_scatter(jnp.einsum('grc,cd->grd', selected, w_out, preferred_ele...  15 us
    ppermute x5, starting transfers between devices, shifted(): return lax.ppermute(value, axis, pairs)  12.3 us
    gather x4, local copies, waits for them, and re-layouts, body(): pages_sent = pool[tables[held_request, :MIGP]]  11.9 us
    gather x1, local copies, waits for them, and re-layouts, gather_pages(): picked = pool[tables]  11.2 us
    dot_general x1, matrix products, body(): jnp.einsum('xjkd,dv->jxkv', gathered, w_vocab, preferred_element_type=jnp...  11 us
  transfers between devices with their start and end apart: 11, of which 5 were waited for; matrix products, arithmetic and copies ran while one was open for 19% of the time, Pallas kernels for 0%

profile of v1, /device:TPU:1, one launch (start us, length us, event | category | flops | bytes accessed | tf_op | source)
XLA Modules:
  0.0 412.7 jit_solution(5128230847193110954)
XLA Ops:
  27.9 2.6 gather_fusion
  30.5 9.9 %collective-permute-start.1 = (bf16[2,64,640]{2,1,0:T(8,128)(2,1)S(1)}, bf16[2,64,640]{2,1,0:T(8,128)(2,1)S(1)}, u32[]{:S(2)}, u32[]{:S(2)}) collective-permute-start(bf16[2,64,640]{2,1,0:T(8,128)(2,1)S(1)} %gather_fusion), channel_id=1, source_target_pairs={{0,126},{1,127},{2,0},{3,1},{4,2},{5,3},{6,4},{7,5},{8,6},{9,7},{1... | collective-permute-start | bytes 491528 | tf_op jit(solution)/shard_map/ppermute | solution.py:33
  40.4 2.7 gather_fusion.1
  44.2 3.3 gather_fusion.2
  48.2 3.3 gather_fusion.3
  52.5 1.6 fusion.27
  54.2 2.5 collective-permute-start
  56.6 4.2 %constant_dynamic-update-slice_fusion.4 = bf16[54,64,640]{2,1,0:T(8,128)(2,1)} fusion(bf16[1,46,64,640]{3,2,1,0:T(8,128)(2,1)} %param.16), kind=kLoop, calls=%fused_computation.73 | loop fusion | bytes 7536640
  63.2 3.7 fusion.2
  68.5 1.6 constant_dynamic-update-slice_fusion.1
  71.7 11.2 %gather_fusion.4 = bf16[192,64,640]{2,1,0:T(8,128)(2,1)} fusion(bf16[54,64,640]{2,1,0:T(8,128)(2,1)} %constant_dynamic-update-slice_fusion, s32[1024]{0:T(1024)S(1)} %pad_clamp_fusion), kind=kCustom, calls=%fused_computation.4 | custom fusion | bytes 31458048 | tf_op jit(solution)/shard_map/gather | solution.py:72
  82.9 16.8 %fusion.69 = (bf16[24,512,320]{2,1,0:T(8,128)(2,1)}, bf16[24,512,320]{2,1,0:T(8,128)(2,1)}) fusion(bf16[24,512,640]{2,1,0:T(8,128)(2,1)} %bitcast.134), kind=kLoop, calls=%fused_computation.132 | loop fusion | bytes 31457280 | tf_op jit(solution)/shard_map/slice | solution.py:44
  99.7 11.6 %copy.45 = bf16[24,512,320]{1,2,0:T(8,128)(2,1)} copy(bf16[24,512,320]{2,1,0:T(8,128)(2,1)} %get-tuple-element.17) | data formatting | bytes 15728640
  111.3 11.5 %copy.46 = bf16[24,512,320]{1,2,0:T(8,128)(2,1)} copy(bf16[24,512,320]{2,1,0:T(8,128)(2,1)} %get-tuple-element.18) | data formatting | bytes 15728640
  124.3 4.5 %fusion.70 = (f32[24,5,4]{2,1,0:T(8,128)S(1)}, f32[24,5,4,512]{3,2,1,0:T(4,128)S(1)}) fusion(bf16[24,5,4,64]{3,2,1,0:T(4,128)(2,1)S(1)} %reshape.355, bf16[24,512,5,64]{1,3,2,0:T(8,128)(2,1)} %bitcast.135, pred[24,512]{1,0:T(8,128)(4,1)S(1)} %iota_compare_fusion), kind=kOutput, calls=%fused_computation.133 | convolution fusion | flops 32194080 | bytes 8923008 | tf_op jit(solution)/shard_map/rkgd,rskd->rkgs/dot_general | solution.py:46
  130.5 5.8 %fusion.14 = bf16[24,5,4,64]{3,2,1,0:T(4,128)(2,1)S(1)} fusion(bf16[24,512,5,64]{1,3,2,0:T(8,128)(2,1)} %bitcast.136, f32[24,5,4,512]{3,2,1,0:T(4,128)} %copy-done.1, f32[24,5,4]{2,1,0:T(8,128)S(1)} %fusion.36, f32[24,5,4]{2,1,0:T(8,128)S(1)} %get-tuple-element.20, f32[24,5,64]{2,1,0:T(8,128)S(1)} %reshape.363, f32[24,5,4]{2,1,0:T(8,128)S(1)} %get-tuple-element.19), kind=kOutput, calls=%fused_computation.17 | convolution fusion | flops 32071680 | bytes 8945280 | tf_op jit(solution)/shard_map/rkgs,rskd->rkgd/dot_general | solution.py:60
  137.2 3.9 collective-permute-done.5
  142.4 15.0 %reduce-scatter.5.cloned.1.call-done = bf16[1,24,2048]{2,1,0:T(8,128)(2,1)} async-done(((bf16[2,24,2048]{2,1,0:T(8,128)(2,1)}), bf16[1,24,2048]{2,1,0:T(8,128)(2,1)}) %reduce-scatter.5.cloned.1.call-update) | async-done | bytes 98320 | tf_op jit(solution)/shard_map/reduce_scatter | solution.py:159
  159.6 4.9 %collective-permute-done.6 = bf16[24,2048]{1,0:T(8,128)(2,1)S(1)} collective-permute-done((bf16[24,2048]{1,0:T(8,128)(2,1)S(1)}, bf16[24,2048]{1,0:T(8,128)(2,1)S(1)}, u32[]{:S(2)}, u32[]{:S(2)}) %collective-permute-start.6) | collective-permute-done | bytes 98336 | tf_op jit(solution)/shard_map/ppermute | solution.py:27
  165.2 2.8 collective-permute-done.7
  168.7 221.7 %all-gather.4.cloned.1.call-done = bf16[128,12,2048]{2,1,0:T(8,128)(2,1)} async-done(((bf16[1,12,2048]{2,1,0:T(8,128)(2,1)}), bf16[128,12,2048]{2,1,0:T(8,128)(2,1)}) %all-gather.4.cloned.1.call-update) | async-done | bytes 6291472 | tf_op jit(solution)/shard_map/all_gather | solution.py:180
  390.4 11.0 %fusion.9 = f32[64,2,12,250]{3,0,2,1:T(8,128)S(1)} fusion(bf16[2,64,12,2048]{3,2,1,0:T(8,128)(2,1)} %bitcast.147, bf16[2048,250]{1,0:T(8,128)(2,1)} %param.15), kind=kOutput, calls=%fused_computation.12 | convolution fusion | flops 1572864000 | bytes 8851456 | tf_op jit(solution)/shard_map/xjkd,dv->jxkv/dot_general | solution.py:182
  401.4 2.3 copy.38
  403.7 2.5 reshape.361
  (78 shorter events, 23.3 us)
Async XLA Ops:
  6.5 134.6 %copy-start = (bf16[640,2048]{1,0:T(8,128)(2,1)S(1)}, bf16[640,2048]{1,0:T(8,128)(2,1)}, u32[]{:S(2)}) copy-start(bf16[640,2048]{1,0:T(8,128)(2,1)} %param.13) | copy-start | bytes 7864324
  6.5 116.3 %reduce-scatter.7.cloned.1.call-start = ((), (), s32[]{:S(2)}) async-start(), calls=%async_computation.4 | async-start | bytes 552960
  30.5 36.6 %collective-permute-start.1 = (bf16[2,64,640]{2,1,0:T(8,128)(2,1)S(1)}, bf16[2,64,640]{2,1,0:T(8,128)(2,1)S(1)}, u32[]{:S(2)}, u32[]{:S(2)}) collective-permute-start(bf16[2,64,640]{2,1,0:T(8,128)(2,1)S(1)} %gather_fusion), channel_id=1, source_target_pairs={{0,126},{1,127},{2,0},{3,1},{4,2},{5,3},{6,4},{7,5},{8,6},{9,7},{1... | collective-permute-start | bytes 491528 | tf_op jit(solution)/shard_map/ppermute | solution.py:33
  40.4 20.5 %copy-start.2 = (bf16[1,24,2048]{2,1,0:T(8,128)(2,1)S(1)}, bf16[1,24,2048]{2,1,0:T(8,128)(2,1)}, u32[]{:S(2)}) copy-start(bf16[1,24,2048]{2,1,0:T(8,128)(2,1)} %param.10) | copy-start | bytes 294916
  40.4 20.5 %copy-start.3 = (f32[2048]{0:T(1024)S(1)}, f32[2048]{0:T(1024)}, u32[]{:S(2)}) copy-start(f32[2048]{0:T(1024)} %param.11) | copy-start | bytes 24580
  43.1 24.7 %collective-permute-start.2 = (bf16[2,64,640]{2,1,0:T(8,128)(2,1)S(1)}, bf16[2,64,640]{2,1,0:T(8,128)(2,1)S(1)}, u32[]{:S(2)}, u32[]{:S(2)}) collective-permute-start(bf16[2,64,640]{2,1,0:T(8,128)(2,1)S(1)} %gather_fusion.1), channel_id=1, source_target_pairs={{0,127},{1,0},{2,1},{3,2},{4,3},{5,4},{6,5},{7,6},{8,7},{9,8},{10,... | collective-permute-start | bytes 491528 | tf_op jit(solution)/shard_map/ppermute | solution.py:33
  47.5 21.1 %collective-permute-start.3 = (bf16[2,64,640]{2,1,0:T(8,128)(2,1)}, bf16[2,64,640]{2,1,0:T(8,128)(2,1)}, u32[]{:S(2)}, u32[]{:S(2)}) collective-permute-start(bf16[2,64,640]{2,1,0:T(8,128)(2,1)} %gather_fusion.2), channel_id=1, source_target_pairs={{0,1},{1,2},{2,3},{3,4},{4,5},{5,6},{6,7},{7,8},{8,9},{9,10},{10,1... | collective-permute-start | bytes 491528 | tf_op jit(solution)/shard_map/ppermute | solution.py:33
  51.5 18.6 %collective-permute-start.4 = (bf16[2,64,640]{2,1,0:T(8,128)(2,1)}, bf16[2,64,640]{2,1,0:T(8,128)(2,1)}, u32[]{:S(2)}, u32[]{:S(2)}) collective-permute-start(bf16[2,64,640]{2,1,0:T(8,128)(2,1)} %gather_fusion.3), channel_id=1, source_target_pairs={{0,2},{1,3},{2,4},{3,5},{4,6},{5,7},{6,8},{7,9},{8,10},{9,11},{10,... | collective-permute-start | bytes 491528 | tf_op jit(solution)/shard_map/ppermute | solution.py:33
  54.2 9.0 %collective-permute-start = (bf16[24,2048]{1,0:T(8,128)(2,1)}, bf16[24,2048]{1,0:T(8,128)(2,1)}, u32[]{:S(2)}, u32[]{:S(2)}) collective-permute-start(bf16[24,2048]{1,0:T(8,128)(2,1)} %fusion.27), channel_id=1, source_target_pairs={{0,128},{128,0},{1,129},{129,1},{2,130},{130,2},{3,131},{131,3},{4... | collective-permute-start | bytes 294920 | tf_op jit(solution)/shard_map/ppermute | solution.py:27
  66.9 90.5 %reduce-scatter.5.cloned.1.call-start = ((), (), s32[]{:S(2)}) async-start(), calls=%async_computation.2 | async-start | bytes 294912 | tf_op jit(solution)/shard_map/reduce_scatter | solution.py:159
  128.8 0.9 copy-start.1
  136.3 22.2 %copy-start.4 = (f32[2048]{0:T(1024)S(1)}, f32[2048]{0:T(1024)}, u32[]{:S(2)}) copy-start(f32[2048]{0:T(1024)} %param.14) | copy-start | bytes 24580
  136.4 4.7 %collective-permute-start.5 = (bf16[24,1280]{1,0:T(8,128)(2,1)S(1)}, bf16[24,1280]{1,0:T(8,128)(2,1)S(1)}, u32[]{:S(2)}, u32[]{:S(2)}) collective-permute-start(bf16[24,1280]{1,0:T(8,128)(2,1)S(1)} %convert_element_type.86), channel_id=1, source_target_pairs={{0,128},{128,0},{1,129},{129,1},{2,130},{130,2},{3,131},{131,3},{4... | collective-permute-start | bytes 184328 | tf_op jit(solution)/shard_map/ppermute | solution.py:27
  142.4 248.0 %all-gather.4.cloned.1.call-start = ((), (), s32[]{:S(2)}) async-start(), calls=%async_computation.3 | async-start | bytes 8454144 | tf_op jit(solution)/shard_map/all_gather | solution.py:180
  159.5 5.1 %collective-permute-start.6 = (bf16[24,2048]{1,0:T(8,128)(2,1)S(1)}, bf16[24,2048]{1,0:T(8,128)(2,1)S(1)}, u32[]{:S(2)}, u32[]{:S(2)}) collective-permute-start(bf16[24,2048]{1,0:T(8,128)(2,1)S(1)} %multiply_convert_fusion), channel_id=1, source_target_pairs={{0,128},{128,0},{1,129},{129,1},{2,130},{130,2},{3,131},{131,3},{4... | collective-permute-start | bytes 294920 | tf_op jit(solution)/shard_map/ppermute | solution.py:27
  164.6 3.4 collective-permute-start.7
Sparse Core Ops, SparseCore 0:
  67.0 15.9 reduce-scatter.6
  142.5 14.8 reduce-scatter.4
  168.8 221.5 all-gather.3

commit v2 on v1

--- a/solution.py
+++ b/solution.py
@@ -3,6 +3,7 @@
 import jax
 import jax.numpy as jnp
 from jax import lax
+from jax.sharding import Mesh
 from jax.sharding import PartitionSpec as P
 
 QH = 20
@@ -11,6 +12,8 @@
 MAXP = 8
 MIGP = 2
 HOP = 2
+REQ = ("x_lo", "y", "z", "core")
+REQ_SPLIT = (2, 4, 8, 2)
 
 
 epsilon = 1e-06
@@ -85,8 +88,8 @@
     page_table,
     migrations,
 ):
-    device = lax.axis_index("req")
-    devices = lax.axis_size("req")
+    device = lax.axis_index(REQ)
+    devices = lax.axis_size(REQ)
     side = lax.axis_index("guide")
     local_rows = hidden_in.shape[1]
     group = QH // KVH
@@ -138,7 +141,7 @@
         )
         held_request = listing[jnp.argmax(holding), 0]
         pages_sent = pool[tables[held_request, :MIGP]]
-        arrivals.append(shifted(pages_sent, "req", offset))
+        arrivals.append(shifted(pages_sent, REQ, offset))
     extended = jnp.concatenate([pool] + arrivals, axis=0)
     page_column = jnp.minimum(jnp.arange(MAXP, dtype=jnp.int32), MIGP - 1)
     moved_pages = pool_pages + slot_of[:, None] * MIGP + page_column[None, :]
@@ -175,28 +178,31 @@
     upper = device // half_devices
     kept = lax.dynamic_slice_in_dim(combined, upper * half_rows, half_rows, 0)
     sent = lax.dynamic_slice_in_dim(combined, (1 - upper) * half_rows, half_rows, 0)
-    swapped = shifted(sent, "req", half_devices)
+    swapped = shifted(sent, REQ, half_devices)
     mine = jnp.where(upper == side, kept, swapped)
-    gathered = lax.all_gather(mine, "req", axis=0, tiled=False)
-    gathered = gathered.reshape(2, half_devices, half_rows, gathered.shape[-1])
+    gathered = lax.all_gather(mine, "x_lo", axis=0, tiled=False)
+    gathered = lax.all_gather(gathered, "y", axis=0, tiled=False)
+    gathered = lax.all_gather(gathered, "z", axis=1, tiled=False)
+    gathered = lax.all_gather(gathered, "core", axis=2, tiled=False)
     logits = jnp.einsum(
-        "xjkd,dv->jxkv", gathered, w_vocab, preferred_element_type=jnp.float32
+        "yzcxkd,dv->yzcxkv", gathered, w_vocab, preferred_element_type=jnp.float32
     )
     return logits.reshape(half_devices * local_rows, logits.shape[-1])
 
 
 def solution(mesh):
+    split = Mesh(mesh.devices.reshape((mesh.devices.shape[0],) + REQ_SPLIT), ("guide",) + REQ)
     in_specs = (
-        P("guide", "req", None),
+        P("guide", REQ, None),
         P(),
         P("guide", None),
         P("guide", None),
         P(),
-        P(None, "req"),
-        P("guide", "req", None, None),
+        P(None, REQ),
+        P("guide", REQ, None, None),
         P("guide", None),
         P("guide", None, None),
         P("guide", None, None),
     )
-    out_specs = P("guide", "req")
-    return jax.shard_map(body, mesh=mesh, in_specs=in_specs, out_specs=out_specs, check_vma=False)
+    out_specs = P("guide", REQ)
+    return jax.shard_map(body, mesh=split, in_specs=in_specs, out_specs=out_specs, check_vma=False)

time: 414 us -> 287 us (0.69)
  waiting for transfers between devices: 248 us -> 113 us
  blocking collectives: 0 us -> 14.8 us
    all_gather x1 -> x2, waiting for transfers between devices: 222 us -> 86.1 us  [the longest x1 59.9 us: body(): gathered = lax.all_gather(gathered, 'z', axis=1, tiled=False)]
    all_gather x0 -> x2, blocking collectives: none -> 14.8 us  [the longest x1 11 us: body(): gathered = lax.all_gather(gathered, 'y', axis=0, tiled=False)]
  transfers between devices with their start and end apart: 11 -> 12, of which waited for: 5 -> 6; matrix products, arithmetic and copies ran while one was open for 19% -> 27% of each run, Pallas kernels for 0% -> 0%
where the time goes in v2:
time: 287 us; the launch traced here: 285 us
  waiting for transfers between devices  113 us (39%)
  local copies, waits for them, and re-layouts  80.2 us (28%)
  between operations  28.6 us (10%)
  matrix products  22.8 us (8%)
  starting transfers between devices  15.8 us (6%)
  blocking collectives  14.8 us (5%)
  other arithmetic  10.6 us (4%)
    all_gather x1, waiting for transfers between devices, body(): gathered = lax.all_gather(gathered, 'z', axis=1, tiled=False)  59.9 us
    unnamed x17, local copies, waits for them, and re-layouts  32.1 us
    all_gather x1, waiting for transfers between devices, body(): gathered = lax.all_gather(gathered, 'core', axis=2, tiled=False)  26.2 us
    slice x1, local copies, waits for them, and re-layouts, masked_scores(): key_rows = page_rows[:, :, :half_width].reshape(count, span, KVH, HD)  16.8 us
    reduce_scatter x1, waiting for transfers between devices, body(): lax.psum_scatter(jnp.einsum('grc,cd->grd', selected, w_out, preferred_ele...  15 us
    ppermute x5, starting transfers between devices, shifted(): return lax.ppermute(value, axis, pairs)  12 us
    gather x4, local copies, waits for them, and re-layouts, body(): pages_sent = pool[tables[held_request, :MIGP]]  11.9 us
    gather x1, local copies, waits for them, and re-layouts, gather_pages(): picked = pool[tables]  11.2 us
  transfers between devices with their start and end apart: 12, of which 6 were waited for; matrix products, arithmetic and copies ran while one was open for 27% of the time, Pallas kernels for 0%

profile of v2, /device:TPU:1, one launch (start us, length us, event | category | flops | bytes accessed | tf_op | source)
XLA Modules:
  0.0 285.4 jit_solution(1852995694674930575)
XLA Ops:
  27.9 2.6 gather_fusion
  30.6 9.8 %collective-permute-start.1 = (bf16[2,64,640]{2,1,0:T(8,128)(2,1)S(1)}, bf16[2,64,640]{2,1,0:T(8,128)(2,1)S(1)}, u32[]{:S(2)}, u32[]{:S(2)}) collective-permute-start(bf16[2,64,640]{2,1,0:T(8,128)(2,1)S(1)} %gather_fusion), channel_id=1, source_target_pairs={{0,126},{1,127},{2,0},{3,1},{4,2},{5,3},{6,4},{7,5},{8,6},{9,7},{1... | collective-permute-start | bytes 491528 | tf_op jit(solution)/shard_map/ppermute | solution.py:36
  40.4 2.7 gather_fusion.1
  44.1 3.3 %gather_fusion.2 = bf16[2,64,640]{2,1,0:T(8,128)(2,1)} fusion(bf16[46,64,640]{2,1,0:T(8,128)(2,1)} %bitcast.140, s32[1024]{0:T(1024)S(1)} %pad_clamp_fusion.2), kind=kCustom, calls=%fused_computation.2 | custom fusion | bytes 327688 | tf_op jit(solution)/shard_map/gather | solution.py:143
  48.2 3.3 %gather_fusion.3 = bf16[2,64,640]{2,1,0:T(8,128)(2,1)} fusion(bf16[46,64,640]{2,1,0:T(8,128)(2,1)} %bitcast.141, s32[1024]{0:T(1024)S(1)} %pad_clamp_fusion.1), kind=kCustom, calls=%fused_computation.3 | custom fusion | bytes 327688 | tf_op jit(solution)/shard_map/gather | solution.py:143
  54.2 2.4 collective-permute-start
  56.6 4.2 %constant_dynamic-update-slice_fusion.4 = bf16[54,64,640]{2,1,0:T(8,128)(2,1)} fusion(bf16[1,46,64,640]{3,2,1,0:T(8,128)(2,1)} %param.16), kind=kLoop, calls=%fused_computation.71 | loop fusion | bytes 7536640
  63.1 3.7 %fusion = f32[2,24,1920]{2,1,0:T(8,128)} fusion(bf16[1024,1920]{1,0:T(8,128)(2,1)} %param.12, s32[]{:T(128)S(6)} %select_n.203, bf16[1,24,2048]{2,1,0:T(8,128)(2,1)} %bitcast.2, bf16[1,24,2048]{2,1,0:T(8,128)(2,1)S(1)} %fusion.25, pred[]{:T(512)S(6)} %eq.85), kind=kOutput, calls=%fused_computation.5 | convolution fusion | flops 189186048 | bytes 4497413 | tf_op jit(solution)/shard_map/grd,df->grf/dot_general | solution.py:111
  71.7 11.2 %gather_fusion.4 = bf16[192,64,640]{2,1,0:T(8,128)(2,1)} fusion(bf16[54,64,640]{2,1,0:T(8,128)(2,1)} %constant_dynamic-update-slice_fusion, s32[1024]{0:T(1024)S(1)} %pad_clamp_fusion), kind=kCustom, calls=%fused_computation.4 | custom fusion | bytes 31458048 | tf_op jit(solution)/shard_map/gather | solution.py:75
  82.9 16.8 %fusion.65 = (bf16[24,512,320]{2,1,0:T(8,128)(2,1)}, bf16[24,512,320]{2,1,0:T(8,128)(2,1)}) fusion(bf16[24,512,640]{2,1,0:T(8,128)(2,1)} %bitcast.135), kind=kLoop, calls=%fused_computation.130 | loop fusion | bytes 31457280 | tf_op jit(solution)/shard_map/slice | solution.py:47
  99.7 11.6 %copy.28 = bf16[24,512,320]{1,2,0:T(8,128)(2,1)} copy(bf16[24,512,320]{2,1,0:T(8,128)(2,1)} %get-tuple-element.17) | data formatting | bytes 15728640
  111.3 11.5 %copy.29 = bf16[24,512,320]{1,2,0:T(8,128)(2,1)} copy(bf16[24,512,320]{2,1,0:T(8,128)(2,1)} %get-tuple-element.18) | data formatting | bytes 15728640
  124.3 4.5 %fusion.66 = (f32[24,5,4]{2,1,0:T(8,128)S(1)}, f32[24,5,4,512]{3,2,1,0:T(4,128)S(1)}) fusion(bf16[24,5,4,64]{3,2,1,0:T(4,128)(2,1)S(1)} %reshape.352, bf16[24,512,5,64]{1,3,2,0:T(8,128)(2,1)} %bitcast.136, pred[24,512]{1,0:T(8,128)(4,1)S(1)} %iota_compare_fusion), kind=kOutput, calls=%fused_computation.131 | convolution fusion | flops 32194080 | bytes 8923008 | tf_op jit(solution)/shard_map/rkgd,rskd->rkgs/dot_general | solution.py:49
  130.5 5.8 %fusion.9 = bf16[24,5,4,64]{3,2,1,0:T(4,128)(2,1)S(1)} fusion(bf16[24,512,5,64]{1,3,2,0:T(8,128)(2,1)} %bitcast.137, f32[24,5,4,512]{3,2,1,0:T(4,128)} %copy-done.1, f32[24,5,4]{2,1,0:T(8,128)S(1)} %fusion.32, f32[24,5,4]{2,1,0:T(8,128)S(1)} %get-tuple-element.20, f32[24,5,64]{2,1,0:T(8,128)S(1)} %reshape.359, f32[24,5,4]{2,1,0:T(8,128)S(1)} %get-tuple-element.19), kind=kOutput, calls=%fused_computation.14 | convolution fusion | flops 32071680 | bytes 8945280 | tf_op jit(solution)/shard_map/rkgs,rskd->rkgd/dot_general | solution.py:63
  137.3 3.8 %collective-permute-done.5 = bf16[24,1280]{1,0:T(8,128)(2,1)S(1)} collective-permute-done((bf16[24,1280]{1,0:T(8,128)(2,1)S(1)}, bf16[24,1280]{1,0:T(8,128)(2,1)S(1)}, u32[]{:S(2)}, u32[]{:S(2)}) %collective-permute-start.5) | collective-permute-done | bytes 61472 | tf_op jit(solution)/shard_map/ppermute | solution.py:30
  142.4 15.0 %reduce-scatter.5.cloned.1.call-done = bf16[1,24,2048]{2,1,0:T(8,128)(2,1)} async-done(((bf16[2,24,2048]{2,1,0:T(8,128)(2,1)}), bf16[1,24,2048]{2,1,0:T(8,128)(2,1)}) %reduce-scatter.5.cloned.1.call-update) | async-done | bytes 98320 | tf_op jit(solution)/shard_map/reduce_scatter | solution.py:162
  159.6 4.9 %collective-permute-done.6 = bf16[24,2048]{1,0:T(8,128)(2,1)S(1)} collective-permute-done((bf16[24,2048]{1,0:T(8,128)(2,1)S(1)}, bf16[24,2048]{1,0:T(8,128)(2,1)S(1)}, u32[]{:S(2)}, u32[]{:S(2)}) %collective-permute-start.6) | collective-permute-done | bytes 98336 | tf_op jit(solution)/shard_map/ppermute | solution.py:30
  165.0 2.8 collective-permute-done.7
  167.8 3.8 %all-gather.4 = bf16[2,12,2048]{2,1,0:T(8,128)(2,1)S(1)} all-gather(bf16[1,12,2048]{2,1,0:T(8,128)(2,1)S(1)} %select_bitcast_fusion), channel_id=2, replica_groups=mesh['guide'=2,'x_lo'=2,'y'=4,'z'=8,'core'=2] {'x_lo'}, dimensions={0}, use_global_device_ids=true | all-gather | bytes 147456 | tf_op jit(solution)/shard_map/all_gather | solution.py:183
  171.6 11.0 %all-gather.1 = bf16[8,12,2048]{2,1,0:T(8,128)(2,1)} all-gather(bf16[2,12,2048]{2,1,0:T(8,128)(2,1)S(1)} %all-gather.4), channel_id=3, replica_groups=mesh['guide'=2,'x_lo'=2,'y'=4,'z'=8,'core'=2] {'y'}, dimensions={0}, use_global_device_ids=true | all-gather | bytes 491520 | tf_op jit(solution)/shard_map/all_gather | solution.py:184
  182.9 59.9 %all-gather.8.cloned.1.call-done = bf16[4,16,12,2048]{3,2,1,0:T(8,128)(2,1)} async-done(((bf16[4,2,12,2048]{3,2,1,0:T(8,128)(2,1)}), bf16[4,16,12,2048]{3,2,1,0:T(8,128)(2,1)}) %all-gather.8.cloned.1.call-update) | async-done | bytes 3145744 | tf_op jit(solution)/shard_map/all_gather | solution.py:185
  242.8 26.2 %all-gather.10.cloned.1.call-done = bf16[4,8,4,12,2048]{4,3,2,1,0:T(8,128)(2,1)} async-done(((bf16[4,8,2,12,2048]{4,3,2,1,0:T(8,128)(2,1)}), bf16[4,8,4,12,2048]{4,3,2,1,0:T(8,128)(2,1)}) %all-gather.10.cloned.1.call-update) | async-done | bytes 6291472 | tf_op jit(solution)/shard_map/all_gather | solution.py:186
  269.0 7.4 %fusion.10 = f32[4,8,2,2,12,250]{5,4,3,2,1,0:T(8,128)} fusion(bf16[4,8,2,2,12,2048]{5,4,3,2,1,0:T(8,128)(2,1)} %bitcast.150, bf16[2048,250]{1,0:T(8,128)(2,1)} %param.15), kind=kOutput, calls=%fused_computation.15 | convolution fusion | flops 1572864000 | bytes 8851456 | tf_op jit(solution)/shard_map/yzcxkd,dv->yzcxkv/dot_general | solution.py:187
  276.4 2.5 reshape.357
  (82 shorter events, 26.1 us)
Async XLA Ops:
  6.5 134.6 %copy-start = (bf16[640,2048]{1,0:T(8,128)(2,1)S(1)}, bf16[640,2048]{1,0:T(8,128)(2,1)}, u32[]{:S(2)}) copy-start(bf16[640,2048]{1,0:T(8,128)(2,1)} %param.13) | copy-start | bytes 7864324
  6.5 116.3 %reduce-scatter.7.cloned.1.call-start = ((), (), s32[]{:S(2)}) async-start(), calls=%async_computation.5 | async-start | bytes 552960
  30.6 36.5 %collective-permute-start.1 = (bf16[2,64,640]{2,1,0:T(8,128)(2,1)S(1)}, bf16[2,64,640]{2,1,0:T(8,128)(2,1)S(1)}, u32[]{:S(2)}, u32[]{:S(2)}) collective-permute-start(bf16[2,64,640]{2,1,0:T(8,128)(2,1)S(1)} %gather_fusion), channel_id=1, source_target_pairs={{0,126},{1,127},{2,0},{3,1},{4,2},{5,3},{6,4},{7,5},{8,6},{9,7},{1... | collective-permute-start | bytes 491528 | tf_op jit(solution)/shard_map/ppermute | solution.py:36
  40.4 20.5 %copy-start.2 = (bf16[1,24,2048]{2,1,0:T(8,128)(2,1)S(1)}, bf16[1,24,2048]{2,1,0:T(8,128)(2,1)}, u32[]{:S(2)}) copy-start(bf16[1,24,2048]{2,1,0:T(8,128)(2,1)} %param.10) | copy-start | bytes 294916
  40.4 20.5 %copy-start.3 = (f32[2048]{0:T(1024)S(1)}, f32[2048]{0:T(1024)}, u32[]{:S(2)}) copy-start(f32[2048]{0:T(1024)} %param.11) | copy-start | bytes 24580
  43.1 24.7 %collective-permute-start.2 = (bf16[2,64,640]{2,1,0:T(8,128)(2,1)S(1)}, bf16[2,64,640]{2,1,0:T(8,128)(2,1)S(1)}, u32[]{:S(2)}, u32[]{:S(2)}) collective-permute-start(bf16[2,64,640]{2,1,0:T(8,128)(2,1)S(1)} %gather_fusion.1), channel_id=1, source_target_pairs={{0,127},{1,0},{2,1},{3,2},{4,3},{5,4},{6,5},{7,6},{8,7},{9,8},{10,... | collective-permute-start | bytes 491528 | tf_op jit(solution)/shard_map/ppermute | solution.py:36
  47.4 21.1 %collective-permute-start.3 = (bf16[2,64,640]{2,1,0:T(8,128)(2,1)}, bf16[2,64,640]{2,1,0:T(8,128)(2,1)}, u32[]{:S(2)}, u32[]{:S(2)}) collective-permute-start(bf16[2,64,640]{2,1,0:T(8,128)(2,1)} %gather_fusion.2), channel_id=1, source_target_pairs={{0,1},{1,2},{2,3},{3,4},{4,5},{5,6},{6,7},{7,8},{8,9},{9,10},{10,1... | collective-permute-start | bytes 491528 | tf_op jit(solution)/shard_map/ppermute | solution.py:36
  51.5 18.6 %collective-permute-start.4 = (bf16[2,64,640]{2,1,0:T(8,128)(2,1)}, bf16[2,64,640]{2,1,0:T(8,128)(2,1)}, u32[]{:S(2)}, u32[]{:S(2)}) collective-permute-start(bf16[2,64,640]{2,1,0:T(8,128)(2,1)} %gather_fusion.3), channel_id=1, source_target_pairs={{0,2},{1,3},{2,4},{3,5},{4,6},{5,7},{6,8},{7,9},{8,10},{9,11},{10,... | collective-permute-start | bytes 491528 | tf_op jit(solution)/shard_map/ppermute | solution.py:36
  54.2 9.0 %collective-permute-start = (bf16[24,2048]{1,0:T(8,128)(2,1)}, bf16[24,2048]{1,0:T(8,128)(2,1)}, u32[]{:S(2)}, u32[]{:S(2)}) collective-permute-start(bf16[24,2048]{1,0:T(8,128)(2,1)} %fusion.23), channel_id=1, source_target_pairs={{0,128},{128,0},{1,129},{129,1},{2,130},{130,2},{3,131},{131,3},{4... | collective-permute-start | bytes 294920 | tf_op jit(solution)/shard_map/ppermute | solution.py:30
  66.9 90.6 %reduce-scatter.5.cloned.1.call-start = ((), (), s32[]{:S(2)}) async-start(), calls=%async_computation.2 | async-start | bytes 294912 | tf_op jit(solution)/shard_map/reduce_scatter | solution.py:162
  128.8 0.9 copy-start.1
  136.3 22.2 %copy-start.4 = (f32[2048]{0:T(1024)S(1)}, f32[2048]{0:T(1024)}, u32[]{:S(2)}) copy-start(f32[2048]{0:T(1024)} %param.14) | copy-start | bytes 24580
  136.4 4.7 %collective-permute-start.5 = (bf16[24,1280]{1,0:T(8,128)(2,1)S(1)}, bf16[24,1280]{1,0:T(8,128)(2,1)S(1)}, u32[]{:S(2)}, u32[]{:S(2)}) collective-permute-start(bf16[24,1280]{1,0:T(8,128)(2,1)S(1)} %convert_element_type.86), channel_id=1, source_target_pairs={{0,128},{128,0},{1,129},{129,1},{2,130},{130,2},{3,131},{131,3},{4... | collective-permute-start | bytes 184328 | tf_op jit(solution)/shard_map/ppermute | solution.py:30
  142.3 100.5 %all-gather.8.cloned.1.call-start = ((), (), s32[]{:S(2)}) async-start(), calls=%async_computation.3 | async-start | bytes 4718592 | tf_op jit(solution)/shard_map/all_gather | solution.py:185
  159.5 5.1 %collective-permute-start.6 = (bf16[24,2048]{1,0:T(8,128)(2,1)S(1)}, bf16[24,2048]{1,0:T(8,128)(2,1)S(1)}, u32[]{:S(2)}, u32[]{:S(2)}) collective-permute-start(bf16[24,2048]{1,0:T(8,128)(2,1)S(1)} %multiply_convert_fusion), channel_id=1, source_target_pairs={{0,128},{128,0},{1,129},{129,1},{2,130},{130,2},{3,131},{131,3},{4... | collective-permute-start | bytes 294920 | tf_op jit(solution)/shard_map/ppermute | solution.py:30
  164.6 3.2 %collective-permute-start.7 = (bf16[12,2048]{1,0:T(8,128)(2,1)S(1)}, bf16[12,2048]{1,0:T(8,128)(2,1)S(1)}, u32[]{:S(2)}, u32[]{:S(2)}) collective-permute-start(bf16[12,2048]{1,0:T(8,128)(2,1)S(1)} %constant_dynamic-slice_fusion), channel_id=1, source_target_pairs={{0,64},{1,65},{2,66},{3,67},{4,68},{5,69},{6,70},{7,71},{8,72},{9,... | collective-permute-start | bytes 147464 | tf_op jit(solution)/shard_map/ppermute | solution.py:36
  182.6 86.4 %all-gather.10.cloned.1.call-start = ((), (), s32[]{:S(2)}) async-start(), calls=%async_computation.4 | async-start | bytes 12582912 | tf_op jit(solution)/shard_map/all_gather | solution.py:186
Sparse Core Ops, SparseCore 0:
  67.0 15.9 reduce-scatter.6
  142.5 14.8 reduce-scatter.4
  182.7 60.0 all-gather.7
  244.5 24.5 all-gather.9

commit v3 on v2

--- a/solution.py
+++ b/solution.py
@@ -74,6 +74,19 @@
 def gather_pages(pool, tables):
     picked = pool[tables]
     return picked.reshape(tables.shape[0], tables.shape[1] * pool.shape[1], pool.shape[2])
+
+
+def dense_scores(queries, page_rows, counts):
+    count = page_rows.shape[0] * page_rows.shape[1]
+    half_width = page_rows.shape[2] // 2
+    flat = page_rows.reshape(count, page_rows.shape[2])
+    key_rows = flat[:, :half_width].reshape(count, KVH, HD)
+    value_rows = flat[:, half_width:].reshape(count, KVH, HD)
+    scores = jnp.einsum(
+        "rkgd,tkd->rkgt", queries, key_rows, preferred_element_type=jnp.float32
+    ) * (1.0 / math.sqrt(HD))
+    scores = jnp.where(counts[:, None, None, :] > 0, scores, -jnp.inf)
+    return (scores, value_rows)
 
 
 def body(
@@ -142,13 +155,45 @@
         held_request = listing[jnp.argmax(holding), 0]
         pages_sent = pool[tables[held_request, :MIGP]]
         arrivals.append(shifted(pages_sent, REQ, offset))
-    extended = jnp.concatenate([pool] + arrivals, axis=0)
+    arrived = jnp.concatenate(arrivals, axis=0)
     page_column = jnp.minimum(jnp.arange(MAXP, dtype=jnp.int32), MIGP - 1)
     moved_pages = pool_pages + slot_of[:, None] * MIGP + page_column[None, :]
     used_table = jnp.where(is_moved[:, None], moved_pages, own_table)
-    tops, sums, accs = attend_all(
-        queries, gather_pages(extended, used_table), own_lengths, own_score, new_values
-    )
+    page_rows = pool.shape[1]
+    living = (
+        jnp.arange(MAXP, dtype=jnp.int32)[:, None] * page_rows
+        + jnp.arange(page_rows, dtype=jnp.int32)[None, :]
+    )[None] < own_lengths[:, None, None]
+    living = living.astype(jnp.float32)
+    all_pages = jnp.arange(pool_pages + arrived.shape[0], dtype=jnp.int32)
+    hits = (used_table[:, :, None] == all_pages[None, None, :]).astype(jnp.float32)
+    counts = jnp.einsum("rsp,rsw->rpw", hits, living).reshape(local_rows, -1)
+    pool_counts = counts[:, : pool_pages * page_rows]
+    arrived_counts = counts[:, pool_pages * page_rows :]
+    pool_scores, pool_values = dense_scores(queries, pool, pool_counts)
+    arrived_scores, arrived_values = dense_scores(queries, arrived, arrived_counts)
+    tops = jnp.maximum(
+        jnp.maximum(jnp.max(pool_scores, axis=-1), jnp.max(arrived_scores, axis=-1)), own_score
+    )
+    own_weight = jnp.exp(own_score - tops)
+    sums = own_weight
+    accs = own_weight.astype(jnp.bfloat16).astype(jnp.float32)[..., None] * new_values.astype(
+        jnp.float32
+    )[:, :, None, :]
+    for scores, values, count in (
+        (pool_scores, pool_values, pool_counts),
+        (arrived_scores, arrived_values, arrived_counts),
+    ):
+        weights = jnp.exp(scores - tops[..., None])
+        sums = sums + jnp.sum(weights * count[:, None, None, :], axis=-1)
+        rounded = weights.astype(jnp.bfloat16).astype(jnp.float32) * count[:, None, None, :]
+        accs = accs + jnp.einsum(
+            "rkgt,tkd->rkgd",
+            rounded,
+            values.astype(jnp.float32),
+            precision=lax.Precision.HIGHEST,
+            preferred_element_type=jnp.float32,
+        )
     attended = (accs / sums[..., None]).reshape(local_rows, query_width).astype(jnp.bfloat16)
     partner_attended = from_partner(attended, "guide", 0)
     both_attended = jnp.where(

time: 287 us -> 254 us (0.89)
  local copies, waits for them, and re-layouts: 80.2 us -> 38.3 us
  waiting for transfers between devices: 113 us -> 122 us
    unnamed x17 -> x19, local copies, waits for them, and re-layouts: 32.1 us -> 9.94 us
    gather x1 -> x0, local copies, waits for them, and re-layouts: 11.2 us -> none  [gather_pages(): picked = pool[tables]]
    slice x1 -> x4, local copies, waits for them, and re-layouts: 16.8 us -> 6.62 us  [the longest x1 5.69 us: dense_scores(): key_rows = flat[:, :half_width].reshape(count, KVH, HD)]
    unnamed x5, waiting for transfers between devices: 0.07 us -> 5.66 us
    reduce_scatter x1, waiting for transfers between devices: 15 us -> 18.2 us  [body(): lax.psum_scatter(jnp.einsum('grc,cd->grd', selected, w_out, preferred_ele...]
    dot_general x2 -> x5, matrix products: 10.3 us -> 9.01 us  [the longest x2 4.7 us: body(): jnp.einsum('rkgt,tkd->rkgd', rounded, values.astype(jnp.float32), precisi...]
  transfers between devices with their start and end apart: 12 -> 12, of which waited for: 6 -> 7; matrix products, arithmetic and copies ran while one was open for 27% -> 18% of each run, Pallas kernels for 0% -> 0%
where the time goes in v3:
time: 254 us; the launch traced here: 253 us
  waiting for transfers between devices  122 us (48%)
  local copies, waits for them, and re-layouts  38.3 us (15%)
  between operations  28.7 us (11%)
  matrix products  21.5 us (8%)
  blocking collectives  15 us (6%)
  starting transfers between devices  13.9 us (5%)
  other arithmetic  13.4 us (5%)
    all_gather x1, waiting for transfers between devices, body(): gathered = lax.all_gather(gathered, 'z', axis=1, tiled=False)  60.2 us
    all_gather x1, waiting for transfers between devices, body(): gathered = lax.all_gather(gathered, 'core', axis=2, tiled=False)  26.2 us
    reduce_scatter x1, waiting for transfers between devices, body(): lax.psum_scatter(jnp.einsum('grc,cd->grd', selected, w_out, preferred_ele...  18.2 us
    gather x4, local copies, waits for them, and re-layouts, body(): pages_sent = pool[tables[held_request, :MIGP]]  13.2 us
    all_gather x1, blocking collectives, body(): gathered = lax.all_gather(gathered, 'y', axis=0, tiled=False)  10.9 us
    unnamed x19, local copies, waits for them, and re-layouts  9.94 us
    ppermute x5, starting transfers between devices, shifted(): return lax.ppermute(value, axis, pairs)  9.71 us
    ppermute x3, waiting for transfers between devices, from_partner(): return lax.ppermute(block, axis, route)  9.36 us
  transfers between devices with their start and end apart: 12, of which 7 were waited for; matrix products, arithmetic and copies ran while one was open for 18% of the time, Pallas kernels for 0%

profile of v3, /device:TPU:1, one launch (start us, length us, event | category | flops | bytes accessed | tf_op | source)
XLA Modules:
  0.0 253.2 jit_solution(9363147862986664306)
XLA Ops:
  8.7 3.7 %collective-permute-start = (bf16[24,2048]{1,0:T(8,128)(2,1)S(1)}, bf16[24,2048]{1,0:T(8,128)(2,1)}, u32[]{:S(2)}, u32[]{:S(2)}) collective-permute-start(bf16[24,2048]{1,0:T(8,128)(2,1)S(1)} %fusion.44), channel_id=1, source_target_pairs={{0,128},{128,0},{1,129},{129,1},{2,130},{130,2},{3,131},{131,3},{4... | collective-permute-start | bytes 294920 | tf_op jit(solution)/shard_map/ppermute | solution.py:30
  33.5 3.3 %gather_fusion.2 = bf16[2,64,640]{2,1,0:T(8,128)(2,1)} fusion(bf16[46,64,640]{2,1,0:T(8,128)(2,1)} %bitcast.178, s32[1024]{0:T(1024)S(1)} %pad_clamp_fusion.1), kind=kCustom, calls=%fused_computation.2 | custom fusion | bytes 327688 | tf_op jit(solution)/shard_map/gather | solution.py:156
  36.9 2.4 collective-permute-start.3
  39.3 3.3 %gather_fusion = bf16[2,64,640]{2,1,0:T(8,128)(2,1)} fusion(bf16[46,64,640]{2,1,0:T(8,128)(2,1)} %bitcast.179, s32[1024]{0:T(1024)S(1)} %pad_clamp_fusion.3), kind=kCustom, calls=%fused_computation | custom fusion | bytes 327688 | tf_op jit(solution)/shard_map/gather | solution.py:156
  42.6 5.6 %collective-permute-start.1 = (bf16[2,64,640]{2,1,0:T(8,128)(2,1)}, bf16[2,64,640]{2,1,0:T(8,128)(2,1)S(1)}, u32[]{:S(2)}, u32[]{:S(2)}) collective-permute-start(bf16[2,64,640]{2,1,0:T(8,128)(2,1)} %gather_fusion), channel_id=1, source_target_pairs={{0,126},{1,127},{2,0},{3,1},{4,2},{5,3},{6,4},{7,5},{8,6},{9,7},{1... | collective-permute-start | bytes 491528 | tf_op jit(solution)/shard_map/ppermute | solution.py:36
  48.2 3.3 %gather_fusion.3 = bf16[2,64,640]{2,1,0:T(8,128)(2,1)} fusion(bf16[46,64,640]{2,1,0:T(8,128)(2,1)} %bitcast.180, s32[1024]{0:T(1024)S(1)} %pad_clamp_fusion), kind=kCustom, calls=%fused_computation.3 | custom fusion | bytes 327688 | tf_op jit(solution)/shard_map/gather | solution.py:156
  51.5 3.3 %gather_fusion.1 = bf16[2,64,640]{2,1,0:T(8,128)(2,1)} fusion(bf16[46,64,640]{2,1,0:T(8,128)(2,1)} %bitcast.181, s32[1024]{0:T(1024)S(1)} %pad_clamp_fusion.2), kind=kCustom, calls=%fused_computation.1 | custom fusion | bytes 327688 | tf_op jit(solution)/shard_map/gather | solution.py:156
  59.2 5.7 %fusion.92 = (bf16[2944,320]{1,0:T(8,128)(2,1)}, bf16[2944,320]{1,0:T(8,128)(2,1)}) fusion(bf16[2944,640]{1,0:T(8,128)(2,1)} %bitcast.182), kind=kLoop, calls=%fused_computation.157 | loop fusion | bytes 7536640 | tf_op jit(solution)/shard_map/slice | solution.py:83
  67.5 3.7 %fusion.5 = f32[2,24,1920]{2,1,0:T(8,128)} fusion(bf16[1024,1920]{1,0:T(8,128)(2,1)} %param.12, s32[]{:T(128)S(6)} %select_n.196, bf16[1,24,2048]{2,1,0:T(8,128)(2,1)} %bitcast.1, bf16[1,24,2048]{2,1,0:T(8,128)(2,1)S(1)} %fusion.46, pred[]{:T(512)S(6)} %eq.98), kind=kOutput, calls=%fused_computation.13 | convolution fusion | flops 189186048 | bytes 4497413 | tf_op jit(solution)/shard_map/grd,df->grf/dot_general | solution.py:124
  72.2 4.1 %copy.65 = bf16[2944,320]{0,1:T(8,128)(2,1)} copy(bf16[2944,320]{1,0:T(8,128)(2,1)} %get-tuple-element.19) | data formatting | bytes 3768320
  76.3 4.1 %copy.67 = bf16[2944,320]{0,1:T(8,128)(2,1)} copy(bf16[2944,320]{1,0:T(8,128)(2,1)} %get-tuple-element.20) | data formatting | bytes 3768320
  82.8 5.6 %reduce-scatter.7.cloned.1.call-done = f32[1,24,1920]{2,1,0:T(8,128)} async-done(((f32[2,24,1920]{2,1,0:T(8,128)}), f32[1,24,1920]{2,1,0:T(8,128)}) %reduce-scatter.7.cloned.1.call-update) | async-done | bytes 184336
  91.1 2.6 %bitcast_reduce_fusion = (f32[24,5,4]{0,2,1:T(4,128)S(1)}, f32[5,24,4,2944]{3,1,2,0:T(8,128)S(1)}) fusion(pred[24,2944]{1,0:T(8,128)(4,1)S(1)} %broadcast_compare_fusion, bf16[2944,5,64,1]{0,2,3,1:T(8,128)(2,1)} %bitcast.177, bf16[24,5,4,64]{3,2,1,0:T(4,128)(2,1)S(1)} %reshape.335), kind=kOutput, calls=%fused_computation.5 | convolution fusion | flops 185118240 | bytes 7670656 | tf_op jit(solution)/shard_map/rkgd,tkd->rkgt/dot_general | solution.py:85
  95.8 4.0 %fusion.25 = f32[24,5,4,64]{3,0,2,1:T(8,128)S(1)} fusion(bf16[2944,5,64,1]{0,2,3,1:T(8,128)(2,1)S(1)} %bitcast.186, f32[5,24,4,2944]{3,1,2,0:T(8,128)S(1)} %get-tuple-element.32, f32[24,2944]{1,0:T(8,128)S(1)} %copy-done.3, f32[24,5,4]{0,2,1:T(4,128)S(1)} %get-tuple-element.18, pred[24,2944]{1,0:T(8,128)(4,1)S(1)} %broadcast_compare_fusion, ...), kind=kOutput, calls=%fused_computation.30 | convolution fusion | flops 1093816320 | bytes 8047360 | tf_op jit(solution)/shard_map/rkgt,tkd->rkgd/dot_general | solution.py:190
  101.0 4.4 %collective-permute-done.5 = bf16[24,1280]{1,0:T(8,128)(2,1)S(1)} collective-permute-done((bf16[24,1280]{1,0:T(8,128)(2,1)S(1)}, bf16[24,1280]{1,0:T(8,128)(2,1)S(1)}, u32[]{:S(2)}, u32[]{:S(2)}) %collective-permute-start.5) | collective-permute-done | bytes 61472 | tf_op jit(solution)/shard_map/ppermute | solution.py:30
  106.7 18.2 %reduce-scatter.5.cloned.1.call-done = bf16[1,24,2048]{2,1,0:T(8,128)(2,1)} async-done(((bf16[2,24,2048]{2,1,0:T(8,128)(2,1)}), bf16[1,24,2048]{2,1,0:T(8,128)(2,1)}) %reduce-scatter.5.cloned.1.call-update) | async-done | bytes 98320 | tf_op jit(solution)/shard_map/reduce_scatter | solution.py:207
  127.1 4.9 %collective-permute-done.6 = bf16[24,2048]{1,0:T(8,128)(2,1)S(1)} collective-permute-done((bf16[24,2048]{1,0:T(8,128)(2,1)S(1)}, bf16[24,2048]{1,0:T(8,128)(2,1)S(1)}, u32[]{:S(2)}, u32[]{:S(2)}) %collective-permute-start.6) | collective-permute-done | bytes 98336 | tf_op jit(solution)/shard_map/ppermute | solution.py:30
  132.5 2.8 %collective-permute-done.7 = bf16[12,2048]{1,0:T(8,128)(2,1)S(1)} collective-permute-done((bf16[12,2048]{1,0:T(8,128)(2,1)S(1)}, bf16[12,2048]{1,0:T(8,128)(2,1)S(1)}, u32[]{:S(2)}, u32[]{:S(2)}) %collective-permute-start.7) | collective-permute-done | bytes 49184 | tf_op jit(solution)/shard_map/ppermute | solution.py:36
  135.4 4.0 %all-gather.4 = bf16[2,12,2048]{2,1,0:T(8,128)(2,1)S(1)} all-gather(bf16[1,12,2048]{2,1,0:T(8,128)(2,1)S(1)} %select_bitcast_fusion), channel_id=2, replica_groups=mesh['guide'=2,'x_lo'=2,'y'=4,'z'=8,'core'=2] {'x_lo'}, dimensions={0}, use_global_device_ids=true | all-gather | bytes 147456 | tf_op jit(solution)/shard_map/all_gather | solution.py:228
  139.4 10.9 %all-gather.1 = bf16[8,12,2048]{2,1,0:T(8,128)(2,1)} all-gather(bf16[2,12,2048]{2,1,0:T(8,128)(2,1)S(1)} %all-gather.4), channel_id=3, replica_groups=mesh['guide'=2,'x_lo'=2,'y'=4,'z'=8,'core'=2] {'y'}, dimensions={0}, use_global_device_ids=true | all-gather | bytes 491520 | tf_op jit(solution)/shard_map/all_gather | solution.py:229
  150.4 60.2 %all-gather.8.cloned.1.call-done = bf16[4,16,12,2048]{3,2,1,0:T(8,128)(2,1)} async-done(((bf16[4,2,12,2048]{3,2,1,0:T(8,128)(2,1)}), bf16[4,16,12,2048]{3,2,1,0:T(8,128)(2,1)}) %all-gather.8.cloned.1.call-update) | async-done | bytes 3145744 | tf_op jit(solution)/shard_map/all_gather | solution.py:230
  210.6 26.2 %all-gather.10.cloned.1.call-done = bf16[4,8,4,12,2048]{4,3,2,1,0:T(8,128)(2,1)} async-done(((bf16[4,8,2,12,2048]{4,3,2,1,0:T(8,128)(2,1)}), bf16[4,8,4,12,2048]{4,3,2,1,0:T(8,128)(2,1)}) %all-gather.10.cloned.1.call-update) | async-done | bytes 6291472 | tf_op jit(solution)/shard_map/all_gather | solution.py:231
  236.8 7.4 %fusion.29 = f32[4,8,2,2,12,250]{5,4,3,2,1,0:T(8,128)} fusion(bf16[4,8,2,2,12,2048]{5,4,3,2,1,0:T(8,128)(2,1)} %bitcast.195, bf16[2048,250]{1,0:T(8,128)(2,1)} %param.15), kind=kOutput, calls=%fused_computation.32 | convolution fusion | flops 1572864000 | bytes 8851456 | tf_op jit(solution)/shard_map/yzcxkd,dv->yzcxkv/dot_general | solution.py:232
  244.1 2.5 reshape.343
  (95 shorter events, 28.3 us)
Async XLA Ops:
  6.5 98.9 %copy-start = (bf16[640,2048]{1,0:T(8,128)(2,1)S(1)}, bf16[640,2048]{1,0:T(8,128)(2,1)}, u32[]{:S(2)}) copy-start(bf16[640,2048]{1,0:T(8,128)(2,1)} %param.13) | copy-start | bytes 7864324
  6.5 81.9 %reduce-scatter.7.cloned.1.call-start = ((), (), s32[]{:S(2)}) async-start(), calls=%async_computation.5 | async-start | bytes 552960
  8.7 58.8 %collective-permute-start = (bf16[24,2048]{1,0:T(8,128)(2,1)S(1)}, bf16[24,2048]{1,0:T(8,128)(2,1)}, u32[]{:S(2)}, u32[]{:S(2)}) collective-permute-start(bf16[24,2048]{1,0:T(8,128)(2,1)S(1)} %fusion.44), channel_id=1, source_target_pairs={{0,128},{128,0},{1,129},{129,1},{2,130},{130,2},{3,131},{131,3},{4... | collective-permute-start | bytes 294920 | tf_op jit(solution)/shard_map/ppermute | solution.py:30
  36.9 43.5 %collective-permute-start.3 = (bf16[2,64,640]{2,1,0:T(8,128)(2,1)}, bf16[2,64,640]{2,1,0:T(8,128)(2,1)S(1)}, u32[]{:S(2)}, u32[]{:S(2)}) collective-permute-start(bf16[2,64,640]{2,1,0:T(8,128)(2,1)} %gather_fusion.2), channel_id=1, source_target_pairs={{0,1},{1,2},{2,3},{3,4},{4,5},{5,6},{6,7},{7,8},{8,9},{9,10},{10,1... | collective-permute-start | bytes 491528 | tf_op jit(solution)/shard_map/ppermute | solution.py:36
  42.6 37.8 %collective-permute-start.1 = (bf16[2,64,640]{2,1,0:T(8,128)(2,1)}, bf16[2,64,640]{2,1,0:T(8,128)(2,1)S(1)}, u32[]{:S(2)}, u32[]{:S(2)}) collective-permute-start(bf16[2,64,640]{2,1,0:T(8,128)(2,1)} %gather_fusion), channel_id=1, source_target_pairs={{0,126},{1,127},{2,0},{3,1},{4,2},{5,3},{6,4},{7,5},{8,6},{9,7},{1... | collective-permute-start | bytes 491528 | tf_op jit(solution)/shard_map/ppermute | solution.py:36
  51.5 28.9 %collective-permute-start.4 = (bf16[2,64,640]{2,1,0:T(8,128)(2,1)}, bf16[2,64,640]{2,1,0:T(8,128)(2,1)}, u32[]{:S(2)}, u32[]{:S(2)}) collective-permute-start(bf16[2,64,640]{2,1,0:T(8,128)(2,1)} %gather_fusion.3), channel_id=1, source_target_pairs={{0,2},{1,3},{2,4},{3,5},{4,6},{5,7},{6,8},{7,9},{8,10},{9,11},{10,... | collective-permute-start | bytes 491528 | tf_op jit(solution)/shard_map/ppermute | solution.py:36
  54.8 25.6 %collective-permute-start.2 = (bf16[2,64,640]{2,1,0:T(8,128)(2,1)}, bf16[2,64,640]{2,1,0:T(8,128)(2,1)}, u32[]{:S(2)}, u32[]{:S(2)}) collective-permute-start(bf16[2,64,640]{2,1,0:T(8,128)(2,1)} %gather_fusion.1), channel_id=1, source_target_pairs={{0,127},{1,0},{2,1},{3,2},{4,3},{5,4},{6,5},{7,6},{8,7},{9,8},{10,... | collective-permute-start | bytes 491528 | tf_op jit(solution)/shard_map/ppermute | solution.py:36
  71.2 53.7 %reduce-scatter.5.cloned.1.call-start = ((), (), s32[]{:S(2)}) async-start(), calls=%async_computation.2 | async-start | bytes 294912 | tf_op jit(solution)/shard_map/reduce_scatter | solution.py:207
  91.1 2.7 %copy-start.3 = (f32[24,2944]{1,0:T(8,128)S(1)}, f32[24,2944]{1,0:T(8,128)}, u32[]{:S(2)}) copy-start(f32[24,2944]{1,0:T(8,128)} %slice.65) | copy-start | bytes 847876
  93.7 2.0 copy-start.2
  93.7 2.0 copy-start.5
  95.8 4.0 %copy-start.4 = (bf16[512,320]{0,1:T(8,128)(2,1)S(1)}, bf16[512,320]{0,1:T(8,128)(2,1)}, u32[]{:S(2)}) copy-start(bf16[512,320]{0,1:T(8,128)(2,1)} %copy.68) | copy-start | bytes 983044
  99.8 25.2 %copy-start.1 = (bf16[1,24,2048]{2,1,0:T(8,128)(2,1)S(1)}, bf16[1,24,2048]{2,1,0:T(8,128)(2,1)}, u32[]{:S(2)}) copy-start(bf16[1,24,2048]{2,1,0:T(8,128)(2,1)} %param.10) | copy-start | bytes 294916
  99.8 26.2 %copy-start.6 = (f32[2048]{0:T(1024)S(1)}, f32[2048]{0:T(1024)}, u32[]{:S(2)}) copy-start(f32[2048]{0:T(1024)} %param.14) | copy-start | bytes 24580
  100.7 4.7 %collective-permute-start.5 = (bf16[24,1280]{1,0:T(8,128)(2,1)S(1)}, bf16[24,1280]{1,0:T(8,128)(2,1)S(1)}, u32[]{:S(2)}, u32[]{:S(2)}) collective-permute-start(bf16[24,1280]{1,0:T(8,128)(2,1)S(1)} %convert_element_type.102), channel_id=1, source_target_pairs={{0,128},{128,0},{1,129},{129,1},{2,130},{130,2},{3,131},{131,3},{4... | collective-permute-start | bytes 184328 | tf_op jit(solution)/shard_map/ppermute | solution.py:30
  106.7 103.9 %all-gather.8.cloned.1.call-start = ((), (), s32[]{:S(2)}) async-start(), calls=%async_computation.3 | async-start | bytes 4718592 | tf_op jit(solution)/shard_map/all_gather | solution.py:230
  127.0 5.1 %collective-permute-start.6 = (bf16[24,2048]{1,0:T(8,128)(2,1)S(1)}, bf16[24,2048]{1,0:T(8,128)(2,1)S(1)}, u32[]{:S(2)}, u32[]{:S(2)}) collective-permute-start(bf16[24,2048]{1,0:T(8,128)(2,1)S(1)} %multiply_convert_fusion), channel_id=1, source_target_pairs={{0,128},{128,0},{1,129},{129,1},{2,130},{130,2},{3,131},{131,3},{4... | collective-permute-start | bytes 294920 | tf_op jit(solution)/shard_map/ppermute | solution.py:30
  132.1 3.2 %collective-permute-start.7 = (bf16[12,2048]{1,0:T(8,128)(2,1)S(1)}, bf16[12,2048]{1,0:T(8,128)(2,1)S(1)}, u32[]{:S(2)}, u32[]{:S(2)}) collective-permute-start(bf16[12,2048]{1,0:T(8,128)(2,1)S(1)} %constant_dynamic-slice_fusion), channel_id=1, source_target_pairs={{0,64},{1,65},{2,66},{3,67},{4,68},{5,69},{6,70},{7,71},{8,72},{9,... | collective-permute-start | bytes 147464 | tf_op jit(solution)/shard_map/ppermute | solution.py:36
  150.4 86.4 %all-gather.10.cloned.1.call-start = ((), (), s32[]{:S(2)}) async-start(), calls=%async_computation.4 | async-start | bytes 12582912 | tf_op jit(solution)/shard_map/all_gather | solution.py:231
Sparse Core Ops, SparseCore 0:
  71.3 17.0 reduce-scatter.6
  106.8 18.1 reduce-scatter.4
  150.5 60.0 all-gather.7
  212.2 24.5 all-gather.9

commit v4 on v3

--- a/solution.py
+++ b/solution.py
@@ -34,6 +34,11 @@
     count = lax.axis_size(axis)
     pairs = [(source, (source + steps) % count) for source in range(count)]
     return lax.ppermute(value, axis, pairs)
+
+
+def xor_partner(block, axes, offset):
+    count = lax.axis_size(axes)
+    return lax.ppermute(block, axes, [(source, source ^ offset) for source in range(count)])
 
 
 def rms_scale(values, gain):
@@ -195,6 +200,10 @@
             preferred_element_type=jnp.float32,
         )
     attended = (accs / sums[..., None]).reshape(local_rows, query_width).astype(jnp.bfloat16)
+    near = ("x_lo", "core")
+    members = lax.axis_size(near)
+    blocks = [w_vocab] + [xor_partner(w_vocab, near, offset) for offset in range(1, members)]
+    blocks, attended = lax.optimization_barrier((blocks, attended))
     partner_attended = from_partner(attended, "guide", 0)
     both_attended = jnp.where(
         side == 0, jnp.stack([attended, partner_attended]), jnp.stack([partner_attended, attended])
@@ -225,14 +234,31 @@
     sent = lax.dynamic_slice_in_dim(combined, (1 - upper) * half_rows, half_rows, 0)
     swapped = shifted(sent, REQ, half_devices)
     mine = jnp.where(upper == side, kept, swapped)
-    gathered = lax.all_gather(mine, "x_lo", axis=0, tiled=False)
-    gathered = lax.all_gather(gathered, "y", axis=0, tiled=False)
+    gathered = lax.all_gather(mine, "y", axis=0, tiled=False)
     gathered = lax.all_gather(gathered, "z", axis=1, tiled=False)
-    gathered = lax.all_gather(gathered, "core", axis=2, tiled=False)
     logits = jnp.einsum(
-        "yzcxkd,dv->yzcxkv", gathered, w_vocab, preferred_element_type=jnp.float32
-    )
-    return logits.reshape(half_devices * local_rows, logits.shape[-1])
+        "yzkd,mdv->myzkv",
+        gathered,
+        jnp.stack(blocks),
+        preferred_element_type=jnp.float32,
+    )
+    parts = [logits[0]] + [
+        xor_partner(logits[offset], near, offset) for offset in range(1, members)
+    ]
+    core = lax.axis_index("core")
+    cores = lax.axis_size("core")
+    x_low = lax.axis_index("x_lo")
+    ordered = []
+    for source_core in range(cores):
+        for source_x in range(members // cores):
+            wanted = (source_x ^ x_low) * cores + (source_core ^ core)
+            pick = parts[0]
+            for offset in range(1, members):
+                pick = jnp.where(wanted == offset, parts[offset], pick)
+            ordered.append(pick)
+    placed = jnp.stack(ordered).reshape((cores, members // cores) + parts[0].shape)
+    placed = jnp.transpose(placed, (2, 3, 0, 1, 4, 5))
+    return placed.reshape(half_devices * local_rows, placed.shape[-1])
 
 
 def solution(mesh):

time: 254 us -> 268 us (1.055)
  starting transfers between devices: 13.9 us -> 25.6 us
  blocking collectives: 15 us -> 9.94 us
  local copies, waits for them, and re-layouts: 38.3 us -> 42.9 us
    ppermute x0 -> x6, waiting for transfers between devices: none -> 50.8 us  [xor_partner(): lax.ppermute(block, axes, [(source, source ^ offset) for source in range(...]
    all_gather x1 -> x0, waiting for transfers between devices: 26.2 us -> none  [body(): gathered = lax.all_gather(gathered, 'core', axis=2, tiled=False)]
    all_gather x1, waiting for transfers between devices: 60.2 us -> 40.4 us  [body(): gathered = lax.all_gather(gathered, 'z', axis=1, tiled=False)]
    ppermute x0 -> x6, starting transfers between devices: none -> 8.47 us  [xor_partner(): lax.ppermute(block, axes, [(source, source ^ offset) for source in range(...]
    all_gather x2 -> x1, blocking collectives: 15 us -> 9.94 us  [body(): gathered = lax.all_gather(mine, 'y', axis=0, tiled=False)]
    unnamed x19 -> x17, local copies, waits for them, and re-layouts: 9.94 us -> 11.5 us
    unnamed x5 -> x4, waiting for transfers between devices: 5.66 us -> 5.74 us
  transfers between devices with their start and end apart: 12 -> 17, of which waited for: 7 -> 10; matrix products, arithmetic and copies ran while one was open for 18% -> 19% of each run, Pallas kernels for 0% -> 0%
where the time goes in v4:
time: 268 us; the launch traced here: 267 us
  waiting for transfers between devices  124 us (46%)
  local copies, waits for them, and re-layouts  42.9 us (16%)
  between operations  28.7 us (11%)
  starting transfers between devices  25.6 us (10%)
  matrix products  21.1 us (8%)
  other arithmetic  15.3 us (6%)
  blocking collectives  9.94 us (4%)
    ppermute x6, waiting for transfers between devices, xor_partner(): lax.ppermute(block, axes, [(source, source ^ offset) for source in range(...  50.8 us
    all_gather x1, waiting for transfers between devices, body(): gathered = lax.all_gather(gathered, 'z', axis=1, tiled=False)  40.4 us
    reduce_scatter x1, waiting for transfers between devices, body(): lax.psum_scatter(jnp.einsum('grc,cd->grd', selected, w_out, preferred_ele...  16.9 us
    gather x4, local copies, waits for them, and re-layouts, body(): pages_sent = pool[tables[held_request, :MIGP]]  13.2 us
    ppermute x5, starting transfers between devices, shifted(): return lax.ppermute(value, axis, pairs)  11.9 us
    unnamed x17, local copies, waits for them, and re-layouts  11.5 us
    all_gather x1, blocking collectives, body(): gathered = lax.all_gather(mine, 'y', axis=0, tiled=False)  9.94 us
    ppermute x6, starting transfers between devices, xor_partner(): lax.ppermute(block, axes, [(source, source ^ offset) for source in range(...  8.47 us
  transfers between devices with their start and end apart: 17, of which 10 were waited for; matrix products, arithmetic and copies ran while one was open for 19% of the time, Pallas kernels for 0%

profile of v4, /device:TPU:1, one launch (start us, length us, event | category | flops | bytes accessed | tf_op | source)
XLA Modules:
  0.0 267.1 jit_solution(16432853598983075416)
XLA Ops:
  27.9 3.3 %gather_fusion = bf16[2,64,640]{2,1,0:T(8,128)(2,1)} fusion(bf16[46,64,640]{2,1,0:T(8,128)(2,1)} %bitcast.219, s32[1024]{0:T(1024)S(1)} %pad_clamp_fusion.3), kind=kCustom, calls=%fused_computation | custom fusion | bytes 327688 | tf_op jit(solution)/shard_map/gather | solution.py:161
  31.2 9.7 %collective-permute-start.4 = (bf16[2,64,640]{2,1,0:T(8,128)(2,1)}, bf16[2,64,640]{2,1,0:T(8,128)(2,1)S(1)}, u32[]{:S(2)}, u32[]{:S(2)}) collective-permute-start(bf16[2,64,640]{2,1,0:T(8,128)(2,1)} %gather_fusion), channel_id=1, source_target_pairs={{0,126},{1,127},{2,0},{3,1},{4,2},{5,3},{6,4},{7,5},{8,6},{9,7},{1... | collective-permute-start | bytes 491528 | tf_op jit(solution)/shard_map/ppermute | solution.py:36
  40.9 3.3 %gather_fusion.1 = bf16[2,64,640]{2,1,0:T(8,128)(2,1)} fusion(bf16[46,64,640]{2,1,0:T(8,128)(2,1)} %bitcast.220, s32[1024]{0:T(1024)S(1)} %pad_clamp_fusion.2), kind=kCustom, calls=%fused_computation.1 | custom fusion | bytes 327688 | tf_op jit(solution)/shard_map/gather | solution.py:161
  45.2 3.3 %gather_fusion.2 = bf16[2,64,640]{2,1,0:T(8,128)(2,1)} fusion(bf16[46,64,640]{2,1,0:T(8,128)(2,1)} %bitcast.221, s32[1024]{0:T(1024)S(1)} %pad_clamp_fusion.1), kind=kCustom, calls=%fused_computation.2 | custom fusion | bytes 327688 | tf_op jit(solution)/shard_map/gather | solution.py:161
  49.3 3.3 %gather_fusion.3 = bf16[2,64,640]{2,1,0:T(8,128)(2,1)} fusion(bf16[46,64,640]{2,1,0:T(8,128)(2,1)} %bitcast.222, s32[1024]{0:T(1024)S(1)} %pad_clamp_fusion), kind=kCustom, calls=%fused_computation.3 | custom fusion | bytes 327688 | tf_op jit(solution)/shard_map/gather | solution.py:161
  54.6 2.6 collective-permute-start.3
  60.3 5.9 %fusion.103 = (bf16[2944,320]{1,0:T(8,128)(2,1)}, bf16[2944,320]{1,0:T(8,128)(2,1)}) fusion(bf16[2944,640]{1,0:T(8,128)(2,1)} %bitcast.223), kind=kLoop, calls=%fused_computation.177 | loop fusion | bytes 7536640 | tf_op jit(solution)/shard_map/slice | solution.py:88
  69.6 3.7 %fusion.12 = f32[2,24,1920]{2,1,0:T(8,128)} fusion(bf16[1024,1920]{1,0:T(8,128)(2,1)} %param.12, s32[]{:T(128)S(6)} %select_n.267, bf16[1,24,2048]{2,1,0:T(8,128)(2,1)} %bitcast.1, bf16[1,24,2048]{2,1,0:T(8,128)(2,1)S(1)} %fusion.54, pred[]{:T(512)S(6)} %eq.134), kind=kOutput, calls=%fused_computation.21 | convolution fusion | flops 189186048 | bytes 4497413 | tf_op jit(solution)/shard_map/grd,df->grf/dot_general | solution.py:129
  74.1 4.1 %copy.74 = bf16[2944,320]{0,1:T(8,128)(2,1)} copy(bf16[2944,320]{1,0:T(8,128)(2,1)} %get-tuple-element.29) | data formatting | bytes 3768320
  78.2 4.1 %copy.76 = bf16[2944,320]{0,1:T(8,128)(2,1)} copy(bf16[2944,320]{1,0:T(8,128)(2,1)} %get-tuple-element.30) | data formatting | bytes 3768320
  86.5 5.7 %reduce-scatter.7.cloned.1.call-done = f32[1,24,1920]{2,1,0:T(8,128)} async-done(((f32[2,24,1920]{2,1,0:T(8,128)}), f32[1,24,1920]{2,1,0:T(8,128)}) %reduce-scatter.7.cloned.1.call-update) | async-done | bytes 184336
  95.2 2.6 bitcast_reduce_fusion
  99.9 4.0 %fusion.37 = f32[24,5,4,64]{3,0,2,1:T(8,128)S(1)} fusion(bf16[2944,5,64,1]{0,2,3,1:T(8,128)(2,1)S(1)} %bitcast.225, f32[5,24,4,2944]{3,1,2,0:T(8,128)S(1)} %get-tuple-element.49, f32[24,2944]{1,0:T(8,128)S(1)} %copy-done.4, f32[24,5,4]{0,2,1:T(4,128)S(1)} %get-tuple-element.28, pred[24,2944]{1,0:T(8,128)(4,1)S(1)} %broadcast_compare_fusion, ...), kind=kOutput, calls=%fused_computation.43 | convolution fusion | flops 1093816320 | bytes 8047360 | tf_op jit(solution)/shard_map/rkgt,tkd->rkgd/dot_general | solution.py:195
  104.8 4.5 %collective-permute-done.1 = bf16[2048,250]{1,0:T(8,128)(2,1)} collective-permute-done((bf16[2048,250]{1,0:T(8,128)(2,1)}, bf16[2048,250]{1,0:T(8,128)(2,1)}, u32[]{:S(2)}, u32[]{:S(2)}) %collective-permute-start.1) | collective-permute-done | bytes 1024032 | tf_op jit(solution)/shard_map/ppermute | solution.py:41
  109.3 22.5 %collective-permute-done.2 = bf16[2048,250]{1,0:T(8,128)(2,1)} collective-permute-done((bf16[2048,250]{1,0:T(8,128)(2,1)}, bf16[2048,250]{1,0:T(8,128)(2,1)}, u32[]{:S(2)}, u32[]{:S(2)}) %collective-permute-start.2) | collective-permute-done | bytes 1024032 | tf_op jit(solution)/shard_map/ppermute | solution.py:41
  137.7 16.9 %reduce-scatter.5.cloned.1.call-done = bf16[1,24,2048]{2,1,0:T(8,128)(2,1)} async-done(((bf16[2,24,2048]{2,1,0:T(8,128)(2,1)}), bf16[1,24,2048]{2,1,0:T(8,128)(2,1)}) %reduce-scatter.5.cloned.1.call-update) | async-done | bytes 98320 | tf_op jit(solution)/shard_map/reduce_scatter | solution.py:216
  156.7 4.9 %collective-permute-done.9 = bf16[24,2048]{1,0:T(8,128)(2,1)S(1)} collective-permute-done((bf16[24,2048]{1,0:T(8,128)(2,1)S(1)}, bf16[24,2048]{1,0:T(8,128)(2,1)S(1)}, u32[]{:S(2)}, u32[]{:S(2)}) %collective-permute-start.9) | collective-permute-done | bytes 98336 | tf_op jit(solution)/shard_map/ppermute | solution.py:30
  162.2 2.8 %collective-permute-done.10 = bf16[12,2048]{1,0:T(8,128)(2,1)S(1)} collective-permute-done((bf16[12,2048]{1,0:T(8,128)(2,1)S(1)}, bf16[12,2048]{1,0:T(8,128)(2,1)S(1)}, u32[]{:S(2)}, u32[]{:S(2)}) %collective-permute-start.10) | collective-permute-done | bytes 49184 | tf_op jit(solution)/shard_map/ppermute | solution.py:36
  165.0 9.9 %all-gather.2 = bf16[4,12,2048]{2,1,0:T(8,128)(2,1)S(1)} all-gather(bf16[1,12,2048]{2,1,0:T(8,128)(2,1)S(1)} %select_bitcast_fusion.4), channel_id=2, replica_groups=mesh['guide'=2,'x_lo'=2,'y'=4,'z'=8,'core'=2] {'y'}, dimensions={0}, use_global_device_ids=true | all-gather | bytes 245760 | tf_op jit(solution)/shard_map/all_gather | solution.py:237
  175.8 40.4 %all-gather.5.cloned.1.call-done = bf16[4,96,2048]{2,0,1:T(4,128)(2,1)} async-done(((bf16[4,12,2048]{2,0,1:T(4,128)(2,1)}), bf16[4,96,2048]{2,0,1:T(4,128)(2,1)}) %all-gather.5.cloned.1.call-update) | async-done | bytes 1572880 | tf_op jit(solution)/shard_map/all_gather | solution.py:238
  216.2 6.0 %fusion.27 = f32[4,4,8,12,250]{4,3,2,1,0:T(8,128)S(1)} fusion(bf16[4,8,12,2048]{3,0,2,1:T(4,128)(2,1)} %bitcast.235, bf16[1,2048,250]{2,1,0:T(8,128)(2,1)} %bitcast.43, bf16[1,2048,250]{2,1,0:T(8,128)(2,1)} %bitcast.42, bf16[1,2048,250]{2,1,0:T(8,128)(2,1)} %bitcast.41, bf16[1,2048,250]{2,1,0:T(8,128)(2,1)} %bitcast.236), kind=kOutput, calls=%fused_computation.35 | convolution fusion | flops 1589248000 | bytes 7204864 | tf_op jit(solution)/shard_map/yzkd,mdv->myzkv/dot_general | solution.py:239
  224.7 5.6 %collective-permute-start.11 = (f32[4,8,12,250]{3,2,1,0:T(8,128)}, f32[4,8,12,250]{3,2,1,0:T(8,128)S(1)}, u32[]{:S(2)}, u32[]{:S(2)}) collective-permute-start(f32[4,8,12,250]{3,2,1,0:T(8,128)} %get-tuple-element.37), channel_id=1, source_target_pairs={{0,65},{1,64},{64,1},{65,0},{2,67},{3,66},{66,3},{67,2},{4,69},{5,... | collective-permute-start | bytes 1152008 | tf_op jit(solution)/shard_map/ppermute | solution.py:41
  230.7 12.5 %collective-permute-done.11 = f32[4,8,12,250]{3,2,1,0:T(8,128)S(1)} collective-permute-done((f32[4,8,12,250]{3,2,1,0:T(8,128)}, f32[4,8,12,250]{3,2,1,0:T(8,128)S(1)}, u32[]{:S(2)}, u32[]{:S(2)}) %collective-permute-start.11) | collective-permute-done | bytes 384032 | tf_op jit(solution)/shard_map/ppermute | solution.py:41
  243.2 11.3 %collective-permute-done.12 = f32[4,8,12,250]{3,2,1,0:T(8,128)} collective-permute-done((f32[4,8,12,250]{3,2,1,0:T(8,128)}, f32[4,8,12,250]{3,2,1,0:T(8,128)}, u32[]{:S(2)}, u32[]{:S(2)}) %collective-permute-start.12) | collective-permute-done | bytes 384032 | tf_op jit(solution)/shard_map/ppermute | solution.py:41
  (105 shorter events, 45.6 us)
Async XLA Ops:
  6.5 129.8 %copy-start = (bf16[640,2048]{1,0:T(8,128)(2,1)S(1)}, bf16[640,2048]{1,0:T(8,128)(2,1)}, u32[]{:S(2)}) copy-start(bf16[640,2048]{1,0:T(8,128)(2,1)} %param.13) | copy-start | bytes 7864324
  6.5 85.6 %reduce-scatter.7.cloned.1.call-start = ((), (), s32[]{:S(2)}) async-start(), calls=%async_computation.4 | async-start | bytes 552960
  31.2 51.2 %collective-permute-start.4 = (bf16[2,64,640]{2,1,0:T(8,128)(2,1)}, bf16[2,64,640]{2,1,0:T(8,128)(2,1)S(1)}, u32[]{:S(2)}, u32[]{:S(2)}) collective-permute-start(bf16[2,64,640]{2,1,0:T(8,128)(2,1)} %gather_fusion), channel_id=1, source_target_pairs={{0,126},{1,127},{2,0},{3,1},{4,2},{5,3},{6,4},{7,5},{8,6},{9,7},{1... | collective-permute-start | bytes 491528 | tf_op jit(solution)/shard_map/ppermute | solution.py:36
  44.2 38.2 %collective-permute-start.5 = (bf16[2,64,640]{2,1,0:T(8,128)(2,1)}, bf16[2,64,640]{2,1,0:T(8,128)(2,1)S(1)}, u32[]{:S(2)}, u32[]{:S(2)}) collective-permute-start(bf16[2,64,640]{2,1,0:T(8,128)(2,1)} %gather_fusion.1), channel_id=1, source_target_pairs={{0,127},{1,0},{2,1},{3,2},{4,3},{5,4},{6,5},{7,6},{8,7},{9,8},{10,... | collective-permute-start | bytes 491528 | tf_op jit(solution)/shard_map/ppermute | solution.py:36
  48.5 35.5 %collective-permute-start.6 = (bf16[2,64,640]{2,1,0:T(8,128)(2,1)}, bf16[2,64,640]{2,1,0:T(8,128)(2,1)}, u32[]{:S(2)}, u32[]{:S(2)}) collective-permute-start(bf16[2,64,640]{2,1,0:T(8,128)(2,1)} %gather_fusion.2), channel_id=1, source_target_pairs={{0,1},{1,2},{2,3},{3,4},{4,5},{5,6},{6,7},{7,8},{8,9},{9,10},{10,1... | collective-permute-start | bytes 491528 | tf_op jit(solution)/shard_map/ppermute | solution.py:36
  52.6 31.5 %collective-permute-start.7 = (bf16[2,64,640]{2,1,0:T(8,128)(2,1)}, bf16[2,64,640]{2,1,0:T(8,128)(2,1)}, u32[]{:S(2)}, u32[]{:S(2)}) collective-permute-start(bf16[2,64,640]{2,1,0:T(8,128)(2,1)} %gather_fusion.3), channel_id=1, source_target_pairs={{0,2},{1,3},{2,4},{3,5},{4,6},{5,7},{6,8},{7,9},{8,10},{9,11},{10,... | collective-permute-start | bytes 491528 | tf_op jit(solution)/shard_map/ppermute | solution.py:36
  54.6 14.2 %collective-permute-start.3 = (bf16[24,2048]{1,0:T(8,128)(2,1)S(1)}, bf16[24,2048]{1,0:T(8,128)(2,1)}, u32[]{:S(2)}, u32[]{:S(2)}) collective-permute-start(bf16[24,2048]{1,0:T(8,128)(2,1)S(1)} %fusion.52), channel_id=1, source_target_pairs={{0,128},{128,0},{1,129},{129,1},{2,130},{130,2},{3,131},{131,3},{4... | collective-permute-start | bytes 294920 | tf_op jit(solution)/shard_map/ppermute | solution.py:30
  68.8 36.0 %collective-permute-start = (bf16[2048,250]{1,0:T(8,128)(2,1)}, bf16[2048,250]{1,0:T(8,128)(2,1)}, u32[]{:S(2)}, u32[]{:S(2)}) collective-permute-start(bf16[2048,250]{1,0:T(8,128)(2,1)} %param.15), channel_id=1, source_target_pairs={{0,1},{1,0},{64,65},{65,64},{2,3},{3,2},{66,67},{67,66},{4,5},{5,4... | collective-permute-start | bytes 3072008 | tf_op jit(solution)/shard_map/ppermute | solution.py:41
  73.3 81.3 %reduce-scatter.5.cloned.1.call-start = ((), (), s32[]{:S(2)}) async-start(), calls=%async_computation.2 | async-start | bytes 294912 | tf_op jit(solution)/shard_map/reduce_scatter | solution.py:216
  82.3 27.0 %collective-permute-start.1 = (bf16[2048,250]{1,0:T(8,128)(2,1)}, bf16[2048,250]{1,0:T(8,128)(2,1)}, u32[]{:S(2)}, u32[]{:S(2)}) collective-permute-start(bf16[2048,250]{1,0:T(8,128)(2,1)} %param.15), channel_id=1, source_target_pairs={{0,64},{1,65},{64,0},{65,1},{2,66},{3,67},{66,2},{67,3},{4,68},{5,... | collective-permute-start | bytes 3072008 | tf_op jit(solution)/shard_map/ppermute | solution.py:41
  82.5 49.3 %collective-permute-start.2 = (bf16[2048,250]{1,0:T(8,128)(2,1)}, bf16[2048,250]{1,0:T(8,128)(2,1)}, u32[]{:S(2)}, u32[]{:S(2)}) collective-permute-start(bf16[2048,250]{1,0:T(8,128)(2,1)} %param.15), channel_id=1, source_target_pairs={{0,65},{1,64},{64,1},{65,0},{2,67},{3,66},{66,3},{67,2},{4,69},{5,... | collective-permute-start | bytes 3072008 | tf_op jit(solution)/shard_map/ppermute | solution.py:41
  95.2 2.6 copy-start.4
  97.8 2.0 copy-start.3
  103.9 50.7 %copy-start.1 = (bf16[1,24,2048]{2,1,0:T(8,128)(2,1)S(1)}, bf16[1,24,2048]{2,1,0:T(8,128)(2,1)}, u32[]{:S(2)}) copy-start(bf16[1,24,2048]{2,1,0:T(8,128)(2,1)} %param.10) | copy-start | bytes 294916
  103.9 51.8 %copy-start.5 = (f32[2048]{0:T(1024)S(1)}, f32[2048]{0:T(1024)}, u32[]{:S(2)}) copy-start(f32[2048]{0:T(1024)} %param.14) | copy-start | bytes 24580
  131.8 4.6 %collective-permute-start.8 = (bf16[24,1280]{1,0:T(8,128)(2,1)S(1)}, bf16[24,1280]{1,0:T(8,128)(2,1)S(1)}, u32[]{:S(2)}, u32[]{:S(2)}) collective-permute-start(bf16[24,1280]{1,0:T(8,128)(2,1)S(1)} %convert_element_type.91), channel_id=1, source_target_pairs={{0,128},{128,0},{1,129},{129,1},{2,130},{130,2},{3,131},{131,3},{4... | collective-permute-start | bytes 184328 | tf_op jit(solution)/shard_map/ppermute | solution.py:30
  137.6 78.6 %all-gather.5.cloned.1.call-start = ((), (), s32[]{:S(2)}) async-start(), calls=%async_computation.3 | async-start | bytes 1769472 | tf_op jit(solution)/shard_map/all_gather | solution.py:238
  156.6 5.1 %collective-permute-start.9 = (bf16[24,2048]{1,0:T(8,128)(2,1)S(1)}, bf16[24,2048]{1,0:T(8,128)(2,1)S(1)}, u32[]{:S(2)}, u32[]{:S(2)}) collective-permute-start(bf16[24,2048]{1,0:T(8,128)(2,1)S(1)} %multiply_convert_fusion), channel_id=1, source_target_pairs={{0,128},{128,0},{1,129},{129,1},{2,130},{130,2},{3,131},{131,3},{4... | collective-permute-start | bytes 294920 | tf_op jit(solution)/shard_map/ppermute | solution.py:30
  161.8 3.2 %collective-permute-start.10 = (bf16[12,2048]{1,0:T(8,128)(2,1)S(1)}, bf16[12,2048]{1,0:T(8,128)(2,1)S(1)}, u32[]{:S(2)}, u32[]{:S(2)}) collective-permute-start(bf16[12,2048]{1,0:T(8,128)(2,1)S(1)} %constant_dynamic-slice_fusion), channel_id=1, source_target_pairs={{0,64},{1,65},{2,66},{3,67},{4,68},{5,69},{6,70},{7,71},{8,72},{9,... | collective-permute-start | bytes 147464 | tf_op jit(solution)/shard_map/ppermute | solution.py:36
  222.2 1.4 copy-start.2
  224.7 18.5 %collective-permute-start.11 = (f32[4,8,12,250]{3,2,1,0:T(8,128)}, f32[4,8,12,250]{3,2,1,0:T(8,128)S(1)}, u32[]{:S(2)}, u32[]{:S(2)}) collective-permute-start(f32[4,8,12,250]{3,2,1,0:T(8,128)} %get-tuple-element.37), channel_id=1, source_target_pairs={{0,65},{1,64},{64,1},{65,0},{2,67},{3,66},{66,3},{67,2},{4,69},{5,... | collective-permute-start | bytes 1152008 | tf_op jit(solution)/shard_map/ppermute | solution.py:41
  230.3 24.3 %collective-permute-start.12 = (f32[4,8,12,250]{3,2,1,0:T(8,128)}, f32[4,8,12,250]{3,2,1,0:T(8,128)}, u32[]{:S(2)}, u32[]{:S(2)}) collective-permute-start(f32[4,8,12,250]{3,2,1,0:T(8,128)} %get-tuple-element.36), channel_id=1, source_target_pairs={{0,64},{1,65},{64,0},{65,1},{2,66},{3,67},{66,2},{67,3},{4,68},{5,... | collective-permute-start | bytes 1152008 | tf_op jit(solution)/shard_map/ppermute | solution.py:41
  230.6 24.0 %collective-permute-start.13 = (f32[4,8,12,250]{3,2,1,0:T(8,128)}, f32[4,8,12,250]{3,2,1,0:T(8,128)}, u32[]{:S(2)}, u32[]{:S(2)}) collective-permute-start(f32[4,8,12,250]{3,2,1,0:T(8,128)} %get-tuple-element.35), channel_id=1, source_target_pairs={{0,1},{1,0},{64,65},{65,64},{2,3},{3,2},{66,67},{67,66},{4,5},{5,4... | collective-permute-start | bytes 1152008 | tf_op jit(solution)/shard_map/ppermute | solution.py:41
Sparse Core Ops, SparseCore 0:
  73.4 18.7 reduce-scatter.6
  137.7 16.8 reduce-scatter.4
  175.9 40.1 all-gather.4

commit v5 on v3

--- a/solution.py
+++ b/solution.py
@@ -120,12 +120,10 @@
     inner_half = w_qkv.shape[0]
     normed_part = lax.dynamic_slice_in_dim(both_normed, side * inner_half, inner_half, 2)
     selected = normed_part
-    joined = lax.psum_scatter(
-        jnp.einsum("grd,df->grf", selected, w_qkv, preferred_element_type=jnp.float32),
-        "guide",
-        scatter_dimension=0,
-        tiled=True,
-    )[0].astype(jnp.bfloat16)
+    qkv_parts = jnp.einsum("grd,df->grf", selected, w_qkv, preferred_element_type=jnp.float32)
+    own_qkv = jnp.where(side == 0, qkv_parts[0], qkv_parts[1])
+    other_qkv = jnp.where(side == 0, qkv_parts[1], qkv_parts[0])
+    joined = (own_qkv + from_partner(other_qkv, "guide", 0)).astype(jnp.bfloat16)
     queries = joined[:, :query_width].reshape(local_rows, KVH, group, HD)
     new_keys = joined[:, query_width : query_width + key_width].reshape(local_rows, KVH, HD)
     new_values = joined[:, query_width + key_width :].reshape(local_rows, KVH, HD)
@@ -202,37 +200,30 @@
     head_half = w_out.shape[0]
     attended_part = lax.dynamic_slice_in_dim(both_attended, side * head_half, head_half, 2)
     selected = attended_part
-    state_after = (
-        states_in
-        + lax.psum_scatter(
-            jnp.einsum("grc,cd->grd", selected, w_out, preferred_element_type=jnp.float32).astype(
-                jnp.bfloat16
-            ),
-            "guide",
-            scatter_dimension=0,
-            tiled=True,
-        ).astype(jnp.float32)[0]
+    out_parts = jnp.einsum("grc,cd->grd", selected, w_out, preferred_element_type=jnp.float32)
+    own_out = jnp.where(side == 0, out_parts[0], out_parts[1])
+    other_out = jnp.where(side == 0, out_parts[1], out_parts[0]).astype(jnp.bfloat16)
+    state_after = states_in + (
+        own_out + from_partner(other_out, "guide", 0).astype(jnp.float32)
     )
     final = rms_scale(state_after, final_gain).astype(jnp.bfloat16)
-    partner_final = from_partner(final, "guide", 0)
-    cond = jnp.where(side == 0, final, partner_final).astype(jnp.float32)
-    uncond = jnp.where(side == 0, partner_final, final).astype(jnp.float32)
+    pair = ("guide", "x_lo")
+    from_side = lax.ppermute(final, pair, [(0, 1), (3, 2)])
+    from_diagonal = lax.ppermute(final, pair, [(2, 1), (1, 2)])
+    from_guide = lax.ppermute(final, pair, [(2, 0), (1, 3)])
+    home = lax.axis_index("x_lo") == side
+    same_group = jnp.where(home, final, from_side)
+    other_group = jnp.where(home, from_guide, from_diagonal)
+    cond = jnp.where(side == 0, same_group, other_group).astype(jnp.float32)
+    uncond = jnp.where(side == 0, other_group, same_group).astype(jnp.float32)
     combined = (uncond + guidance * (cond - uncond)).astype(jnp.bfloat16)
-    half_devices = devices // 2
-    half_rows = local_rows // 2
-    upper = device // half_devices
-    kept = lax.dynamic_slice_in_dim(combined, upper * half_rows, half_rows, 0)
-    sent = lax.dynamic_slice_in_dim(combined, (1 - upper) * half_rows, half_rows, 0)
-    swapped = shifted(sent, REQ, half_devices)
-    mine = jnp.where(upper == side, kept, swapped)
-    gathered = lax.all_gather(mine, "x_lo", axis=0, tiled=False)
-    gathered = lax.all_gather(gathered, "y", axis=0, tiled=False)
+    gathered = lax.all_gather(combined, "y", axis=0, tiled=False)
     gathered = lax.all_gather(gathered, "z", axis=1, tiled=False)
     gathered = lax.all_gather(gathered, "core", axis=2, tiled=False)
     logits = jnp.einsum(
-        "yzcxkd,dv->yzcxkv", gathered, w_vocab, preferred_element_type=jnp.float32
-    )
-    return logits.reshape(half_devices * local_rows, logits.shape[-1])
+        "yzcrd,dv->yzcrv", gathered, w_vocab, preferred_element_type=jnp.float32
+    )
+    return logits.reshape(-1, logits.shape[-1])
 
 
 def solution(mesh):

time: 254 us -> 218 us (0.86)
  waiting for transfers between devices: 122 us -> 87.1 us
  starting transfers between devices: 13.9 us -> 21.8 us
  blocking collectives: 15 us -> 10.4 us
  matrix products: 21.5 us -> 18.7 us
    reduce_scatter x1 -> x0, waiting for transfers between devices: 18.2 us -> none  [body(): lax.psum_scatter(jnp.einsum('grc,cd->grd', selected, w_out, preferred_ele...]
    all_gather x1, waiting for transfers between devices: 60.2 us -> 51.9 us  [body(): gathered = lax.all_gather(gathered, 'z', axis=1, tiled=False)]
    unnamed x5 -> x2, waiting for transfers between devices: 5.66 us -> 0.03 us
    ppermute x0 -> x3, waiting for transfers between devices: none -> 4.88 us  [the longest x1 4.88 us: body(): from_guide = lax.ppermute(final, pair, [(2, 0), (1, 3)])]
    all_gather x2 -> x1, blocking collectives: 15 us -> 10.4 us  [body(): gathered = lax.all_gather(combined, 'y', axis=0, tiled=False)]
    ppermute x0 -> x3, starting transfers between devices: none -> 4.55 us  [the longest x1 2.59 us: body(): from_side = lax.ppermute(final, pair, [(0, 1), (3, 2)])]
    ppermute x3 -> x4, starting transfers between devices: 3.85 us -> 8.18 us  [from_partner(): return lax.ppermute(block, axis, route)]
    ppermute x5 -> x4, waiting for transfers between devices: 2.84 us -> 0.01 us  [shifted(): return lax.ppermute(value, axis, pairs)]
  transfers between devices with their start and end apart: 12 -> 13, of which waited for: 7 -> 5; matrix products, arithmetic and copies ran while one was open for 18% -> 22% of each run, Pallas kernels for 0% -> 0%
where the time goes in v5:
time: 218 us; the launch traced here: 217 us
  waiting for transfers between devices  87.1 us (40%)
  local copies, waits for them, and re-layouts  37.5 us (17%)
  between operations  28.9 us (13%)
  starting transfers between devices  21.8 us (10%)
  matrix products  18.7 us (9%)
  other arithmetic  12.6 us (6%)
  blocking collectives  10.4 us (5%)
    all_gather x1, waiting for transfers between devices, body(): gathered = lax.all_gather(gathered, 'z', axis=1, tiled=False)  51.9 us
    all_gather x1, waiting for transfers between devices, body(): gathered = lax.all_gather(gathered, 'core', axis=2, tiled=False)  23.5 us
    gather x4, local copies, waits for them, and re-layouts, body(): pages_sent = pool[tables[held_request, :MIGP]]  13.2 us
    unnamed x19, local copies, waits for them, and re-layouts  11.7 us
    all_gather x1, blocking collectives, body(): gathered = lax.all_gather(combined, 'y', axis=0, tiled=False)  10.4 us
    ppermute x4, starting transfers between devices, shifted(): return lax.ppermute(value, axis, pairs)  9.05 us
    ppermute x4, starting transfers between devices, from_partner(): return lax.ppermute(block, axis, route)  8.18 us
    ppermute x4, waiting for transfers between devices, from_partner(): return lax.ppermute(block, axis, route)  6.8 us
  transfers between devices with their start and end apart: 13, of which 5 were waited for; matrix products, arithmetic and copies ran while one was open for 22% of the time, Pallas kernels for 0%

profile of v5, /device:TPU:1, one launch (start us, length us, event | category | flops | bytes accessed | tf_op | source)
XLA Modules:
  0.0 217.1 jit_solution(13390418738207180168)
XLA Ops:
  8.7 3.7 %collective-permute-start = (bf16[24,2048]{1,0:T(8,128)(2,1)S(1)}, bf16[24,2048]{1,0:T(8,128)(2,1)}, u32[]{:S(2)}, u32[]{:S(2)}) collective-permute-start(bf16[24,2048]{1,0:T(8,128)(2,1)S(1)} %fusion.41), channel_id=1, source_target_pairs={{0,128},{128,0},{1,129},{129,1},{2,130},{130,2},{3,131},{131,3},{4... | collective-permute-start | bytes 294920 | tf_op jit(solution)/shard_map/ppermute | solution.py:30
  33.5 3.3 %gather_fusion.3 = bf16[2,64,640]{2,1,0:T(8,128)(2,1)} fusion(bf16[46,64,640]{2,1,0:T(8,128)(2,1)} %bitcast.178, s32[1024]{0:T(1024)S(1)} %pad_clamp_fusion), kind=kCustom, calls=%fused_computation.3 | custom fusion | bytes 327688 | tf_op jit(solution)/shard_map/gather | solution.py:154
  36.8 1.7 collective-permute-start.5
  38.5 3.3 %gather_fusion.2 = bf16[2,64,640]{2,1,0:T(8,128)(2,1)} fusion(bf16[46,64,640]{2,1,0:T(8,128)(2,1)} %bitcast.179, s32[1024]{0:T(1024)S(1)} %pad_clamp_fusion.1), kind=kCustom, calls=%fused_computation.2 | custom fusion | bytes 327688 | tf_op jit(solution)/shard_map/gather | solution.py:154
  41.8 2.7 %collective-permute-start.4 = (bf16[2,64,640]{2,1,0:T(8,128)(2,1)}, bf16[2,64,640]{2,1,0:T(8,128)(2,1)}, u32[]{:S(2)}, u32[]{:S(2)}) collective-permute-start(bf16[2,64,640]{2,1,0:T(8,128)(2,1)} %gather_fusion.2), channel_id=1, source_target_pairs={{0,1},{1,2},{2,3},{3,4},{4,5},{5,6},{6,7},{7,8},{8,9},{9,10},{10,1... | collective-permute-start | bytes 491528 | tf_op jit(solution)/shard_map/ppermute | solution.py:36
  44.6 3.3 %gather_fusion.1 = bf16[2,64,640]{2,1,0:T(8,128)(2,1)} fusion(bf16[46,64,640]{2,1,0:T(8,128)(2,1)} %bitcast.180, s32[1024]{0:T(1024)S(1)} %pad_clamp_fusion.2), kind=kCustom, calls=%fused_computation.1 | custom fusion | bytes 327688 | tf_op jit(solution)/shard_map/gather | solution.py:154
  47.9 3.3 %gather_fusion = bf16[2,64,640]{2,1,0:T(8,128)(2,1)} fusion(bf16[46,64,640]{2,1,0:T(8,128)(2,1)} %bitcast.181, s32[1024]{0:T(1024)S(1)} %pad_clamp_fusion.3), kind=kCustom, calls=%fused_computation | custom fusion | bytes 327688 | tf_op jit(solution)/shard_map/gather | solution.py:154
  51.2 4.6 %collective-permute-start.2 = (bf16[2,64,640]{2,1,0:T(8,128)(2,1)}, bf16[2,64,640]{2,1,0:T(8,128)(2,1)}, u32[]{:S(2)}, u32[]{:S(2)}) collective-permute-start(bf16[2,64,640]{2,1,0:T(8,128)(2,1)} %gather_fusion), channel_id=1, source_target_pairs={{0,126},{1,127},{2,0},{3,1},{4,2},{5,3},{6,4},{7,5},{8,6},{9,7},{1... | collective-permute-start | bytes 491528 | tf_op jit(solution)/shard_map/ppermute | solution.py:36
  56.8 5.7 %fusion.92 = (bf16[2944,320]{1,0:T(8,128)(2,1)}, bf16[2944,320]{1,0:T(8,128)(2,1)}) fusion(bf16[2944,640]{1,0:T(8,128)(2,1)} %bitcast.182), kind=kLoop, calls=%fused_computation.159 | loop fusion | bytes 7536640 | tf_op jit(solution)/shard_map/slice | solution.py:83
  68.0 4.1 %copy.49 = bf16[2944,320]{0,1:T(8,128)(2,1)} copy(bf16[2944,320]{1,0:T(8,128)(2,1)} %get-tuple-element.22) | data formatting | bytes 3768320
  72.1 4.1 %copy.47 = bf16[2944,320]{0,1:T(8,128)(2,1)} copy(bf16[2944,320]{1,0:T(8,128)(2,1)} %get-tuple-element.21) | data formatting | bytes 3768320
  76.2 2.9 %fusion.5 = f32[2,24,1920]{2,1,0:T(8,128)S(1)} fusion(bf16[1024,1920]{1,0:T(8,128)(2,1)} %param.12, s32[]{:T(128)S(6)} %select_n.223, bf16[1,24,2048]{2,1,0:T(8,128)(2,1)} %bitcast.1, bf16[1,24,2048]{2,1,0:T(8,128)(2,1)S(1)} %fusion.43, pred[]{:T(512)S(6)} %eq.101), kind=kOutput, calls=%fused_computation.13 | convolution fusion | flops 189186048 | bytes 4497413 | tf_op jit(solution)/shard_map/grd,df->grf/dot_general | solution.py:123
  79.8 1.7 collective-permute-start.1
  83.7 1.9 copy.48
  88.3 2.6 %bitcast_reduce_fusion = (f32[24,5,4]{0,2,1:T(4,128)S(1)}, f32[5,24,4,2944]{3,1,2,0:T(8,128)S(1)}) fusion(pred[24,2944]{1,0:T(8,128)(4,1)S(1)} %broadcast_compare_fusion, bf16[2944,5,64,1]{0,2,3,1:T(8,128)(2,1)} %bitcast.177, bf16[24,5,4,64]{3,2,1,0:T(4,128)(2,1)S(1)} %reshape.343), kind=kOutput, calls=%fused_computation.5 | convolution fusion | flops 185118240 | bytes 7670656 | tf_op jit(solution)/shard_map/rkgd,tkd->rkgt/dot_general | solution.py:85
  93.2 4.0 %fusion.22 = f32[24,5,4,64]{3,0,2,1:T(8,128)S(1)} fusion(bf16[2944,5,64,1]{0,2,3,1:T(8,128)(2,1)S(1)} %bitcast.185, f32[5,24,4,2944]{3,1,2,0:T(8,128)S(1)} %get-tuple-element.34, f32[24,2944]{1,0:T(8,128)S(1)} %copy-done.4, f32[24,5,4]{0,2,1:T(4,128)S(1)} %get-tuple-element.20, pred[24,2944]{1,0:T(8,128)(4,1)S(1)} %broadcast_compare_fusion, ...), kind=kOutput, calls=%fused_computation.29 | convolution fusion | flops 1093816320 | bytes 8047360 | tf_op jit(solution)/shard_map/rkgt,tkd->rkgd/dot_general | solution.py:188
  99.7 3.1 %collective-permute-done.6 = bf16[24,1280]{1,0:T(8,128)(2,1)S(1)} collective-permute-done((bf16[24,1280]{1,0:T(8,128)(2,1)S(1)}, bf16[24,1280]{1,0:T(8,128)(2,1)S(1)}, u32[]{:S(2)}, u32[]{:S(2)}) %collective-permute-start.6) | collective-permute-done | bytes 61472 | tf_op jit(solution)/shard_map/ppermute | solution.py:30
  104.8 3.7 %collective-permute-done.7 = bf16[24,2048]{1,0:T(8,128)(2,1)S(1)} collective-permute-done((bf16[24,2048]{1,0:T(8,128)(2,1)S(1)}, bf16[24,2048]{1,0:T(8,128)(2,1)S(1)}, u32[]{:S(2)}, u32[]{:S(2)}) %collective-permute-start.7) | collective-permute-done | bytes 98336 | tf_op jit(solution)/shard_map/ppermute | solution.py:30
  108.8 2.6 %collective-permute-start.10 = (bf16[24,2048]{1,0:T(8,128)(2,1)S(1)}, bf16[24,2048]{1,0:T(8,128)(2,1)S(1)}, u32[]{:S(2)}, u32[]{:S(2)}) collective-permute-start(bf16[24,2048]{1,0:T(8,128)(2,1)S(1)} %multiply_convert_fusion), channel_id=1, source_target_pairs={{0,64},{192,128},{1,65},{193,129},{2,66},{194,130},{3,67},{195,131... | collective-permute-start | bytes 294920 | tf_op jit(solution)/shard_map/ppermute | solution.py:211
  113.3 4.9 %collective-permute-done.8 = bf16[24,2048]{1,0:T(8,128)(2,1)S(1)} collective-permute-done((bf16[24,2048]{1,0:T(8,128)(2,1)S(1)}, bf16[24,2048]{1,0:T(8,128)(2,1)S(1)}, u32[]{:S(2)}, u32[]{:S(2)}) %collective-permute-start.8) | collective-permute-done | bytes 98336 | tf_op jit(solution)/shard_map/ppermute | solution.py:213
  118.4 10.4 %all-gather = bf16[96,2048]{1,0:T(8,128)(2,1)} all-gather(bf16[24,2048]{1,0:T(8,128)(2,1)S(1)} %fusion.38), channel_id=2, replica_groups=mesh['guide'=2,'x_lo'=2,'y'=4,'z'=8,'core'=2] {'y'}, dimensions={0}, use_global_device_ids=true | all-gather | bytes 491520 | tf_op jit(solution)/shard_map/all_gather | solution.py:220
  128.8 51.9 %all-gather.6.cloned.1.call-done = bf16[4,192,2048]{2,1,0:T(8,128)(2,1)} async-done(((bf16[4,24,2048]{2,1,0:T(8,128)(2,1)}), bf16[4,192,2048]{2,1,0:T(8,128)(2,1)}) %all-gather.6.cloned.1.call-update) | async-done | bytes 3145744 | tf_op jit(solution)/shard_map/all_gather | solution.py:221
  180.7 23.5 %all-gather.8.cloned.1.call-done = bf16[4,8,48,2048]{3,2,1,0:T(8,128)(2,1)} async-done(((bf16[4,8,24,2048]{3,2,1,0:T(8,128)(2,1)}), bf16[4,8,48,2048]{3,2,1,0:T(8,128)(2,1)}) %all-gather.8.cloned.1.call-update) | async-done | bytes 6291472 | tf_op jit(solution)/shard_map/all_gather | solution.py:222
  204.2 6.0 %fusion.26 = f32[4,8,2,24,250]{4,3,2,1,0:T(8,128)} fusion(bf16[4,8,2,24,2048]{4,3,2,1,0:T(8,128)(2,1)} %bitcast.195, bf16[2048,250]{1,0:T(8,128)(2,1)} %param.15), kind=kOutput, calls=%fused_computation.31 | convolution fusion | flops 1572864000 | bytes 8851456 | tf_op jit(solution)/shard_map/yzcrd,dv->yzcrv/dot_general | solution.py:223
  (93 shorter events, 29.2 us)
Async XLA Ops:
  6.5 96.3 %copy-start = (bf16[640,2048]{1,0:T(8,128)(2,1)S(1)}, bf16[640,2048]{1,0:T(8,128)(2,1)}, u32[]{:S(2)}) copy-start(bf16[640,2048]{1,0:T(8,128)(2,1)} %param.13) | copy-start | bytes 7864324
  6.5 174.1 %all-gather.6.cloned.1.call-start = ((), (), s32[]{:S(2)}) async-start(), calls=%async_computation | async-start | bytes 3538944 | tf_op jit(solution)/shard_map/all_gather | solution.py:221
  8.7 67.5 %collective-permute-start = (bf16[24,2048]{1,0:T(8,128)(2,1)S(1)}, bf16[24,2048]{1,0:T(8,128)(2,1)}, u32[]{:S(2)}, u32[]{:S(2)}) collective-permute-start(bf16[24,2048]{1,0:T(8,128)(2,1)S(1)} %fusion.41), channel_id=1, source_target_pairs={{0,128},{128,0},{1,129},{129,1},{2,130},{130,2},{3,131},{131,3},{4... | collective-permute-start | bytes 294920 | tf_op jit(solution)/shard_map/ppermute | solution.py:30
  36.8 44.7 %collective-permute-start.5 = (bf16[2,64,640]{2,1,0:T(8,128)(2,1)}, bf16[2,64,640]{2,1,0:T(8,128)(2,1)S(1)}, u32[]{:S(2)}, u32[]{:S(2)}) collective-permute-start(bf16[2,64,640]{2,1,0:T(8,128)(2,1)} %gather_fusion.3), channel_id=1, source_target_pairs={{0,2},{1,3},{2,4},{3,5},{4,6},{5,7},{6,8},{7,9},{8,10},{9,11},{10,... | collective-permute-start | bytes 491528 | tf_op jit(solution)/shard_map/ppermute | solution.py:36
  41.8 39.7 %collective-permute-start.4 = (bf16[2,64,640]{2,1,0:T(8,128)(2,1)}, bf16[2,64,640]{2,1,0:T(8,128)(2,1)}, u32[]{:S(2)}, u32[]{:S(2)}) collective-permute-start(bf16[2,64,640]{2,1,0:T(8,128)(2,1)} %gather_fusion.2), channel_id=1, source_target_pairs={{0,1},{1,2},{2,3},{3,4},{4,5},{5,6},{6,7},{7,8},{8,9},{9,10},{10,1... | collective-permute-start | bytes 491528 | tf_op jit(solution)/shard_map/ppermute | solution.py:36
  47.9 33.7 %collective-permute-start.3 = (bf16[2,64,640]{2,1,0:T(8,128)(2,1)}, bf16[2,64,640]{2,1,0:T(8,128)(2,1)}, u32[]{:S(2)}, u32[]{:S(2)}) collective-permute-start(bf16[2,64,640]{2,1,0:T(8,128)(2,1)} %gather_fusion.1), channel_id=1, source_target_pairs={{0,127},{1,0},{2,1},{3,2},{4,3},{5,4},{6,5},{7,6},{8,7},{9,8},{10,... | collective-permute-start | bytes 491528 | tf_op jit(solution)/shard_map/ppermute | solution.py:36
  51.2 30.4 %collective-permute-start.2 = (bf16[2,64,640]{2,1,0:T(8,128)(2,1)}, bf16[2,64,640]{2,1,0:T(8,128)(2,1)}, u32[]{:S(2)}, u32[]{:S(2)}) collective-permute-start(bf16[2,64,640]{2,1,0:T(8,128)(2,1)} %gather_fusion), channel_id=1, source_target_pairs={{0,126},{1,127},{2,0},{3,1},{4,2},{5,3},{6,4},{7,5},{8,6},{9,7},{1... | collective-permute-start | bytes 491528 | tf_op jit(solution)/shard_map/ppermute | solution.py:36
  79.8 6.6 %collective-permute-start.1 = (f32[24,1920]{1,0:T(8,128)}, f32[24,1920]{1,0:T(8,128)}, u32[]{:S(2)}, u32[]{:S(2)}) collective-permute-start(f32[24,1920]{1,0:T(8,128)} %select_bitcast_fusion), channel_id=1, source_target_pairs={{0,128},{128,0},{1,129},{129,1},{2,130},{130,2},{3,131},{131,3},{4... | collective-permute-start | bytes 552968 | tf_op jit(solution)/shard_map/ppermute | solution.py:30
  86.5 4.4 %copy-start.3 = (bf16[512,320]{0,1:T(8,128)(2,1)S(1)}, bf16[512,320]{0,1:T(8,128)(2,1)}, u32[]{:S(2)}) copy-start(bf16[512,320]{0,1:T(8,128)(2,1)} %copy.48) | copy-start | bytes 983044
  88.3 3.3 %copy-start.4 = (f32[24,2944]{1,0:T(8,128)S(1)}, f32[24,2944]{1,0:T(8,128)}, u32[]{:S(2)}) copy-start(f32[24,2944]{1,0:T(8,128)} %slice.87) | copy-start | bytes 847876
  90.8 2.4 %copy-start.1 = (bf16[2944,320]{0,1:T(8,128)(2,1)S(1)}, bf16[2944,320]{0,1:T(8,128)(2,1)}, u32[]{:S(2)}) copy-start(bf16[2944,320]{0,1:T(8,128)(2,1)} %copy.49) | copy-start | bytes 5652484
  93.2 4.0 %copy-start.5 = (bf16[512,320]{0,1:T(8,128)(2,1)S(1)}, bf16[512,320]{0,1:T(8,128)(2,1)}, u32[]{:S(2)}) copy-start(bf16[512,320]{0,1:T(8,128)(2,1)} %copy.50) | copy-start | bytes 983044
  97.2 11.3 %copy-start.2 = (bf16[1,24,2048]{2,1,0:T(8,128)(2,1)S(1)}, bf16[1,24,2048]{2,1,0:T(8,128)(2,1)}, u32[]{:S(2)}) copy-start(bf16[1,24,2048]{2,1,0:T(8,128)(2,1)} %param.10) | copy-start | bytes 294916
  97.2 11.4 %copy-start.6 = (f32[2048]{0:T(1024)S(1)}, f32[2048]{0:T(1024)}, u32[]{:S(2)}) copy-start(f32[2048]{0:T(1024)} %param.14) | copy-start | bytes 24580
  98.2 4.7 %collective-permute-start.6 = (bf16[24,1280]{1,0:T(8,128)(2,1)S(1)}, bf16[24,1280]{1,0:T(8,128)(2,1)S(1)}, u32[]{:S(2)}, u32[]{:S(2)}) collective-permute-start(bf16[24,1280]{1,0:T(8,128)(2,1)S(1)} %convert_element_type.103), channel_id=1, source_target_pairs={{0,128},{128,0},{1,129},{129,1},{2,130},{130,2},{3,131},{131,3},{4... | collective-permute-start | bytes 184328 | tf_op jit(solution)/shard_map/ppermute | solution.py:30
  103.4 5.1 %collective-permute-start.7 = (bf16[24,2048]{1,0:T(8,128)(2,1)S(1)}, bf16[24,2048]{1,0:T(8,128)(2,1)S(1)}, u32[]{:S(2)}, u32[]{:S(2)}) collective-permute-start(bf16[24,2048]{1,0:T(8,128)(2,1)S(1)} %fusion.48), channel_id=1, source_target_pairs={{0,128},{128,0},{1,129},{129,1},{2,130},{130,2},{3,131},{131,3},{4... | collective-permute-start | bytes 294920 | tf_op jit(solution)/shard_map/ppermute | solution.py:30
  108.8 4.6 %collective-permute-start.10 = (bf16[24,2048]{1,0:T(8,128)(2,1)S(1)}, bf16[24,2048]{1,0:T(8,128)(2,1)S(1)}, u32[]{:S(2)}, u32[]{:S(2)}) collective-permute-start(bf16[24,2048]{1,0:T(8,128)(2,1)S(1)} %multiply_convert_fusion), channel_id=1, source_target_pairs={{0,64},{192,128},{1,65},{193,129},{2,66},{194,130},{3,67},{195,131... | collective-permute-start | bytes 294920 | tf_op jit(solution)/shard_map/ppermute | solution.py:211
  111.3 6.9 %collective-permute-start.8 = (bf16[24,2048]{1,0:T(8,128)(2,1)S(1)}, bf16[24,2048]{1,0:T(8,128)(2,1)S(1)}, u32[]{:S(2)}, u32[]{:S(2)}) collective-permute-start(bf16[24,2048]{1,0:T(8,128)(2,1)S(1)} %multiply_convert_fusion), channel_id=1, source_target_pairs={{128,0},{64,192},{129,1},{65,193},{130,2},{66,194},{131,3},{67,195... | collective-permute-start | bytes 294920 | tf_op jit(solution)/shard_map/ppermute | solution.py:213
  112.6 5.6 %collective-permute-start.9 = (bf16[24,2048]{1,0:T(8,128)(2,1)S(1)}, bf16[24,2048]{1,0:T(8,128)(2,1)S(1)}, u32[]{:S(2)}, u32[]{:S(2)}) collective-permute-start(bf16[24,2048]{1,0:T(8,128)(2,1)S(1)} %multiply_convert_fusion), channel_id=1, source_target_pairs={{128,64},{64,128},{129,65},{65,129},{130,66},{66,130},{131,67},{67... | collective-permute-start | bytes 294920 | tf_op jit(solution)/shard_map/ppermute | solution.py:212
  128.8 75.4 %all-gather.8.cloned.1.call-start = ((), (), s32[]{:S(2)}) async-start(), calls=%async_computation.1 | async-start | bytes 9437184 | tf_op jit(solution)/shard_map/all_gather | solution.py:222
Sparse Core Ops, SparseCore 0:
  128.9 51.7 all-gather.5
  182.5 21.6 all-gather.7

commit v6 on v5

--- a/solution.py
+++ b/solution.py
@@ -144,15 +144,18 @@
     old_owner = jnp.sum(jnp.where(matches, listing[None, :, 1], 0), axis=1)
     distance = jnp.remainder(device - old_owner, devices)
     slot_of = jnp.where(distance <= HOP, HOP + distance - 1, HOP - (devices - distance))
-    arrivals = []
-    for number in range(slots):
-        offset = offsets[number]
-        holding = (listing[:, 1] == device) & (
-            listing[:, 2] == jnp.remainder(device + offset, devices)
-        )
-        held_request = listing[jnp.argmax(holding), 0]
-        pages_sent = pool[tables[held_request, :MIGP]]
-        arrivals.append(shifted(pages_sent, REQ, offset))
+    targets = jnp.remainder(device + jnp.array(offsets, jnp.int32), devices)
+    holding = (listing[None, :, 1] == device) & (listing[None, :, 2] == targets[:, None])
+    held_request = jnp.sum(jnp.where(holding, listing[None, :, 0], 0), axis=1)
+    request_hit = jnp.arange(tables.shape[0], dtype=jnp.int32)[None, :] == held_request[:, None]
+    sent_ids = jnp.sum(jnp.where(request_hit[:, :, None], tables[None, :, :MIGP], 0), axis=1)
+    page_hit = (
+        sent_ids[:, :, None] == jnp.arange(pool_pages, dtype=jnp.int32)[None, None, :]
+    ).astype(jnp.bfloat16)
+    pages_sent = jnp.einsum(
+        "smp,pwc->smwc", page_hit, pool, preferred_element_type=jnp.float32
+    ).astype(jnp.bfloat16)
+    arrivals = [shifted(pages_sent[number], REQ, offsets[number]) for number in range(slots)]
     arrived = jnp.concatenate(arrivals, axis=0)
     page_column = jnp.minimum(jnp.arange(MAXP, dtype=jnp.int32), MIGP - 1)
     moved_pages = pool_pages + slot_of[:, None] * MIGP + page_column[None, :]

time: 218 us -> 193 us (0.89)
  between operations: 28.9 us -> 13.8 us
  local copies, waits for them, and re-layouts: 37.5 us -> 24.8 us
  matrix products: 18.7 us -> 23.9 us
    gather x4 -> x0, local copies, waits for them, and re-layouts: 13.2 us -> none  [body(): pages_sent = pool[tables[held_request, :MIGP]]]
    dot_general x0 -> x1, matrix products: none -> 5.17 us  [body(): jnp.einsum('smp,pwc->smwc', page_hit, pool, preferred_element_type=jnp.fl...]
    another operation x4 -> x0, other arithmetic: 2.78 us -> none  [body(): held_request = listing[jnp.argmax(holding), 0]]
    unnamed x19 -> x31, local copies, waits for them, and re-layouts: 11.7 us -> 14.4 us
    dynamic_slice x2 -> x0, local copies, waits for them, and re-layouts: 2.46 us -> none  [the longest x1 1.48 us: body(): held_request = listing[jnp.argmax(holding), 0]]
    slice x1, local copies, waits for them, and re-layouts: 5.71 us -> 3.42 us  [dense_scores(): key_rows = flat[:, :half_width].reshape(count, KVH, HD)]
  transfers between devices with their start and end apart: 13 -> 13, of which waited for: 5 -> 5; matrix products, arithmetic and copies ran while one was open for 22% -> 20% of each run, Pallas kernels for 0% -> 0%
where the time goes in v6:
time: 193 us; the launch traced here: 192 us
  waiting for transfers between devices  87.1 us (45%)
  local copies, waits for them, and re-layouts  24.8 us (13%)
  matrix products  23.9 us (12%)
  starting transfers between devices  21.9 us (11%)
  between operations  13.8 us (7%)
  other arithmetic  10.5 us (5%)
  blocking collectives  10.4 us (5%)
    all_gather x1, waiting for transfers between devices, body(): gathered = lax.all_gather(gathered, 'z', axis=1, tiled=False)  51.8 us
    all_gather x1, waiting for transfers between devices, body(): gathered = lax.all_gather(gathered, 'core', axis=2, tiled=False)  23.5 us
    unnamed x31, local copies, waits for them, and re-layouts  14.4 us
    all_gather x1, blocking collectives, body(): gathered = lax.all_gather(combined, 'y', axis=0, tiled=False)  10.4 us
    ppermute x4, starting transfers between devices, shifted(): return lax.ppermute(value, axis, pairs)  9.02 us
    ppermute x4, starting transfers between devices, from_partner(): return lax.ppermute(block, axis, route)  8.18 us
    ppermute x4, waiting for transfers between devices, from_partner(): return lax.ppermute(block, axis, route)  6.8 us
    dot_general x1, matrix products, body(): jnp.einsum('yzcrd,dv->yzcrv', gathered, w_vocab, preferred_element_type=j...  6.03 us
  transfers between devices with their start and end apart: 13, of which 5 were waited for; matrix products, arithmetic and copies ran while one was open for 20% of the time, Pallas kernels for 0%

profile of v6, /device:TPU:1, one launch (start us, length us, event | category | flops | bytes accessed | tf_op | source)
XLA Modules:
  0.0 192.4 jit_solution(14110515030179904760)
XLA Ops:
  8.7 3.7 %collective-permute-start = (bf16[24,2048]{1,0:T(8,128)(2,1)S(1)}, bf16[24,2048]{1,0:T(8,128)(2,1)}, u32[]{:S(2)}, u32[]{:S(2)}) collective-permute-start(bf16[24,2048]{1,0:T(8,128)(2,1)S(1)} %fusion.47), channel_id=1, source_target_pairs={{0,128},{128,0},{1,129},{129,1},{2,130},{130,2},{3,131},{131,3},{4... | collective-permute-start | bytes 294920 | tf_op jit(solution)/shard_map/ppermute | solution.py:30
  15.1 5.2 %fusion.18 = bf16[4,2,64,640]{3,0,2,1:T(4,128)(2,1)S(1)} fusion(bf16[46,64,640]{2,1,0:T(8,128)(2,1)} %bitcast.156, s32[4,2]{0,1:T(2,128)S(1)} %select_reduce_fusion), kind=kOutput, calls=%fused_computation.21 | convolution fusion | flops 30474608 | bytes 4423712 | tf_op jit(solution)/shard_map/smp,pwc->smwc/dot_general | solution.py:155
  22.0 1.6 collective-permute-start.5
  24.3 2.8 %collective-permute-start.4 = (bf16[2,64,640]{2,1,0:T(8,128)(2,1)}, bf16[2,64,640]{2,1,0:T(8,128)(2,1)}, u32[]{:S(2)}, u32[]{:S(2)}) collective-permute-start(bf16[2,64,640]{2,1,0:T(8,128)(2,1)} %bitcast.152), channel_id=1, source_target_pairs={{0,1},{1,2},{2,3},{3,4},{4,5},{5,6},{6,7},{7,8},{8,9},{9,10},{10,1... | collective-permute-start | bytes 491528 | tf_op jit(solution)/shard_map/ppermute | solution.py:36
  28.4 4.6 %collective-permute-start.2 = (bf16[2,64,640]{2,1,0:T(8,128)(2,1)}, bf16[2,64,640]{2,1,0:T(8,128)(2,1)}, u32[]{:S(2)}, u32[]{:S(2)}) collective-permute-start(bf16[2,64,640]{2,1,0:T(8,128)(2,1)} %bitcast.154), channel_id=1, source_target_pairs={{0,126},{1,127},{2,0},{3,1},{4,2},{5,3},{6,4},{7,5},{8,6},{9,7},{1... | collective-permute-start | bytes 491528 | tf_op jit(solution)/shard_map/ppermute | solution.py:36
  33.2 3.4 %fusion.88 = (bf16[2944,320]{1,0:T(8,128)(2,1)}, bf16[2944,320]{1,0:T(8,128)(2,1)}) fusion(bf16[2944,640]{1,0:T(8,128)(2,1)S(1)} %bitcast.157), kind=kLoop, calls=%fused_computation.140 | loop fusion | bytes 7536640 | tf_op jit(solution)/shard_map/slice | solution.py:83
  43.3 4.1 %copy.102 = bf16[2944,320]{0,1:T(8,128)(2,1)} copy(bf16[2944,320]{1,0:T(8,128)(2,1)} %get-tuple-element.10) | data formatting | bytes 3768320
  47.4 4.1 %copy.100 = bf16[2944,320]{0,1:T(8,128)(2,1)} copy(bf16[2944,320]{1,0:T(8,128)(2,1)} %get-tuple-element.9) | data formatting | bytes 3768320
  51.5 2.9 %fusion.7 = f32[2,24,1920]{2,1,0:T(8,128)S(1)} fusion(bf16[1024,1920]{1,0:T(8,128)(2,1)} %param.13, s32[]{:T(128)S(6)} %select_n.145, bf16[1,24,2048]{2,1,0:T(8,128)(2,1)} %bitcast.1, bf16[1,24,2048]{2,1,0:T(8,128)(2,1)S(1)} %fusion.49, pred[]{:T(512)S(6)} %eq.101), kind=kOutput, calls=%fused_computation.11 | convolution fusion | flops 189186048 | bytes 4497413 | tf_op jit(solution)/shard_map/grd,df->grf/dot_general | solution.py:123
  55.1 1.7 collective-permute-start.1
  58.9 1.9 copy.101
  63.5 2.6 %bitcast_reduce_fusion = (f32[24,5,4]{0,2,1:T(4,128)S(1)}, f32[5,24,4,2944]{3,1,2,0:T(8,128)S(1)}) fusion(pred[24,2944]{1,0:T(8,128)(4,1)S(1)} %broadcast_compare_fusion, bf16[2944,5,64,1]{0,2,3,1:T(8,128)(2,1)} %bitcast.158, bf16[24,5,4,64]{3,2,1,0:T(4,128)(2,1)S(1)} %reshape.239), kind=kOutput, calls=%fused_computation.1 | convolution fusion | flops 185118240 | bytes 7670656 | tf_op jit(solution)/shard_map/rkgd,tkd->rkgt/dot_general | solution.py:85
  66.9 1.6 multiply_reduce_fusion
  68.5 4.0 %fusion.28 = f32[24,5,4,64]{3,0,2,1:T(8,128)S(1)} fusion(bf16[2944,5,64,1]{0,2,3,1:T(8,128)(2,1)S(1)} %bitcast.161, f32[5,24,4,2944]{3,1,2,0:T(8,128)S(1)} %get-tuple-element.23, f32[24,2944]{1,0:T(8,128)S(1)} %copy-done.5, f32[24,5,4]{0,2,1:T(4,128)S(1)} %get-tuple-element.8, pred[24,2944]{1,0:T(8,128)(4,1)S(1)} %broadcast_compare_fusion, ...), kind=kOutput, calls=%fused_computation.29 | convolution fusion | flops 1093816320 | bytes 8047360 | tf_op jit(solution)/shard_map/rkgt,tkd->rkgd/dot_general | solution.py:191
  73.4 1.4 collective-permute-start.6
  75.0 3.1 %collective-permute-done.6 = bf16[24,1280]{1,0:T(8,128)(2,1)S(1)} collective-permute-done((bf16[24,1280]{1,0:T(8,128)(2,1)S(1)}, bf16[24,1280]{1,0:T(8,128)(2,1)S(1)}, u32[]{:S(2)}, u32[]{:S(2)}) %collective-permute-start.6) | collective-permute-done | bytes 61472 | tf_op jit(solution)/shard_map/ppermute | solution.py:30
  78.7 1.4 collective-permute-start.7
  80.1 3.7 %collective-permute-done.7 = bf16[24,2048]{1,0:T(8,128)(2,1)S(1)} collective-permute-done((bf16[24,2048]{1,0:T(8,128)(2,1)S(1)}, bf16[24,2048]{1,0:T(8,128)(2,1)S(1)}, u32[]{:S(2)}, u32[]{:S(2)}) %collective-permute-start.7) | collective-permute-done | bytes 98336 | tf_op jit(solution)/shard_map/ppermute | solution.py:30
  84.0 2.7 %collective-permute-start.10 = (bf16[24,2048]{1,0:T(8,128)(2,1)S(1)}, bf16[24,2048]{1,0:T(8,128)(2,1)S(1)}, u32[]{:S(2)}, u32[]{:S(2)}) collective-permute-start(bf16[24,2048]{1,0:T(8,128)(2,1)S(1)} %multiply_convert_fusion), channel_id=1, source_target_pairs={{0,64},{192,128},{1,65},{193,129},{2,66},{194,130},{3,67},{195,131... | collective-permute-start | bytes 294920 | tf_op jit(solution)/shard_map/ppermute | solution.py:214
  88.7 4.9 %collective-permute-done.8 = bf16[24,2048]{1,0:T(8,128)(2,1)S(1)} collective-permute-done((bf16[24,2048]{1,0:T(8,128)(2,1)S(1)}, bf16[24,2048]{1,0:T(8,128)(2,1)S(1)}, u32[]{:S(2)}, u32[]{:S(2)}) %collective-permute-start.8) | collective-permute-done | bytes 98336 | tf_op jit(solution)/shard_map/ppermute | solution.py:216
  93.7 10.4 %all-gather = bf16[96,2048]{1,0:T(8,128)(2,1)} all-gather(bf16[24,2048]{1,0:T(8,128)(2,1)S(1)} %fusion.44), channel_id=2, replica_groups=mesh['guide'=2,'x_lo'=2,'y'=4,'z'=8,'core'=2] {'y'}, dimensions={0}, use_global_device_ids=true | all-gather | bytes 491520 | tf_op jit(solution)/shard_map/all_gather | solution.py:223
  104.2 51.8 %all-gather.6.cloned.1.call-done = bf16[4,192,2048]{2,1,0:T(8,128)(2,1)} async-done(((bf16[4,24,2048]{2,1,0:T(8,128)(2,1)}), bf16[4,192,2048]{2,1,0:T(8,128)(2,1)}) %all-gather.6.cloned.1.call-update) | async-done | bytes 3145744 | tf_op jit(solution)/shard_map/all_gather | solution.py:224
  156.0 23.5 %all-gather.8.cloned.1.call-done = bf16[4,8,48,2048]{3,2,1,0:T(8,128)(2,1)} async-done(((bf16[4,8,24,2048]{3,2,1,0:T(8,128)(2,1)}), bf16[4,8,48,2048]{3,2,1,0:T(8,128)(2,1)}) %all-gather.8.cloned.1.call-update) | async-done | bytes 6291472 | tf_op jit(solution)/shard_map/all_gather | solution.py:225
  179.5 6.0 %fusion.32 = f32[4,8,2,24,250]{4,3,2,1,0:T(8,128)} fusion(bf16[4,8,2,24,2048]{4,3,2,1,0:T(8,128)(2,1)} %bitcast.169, bf16[2048,250]{1,0:T(8,128)(2,1)} %param.16), kind=kOutput, calls=%fused_computation.31 | convolution fusion | flops 1572864000 | bytes 8851456 | tf_op jit(solution)/shard_map/yzcrd,dv->yzcrv/dot_general | solution.py:226
  (97 shorter events, 25.6 us)
Async XLA Ops:
  6.5 71.6 %copy-start = (bf16[640,2048]{1,0:T(8,128)(2,1)S(1)}, bf16[640,2048]{1,0:T(8,128)(2,1)}, u32[]{:S(2)}) copy-start(bf16[640,2048]{1,0:T(8,128)(2,1)} %param.14) | copy-start | bytes 7864324
  6.5 149.5 %all-gather.6.cloned.1.call-start = ((), (), s32[]{:S(2)}) async-start(), calls=%async_computation | async-start | bytes 3538944 | tf_op jit(solution)/shard_map/all_gather | solution.py:224
  8.7 42.7 %collective-permute-start = (bf16[24,2048]{1,0:T(8,128)(2,1)S(1)}, bf16[24,2048]{1,0:T(8,128)(2,1)}, u32[]{:S(2)}, u32[]{:S(2)}) collective-permute-start(bf16[24,2048]{1,0:T(8,128)(2,1)S(1)} %fusion.47), channel_id=1, source_target_pairs={{0,128},{128,0},{1,129},{129,1},{2,130},{130,2},{3,131},{131,3},{4... | collective-permute-start | bytes 294920 | tf_op jit(solution)/shard_map/ppermute | solution.py:30
  15.1 18.0 %copy-start.3 = (bf16[1,24,2048]{2,1,0:T(8,128)(2,1)S(1)}, bf16[1,24,2048]{2,1,0:T(8,128)(2,1)}, u32[]{:S(2)}) copy-start(bf16[1,24,2048]{2,1,0:T(8,128)(2,1)} %param.11) | copy-start | bytes 294916
  15.1 18.0 %copy-start.10 = (f32[2048]{0:T(1024)S(1)}, f32[2048]{0:T(1024)}, u32[]{:S(2)}) copy-start(f32[2048]{0:T(1024)} %param.12) | copy-start | bytes 24580
  15.1 18.1 %copy-start.1 = (bf16[1,46,64,640]{3,2,1,0:T(8,128)(2,1)S(1)}, bf16[1,46,64,640]{3,2,1,0:T(8,128)(2,1)}, u32[]{:S(2)}) copy-start(bf16[1,46,64,640]{3,2,1,0:T(8,128)(2,1)} %param.17) | copy-start | bytes 11304964
  22.0 34.8 %collective-permute-start.5 = (bf16[2,64,640]{2,1,0:T(8,128)(2,1)}, bf16[2,64,640]{2,1,0:T(8,128)(2,1)S(1)}, u32[]{:S(2)}, u32[]{:S(2)}) collective-permute-start(bf16[2,64,640]{2,1,0:T(8,128)(2,1)} %bitcast.151), channel_id=1, source_target_pairs={{0,2},{1,3},{2,4},{3,5},{4,6},{5,7},{6,8},{7,9},{8,10},{9,11},{10,... | collective-permute-start | bytes 491528 | tf_op jit(solution)/shard_map/ppermute | solution.py:36
  24.3 32.5 %collective-permute-start.4 = (bf16[2,64,640]{2,1,0:T(8,128)(2,1)}, bf16[2,64,640]{2,1,0:T(8,128)(2,1)}, u32[]{:S(2)}, u32[]{:S(2)}) collective-permute-start(bf16[2,64,640]{2,1,0:T(8,128)(2,1)} %bitcast.152), channel_id=1, source_target_pairs={{0,1},{1,2},{2,3},{3,4},{4,5},{5,6},{6,7},{7,8},{8,9},{9,10},{10,1... | collective-permute-start | bytes 491528 | tf_op jit(solution)/shard_map/ppermute | solution.py:36
  27.7 29.1 %collective-permute-start.3 = (bf16[2,64,640]{2,1,0:T(8,128)(2,1)}, bf16[2,64,640]{2,1,0:T(8,128)(2,1)}, u32[]{:S(2)}, u32[]{:S(2)}) collective-permute-start(bf16[2,64,640]{2,1,0:T(8,128)(2,1)} %bitcast.153), channel_id=1, source_target_pairs={{0,127},{1,0},{2,1},{3,2},{4,3},{5,4},{6,5},{7,6},{8,7},{9,8},{10,... | collective-permute-start | bytes 491528 | tf_op jit(solution)/shard_map/ppermute | solution.py:36
  28.4 28.4 %collective-permute-start.2 = (bf16[2,64,640]{2,1,0:T(8,128)(2,1)}, bf16[2,64,640]{2,1,0:T(8,128)(2,1)}, u32[]{:S(2)}, u32[]{:S(2)}) collective-permute-start(bf16[2,64,640]{2,1,0:T(8,128)(2,1)} %bitcast.154), channel_id=1, source_target_pairs={{0,126},{1,127},{2,0},{3,1},{4,2},{5,3},{6,4},{7,5},{8,6},{9,7},{1... | collective-permute-start | bytes 491528 | tf_op jit(solution)/shard_map/ppermute | solution.py:36
  55.1 6.6 %collective-permute-start.1 = (f32[24,1920]{1,0:T(8,128)}, f32[24,1920]{1,0:T(8,128)}, u32[]{:S(2)}, u32[]{:S(2)}) collective-permute-start(f32[24,1920]{1,0:T(8,128)} %select_bitcast_fusion), channel_id=1, source_target_pairs={{0,128},{128,0},{1,129},{129,1},{2,130},{130,2},{3,131},{131,3},{4... | collective-permute-start | bytes 552968 | tf_op jit(solution)/shard_map/ppermute | solution.py:30
  63.5 2.6 %copy-start.4 = (bf16[512,320]{0,1:T(8,128)(2,1)S(1)}, bf16[512,320]{0,1:T(8,128)(2,1)}, u32[]{:S(2)}) copy-start(bf16[512,320]{0,1:T(8,128)(2,1)} %copy.101) | copy-start | bytes 983044
  63.5 2.6 %copy-start.8 = (pred[24,512]{1,0:T(8,128)(4,1)S(1)}, pred[24,512]{1,0:T(8,128)(4,1)}, u32[]{:S(2)}) copy-start(pred[24,512]{1,0:T(8,128)(4,1)} %broadcast_compare_fusion.1) | copy-start | bytes 36868
  63.5 3.0 %copy-start.7 = (f32[24,512]{1,0:T(8,128)S(1)}, f32[24,512]{1,0:T(8,128)}, u32[]{:S(2)}) copy-start(f32[24,512]{1,0:T(8,128)} %slice.96) | copy-start | bytes 147460
  63.5 3.4 %copy-start.5 = (f32[24,2944]{1,0:T(8,128)S(1)}, f32[24,2944]{1,0:T(8,128)}, u32[]{:S(2)}) copy-start(f32[24,2944]{1,0:T(8,128)} %slice.94) | copy-start | bytes 847876
  66.5 2.0 %copy-start.2 = (bf16[2944,320]{0,1:T(8,128)(2,1)S(1)}, bf16[2944,320]{0,1:T(8,128)(2,1)}, u32[]{:S(2)}) copy-start(bf16[2944,320]{0,1:T(8,128)(2,1)} %copy.102) | copy-start | bytes 5652484
  68.5 4.0 %copy-start.6 = (bf16[512,320]{0,1:T(8,128)(2,1)S(1)}, bf16[512,320]{0,1:T(8,128)(2,1)}, u32[]{:S(2)}) copy-start(bf16[512,320]{0,1:T(8,128)(2,1)} %copy.103) | copy-start | bytes 983044
  72.5 11.4 %copy-start.9 = (f32[2048]{0:T(1024)S(1)}, f32[2048]{0:T(1024)}, u32[]{:S(2)}) copy-start(f32[2048]{0:T(1024)} %param.15) | copy-start | bytes 24580
  73.4 4.7 %collective-permute-start.6 = (bf16[24,1280]{1,0:T(8,128)(2,1)S(1)}, bf16[24,1280]{1,0:T(8,128)(2,1)S(1)}, u32[]{:S(2)}, u32[]{:S(2)}) collective-permute-start(bf16[24,1280]{1,0:T(8,128)(2,1)S(1)} %convert_element_type.108), channel_id=1, source_target_pairs={{0,128},{128,0},{1,129},{129,1},{2,130},{130,2},{3,131},{131,3},{4... | collective-permute-start | bytes 184328 | tf_op jit(solution)/shard_map/ppermute | solution.py:30
  78.7 5.1 %collective-permute-start.7 = (bf16[24,2048]{1,0:T(8,128)(2,1)S(1)}, bf16[24,2048]{1,0:T(8,128)(2,1)S(1)}, u32[]{:S(2)}, u32[]{:S(2)}) collective-permute-start(bf16[24,2048]{1,0:T(8,128)(2,1)S(1)} %fusion.54), channel_id=1, source_target_pairs={{0,128},{128,0},{1,129},{129,1},{2,130},{130,2},{3,131},{131,3},{4... | collective-permute-start | bytes 294920 | tf_op jit(solution)/shard_map/ppermute | solution.py:30
  84.0 4.7 %collective-permute-start.10 = (bf16[24,2048]{1,0:T(8,128)(2,1)S(1)}, bf16[24,2048]{1,0:T(8,128)(2,1)S(1)}, u32[]{:S(2)}, u32[]{:S(2)}) collective-permute-start(bf16[24,2048]{1,0:T(8,128)(2,1)S(1)} %multiply_convert_fusion), channel_id=1, source_target_pairs={{0,64},{192,128},{1,65},{193,129},{2,66},{194,130},{3,67},{195,131... | collective-permute-start | bytes 294920 | tf_op jit(solution)/shard_map/ppermute | solution.py:214
  86.7 6.9 %collective-permute-start.8 = (bf16[24,2048]{1,0:T(8,128)(2,1)S(1)}, bf16[24,2048]{1,0:T(8,128)(2,1)S(1)}, u32[]{:S(2)}, u32[]{:S(2)}) collective-permute-start(bf16[24,2048]{1,0:T(8,128)(2,1)S(1)} %multiply_convert_fusion), channel_id=1, source_target_pairs={{128,0},{64,192},{129,1},{65,193},{130,2},{66,194},{131,3},{67,195... | collective-permute-start | bytes 294920 | tf_op jit(solution)/shard_map/ppermute | solution.py:216
  88.0 5.6 %collective-permute-start.9 = (bf16[24,2048]{1,0:T(8,128)(2,1)S(1)}, bf16[24,2048]{1,0:T(8,128)(2,1)S(1)}, u32[]{:S(2)}, u32[]{:S(2)}) collective-permute-start(bf16[24,2048]{1,0:T(8,128)(2,1)S(1)} %multiply_convert_fusion), channel_id=1, source_target_pairs={{128,64},{64,128},{129,65},{65,129},{130,66},{66,130},{131,67},{67... | collective-permute-start | bytes 294920 | tf_op jit(solution)/shard_map/ppermute | solution.py:215
  104.1 75.4 %all-gather.8.cloned.1.call-start = ((), (), s32[]{:S(2)}) async-start(), calls=%async_computation.1 | async-start | bytes 9437184 | tf_op jit(solution)/shard_map/all_gather | solution.py:225
Sparse Core Ops, SparseCore 0:
  104.2 51.7 all-gather.5
  157.8 21.6 all-gather.7

commit v7 on v6

--- a/solution.py
+++ b/solution.py
@@ -222,9 +222,16 @@
     combined = (uncond + guidance * (cond - uncond)).astype(jnp.bfloat16)
     gathered = lax.all_gather(combined, "y", axis=0, tiled=False)
     gathered = lax.all_gather(gathered, "z", axis=1, tiled=False)
-    gathered = lax.all_gather(gathered, "core", axis=2, tiled=False)
-    logits = jnp.einsum(
-        "yzcrd,dv->yzcrv", gathered, w_vocab, preferred_element_type=jnp.float32
+    core = lax.axis_index("core")
+    twin = lax.ppermute(gathered, "core", [(0, 1), (1, 0)])
+    mine_logits = jnp.einsum("yzrd,dv->yzrv", gathered, w_vocab, preferred_element_type=jnp.float32)
+    twin_logits = jnp.einsum("yzrd,dv->yzrv", twin, w_vocab, preferred_element_type=jnp.float32)
+    logits = jnp.stack(
+        [
+            jnp.where(core == 0, mine_logits, twin_logits),
+            jnp.where(core == 0, twin_logits, mine_logits),
+        ],
+        axis=2,
     )
     return logits.reshape(-1, logits.shape[-1])
 

time: 193 us -> 174 us (0.902)
  waiting for transfers between devices: 87.1 us -> 66 us
    all_gather x1 -> x0, waiting for transfers between devices: 23.5 us -> none  [body(): gathered = lax.all_gather(gathered, 'core', axis=2, tiled=False)]
    ppermute x0 -> x1, waiting for transfers between devices: none -> 2.38 us  [body(): twin = lax.ppermute(gathered, 'core', [(0, 1), (1, 0)])]
    dot_general x1 -> x2, matrix products: 6.03 us -> 6.15 us  [the longest x1 3.24 us: body(): jnp.einsum('yzrd,dv->yzrv', gathered, w_vocab, preferred_element_type=jnp...]
    unnamed x31 -> x33, local copies, waits for them, and re-layouts: 14.4 us -> 14.4 us
  transfers between devices with their start and end apart: 13 -> 13, of which waited for: 5 -> 5; matrix products, arithmetic and copies ran while one was open for 20% -> 24% of each run, Pallas kernels for 0% -> 0%
where the time goes in v7:
time: 174 us
  waiting for transfers between devices  66 us (38%)
  local copies, waits for them, and re-layouts  26.2 us (15%)
  matrix products  24 us (14%)
  starting transfers between devices  22.8 us (13%)
  between operations  13.8 us (8%)
  other arithmetic  10.6 us (6%)
  blocking collectives  10.4 us (6%)
    all_gather x1, waiting for transfers between devices, body(): gathered = lax.all_gather(gathered, 'z', axis=1, tiled=False)  51.9 us
    unnamed x33, local copies, waits for them, and re-layouts  14.4 us
    all_gather x1, blocking collectives, body(): gathered = lax.all_gather(combined, 'y', axis=0, tiled=False)  10.4 us
    ppermute x4, starting transfers between devices, shifted(): return lax.ppermute(value, axis, pairs)  9.02 us
    ppermute x4, starting transfers between devices, from_partner(): return lax.ppermute(block, axis, route)  8.18 us
    ppermute x4, waiting for transfers between devices, from_partner(): return lax.ppermute(block, axis, route)  6.8 us
    dot_general x1, matrix products, body(): jnp.einsum('smp,pwc->smwc', page_hit, pool, preferred_element_type=jnp.fl...  5.17 us
    ppermute x1, waiting for transfers between devices, body(): from_guide = lax.ppermute(final, pair, [(2, 0), (1, 3)])  4.88 us
  transfers between devices with their start and end apart: 13, of which 5 were waited for; matrix products, arithmetic and copies ran while one was open for 24% of the time, Pallas kernels for 0%

profile of v7, /device:TPU:1, one launch (start us, length us, event | category | flops | bytes accessed | tf_op | source)
XLA Modules:
  0.0 173.8 jit_solution(7484438789204227571)
XLA Ops:
  8.7 3.7 %collective-permute-start = (bf16[24,2048]{1,0:T(8,128)(2,1)S(1)}, bf16[24,2048]{1,0:T(8,128)(2,1)}, u32[]{:S(2)}, u32[]{:S(2)}) collective-permute-start(bf16[24,2048]{1,0:T(8,128)(2,1)S(1)} %fusion.49), channel_id=1, source_target_pairs={{0,128},{128,0},{1,129},{129,1},{2,130},{130,2},{3,131},{131,3},{4... | collective-permute-start | bytes 294920 | tf_op jit(solution)/shard_map/ppermute | solution.py:30
  15.1 5.2 %fusion.18 = bf16[4,2,64,640]{3,0,2,1:T(4,128)(2,1)S(1)} fusion(bf16[46,64,640]{2,1,0:T(8,128)(2,1)} %bitcast.164, s32[4,2]{0,1:T(2,128)S(1)} %select_reduce_fusion), kind=kOutput, calls=%fused_computation.22 | convolution fusion | flops 30474608 | bytes 4423712 | tf_op jit(solution)/shard_map/smp,pwc->smwc/dot_general | solution.py:155
  22.0 1.6 collective-permute-start.5
  24.3 2.8 %collective-permute-start.4 = (bf16[2,64,640]{2,1,0:T(8,128)(2,1)}, bf16[2,64,640]{2,1,0:T(8,128)(2,1)}, u32[]{:S(2)}, u32[]{:S(2)}) collective-permute-start(bf16[2,64,640]{2,1,0:T(8,128)(2,1)} %bitcast.160), channel_id=1, source_target_pairs={{0,1},{1,2},{2,3},{3,4},{4,5},{5,6},{6,7},{7,8},{8,9},{9,10},{10,1... | collective-permute-start | bytes 491528 | tf_op jit(solution)/shard_map/ppermute | solution.py:36
  28.4 4.6 %collective-permute-start.2 = (bf16[2,64,640]{2,1,0:T(8,128)(2,1)}, bf16[2,64,640]{2,1,0:T(8,128)(2,1)}, u32[]{:S(2)}, u32[]{:S(2)}) collective-permute-start(bf16[2,64,640]{2,1,0:T(8,128)(2,1)} %bitcast.162), channel_id=1, source_target_pairs={{0,126},{1,127},{2,0},{3,1},{4,2},{5,3},{6,4},{7,5},{8,6},{9,7},{1... | collective-permute-start | bytes 491528 | tf_op jit(solution)/shard_map/ppermute | solution.py:36
  33.2 3.4 %fusion.90 = (bf16[2944,320]{1,0:T(8,128)(2,1)}, bf16[2944,320]{1,0:T(8,128)(2,1)}) fusion(bf16[2944,640]{1,0:T(8,128)(2,1)S(1)} %bitcast.165), kind=kLoop, calls=%fused_computation.145 | loop fusion | bytes 7536640 | tf_op jit(solution)/shard_map/slice | solution.py:83
  43.3 4.1 %copy.107 = bf16[2944,320]{0,1:T(8,128)(2,1)} copy(bf16[2944,320]{1,0:T(8,128)(2,1)} %get-tuple-element.10) | data formatting | bytes 3768320
  47.4 4.1 %copy.105 = bf16[2944,320]{0,1:T(8,128)(2,1)} copy(bf16[2944,320]{1,0:T(8,128)(2,1)} %get-tuple-element.9) | data formatting | bytes 3768320
  51.5 2.9 %fusion.7 = f32[2,24,1920]{2,1,0:T(8,128)S(1)} fusion(bf16[1024,1920]{1,0:T(8,128)(2,1)} %param.13, s32[]{:T(128)S(6)} %select_n.158, bf16[1,24,2048]{2,1,0:T(8,128)(2,1)} %bitcast.1, bf16[1,24,2048]{2,1,0:T(8,128)(2,1)S(1)} %fusion.51, pred[]{:T(512)S(6)} %eq.106), kind=kOutput, calls=%fused_computation.11 | convolution fusion | flops 189186048 | bytes 4497413 | tf_op jit(solution)/shard_map/grd,df->grf/dot_general | solution.py:123
  55.1 1.7 collective-permute-start.1
  58.9 1.9 %copy.106 = bf16[512,320]{0,1:T(8,128)(2,1)} copy(bf16[512,320]{1,0:T(8,128)(2,1)} %get-tuple-element.14) | data formatting | bytes 655360
  63.5 2.6 %bitcast_reduce_fusion = (f32[24,5,4]{0,2,1:T(4,128)S(1)}, f32[5,24,4,2944]{3,1,2,0:T(8,128)S(1)}) fusion(pred[24,2944]{1,0:T(8,128)(4,1)S(1)} %broadcast_compare_fusion, bf16[2944,5,64,1]{0,2,3,1:T(8,128)(2,1)} %bitcast.166, bf16[24,5,4,64]{3,2,1,0:T(4,128)(2,1)S(1)} %reshape.239), kind=kOutput, calls=%fused_computation.1 | convolution fusion | flops 185118240 | bytes 7670656 | tf_op jit(solution)/shard_map/rkgd,tkd->rkgt/dot_general | solution.py:85
  66.9 1.6 multiply_reduce_fusion
  68.5 4.0 %fusion.28 = f32[24,5,4,64]{3,0,2,1:T(8,128)S(1)} fusion(bf16[2944,5,64,1]{0,2,3,1:T(8,128)(2,1)S(1)} %bitcast.168, f32[5,24,4,2944]{3,1,2,0:T(8,128)S(1)} %get-tuple-element.25, f32[24,2944]{1,0:T(8,128)S(1)} %copy-done.5, f32[24,5,4]{0,2,1:T(4,128)S(1)} %get-tuple-element.8, pred[24,2944]{1,0:T(8,128)(4,1)S(1)} %broadcast_compare_fusion, ...), kind=kOutput, calls=%fused_computation.30 | convolution fusion | flops 1093816320 | bytes 8047360 | tf_op jit(solution)/shard_map/rkgt,tkd->rkgd/dot_general | solution.py:191
  73.4 1.4 collective-permute-start.6
  75.0 3.1 %collective-permute-done.6 = bf16[24,1280]{1,0:T(8,128)(2,1)S(1)} collective-permute-done((bf16[24,1280]{1,0:T(8,128)(2,1)S(1)}, bf16[24,1280]{1,0:T(8,128)(2,1)S(1)}, u32[]{:S(2)}, u32[]{:S(2)}) %collective-permute-start.6) | collective-permute-done | bytes 61472 | tf_op jit(solution)/shard_map/ppermute | solution.py:30
  80.1 3.7 %collective-permute-done.7 = bf16[24,2048]{1,0:T(8,128)(2,1)S(1)} collective-permute-done((bf16[24,2048]{1,0:T(8,128)(2,1)S(1)}, bf16[24,2048]{1,0:T(8,128)(2,1)S(1)}, u32[]{:S(2)}, u32[]{:S(2)}) %collective-permute-start.7) | collective-permute-done | bytes 98336 | tf_op jit(solution)/shard_map/ppermute | solution.py:30
  84.0 2.7 %collective-permute-start.10 = (bf16[24,2048]{1,0:T(8,128)(2,1)S(1)}, bf16[24,2048]{1,0:T(8,128)(2,1)S(1)}, u32[]{:S(2)}, u32[]{:S(2)}) collective-permute-start(bf16[24,2048]{1,0:T(8,128)(2,1)S(1)} %multiply_convert_fusion), channel_id=1, source_target_pairs={{0,64},{192,128},{1,65},{193,129},{2,66},{194,130},{3,67},{195,131... | collective-permute-start | bytes 294920 | tf_op jit(solution)/shard_map/ppermute | solution.py:214
  88.7 4.9 %collective-permute-done.8 = bf16[24,2048]{1,0:T(8,128)(2,1)S(1)} collective-permute-done((bf16[24,2048]{1,0:T(8,128)(2,1)S(1)}, bf16[24,2048]{1,0:T(8,128)(2,1)S(1)}, u32[]{:S(2)}, u32[]{:S(2)}) %collective-permute-start.8) | collective-permute-done | bytes 98336 | tf_op jit(solution)/shard_map/ppermute | solution.py:216
  93.7 10.4 %all-gather = bf16[96,2048]{1,0:T(8,128)(2,1)} all-gather(bf16[24,2048]{1,0:T(8,128)(2,1)S(1)} %fusion.46), channel_id=2, replica_groups=mesh['guide'=2,'x_lo'=2,'y'=4,'z'=8,'core'=2] {'y'}, dimensions={0}, use_global_device_ids=true | all-gather | bytes 491520 | tf_op jit(solution)/shard_map/all_gather | solution.py:223
  104.1 51.9 %all-gather.4.cloned.1.call-done = bf16[4,192,2048]{2,1,0:T(8,128)(2,1)} async-done(((bf16[4,24,2048]{2,1,0:T(8,128)(2,1)}), bf16[4,192,2048]{2,1,0:T(8,128)(2,1)}) %all-gather.4.cloned.1.call-update) | async-done | bytes 3145744 | tf_op jit(solution)/shard_map/all_gather | solution.py:224
  156.9 3.2 %fusion.34 = f32[4,8,24,250]{3,2,1,0:T(8,128)S(1)} fusion(bf16[4,8,24,2048]{3,2,1,0:T(8,128)(2,1)} %bitcast.177, bf16[2048,250]{1,0:T(8,128)(2,1)} %param.16), kind=kOutput, calls=%fused_computation.34 | convolution fusion | flops 786432000 | bytes 4937728 | tf_op jit(solution)/shard_map/yzrd,dv->yzrv/dot_general | solution.py:227
  160.2 2.4 %collective-permute-done.11 = bf16[4,8,24,2048]{3,2,1,0:T(8,128)(2,1)} collective-permute-done((bf16[4,8,24,2048]{3,2,1,0:T(8,128)(2,1)}, bf16[4,8,24,2048]{3,2,1,0:T(8,128)(2,1)}, u32[]{:S(2)}, u32[]{:S(2)}) %collective-permute-start.11) | collective-permute-done | bytes 3145760 | tf_op jit(solution)/shard_map/ppermute | solution.py:226
  162.6 2.9 %select_bitcast_fusion.1 = (f32[4,8,1,24,250]{4,3,1,0,2:T(8,128)S(1)}, f32[4,8,1,24,250]{4,3,1,0,2:T(8,128)S(1)}) fusion(f32[4,8,24,250]{3,2,1,0:T(8,128)S(1)} %fusion.34, pred[]{:T(512)S(6)} %eq.105, bf16[4,8,24,2048]{3,2,1,0:T(8,128)(2,1)} %collective-permute-done.11, bf16[2048,250]{1,0:T(8,128)(2,1)S(1)} %copy-done.6), kind=kOutput, calls=%fused_computation.42 | convolution fusion | flops 786816000 | bytes 6473729 | tf_op jit(solution)/shard_map/yzrd,dv->yzrv/dot_general | solution.py:228
  (101 shorter events, 29.3 us)
Async XLA Ops:
  6.5 71.6 %copy-start = (bf16[640,2048]{1,0:T(8,128)(2,1)S(1)}, bf16[640,2048]{1,0:T(8,128)(2,1)}, u32[]{:S(2)}) copy-start(bf16[640,2048]{1,0:T(8,128)(2,1)} %param.14) | copy-start | bytes 7864324
  6.5 149.5 %all-gather.4.cloned.1.call-start = ((), (), s32[]{:S(2)}) async-start(), calls=%async_computation | async-start | bytes 3538944 | tf_op jit(solution)/shard_map/all_gather | solution.py:224
  8.7 42.7 %collective-permute-start = (bf16[24,2048]{1,0:T(8,128)(2,1)S(1)}, bf16[24,2048]{1,0:T(8,128)(2,1)}, u32[]{:S(2)}, u32[]{:S(2)}) collective-permute-start(bf16[24,2048]{1,0:T(8,128)(2,1)S(1)} %fusion.49), channel_id=1, source_target_pairs={{0,128},{128,0},{1,129},{129,1},{2,130},{130,2},{3,131},{131,3},{4... | collective-permute-start | bytes 294920 | tf_op jit(solution)/shard_map/ppermute | solution.py:30
  15.1 18.0 %copy-start.3 = (bf16[1,24,2048]{2,1,0:T(8,128)(2,1)S(1)}, bf16[1,24,2048]{2,1,0:T(8,128)(2,1)}, u32[]{:S(2)}) copy-start(bf16[1,24,2048]{2,1,0:T(8,128)(2,1)} %param.11) | copy-start | bytes 294916
  15.1 18.0 %copy-start.11 = (f32[2048]{0:T(1024)S(1)}, f32[2048]{0:T(1024)}, u32[]{:S(2)}) copy-start(f32[2048]{0:T(1024)} %param.12) | copy-start | bytes 24580
  15.1 18.1 %copy-start.1 = (bf16[1,46,64,640]{3,2,1,0:T(8,128)(2,1)S(1)}, bf16[1,46,64,640]{3,2,1,0:T(8,128)(2,1)}, u32[]{:S(2)}) copy-start(bf16[1,46,64,640]{3,2,1,0:T(8,128)(2,1)} %param.17) | copy-start | bytes 11304964
  22.0 34.8 %collective-permute-start.5 = (bf16[2,64,640]{2,1,0:T(8,128)(2,1)}, bf16[2,64,640]{2,1,0:T(8,128)(2,1)S(1)}, u32[]{:S(2)}, u32[]{:S(2)}) collective-permute-start(bf16[2,64,640]{2,1,0:T(8,128)(2,1)} %bitcast.159), channel_id=1, source_target_pairs={{0,2},{1,3},{2,4},{3,5},{4,6},{5,7},{6,8},{7,9},{8,10},{9,11},{10,... | collective-permute-start | bytes 491528 | tf_op jit(solution)/shard_map/ppermute | solution.py:36
  24.3 32.5 %collective-permute-start.4 = (bf16[2,64,640]{2,1,0:T(8,128)(2,1)}, bf16[2,64,640]{2,1,0:T(8,128)(2,1)}, u32[]{:S(2)}, u32[]{:S(2)}) collective-permute-start(bf16[2,64,640]{2,1,0:T(8,128)(2,1)} %bitcast.160), channel_id=1, source_target_pairs={{0,1},{1,2},{2,3},{3,4},{4,5},{5,6},{6,7},{7,8},{8,9},{9,10},{10,1... | collective-permute-start | bytes 491528 | tf_op jit(solution)/shard_map/ppermute | solution.py:36
  27.7 29.1 %collective-permute-start.3 = (bf16[2,64,640]{2,1,0:T(8,128)(2,1)}, bf16[2,64,640]{2,1,0:T(8,128)(2,1)}, u32[]{:S(2)}, u32[]{:S(2)}) collective-permute-start(bf16[2,64,640]{2,1,0:T(8,128)(2,1)} %bitcast.161), channel_id=1, source_target_pairs={{0,127},{1,0},{2,1},{3,2},{4,3},{5,4},{6,5},{7,6},{8,7},{9,8},{10,... | collective-permute-start | bytes 491528 | tf_op jit(solution)/shard_map/ppermute | solution.py:36
  28.4 28.4 %collective-permute-start.2 = (bf16[2,64,640]{2,1,0:T(8,128)(2,1)}, bf16[2,64,640]{2,1,0:T(8,128)(2,1)}, u32[]{:S(2)}, u32[]{:S(2)}) collective-permute-start(bf16[2,64,640]{2,1,0:T(8,128)(2,1)} %bitcast.162), channel_id=1, source_target_pairs={{0,126},{1,127},{2,0},{3,1},{4,2},{5,3},{6,4},{7,5},{8,6},{9,7},{1... | collective-permute-start | bytes 491528 | tf_op jit(solution)/shard_map/ppermute | solution.py:36
  55.1 6.6 %collective-permute-start.1 = (f32[24,1920]{1,0:T(8,128)}, f32[24,1920]{1,0:T(8,128)}, u32[]{:S(2)}, u32[]{:S(2)}) collective-permute-start(f32[24,1920]{1,0:T(8,128)} %select_bitcast_fusion.2), channel_id=1, source_target_pairs={{0,128},{128,0},{1,129},{129,1},{2,130},{130,2},{3,131},{131,3},{4... | collective-permute-start | bytes 552968 | tf_op jit(solution)/shard_map/ppermute | solution.py:30
  63.5 2.6 %copy-start.4 = (bf16[512,320]{0,1:T(8,128)(2,1)S(1)}, bf16[512,320]{0,1:T(8,128)(2,1)}, u32[]{:S(2)}) copy-start(bf16[512,320]{0,1:T(8,128)(2,1)} %copy.106) | copy-start | bytes 983044
  63.5 2.6 %copy-start.9 = (pred[24,512]{1,0:T(8,128)(4,1)S(1)}, pred[24,512]{1,0:T(8,128)(4,1)}, u32[]{:S(2)}) copy-start(pred[24,512]{1,0:T(8,128)(4,1)} %broadcast_compare_fusion.1) | copy-start | bytes 36868
  63.5 3.0 %copy-start.8 = (f32[24,512]{1,0:T(8,128)S(1)}, f32[24,512]{1,0:T(8,128)}, u32[]{:S(2)}) copy-start(f32[24,512]{1,0:T(8,128)} %slice.96) | copy-start | bytes 147460
  63.5 3.4 %copy-start.5 = (f32[24,2944]{1,0:T(8,128)S(1)}, f32[24,2944]{1,0:T(8,128)}, u32[]{:S(2)}) copy-start(f32[24,2944]{1,0:T(8,128)} %slice.94) | copy-start | bytes 847876
  68.5 4.0 %copy-start.7 = (bf16[512,320]{0,1:T(8,128)(2,1)S(1)}, bf16[512,320]{0,1:T(8,128)(2,1)}, u32[]{:S(2)}) copy-start(bf16[512,320]{0,1:T(8,128)(2,1)} %copy.108) | copy-start | bytes 983044
  72.5 11.4 %copy-start.10 = (f32[2048]{0:T(1024)S(1)}, f32[2048]{0:T(1024)}, u32[]{:S(2)}) copy-start(f32[2048]{0:T(1024)} %param.15) | copy-start | bytes 24580
  73.4 4.7 %collective-permute-start.6 = (bf16[24,1280]{1,0:T(8,128)(2,1)S(1)}, bf16[24,1280]{1,0:T(8,128)(2,1)S(1)}, u32[]{:S(2)}, u32[]{:S(2)}) collective-permute-start(bf16[24,1280]{1,0:T(8,128)(2,1)S(1)} %convert_element_type.108), channel_id=1, source_target_pairs={{0,128},{128,0},{1,129},{129,1},{2,130},{130,2},{3,131},{131,3},{4... | collective-permute-start | bytes 184328 | tf_op jit(solution)/shard_map/ppermute | solution.py:30
  78.7 5.1 %collective-permute-start.7 = (bf16[24,2048]{1,0:T(8,128)(2,1)S(1)}, bf16[24,2048]{1,0:T(8,128)(2,1)S(1)}, u32[]{:S(2)}, u32[]{:S(2)}) collective-permute-start(bf16[24,2048]{1,0:T(8,128)(2,1)S(1)} %fusion.56), channel_id=1, source_target_pairs={{0,128},{128,0},{1,129},{129,1},{2,130},{130,2},{3,131},{131,3},{4... | collective-permute-start | bytes 294920 | tf_op jit(solution)/shard_map/ppermute | solution.py:30
  84.0 4.7 %collective-permute-start.10 = (bf16[24,2048]{1,0:T(8,128)(2,1)S(1)}, bf16[24,2048]{1,0:T(8,128)(2,1)S(1)}, u32[]{:S(2)}, u32[]{:S(2)}) collective-permute-start(bf16[24,2048]{1,0:T(8,128)(2,1)S(1)} %multiply_convert_fusion), channel_id=1, source_target_pairs={{0,64},{192,128},{1,65},{193,129},{2,66},{194,130},{3,67},{195,131... | collective-permute-start | bytes 294920 | tf_op jit(solution)/shard_map/ppermute | solution.py:214
  86.7 6.9 %collective-permute-start.8 = (bf16[24,2048]{1,0:T(8,128)(2,1)S(1)}, bf16[24,2048]{1,0:T(8,128)(2,1)S(1)}, u32[]{:S(2)}, u32[]{:S(2)}) collective-permute-start(bf16[24,2048]{1,0:T(8,128)(2,1)S(1)} %multiply_convert_fusion), channel_id=1, source_target_pairs={{128,0},{64,192},{129,1},{65,193},{130,2},{66,194},{131,3},{67,195... | collective-permute-start | bytes 294920 | tf_op jit(solution)/shard_map/ppermute | solution.py:216
  88.0 5.6 %collective-permute-start.9 = (bf16[24,2048]{1,0:T(8,128)(2,1)S(1)}, bf16[24,2048]{1,0:T(8,128)(2,1)S(1)}, u32[]{:S(2)}, u32[]{:S(2)}) collective-permute-start(bf16[24,2048]{1,0:T(8,128)(2,1)S(1)} %multiply_convert_fusion), channel_id=1, source_target_pairs={{128,64},{64,128},{129,65},{65,129},{130,66},{66,130},{131,67},{67... | collective-permute-start | bytes 294920 | tf_op jit(solution)/shard_map/ppermute | solution.py:215
  156.0 6.5 %collective-permute-start.11 = (bf16[4,8,24,2048]{3,2,1,0:T(8,128)(2,1)}, bf16[4,8,24,2048]{3,2,1,0:T(8,128)(2,1)}, u32[]{:S(2)}, u32[]{:S(2)}) collective-permute-start(bf16[4,8,24,2048]{3,2,1,0:T(8,128)(2,1)} %bitcast.176), channel_id=1, source_target_pairs={{0,1},{1,0},{2,3},{3,2},{4,5},{5,4},{6,7},{7,6},{8,9},{9,8},{10,11... | collective-permute-start | bytes 9437192 | tf_op jit(solution)/shard_map/ppermute | solution.py:226
  156.9 5.6 %copy-start.6 = (bf16[2048,250]{1,0:T(8,128)(2,1)S(1)}, bf16[2048,250]{1,0:T(8,128)(2,1)}, u32[]{:S(2)}) copy-start(bf16[2048,250]{1,0:T(8,128)(2,1)} %param.16) | copy-start | bytes 3072004
  (1 other events, 2.0 us)
Sparse Core Ops, SparseCore 0:
  104.2 51.7 all-gather.3

commit v8 on v7

--- a/solution.py
+++ b/solution.py
@@ -220,8 +220,10 @@
     cond = jnp.where(side == 0, same_group, other_group).astype(jnp.float32)
     uncond = jnp.where(side == 0, other_group, same_group).astype(jnp.float32)
     combined = (uncond + guidance * (cond - uncond)).astype(jnp.bfloat16)
-    gathered = lax.all_gather(combined, "y", axis=0, tiled=False)
-    gathered = lax.all_gather(gathered, "z", axis=1, tiled=False)
+    gathered = lax.all_gather(combined, ("y", "z"), axis=0, tiled=False)
+    gathered = gathered.reshape(
+        (lax.axis_size("y"), lax.axis_size("z")) + combined.shape
+    )
     core = lax.axis_index("core")
     twin = lax.ppermute(gathered, "core", [(0, 1), (1, 0)])
     mine_logits = jnp.einsum("yzrd,dv->yzrv", gathered, w_vocab, preferred_element_type=jnp.float32)

time: 174 us -> 198 us (1.14)
  waiting for transfers between devices: 66 us -> 97.7 us
  blocking collectives: 10.4 us -> 0 us
  starting transfers between devices: 22.8 us -> 26.5 us
    all_gather x1, waiting for transfers between devices: 51.9 us -> 80.4 us  [body(): gathered = lax.all_gather(combined, ('y', 'z'), axis=0, tiled=False)]
    all_gather x1 -> x0, blocking collectives: 10.4 us -> none  [body(): gathered = lax.all_gather(combined, 'y', axis=0, tiled=False)]
    ppermute x1, starting transfers between devices: 0.91 us -> 4.6 us  [body(): twin = lax.ppermute(gathered, 'core', [(0, 1), (1, 0)])]
    ppermute x1, waiting for transfers between devices: 2.38 us -> 5.62 us  [body(): twin = lax.ppermute(gathered, 'core', [(0, 1), (1, 0)])]
    dot_general x1, matrix products: 3.24 us -> 1.06 us  [body(): jnp.einsum('yzrd,dv->yzrv', gathered, w_vocab, preferred_element_type=jnp...]
    unnamed x33 -> x35, local copies, waits for them, and re-layouts: 14.4 us -> 14.4 us
  transfers between devices with their start and end apart: 13 -> 13, of which waited for: 5 -> 5; matrix products, arithmetic and copies ran while one was open for 24% -> 20% of each run, Pallas kernels for 0% -> 0%
where the time goes in v8:
time: 198 us
  waiting for transfers between devices  97.7 us (49%)
  starting transfers between devices  26.5 us (13%)
  local copies, waits for them, and re-layouts  26.2 us (13%)
  matrix products  22.1 us (11%)
  between operations  13.8 us (7%)
  other arithmetic  11.3 us (6%)
    all_gather x1, waiting for transfers between devices, body(): gathered = lax.all_gather(combined, ('y', 'z'), axis=0, tiled=False)  80.4 us
    unnamed x35, local copies, waits for them, and re-layouts  14.4 us
    ppermute x4, starting transfers between devices, shifted(): return lax.ppermute(value, axis, pairs)  9.02 us
    ppermute x4, starting transfers between devices, from_partner(): return lax.ppermute(block, axis, route)  8.22 us
    ppermute x4, waiting for transfers between devices, from_partner(): return lax.ppermute(block, axis, route)  6.76 us
    ppermute x1, waiting for transfers between devices, body(): twin = lax.ppermute(gathered, 'core', [(0, 1), (1, 0)])  5.62 us
    dot_general x1, matrix products, body(): jnp.einsum('smp,pwc->smwc', page_hit, pool, preferred_element_type=jnp.fl...  5.17 us
    ppermute x1, waiting for transfers between devices, body(): from_guide = lax.ppermute(final, pair, [(2, 0), (1, 3)])  4.88 us
  transfers between devices with their start and end apart: 13, of which 5 were waited for; matrix products, arithmetic and copies ran while one was open for 20% of the time, Pallas kernels for 0%

profile of v8, /device:TPU:1, one launch (start us, length us, event | category | flops | bytes accessed | tf_op | source)
XLA Modules:
  0.0 197.5 jit_solution(6038168952499776720)
XLA Ops:
  8.7 3.7 %collective-permute-start = (bf16[24,2048]{1,0:T(8,128)(2,1)S(1)}, bf16[24,2048]{1,0:T(8,128)(2,1)}, u32[]{:S(2)}, u32[]{:S(2)}) collective-permute-start(bf16[24,2048]{1,0:T(8,128)(2,1)S(1)} %fusion.49), channel_id=1, source_target_pairs={{0,128},{128,0},{1,129},{129,1},{2,130},{130,2},{3,131},{131,3},{4... | collective-permute-start | bytes 294920 | tf_op jit(solution)/shard_map/ppermute | solution.py:30
  15.1 5.2 %fusion.18 = bf16[4,2,64,640]{3,0,2,1:T(4,128)(2,1)S(1)} fusion(bf16[46,64,640]{2,1,0:T(8,128)(2,1)} %bitcast.163, s32[4,2]{0,1:T(2,128)S(1)} %select_reduce_fusion), kind=kOutput, calls=%fused_computation.22 | convolution fusion | flops 30474608 | bytes 4423712 | tf_op jit(solution)/shard_map/smp,pwc->smwc/dot_general | solution.py:155
  22.0 1.6 collective-permute-start.5
  24.3 2.8 %collective-permute-start.4 = (bf16[2,64,640]{2,1,0:T(8,128)(2,1)}, bf16[2,64,640]{2,1,0:T(8,128)(2,1)}, u32[]{:S(2)}, u32[]{:S(2)}) collective-permute-start(bf16[2,64,640]{2,1,0:T(8,128)(2,1)} %bitcast.159), channel_id=1, source_target_pairs={{0,1},{1,2},{2,3},{3,4},{4,5},{5,6},{6,7},{7,8},{8,9},{9,10},{10,1... | collective-permute-start | bytes 491528 | tf_op jit(solution)/shard_map/ppermute | solution.py:36
  28.4 4.6 %collective-permute-start.2 = (bf16[2,64,640]{2,1,0:T(8,128)(2,1)}, bf16[2,64,640]{2,1,0:T(8,128)(2,1)}, u32[]{:S(2)}, u32[]{:S(2)}) collective-permute-start(bf16[2,64,640]{2,1,0:T(8,128)(2,1)} %bitcast.161), channel_id=1, source_target_pairs={{0,126},{1,127},{2,0},{3,1},{4,2},{5,3},{6,4},{7,5},{8,6},{9,7},{1... | collective-permute-start | bytes 491528 | tf_op jit(solution)/shard_map/ppermute | solution.py:36
  33.1 3.4 %fusion.90 = (bf16[2944,320]{1,0:T(8,128)(2,1)}, bf16[2944,320]{1,0:T(8,128)(2,1)}) fusion(bf16[2944,640]{1,0:T(8,128)(2,1)S(1)} %bitcast.164), kind=kLoop, calls=%fused_computation.145 | loop fusion | bytes 7536640 | tf_op jit(solution)/shard_map/slice | solution.py:83
  43.3 4.1 %copy.107 = bf16[2944,320]{0,1:T(8,128)(2,1)} copy(bf16[2944,320]{1,0:T(8,128)(2,1)} %get-tuple-element.10) | data formatting | bytes 3768320
  47.3 4.1 %copy.105 = bf16[2944,320]{0,1:T(8,128)(2,1)} copy(bf16[2944,320]{1,0:T(8,128)(2,1)} %get-tuple-element.9) | data formatting | bytes 3768320
  51.4 2.9 %fusion.7 = f32[2,24,1920]{2,1,0:T(8,128)S(1)} fusion(bf16[1024,1920]{1,0:T(8,128)(2,1)} %param.13, s32[]{:T(128)S(6)} %select_n.158, bf16[1,24,2048]{2,1,0:T(8,128)(2,1)} %bitcast.1, bf16[1,24,2048]{2,1,0:T(8,128)(2,1)S(1)} %fusion.51, pred[]{:T(512)S(6)} %eq.106), kind=kOutput, calls=%fused_computation.11 | convolution fusion | flops 189186048 | bytes 4497413 | tf_op jit(solution)/shard_map/grd,df->grf/dot_general | solution.py:123
  55.0 1.7 collective-permute-start.1
  58.9 1.9 copy.106
  63.5 2.6 %bitcast_reduce_fusion = (f32[24,5,4]{0,2,1:T(4,128)S(1)}, f32[5,24,4,2944]{3,1,2,0:T(8,128)S(1)}) fusion(pred[24,2944]{1,0:T(8,128)(4,1)S(1)} %broadcast_compare_fusion, bf16[2944,5,64,1]{0,2,3,1:T(8,128)(2,1)} %bitcast.165, bf16[24,5,4,64]{3,2,1,0:T(4,128)(2,1)S(1)} %reshape.242), kind=kOutput, calls=%fused_computation.1 | convolution fusion | flops 185118240 | bytes 7670656 | tf_op jit(solution)/shard_map/rkgd,tkd->rkgt/dot_general | solution.py:85
  66.8 1.6 multiply_reduce_fusion
  68.5 4.0 %fusion.28 = f32[24,5,4,64]{3,0,2,1:T(8,128)S(1)} fusion(bf16[2944,5,64,1]{0,2,3,1:T(8,128)(2,1)S(1)} %bitcast.169, f32[5,24,4,2944]{3,1,2,0:T(8,128)S(1)} %get-tuple-element.25, f32[24,2944]{1,0:T(8,128)S(1)} %copy-done.6, f32[24,5,4]{0,2,1:T(4,128)S(1)} %get-tuple-element.8, pred[24,2944]{1,0:T(8,128)(4,1)S(1)} %broadcast_compare_fusion, ...), kind=kOutput, calls=%fused_computation.30 | convolution fusion | flops 1093816320 | bytes 8047360 | tf_op jit(solution)/shard_map/rkgt,tkd->rkgd/dot_general | solution.py:191
  73.4 1.4 collective-permute-start.6
  74.9 3.1 %collective-permute-done.6 = bf16[24,1280]{1,0:T(8,128)(2,1)S(1)} collective-permute-done((bf16[24,1280]{1,0:T(8,128)(2,1)S(1)}, bf16[24,1280]{1,0:T(8,128)(2,1)S(1)}, u32[]{:S(2)}, u32[]{:S(2)}) %collective-permute-start.6) | collective-permute-done | bytes 61472 | tf_op jit(solution)/shard_map/ppermute | solution.py:30
  78.6 1.4 collective-permute-start.7
  80.0 3.6 %collective-permute-done.7 = bf16[24,2048]{1,0:T(8,128)(2,1)S(1)} collective-permute-done((bf16[24,2048]{1,0:T(8,128)(2,1)S(1)}, bf16[24,2048]{1,0:T(8,128)(2,1)S(1)}, u32[]{:S(2)}, u32[]{:S(2)}) %collective-permute-start.7) | collective-permute-done | bytes 98336 | tf_op jit(solution)/shard_map/ppermute | solution.py:30
  84.0 2.7 %collective-permute-start.10 = (bf16[24,2048]{1,0:T(8,128)(2,1)S(1)}, bf16[24,2048]{1,0:T(8,128)(2,1)S(1)}, u32[]{:S(2)}, u32[]{:S(2)}) collective-permute-start(bf16[24,2048]{1,0:T(8,128)(2,1)S(1)} %multiply_convert_fusion), channel_id=1, source_target_pairs={{0,64},{192,128},{1,65},{193,129},{2,66},{194,130},{3,67},{195,131... | collective-permute-start | bytes 294920 | tf_op jit(solution)/shard_map/ppermute | solution.py:214
  88.7 4.9 %collective-permute-done.8 = bf16[24,2048]{1,0:T(8,128)(2,1)S(1)} collective-permute-done((bf16[24,2048]{1,0:T(8,128)(2,1)S(1)}, bf16[24,2048]{1,0:T(8,128)(2,1)S(1)}, u32[]{:S(2)}, u32[]{:S(2)}) %collective-permute-start.8) | collective-permute-done | bytes 98336 | tf_op jit(solution)/shard_map/ppermute | solution.py:216
  94.3 80.4 %all-gather.3.cloned.1.call-done = bf16[768,2048]{1,0:T(8,128)(2,1)} async-done(((bf16[24,2048]{1,0:T(8,128)(2,1)}), bf16[768,2048]{1,0:T(8,128)(2,1)}) %all-gather.3.cloned.1.call-update) | async-done | bytes 3145744 | tf_op jit(solution)/shard_map/all_gather | solution.py:223
  174.7 4.6 %collective-permute-start.11 = (bf16[4,8,24,2048]{3,2,1,0:T(8,128)(2,1)}, bf16[4,8,24,2048]{3,2,1,0:T(8,128)(2,1)}, u32[]{:S(2)}, u32[]{:S(2)}) collective-permute-start(bf16[4,8,24,2048]{3,2,1,0:T(8,128)(2,1)} %bitcast.167), channel_id=1, source_target_pairs={{0,1},{1,0},{2,3},{3,2},{4,5},{5,4},{6,7},{7,6},{8,9},{9,8},{10,11... | collective-permute-start | bytes 9437192 | tf_op jit(solution)/shard_map/ppermute | solution.py:228
  179.3 5.6 %collective-permute-done.11 = bf16[4,8,24,2048]{3,2,1,0:T(8,128)(2,1)} collective-permute-done((bf16[4,8,24,2048]{3,2,1,0:T(8,128)(2,1)}, bf16[4,8,24,2048]{3,2,1,0:T(8,128)(2,1)}, u32[]{:S(2)}, u32[]{:S(2)}) %collective-permute-start.11) | collective-permute-done | bytes 3145760 | tf_op jit(solution)/shard_map/ppermute | solution.py:228
  184.9 3.1 %fusion.32 = f32[4,8,24,250]{3,2,1,0:T(8,128)S(1)} fusion(bf16[4,8,24,2048]{3,2,1,0:T(8,128)(2,1)} %collective-permute-done.11, bf16[2048,250]{1,0:T(8,128)(2,1)} %param.16), kind=kOutput, calls=%fused_computation.32 | convolution fusion | flops 786432000 | bytes 4937728 | tf_op jit(solution)/shard_map/yzrd,dv->yzrv/dot_general | solution.py:230
  (102 shorter events, 28.7 us)
Async XLA Ops:
  6.5 71.5 %copy-start = (bf16[640,2048]{1,0:T(8,128)(2,1)S(1)}, bf16[640,2048]{1,0:T(8,128)(2,1)}, u32[]{:S(2)}) copy-start(bf16[640,2048]{1,0:T(8,128)(2,1)} %param.14) | copy-start | bytes 7864324
  6.5 168.2 %all-gather.3.cloned.1.call-start = ((), (), s32[]{:S(2)}) async-start(), calls=%async_computation | async-start | bytes 3244032 | tf_op jit(solution)/shard_map/all_gather | solution.py:223
  8.7 42.7 %collective-permute-start = (bf16[24,2048]{1,0:T(8,128)(2,1)S(1)}, bf16[24,2048]{1,0:T(8,128)(2,1)}, u32[]{:S(2)}, u32[]{:S(2)}) collective-permute-start(bf16[24,2048]{1,0:T(8,128)(2,1)S(1)} %fusion.49), channel_id=1, source_target_pairs={{0,128},{128,0},{1,129},{129,1},{2,130},{130,2},{3,131},{131,3},{4... | collective-permute-start | bytes 294920 | tf_op jit(solution)/shard_map/ppermute | solution.py:30
  15.1 17.9 %copy-start.4 = (bf16[1,24,2048]{2,1,0:T(8,128)(2,1)S(1)}, bf16[1,24,2048]{2,1,0:T(8,128)(2,1)}, u32[]{:S(2)}) copy-start(bf16[1,24,2048]{2,1,0:T(8,128)(2,1)} %param.11) | copy-start | bytes 294916
  15.1 17.9 %copy-start.12 = (f32[2048]{0:T(1024)S(1)}, f32[2048]{0:T(1024)}, u32[]{:S(2)}) copy-start(f32[2048]{0:T(1024)} %param.12) | copy-start | bytes 24580
  15.1 18.0 %copy-start.1 = (bf16[1,46,64,640]{3,2,1,0:T(8,128)(2,1)S(1)}, bf16[1,46,64,640]{3,2,1,0:T(8,128)(2,1)}, u32[]{:S(2)}) copy-start(bf16[1,46,64,640]{3,2,1,0:T(8,128)(2,1)} %param.17) | copy-start | bytes 11304964
  22.0 34.8 %collective-permute-start.5 = (bf16[2,64,640]{2,1,0:T(8,128)(2,1)}, bf16[2,64,640]{2,1,0:T(8,128)(2,1)S(1)}, u32[]{:S(2)}, u32[]{:S(2)}) collective-permute-start(bf16[2,64,640]{2,1,0:T(8,128)(2,1)} %bitcast.158), channel_id=1, source_target_pairs={{0,2},{1,3},{2,4},{3,5},{4,6},{5,7},{6,8},{7,9},{8,10},{9,11},{10,... | collective-permute-start | bytes 491528 | tf_op jit(solution)/shard_map/ppermute | solution.py:36
  24.3 32.5 %collective-permute-start.4 = (bf16[2,64,640]{2,1,0:T(8,128)(2,1)}, bf16[2,64,640]{2,1,0:T(8,128)(2,1)}, u32[]{:S(2)}, u32[]{:S(2)}) collective-permute-start(bf16[2,64,640]{2,1,0:T(8,128)(2,1)} %bitcast.159), channel_id=1, source_target_pairs={{0,1},{1,2},{2,3},{3,4},{4,5},{5,6},{6,7},{7,8},{8,9},{9,10},{10,1... | collective-permute-start | bytes 491528 | tf_op jit(solution)/shard_map/ppermute | solution.py:36
  27.7 29.1 %collective-permute-start.3 = (bf16[2,64,640]{2,1,0:T(8,128)(2,1)}, bf16[2,64,640]{2,1,0:T(8,128)(2,1)}, u32[]{:S(2)}, u32[]{:S(2)}) collective-permute-start(bf16[2,64,640]{2,1,0:T(8,128)(2,1)} %bitcast.160), channel_id=1, source_target_pairs={{0,127},{1,0},{2,1},{3,2},{4,3},{5,4},{6,5},{7,6},{8,7},{9,8},{10,... | collective-permute-start | bytes 491528 | tf_op jit(solution)/shard_map/ppermute | solution.py:36
  28.4 28.4 %collective-permute-start.2 = (bf16[2,64,640]{2,1,0:T(8,128)(2,1)}, bf16[2,64,640]{2,1,0:T(8,128)(2,1)}, u32[]{:S(2)}, u32[]{:S(2)}) collective-permute-start(bf16[2,64,640]{2,1,0:T(8,128)(2,1)} %bitcast.161), channel_id=1, source_target_pairs={{0,126},{1,127},{2,0},{3,1},{4,2},{5,3},{6,4},{7,5},{8,6},{9,7},{1... | collective-permute-start | bytes 491528 | tf_op jit(solution)/shard_map/ppermute | solution.py:36
  55.0 6.6 %collective-permute-start.1 = (f32[24,1920]{1,0:T(8,128)}, f32[24,1920]{1,0:T(8,128)}, u32[]{:S(2)}, u32[]{:S(2)}) collective-permute-start(f32[24,1920]{1,0:T(8,128)} %select_bitcast_fusion.2), channel_id=1, source_target_pairs={{0,128},{128,0},{1,129},{129,1},{2,130},{130,2},{3,131},{131,3},{4... | collective-permute-start | bytes 552968 | tf_op jit(solution)/shard_map/ppermute | solution.py:30
  63.4 2.6 %copy-start.5 = (bf16[512,320]{0,1:T(8,128)(2,1)S(1)}, bf16[512,320]{0,1:T(8,128)(2,1)}, u32[]{:S(2)}) copy-start(bf16[512,320]{0,1:T(8,128)(2,1)} %copy.106) | copy-start | bytes 983044
  63.4 3.0 %copy-start.9 = (f32[24,512]{1,0:T(8,128)S(1)}, f32[24,512]{1,0:T(8,128)}, u32[]{:S(2)}) copy-start(f32[24,512]{1,0:T(8,128)} %slice.96) | copy-start | bytes 147460
  63.5 3.4 %copy-start.6 = (f32[24,2944]{1,0:T(8,128)S(1)}, f32[24,2944]{1,0:T(8,128)}, u32[]{:S(2)}) copy-start(f32[24,2944]{1,0:T(8,128)} %slice.94) | copy-start | bytes 847876
  68.5 4.0 %copy-start.8 = (bf16[512,320]{0,1:T(8,128)(2,1)S(1)}, bf16[512,320]{0,1:T(8,128)(2,1)}, u32[]{:S(2)}) copy-start(bf16[512,320]{0,1:T(8,128)(2,1)} %copy.108) | copy-start | bytes 983044
  72.5 11.4 %copy-start.11 = (f32[2048]{0:T(1024)S(1)}, f32[2048]{0:T(1024)}, u32[]{:S(2)}) copy-start(f32[2048]{0:T(1024)} %param.15) | copy-start | bytes 24580
  73.4 4.7 %collective-permute-start.6 = (bf16[24,1280]{1,0:T(8,128)(2,1)S(1)}, bf16[24,1280]{1,0:T(8,128)(2,1)S(1)}, u32[]{:S(2)}, u32[]{:S(2)}) collective-permute-start(bf16[24,1280]{1,0:T(8,128)(2,1)S(1)} %convert_element_type.108), channel_id=1, source_target_pairs={{0,128},{128,0},{1,129},{129,1},{2,130},{130,2},{3,131},{131,3},{4... | collective-permute-start | bytes 184328 | tf_op jit(solution)/shard_map/ppermute | solution.py:30
  78.6 5.1 %collective-permute-start.7 = (bf16[24,2048]{1,0:T(8,128)(2,1)S(1)}, bf16[24,2048]{1,0:T(8,128)(2,1)S(1)}, u32[]{:S(2)}, u32[]{:S(2)}) collective-permute-start(bf16[24,2048]{1,0:T(8,128)(2,1)S(1)} %fusion.56), channel_id=1, source_target_pairs={{0,128},{128,0},{1,129},{129,1},{2,130},{130,2},{3,131},{131,3},{4... | collective-permute-start | bytes 294920 | tf_op jit(solution)/shard_map/ppermute | solution.py:30
  84.0 4.7 %collective-permute-start.10 = (bf16[24,2048]{1,0:T(8,128)(2,1)S(1)}, bf16[24,2048]{1,0:T(8,128)(2,1)S(1)}, u32[]{:S(2)}, u32[]{:S(2)}) collective-permute-start(bf16[24,2048]{1,0:T(8,128)(2,1)S(1)} %multiply_convert_fusion), channel_id=1, source_target_pairs={{0,64},{192,128},{1,65},{193,129},{2,66},{194,130},{3,67},{195,131... | collective-permute-start | bytes 294920 | tf_op jit(solution)/shard_map/ppermute | solution.py:214
  86.7 6.9 %collective-permute-start.8 = (bf16[24,2048]{1,0:T(8,128)(2,1)S(1)}, bf16[24,2048]{1,0:T(8,128)(2,1)S(1)}, u32[]{:S(2)}, u32[]{:S(2)}) collective-permute-start(bf16[24,2048]{1,0:T(8,128)(2,1)S(1)} %multiply_convert_fusion), channel_id=1, source_target_pairs={{128,0},{64,192},{129,1},{65,193},{130,2},{66,194},{131,3},{67,195... | collective-permute-start | bytes 294920 | tf_op jit(solution)/shard_map/ppermute | solution.py:216
  88.0 5.6 %collective-permute-start.9 = (bf16[24,2048]{1,0:T(8,128)(2,1)S(1)}, bf16[24,2048]{1,0:T(8,128)(2,1)S(1)}, u32[]{:S(2)}, u32[]{:S(2)}) collective-permute-start(bf16[24,2048]{1,0:T(8,128)(2,1)S(1)} %multiply_convert_fusion), channel_id=1, source_target_pairs={{128,64},{64,128},{129,65},{65,129},{130,66},{66,130},{131,67},{67... | collective-permute-start | bytes 294920 | tf_op jit(solution)/shard_map/ppermute | solution.py:215
  174.7 10.2 %collective-permute-start.11 = (bf16[4,8,24,2048]{3,2,1,0:T(8,128)(2,1)}, bf16[4,8,24,2048]{3,2,1,0:T(8,128)(2,1)}, u32[]{:S(2)}, u32[]{:S(2)}) collective-permute-start(bf16[4,8,24,2048]{3,2,1,0:T(8,128)(2,1)} %bitcast.167), channel_id=1, source_target_pairs={{0,1},{1,0},{2,3},{3,2},{4,5},{5,4},{6,7},{7,6},{8,9},{9,8},{10,11... | collective-permute-start | bytes 9437192 | tf_op jit(solution)/shard_map/ppermute | solution.py:228
  179.3 8.8 %copy-start.2 = (bf16[768,2048]{1,0:T(8,128)(2,1)S(1)}, bf16[768,2048]{1,0:T(8,128)(2,1)}, u32[]{:S(2)}) copy-start(bf16[768,2048]{1,0:T(8,128)(2,1)} %all-gather.3.cloned.1.call-done) | copy-start | bytes 9437188
  179.3 8.8 %copy-start.7 = (bf16[2048,250]{1,0:T(8,128)(2,1)S(1)}, bf16[2048,250]{1,0:T(8,128)(2,1)}, u32[]{:S(2)}) copy-start(bf16[2048,250]{1,0:T(8,128)(2,1)} %param.16) | copy-start | bytes 3072004
  (2 other events, 4.6 us)
Sparse Core Ops, SparseCore 0:
  94.5 80.2 all-gather.2

commit v9 on v7

--- a/solution.py
+++ b/solution.py
@@ -196,18 +196,14 @@
             preferred_element_type=jnp.float32,
         )
     attended = (accs / sums[..., None]).reshape(local_rows, query_width).astype(jnp.bfloat16)
-    partner_attended = from_partner(attended, "guide", 0)
-    both_attended = jnp.where(
-        side == 0, jnp.stack([attended, partner_attended]), jnp.stack([partner_attended, attended])
-    )
     head_half = w_out.shape[0]
-    attended_part = lax.dynamic_slice_in_dim(both_attended, side * head_half, head_half, 2)
-    selected = attended_part
-    out_parts = jnp.einsum("grc,cd->grd", selected, w_out, preferred_element_type=jnp.float32)
-    own_out = jnp.where(side == 0, out_parts[0], out_parts[1])
-    other_out = jnp.where(side == 0, out_parts[1], out_parts[0]).astype(jnp.bfloat16)
+    partner_w_out = from_partner(w_out, "guide", 0)
+    partner_w_out, attended = lax.optimization_barrier((partner_w_out, attended))
+    own_heads = lax.dynamic_slice_in_dim(attended, side * head_half, head_half, 1)
+    other_heads = lax.dynamic_slice_in_dim(attended, (1 - side) * head_half, head_half, 1)
     state_after = states_in + (
-        own_out + from_partner(other_out, "guide", 0).astype(jnp.float32)
+        jnp.dot(own_heads, w_out, preferred_element_type=jnp.float32)
+        + jnp.dot(other_heads, partner_w_out, preferred_element_type=jnp.float32)
     )
     final = rms_scale(state_after, final_gain).astype(jnp.bfloat16)
     pair = ("guide", "x_lo")

time: 174 us -> 216 us (1.24)
  waiting for transfers between devices: 66 us -> 103 us
  starting transfers between devices: 22.8 us -> 26.2 us
  matrix products: 24 us -> 26.3 us
    ppermute x4 -> x3, waiting for transfers between devices: 6.8 us -> 50.7 us  [from_partner(): return lax.ppermute(block, axis, route)]
    ppermute x1, waiting for transfers between devices: 4.88 us -> 0.01 us  [body(): from_guide = lax.ppermute(final, pair, [(2, 0), (1, 3)])]
    all_gather x1, waiting for transfers between devices: 51.9 us -> 47.7 us  [body(): gathered = lax.all_gather(gathered, 'z', axis=1, tiled=False)]
    dot_general x1 -> x2, matrix products: 0.54 us -> 4.52 us  [the longest x1 2.32 us: body(): jnp.dot(own_heads, w_out, preferred_element_type=jnp.float32)]
    ppermute x1, starting transfers between devices: 2.69 us -> 6.42 us  [body(): from_side = lax.ppermute(final, pair, [(0, 1), (3, 2)])]
    ppermute x4 -> x3, starting transfers between devices: 8.18 us -> 5.39 us  [from_partner(): return lax.ppermute(block, axis, route)]
    ppermute x4, starting transfers between devices: 9.02 us -> 11.5 us  [shifted(): return lax.ppermute(value, axis, pairs)]
    slice x1, local copies, waits for them, and re-layouts: 3.42 us -> 5.68 us  [dense_scores(): key_rows = flat[:, :half_width].reshape(count, KVH, HD)]
  transfers between devices with their start and end apart: 13 -> 12, of which waited for: 5 -> 4; matrix products, arithmetic and copies ran while one was open for 24% -> 20% of each run, Pallas kernels for 0% -> 0%
where the time goes in v9:
time: 216 us
  waiting for transfers between devices  103 us (48%)
  local copies, waits for them, and re-layouts  26.8 us (12%)
  matrix products  26.3 us (12%)
  starting transfers between devices  26.2 us (12%)
  between operations  13.7 us (6%)
  blocking collectives  11.2 us (5%)
  other arithmetic  8.67 us (4%)
    ppermute x3, waiting for transfers between devices, from_partner(): return lax.ppermute(block, axis, route)  50.7 us
    all_gather x1, waiting for transfers between devices, body(): gathered = lax.all_gather(gathered, 'z', axis=1, tiled=False)  47.7 us
    unnamed x25, local copies, waits for them, and re-layouts  14.5 us
    ppermute x4, starting transfers between devices, shifted(): return lax.ppermute(value, axis, pairs)  11.5 us
    all_gather x1, blocking collectives, body(): gathered = lax.all_gather(combined, 'y', axis=0, tiled=False)  11.2 us
    ppermute x1, starting transfers between devices, body(): from_side = lax.ppermute(final, pair, [(0, 1), (3, 2)])  6.42 us
    slice x1, local copies, waits for them, and re-layouts, dense_scores(): key_rows = flat[:, :half_width].reshape(count, KVH, HD)  5.68 us
    ppermute x3, starting transfers between devices, from_partner(): return lax.ppermute(block, axis, route)  5.39 us
  transfers between devices with their start and end apart: 12, of which 4 were waited for; matrix products, arithmetic and copies ran while one was open for 20% of the time, Pallas kernels for 0%

profile of v9, /device:TPU:1, one launch (start us, length us, event | category | flops | bytes accessed | tf_op | source)
XLA Modules:
  0.0 215.5 jit_solution(6874800022973023390)
XLA Ops:
  9.4 5.1 %fusion.17 = bf16[4,2,64,640]{3,0,2,1:T(4,128)(2,1)S(1)} fusion(bf16[46,64,640]{2,1,0:T(8,128)(2,1)} %bitcast.154, s32[4,2]{0,1:T(2,128)S(1)} %select_reduce_fusion), kind=kOutput, calls=%fused_computation.22 | convolution fusion | flops 30474608 | bytes 4423712 | tf_op jit(solution)/shard_map/smp,pwc->smwc/dot_general | solution.py:155
  16.1 9.8 %collective-permute-start.3 = (bf16[2,64,640]{2,1,0:T(8,128)(2,1)}, bf16[2,64,640]{2,1,0:T(8,128)(2,1)}, u32[]{:S(2)}, u32[]{:S(2)}) collective-permute-start(bf16[2,64,640]{2,1,0:T(8,128)(2,1)} %bitcast.152), channel_id=1, source_target_pairs={{0,126},{1,127},{2,0},{3,1},{4,2},{5,3},{6,4},{7,5},{8,6},{9,7},{1... | collective-permute-start | bytes 491528 | tf_op jit(solution)/shard_map/ppermute | solution.py:36
  29.9 2.5 %collective-permute-start.1 = (bf16[24,2048]{1,0:T(8,128)(2,1)S(1)}, bf16[24,2048]{1,0:T(8,128)(2,1)S(1)}, u32[]{:S(2)}, u32[]{:S(2)}) collective-permute-start(bf16[24,2048]{1,0:T(8,128)(2,1)S(1)} %fusion.47), channel_id=1, source_target_pairs={{0,128},{128,0},{1,129},{129,1},{2,130},{130,2},{3,131},{131,3},{4... | collective-permute-start | bytes 294920 | tf_op jit(solution)/shard_map/ppermute | solution.py:30
  36.0 5.7 %fusion.83 = (bf16[2944,320]{1,0:T(8,128)(2,1)}, bf16[2944,320]{1,0:T(8,128)(2,1)}) fusion(bf16[2944,640]{1,0:T(8,128)(2,1)} %bitcast.155), kind=kLoop, calls=%fused_computation.136 | loop fusion | bytes 7536640 | tf_op jit(solution)/shard_map/slice | solution.py:83
  42.4 3.0 %copy.100 = bf16[2944,320]{0,1:T(8,128)(2,1)S(1)} copy(bf16[2944,320]{1,0:T(8,128)(2,1)} %get-tuple-element.11) | data formatting | bytes 3768320
  45.4 4.1 %copy.102 = bf16[2944,320]{0,1:T(8,128)(2,1)} copy(bf16[2944,320]{1,0:T(8,128)(2,1)} %get-tuple-element.12) | data formatting | bytes 3768320
  50.2 3.0 %fusion.7 = f32[2,24,1920]{2,1,0:T(8,128)S(1)} fusion(bf16[1024,1920]{1,0:T(8,128)(2,1)} %param.13, s32[]{:T(128)S(6)} %select_n.135, bf16[1,24,2048]{2,1,0:T(8,128)(2,1)} %bitcast.162, bf16[1,24,2048]{2,1,0:T(8,128)(2,1)} %fusion.49, pred[]{:T(512)S(6)} %eq.103), kind=kOutput, calls=%fused_computation.11 | convolution fusion | flops 189186048 | bytes 4497413 | tf_op jit(solution)/shard_map/grd,df->grf/dot_general | solution.py:123
  53.9 2.3 %collective-permute-start.2 = (f32[24,1920]{1,0:T(8,128)}, f32[24,1920]{1,0:T(8,128)}, u32[]{:S(2)}, u32[]{:S(2)}) collective-permute-start(f32[24,1920]{1,0:T(8,128)} %select_bitcast_fusion.2), channel_id=1, source_target_pairs={{0,128},{128,0},{1,129},{129,1},{2,130},{130,2},{3,131},{131,3},{4... | collective-permute-start | bytes 552968 | tf_op jit(solution)/shard_map/ppermute | solution.py:30
  58.5 1.9 copy.101
  60.4 1.9 copy.103
  62.3 50.7 %collective-permute-done.2 = f32[24,1920]{1,0:T(8,128)} collective-permute-done((f32[24,1920]{1,0:T(8,128)}, f32[24,1920]{1,0:T(8,128)}, u32[]{:S(2)}, u32[]{:S(2)}) %collective-permute-start.2) | collective-permute-done | bytes 184352 | tf_op jit(solution)/shard_map/ppermute | solution.py:30
  114.8 1.3 fusion.86
  117.5 1.6 multiply_reduce_fusion
  119.2 4.0 %fusion.27 = f32[24,5,4,64]{3,0,2,1:T(8,128)S(1)} fusion(bf16[2944,5,64,1]{0,2,3,1:T(8,128)(2,1)S(1)} %bitcast.158, f32[5,24,4,2944]{3,1,2,0:T(8,128)S(1)} %get-tuple-element.27, f32[24,2944]{1,0:T(8,128)S(1)} %copy-done.3, f32[24,5,4]{0,2,1:T(4,128)S(1)} %get-tuple-element.10, pred[24,2944]{1,0:T(8,128)(4,1)S(1)} %broadcast_compare_fusion, ...), kind=kOutput, calls=%fused_computation.30 | convolution fusion | flops 1093816320 | bytes 8047360 | tf_op jit(solution)/shard_map/rkgt,tkd->rkgd/dot_general | solution.py:191
  124.1 2.2 %fusion.65 = f32[24,2048]{1,0:T(8,128)S(1)} fusion(bf16[640,2048]{1,0:T(8,128)(2,1)} %collective-permute-done, bf16[24,1280]{1,0:T(8,128)(2,1)S(1)} %convert_element_type.88, s32[]{:T(128)S(6)} %select_n.152), kind=kOutput, calls=%fused_computation.88 | convolution fusion | flops 62914560 | bytes 2848772 | tf_op jit(solution)/shard_map/dot_general | solution.py:206
  126.3 2.3 %multiply_reduce_fusion.2 = (f32[24]{0:T(128)S(1)}, f32[24,2048]{1,0:T(8,128)S(1)}) fusion(f32[24,2048]{1,0:T(8,128)S(1)} %fusion.65, bf16[640,2048]{1,0:T(8,128)(2,1)} %param.14, bf16[24,1280]{1,0:T(8,128)(2,1)S(1)} %convert_element_type.88, s32[]{:T(128)S(6)} %select_n.151, bf16[1,24,2048]{2,1,0:T(8,128)(2,1)S(1)} %copy-done.2), kind=kOutput, calls=%fused_computation.64 | convolution fusion | flops 63160296 | bytes 3143780 | tf_op jit(solution)/shard_map/dot_general | solution.py:205
  130.7 6.4 %collective-permute-start.9 = (bf16[24,2048]{1,0:T(8,128)(2,1)S(1)}, bf16[24,2048]{1,0:T(8,128)(2,1)S(1)}, u32[]{:S(2)}, u32[]{:S(2)}) collective-permute-start(bf16[24,2048]{1,0:T(8,128)(2,1)S(1)} %multiply_convert_fusion), channel_id=1, source_target_pairs={{0,64},{192,128},{1,65},{193,129},{2,66},{194,130},{3,67},{195,131... | collective-permute-start | bytes 294920 | tf_op jit(solution)/shard_map/ppermute | solution.py:210
  137.2 1.6 collective-permute-done.9
  138.9 11.2 %all-gather = bf16[96,2048]{1,0:T(8,128)(2,1)} all-gather(bf16[24,2048]{1,0:T(8,128)(2,1)S(1)} %fusion.44), channel_id=2, replica_groups=mesh['guide'=2,'x_lo'=2,'y'=4,'z'=8,'core'=2] {'y'}, dimensions={0}, use_global_device_ids=true | all-gather | bytes 491520 | tf_op jit(solution)/shard_map/all_gather | solution.py:219
  150.1 47.7 %all-gather.4.cloned.1.call-done = bf16[4,192,2048]{2,1,0:T(8,128)(2,1)} async-done(((bf16[4,24,2048]{2,1,0:T(8,128)(2,1)}), bf16[4,192,2048]{2,1,0:T(8,128)(2,1)}) %all-gather.4.cloned.1.call-update) | async-done | bytes 3145744 | tf_op jit(solution)/shard_map/all_gather | solution.py:220
  198.7 3.0 %fusion.33 = f32[4,8,24,250]{3,2,1,0:T(8,128)S(1)} fusion(bf16[4,8,24,2048]{3,2,1,0:T(8,128)(2,1)} %bitcast.167, bf16[2048,250]{1,0:T(8,128)(2,1)S(1)} %copy-done), kind=kOutput, calls=%fused_computation.34 | convolution fusion | flops 786432000 | bytes 4937728 | tf_op jit(solution)/shard_map/yzrd,dv->yzrv/dot_general | solution.py:223
  201.7 2.6 %collective-permute-done.10 = bf16[4,8,24,2048]{3,2,1,0:T(8,128)(2,1)} collective-permute-done((bf16[4,8,24,2048]{3,2,1,0:T(8,128)(2,1)}, bf16[4,8,24,2048]{3,2,1,0:T(8,128)(2,1)}, u32[]{:S(2)}, u32[]{:S(2)}) %collective-permute-start.10) | collective-permute-done | bytes 3145760 | tf_op jit(solution)/shard_map/ppermute | solution.py:222
  204.3 2.9 %select_bitcast_fusion.1 = (f32[4,8,1,24,250]{4,3,1,0,2:T(8,128)S(1)}, f32[4,8,1,24,250]{4,3,1,0,2:T(8,128)S(1)}) fusion(f32[4,8,24,250]{3,2,1,0:T(8,128)S(1)} %fusion.33, pred[]{:T(512)S(6)} %eq.102, bf16[4,8,24,2048]{3,2,1,0:T(8,128)(2,1)} %collective-permute-done.10, bf16[2048,250]{1,0:T(8,128)(2,1)S(1)} %copy-done), kind=kOutput, calls=%fused_computation.42 | convolution fusion | flops 786816000 | bytes 6473729 | tf_op jit(solution)/shard_map/yzrd,dv->yzrv/dot_general | solution.py:224
  207.3 1.4 copy.86
  (89 shorter events, 23.7 us)
Async XLA Ops:
  6.5 192.2 %copy-start = (bf16[2048,250]{1,0:T(8,128)(2,1)S(1)}, bf16[2048,250]{1,0:T(8,128)(2,1)}, u32[]{:S(2)}) copy-start(bf16[2048,250]{1,0:T(8,128)(2,1)} %param.16) | copy-start | bytes 3072004
  6.5 191.2 %all-gather.4.cloned.1.call-start = ((), (), s32[]{:S(2)}) async-start(), calls=%async_computation | async-start | bytes 3538944 | tf_op jit(solution)/shard_map/all_gather | solution.py:220
  9.3 20.3 %copy-start.2 = (bf16[1,24,2048]{2,1,0:T(8,128)(2,1)S(1)}, bf16[1,24,2048]{2,1,0:T(8,128)(2,1)}, u32[]{:S(2)}) copy-start(bf16[1,24,2048]{2,1,0:T(8,128)(2,1)} %param.11) | copy-start | bytes 294916
  9.4 20.5 %copy-start.7 = (f32[2048]{0:T(1024)S(1)}, f32[2048]{0:T(1024)}, u32[]{:S(2)}) copy-start(f32[2048]{0:T(1024)} %param.12) | copy-start | bytes 24580
  16.1 37.8 %collective-permute-start.3 = (bf16[2,64,640]{2,1,0:T(8,128)(2,1)}, bf16[2,64,640]{2,1,0:T(8,128)(2,1)}, u32[]{:S(2)}, u32[]{:S(2)}) collective-permute-start(bf16[2,64,640]{2,1,0:T(8,128)(2,1)} %bitcast.152), channel_id=1, source_target_pairs={{0,126},{1,127},{2,0},{3,1},{4,2},{5,3},{6,4},{7,5},{8,6},{9,7},{1... | collective-permute-start | bytes 491528 | tf_op jit(solution)/shard_map/ppermute | solution.py:36
  26.5 29.7 %collective-permute-start.4 = (bf16[2,64,640]{2,1,0:T(8,128)(2,1)}, bf16[2,64,640]{2,1,0:T(8,128)(2,1)}, u32[]{:S(2)}, u32[]{:S(2)}) collective-permute-start(bf16[2,64,640]{2,1,0:T(8,128)(2,1)} %bitcast.151), channel_id=1, source_target_pairs={{0,127},{1,0},{2,1},{3,2},{4,3},{5,4},{6,5},{7,6},{8,7},{9,8},{10,... | collective-permute-start | bytes 491528 | tf_op jit(solution)/shard_map/ppermute | solution.py:36
  28.2 28.0 %collective-permute-start.5 = (bf16[2,64,640]{2,1,0:T(8,128)(2,1)}, bf16[2,64,640]{2,1,0:T(8,128)(2,1)}, u32[]{:S(2)}, u32[]{:S(2)}) collective-permute-start(bf16[2,64,640]{2,1,0:T(8,128)(2,1)} %bitcast.150), channel_id=1, source_target_pairs={{0,1},{1,2},{2,3},{3,4},{4,5},{5,6},{6,7},{7,8},{8,9},{9,10},{10,1... | collective-permute-start | bytes 491528 | tf_op jit(solution)/shard_map/ppermute | solution.py:36
  29.7 26.5 %collective-permute-start.6 = (bf16[2,64,640]{2,1,0:T(8,128)(2,1)}, bf16[2,64,640]{2,1,0:T(8,128)(2,1)}, u32[]{:S(2)}, u32[]{:S(2)}) collective-permute-start(bf16[2,64,640]{2,1,0:T(8,128)(2,1)} %bitcast.149), channel_id=1, source_target_pairs={{0,2},{1,3},{2,4},{3,5},{4,6},{5,7},{6,8},{7,9},{8,10},{9,11},{10,... | collective-permute-start | bytes 491528 | tf_op jit(solution)/shard_map/ppermute | solution.py:36
  29.9 19.6 %collective-permute-start.1 = (bf16[24,2048]{1,0:T(8,128)(2,1)S(1)}, bf16[24,2048]{1,0:T(8,128)(2,1)S(1)}, u32[]{:S(2)}, u32[]{:S(2)}) collective-permute-start(bf16[24,2048]{1,0:T(8,128)(2,1)S(1)} %fusion.47), channel_id=1, source_target_pairs={{0,128},{128,0},{1,129},{129,1},{2,130},{130,2},{3,131},{131,3},{4... | collective-permute-start | bytes 294920 | tf_op jit(solution)/shard_map/ppermute | solution.py:30
  49.5 0.6 copy-start.5
  49.5 74.6 %collective-permute-start = (bf16[640,2048]{1,0:T(8,128)(2,1)}, bf16[640,2048]{1,0:T(8,128)(2,1)}, u32[]{:S(2)}, u32[]{:S(2)}) collective-permute-start(bf16[640,2048]{1,0:T(8,128)(2,1)} %param.14), channel_id=1, source_target_pairs={{0,128},{128,0},{1,129},{129,1},{2,130},{130,2},{3,131},{131,3},{4... | collective-permute-start | bytes 7864328 | tf_op jit(solution)/shard_map/ppermute | solution.py:30
  53.9 59.2 %collective-permute-start.2 = (f32[24,1920]{1,0:T(8,128)}, f32[24,1920]{1,0:T(8,128)}, u32[]{:S(2)}, u32[]{:S(2)}) collective-permute-start(f32[24,1920]{1,0:T(8,128)} %select_bitcast_fusion.2), channel_id=1, source_target_pairs={{0,128},{128,0},{1,129},{129,1},{2,130},{130,2},{3,131},{131,3},{4... | collective-permute-start | bytes 552968 | tf_op jit(solution)/shard_map/ppermute | solution.py:30
  116.1 1.4 copy-start.3
  117.1 2.0 copy-start.1
  119.1 4.0 %copy-start.4 = (bf16[512,320]{0,1:T(8,128)(2,1)S(1)}, bf16[512,320]{0,1:T(8,128)(2,1)}, u32[]{:S(2)}) copy-start(bf16[512,320]{0,1:T(8,128)(2,1)} %copy.103) | copy-start | bytes 983044
  123.1 5.5 %copy-start.6 = (f32[2048]{0:T(1024)S(1)}, f32[2048]{0:T(1024)}, u32[]{:S(2)}) copy-start(f32[2048]{0:T(1024)} %param.15) | copy-start | bytes 24580
  128.8 8.4 %collective-permute-start.7 = (bf16[24,2048]{1,0:T(8,128)(2,1)S(1)}, bf16[24,2048]{1,0:T(8,128)(2,1)S(1)}, u32[]{:S(2)}, u32[]{:S(2)}) collective-permute-start(bf16[24,2048]{1,0:T(8,128)(2,1)S(1)} %multiply_convert_fusion), channel_id=1, source_target_pairs={{128,0},{64,192},{129,1},{65,193},{130,2},{66,194},{131,3},{67,195... | collective-permute-start | bytes 294920 | tf_op jit(solution)/shard_map/ppermute | solution.py:212
  130.1 7.1 %collective-permute-start.8 = (bf16[24,2048]{1,0:T(8,128)(2,1)S(1)}, bf16[24,2048]{1,0:T(8,128)(2,1)S(1)}, u32[]{:S(2)}, u32[]{:S(2)}) collective-permute-start(bf16[24,2048]{1,0:T(8,128)(2,1)S(1)} %multiply_convert_fusion), channel_id=1, source_target_pairs={{128,64},{64,128},{129,65},{65,129},{130,66},{66,130},{131,67},{67... | collective-permute-start | bytes 294920 | tf_op jit(solution)/shard_map/ppermute | solution.py:211
  130.7 8.0 %collective-permute-start.9 = (bf16[24,2048]{1,0:T(8,128)(2,1)S(1)}, bf16[24,2048]{1,0:T(8,128)(2,1)S(1)}, u32[]{:S(2)}, u32[]{:S(2)}) collective-permute-start(bf16[24,2048]{1,0:T(8,128)(2,1)S(1)} %multiply_convert_fusion), channel_id=1, source_target_pairs={{0,64},{192,128},{1,65},{193,129},{2,66},{194,130},{3,67},{195,131... | collective-permute-start | bytes 294920 | tf_op jit(solution)/shard_map/ppermute | solution.py:210
  197.8 6.5 %collective-permute-start.10 = (bf16[4,8,24,2048]{3,2,1,0:T(8,128)(2,1)}, bf16[4,8,24,2048]{3,2,1,0:T(8,128)(2,1)}, u32[]{:S(2)}, u32[]{:S(2)}) collective-permute-start(bf16[4,8,24,2048]{3,2,1,0:T(8,128)(2,1)} %bitcast.166), channel_id=1, source_target_pairs={{0,1},{1,0},{2,3},{3,2},{4,5},{5,4},{6,7},{7,6},{8,9},{9,8},{10,11... | collective-permute-start | bytes 9437192 | tf_op jit(solution)/shard_map/ppermute | solution.py:222
Sparse Core Ops, SparseCore 0:
  150.2 47.5 all-gather.3

commit v10 on v7

--- a/solution.py
+++ b/solution.py
@@ -76,14 +76,14 @@
     return picked.reshape(tables.shape[0], tables.shape[1] * pool.shape[1], pool.shape[2])
 
 
-def dense_scores(queries, page_rows, counts):
+def dense_scores(blocked, page_rows, counts):
     count = page_rows.shape[0] * page_rows.shape[1]
     half_width = page_rows.shape[2] // 2
     flat = page_rows.reshape(count, page_rows.shape[2])
-    key_rows = flat[:, :half_width].reshape(count, KVH, HD)
-    value_rows = flat[:, half_width:].reshape(count, KVH, HD)
+    key_rows = flat[:, :half_width]
+    value_rows = flat[:, half_width:]
     scores = jnp.einsum(
-        "rkgd,tkd->rkgt", queries, key_rows, preferred_element_type=jnp.float32
+        "rkgc,tc->rkgt", blocked, key_rows, preferred_element_type=jnp.float32
     ) * (1.0 / math.sqrt(HD))
     scores = jnp.where(counts[:, None, None, :] > 0, scores, -jnp.inf)
     return (scores, value_rows)
@@ -171,8 +171,13 @@
     counts = jnp.einsum("rsp,rsw->rpw", hits, living).reshape(local_rows, -1)
     pool_counts = counts[:, : pool_pages * page_rows]
     arrived_counts = counts[:, pool_pages * page_rows :]
-    pool_scores, pool_values = dense_scores(queries, pool, pool_counts)
-    arrived_scores, arrived_values = dense_scores(queries, arrived, arrived_counts)
+    head_match = jnp.arange(KVH)[:, None] == jnp.arange(KVH)[None, :]
+    blocked = jnp.where(
+        head_match[None, :, None, :, None], queries[:, :, :, None, :], jnp.zeros((), queries.dtype)
+    ).reshape(local_rows, KVH, group, key_width)
+    pool_scores, pool_values = dense_scores(blocked, pool, pool_counts)
+    arrived_scores, arrived_values = dense_scores(blocked, arrived, arrived_counts)
+    spread = jnp.zeros((local_rows, KVH, group, key_width), jnp.float32)
     tops = jnp.maximum(
         jnp.maximum(jnp.max(pool_scores, axis=-1), jnp.max(arrived_scores, axis=-1)), own_score
     )
@@ -188,13 +193,16 @@
         weights = jnp.exp(scores - tops[..., None])
         sums = sums + jnp.sum(weights * count[:, None, None, :], axis=-1)
         rounded = weights.astype(jnp.bfloat16).astype(jnp.float32) * count[:, None, None, :]
-        accs = accs + jnp.einsum(
-            "rkgt,tkd->rkgd",
-            rounded,
-            values.astype(jnp.float32),
-            precision=lax.Precision.HIGHEST,
-            preferred_element_type=jnp.float32,
-        )
+        high = rounded.astype(jnp.bfloat16)
+        low = (rounded - high.astype(jnp.float32)).astype(jnp.bfloat16)
+        for piece in (high, low):
+            spread = spread + jnp.einsum(
+                "rkgt,tc->rkgc", piece, values, preferred_element_type=jnp.float32
+            )
+    spread = spread.reshape(local_rows, KVH, group, KVH, HD)
+    accs = accs + jnp.sum(
+        jnp.where(head_match[None, :, None, :, None], spread, 0.0), axis=3
+    )
     attended = (accs / sums[..., None]).reshape(local_rows, query_width).astype(jnp.bfloat16)
     partner_attended = from_partner(attended, "guide", 0)
     both_attended = jnp.where(

time: 174 us -> 175 us (level)
  local copies, waits for them, and re-layouts: 26.2 us -> 16 us
  waiting for transfers between devices: 66 us -> 71 us
  matrix products: 24 us -> 28.1 us
  other arithmetic: 10.6 us -> 13.9 us
  starting transfers between devices: 22.8 us -> 20.7 us
    unnamed x33 -> x37, local copies, waits for them, and re-layouts: 14.4 us -> 4.31 us
    ppermute x4, waiting for transfers between devices: 6.8 us -> 12.1 us  [from_partner(): return lax.ppermute(block, axis, route)]
    slice x2 -> x0, local copies, waits for them, and re-layouts: 4.32 us -> none  [the longest x1 3.42 us: dense_scores(): key_rows = flat[:, :half_width].reshape(count, KVH, HD)]
    dot_general x4 -> x6, matrix products: 7.63 us -> 11.8 us  [the longest x4 6.77 us: body(): jnp.einsum('rkgt,tc->rkgc', piece, values, preferred_element_type=jnp.flo...]
    ppermute x4, starting transfers between devices: 8.18 us -> 4.49 us  [from_partner(): return lax.ppermute(block, axis, route)]
    broadcast_in_dim x0 -> x4, local copies, waits for them, and re-layouts: none -> 3.2 us  [body(): jnp.where(head_match[None, :, None, :, None], queries[:, :, :, None, :],...]
    ppermute x4, starting transfers between devices: 9.02 us -> 11.5 us  [shifted(): return lax.ppermute(value, axis, pairs)]
    reduce_sum x0 -> x1, other arithmetic: none -> 2.32 us  [body(): jnp.sum(jnp.where(head_match[None, :, None, :, None], spread, 0.0), axis=3)]
  transfers between devices with their start and end apart: 13 -> 13, of which waited for: 5 -> 6; matrix products, arithmetic and copies ran while one was open for 24% -> 10% of each run, Pallas kernels for 0% -> 0%
where the time goes in v10:
time: 175 us
  waiting for transfers between devices  71 us (41%)
  matrix products  28.1 us (16%)
  starting transfers between devices  20.7 us (12%)
  local copies, waits for them, and re-layouts  16 us (9%)
  other arithmetic  13.9 us (8%)
  between operations  13.9 us (8%)
  blocking collectives  11.3 us (6%)
    all_gather x1, waiting for transfers between devices, body(): gathered = lax.all_gather(gathered, 'z', axis=1, tiled=False)  51.6 us
    ppermute x4, waiting for transfers between devices, from_partner(): return lax.ppermute(block, axis, route)  12.1 us
    ppermute x4, starting transfers between devices, shifted(): return lax.ppermute(value, axis, pairs)  11.5 us
    all_gather x1, blocking collectives, body(): gathered = lax.all_gather(combined, 'y', axis=0, tiled=False)  11.3 us
    dot_general x4, matrix products, body(): jnp.einsum('rkgt,tc->rkgc', piece, values, preferred_element_type=jnp.flo...  6.77 us
    dot_general x1, matrix products, body(): jnp.einsum('smp,pwc->smwc', page_hit, pool, preferred_element_type=jnp.fl...  5.05 us
    dot_general x2, matrix products, dense_scores(): jnp.einsum('rkgc,tc->rkgt', blocked, key_rows, preferred_element_type=jnp...  5.03 us
    ppermute x1, waiting for transfers between devices, body(): from_guide = lax.ppermute(final, pair, [(2, 0), (1, 3)])  4.88 us
  transfers between devices with their start and end apart: 13, of which 6 were waited for; matrix products, arithmetic and copies ran while one was open for 10% of the time, Pallas kernels for 0%

profile of v10, /device:TPU:1, one launch (start us, length us, event | category | flops | bytes accessed | tf_op | source)
XLA Modules:
  0.0 175.0 jit_solution(8588126387843517482)
XLA Ops:
  9.4 5.1 %fusion.16 = bf16[4,2,64,640]{3,0,2,1:T(4,128)(2,1)S(1)} fusion(bf16[46,64,640]{2,1,0:T(8,128)(2,1)} %bitcast.148, s32[4,2]{0,1:T(2,128)S(1)} %select_reduce_fusion.1), kind=kOutput, calls=%fused_computation.24 | convolution fusion | flops 30474608 | bytes 4423712 | tf_op jit(solution)/shard_map/smp,pwc->smwc/dot_general | solution.py:155
  16.2 9.8 %collective-permute-start.2 = (bf16[2,64,640]{2,1,0:T(8,128)(2,1)}, bf16[2,64,640]{2,1,0:T(8,128)(2,1)}, u32[]{:S(2)}, u32[]{:S(2)}) collective-permute-start(bf16[2,64,640]{2,1,0:T(8,128)(2,1)} %bitcast.146), channel_id=1, source_target_pairs={{0,126},{1,127},{2,0},{3,1},{4,2},{5,3},{6,4},{7,5},{8,6},{9,7},{1... | collective-permute-start | bytes 491528 | tf_op jit(solution)/shard_map/ppermute | solution.py:36
  30.0 2.5 %collective-permute-start = (bf16[24,2048]{1,0:T(8,128)(2,1)S(1)}, bf16[24,2048]{1,0:T(8,128)(2,1)S(1)}, u32[]{:S(2)}, u32[]{:S(2)}) collective-permute-start(bf16[24,2048]{1,0:T(8,128)(2,1)S(1)} %fusion.37), channel_id=1, source_target_pairs={{0,128},{128,0},{1,129},{129,1},{2,130},{130,2},{3,131},{131,3},{4... | collective-permute-start | bytes 294920 | tf_op jit(solution)/shard_map/ppermute | solution.py:30
  38.7 2.9 %fusion.5 = f32[2,24,1920]{2,1,0:T(8,128)S(1)} fusion(bf16[1024,1920]{1,0:T(8,128)(2,1)} %param.13, s32[]{:T(128)S(6)} %select_n.164, bf16[1,24,2048]{2,1,0:T(8,128)(2,1)} %bitcast.156, bf16[1,24,2048]{2,1,0:T(8,128)(2,1)S(1)} %fusion.39, pred[]{:T(512)S(6)} %eq.129), kind=kOutput, calls=%fused_computation.10 | convolution fusion | flops 189186048 | bytes 4497413 | tf_op jit(solution)/shard_map/grd,df->grf/dot_general | solution.py:123
  43.8 2.1 %pad_maximum_fusion.1 = bf16[8,64,640]{2,1,0:T(8,128)(2,1)} fusion(bf16[2,64,640]{2,1,0:T(8,128)(2,1)} %collective-permute-done.5, bf16[2,64,640]{2,1,0:T(8,128)(2,1)} %collective-permute-done.4, bf16[2,64,640]{2,1,0:T(8,128)(2,1)} %collective-permute-done.3, bf16[2,64,640]{2,1,0:T(8,128)(2,1)} %collective-permute-done.2), kind=kLoop, calls=%fused_computation.42 | loop fusion | flops 983040 | bytes 1310720 | tf_op jit(solution)/shard_map/concatenate | solution.py:159
  45.9 3.8 %collective-permute-done.1 = f32[24,1920]{1,0:T(8,128)} collective-permute-done((f32[24,1920]{1,0:T(8,128)}, f32[24,1920]{1,0:T(8,128)}, u32[]{:S(2)}, u32[]{:S(2)}) %collective-permute-start.1) | collective-permute-done | bytes 184352 | tf_op jit(solution)/shard_map/ppermute | solution.py:30
  52.0 1.9 %broadcast_in_dim.161 = bf16[24,5,4,320]{3,0,2,1:T(8,128)(2,1)S(1)} reshape(bf16[24,5,4,5,64]{4,3,0,2,1:T(8,128)(2,1)} %broadcast_in_dim.160) | data formatting | bytes 614400 | tf_op jit(solution)/shard_map/jit(_where)/broadcast_in_dim | solution.py:175
  54.4 1.6 fusion.86
  56.0 3.5 %fusion.1 = (f32[24,5,4]{0,2,1:T(4,128)S(1)}, f32[24,5,4,2944]{3,0,2,1:T(8,128)S(1)}) fusion(pred[24,2944]{1,0:T(8,128)(4,1)S(1)} %copy-done.6, bf16[2944,640]{1,0:T(8,128)(2,1)} %bitcast.149, bf16[24,5,4,320]{3,0,2,1:T(8,128)(2,1)S(1)} %broadcast_in_dim.161, pred[5,320]{1,0:T(8,128)(4,1)S(1)} %broadcast_in_dim.158), kind=kOutput, calls=%fused_computation.6 | convolution fusion | flops 908789248 | bytes 8294848 | tf_op jit(solution)/shard_map/rkgc,tc->rkgt/dot_general | solution.py:85
  60.1 2.1 %multiply_reduce_fusion = f32[24,5,4]{0,2,1:T(4,128)} fusion(f32[24,5,4,2944]{3,0,2,1:T(8,128)S(1)} %get-tuple-element.21, f32[24,2944]{1,0:T(8,128)S(1)} %copy-done.4, f32[24,5,4]{0,2,1:T(4,128)S(1)} %get-tuple-element.8, pred[24,2944]{1,0:T(8,128)(4,1)S(1)} %copy-done.6), kind=kLoop, calls=%fused_computation | loop fusion | flops 7065120 | bytes 6009600 | tf_op jit(solution)/shard_map/reduce_sum | solution.py:194
  62.3 2.6 %fusion.8 = f32[24,5,4,320]{3,0,2,1:T(8,128)S(1)} fusion(f32[24,2944]{1,0:T(8,128)S(1)} %copy-done.4, bf16[2944,640]{1,0:T(8,128)(2,1)S(1)} %bitcast.150, f32[24,5,4,2944]{3,0,2,1:T(8,128)S(1)} %get-tuple-element.21, f32[24,5,4]{0,2,1:T(4,128)S(1)} %get-tuple-element.8, pred[24,2944]{1,0:T(8,128)(4,1)S(1)} %copy-done.6), kind=kOutput, calls=%fused_computation.13 | convolution fusion | flops 914288640 | bytes 8891392 | tf_op jit(solution)/shard_map/rkgt,tc->rkgc/dot_general | solution.py:199
  64.9 2.9 %fusion.20 = f32[24,5,4,320]{3,0,2,1:T(8,128)S(1)} fusion(f32[24,5,4,320]{3,0,2,1:T(8,128)S(1)} %fusion.8, bf16[2944,640]{1,0:T(8,128)(2,1)S(1)} %bitcast.151, f32[24,2944]{1,0:T(8,128)S(1)} %copy-done.4, f32[24,5,4,2944]{3,0,2,1:T(8,128)S(1)} %get-tuple-element.21, f32[24,5,4]{0,2,1:T(4,128)S(1)} %get-tuple-element.8, pred[24,2944]{1,0:T(8,128)(4,1)S(1)} %copy-done.6), kind=kOutput, calls=%fused_computation.29 | convolution fusion | flops 918681600 | bytes 9628672 | tf_op jit(solution)/shard_map/rkgt,tc->rkgc/dot_general | solution.py:199
  70.1 1.6 reshape.291
  71.7 2.3 %select_reduce_fusion = f32[24,5,4,64]{3,0,2,1:T(8,128)S(1)} fusion(f32[24,5,4,5,64]{4,3,0,2,1:T(8,128)} %reshape.291, pred[5,5]{1,0:T(8,128)(4,1)} %copy-done.15), kind=kLoop, calls=%fused_computation.22 | loop fusion | flops 276480 | bytes 737305 | tf_op jit(solution)/shard_map/reduce_sum | solution.py:203
  75.6 3.9 %collective-permute-done.6 = bf16[24,1280]{1,0:T(8,128)(2,1)S(1)} collective-permute-done((bf16[24,1280]{1,0:T(8,128)(2,1)S(1)}, bf16[24,1280]{1,0:T(8,128)(2,1)S(1)}, u32[]{:S(2)}, u32[]{:S(2)}) %collective-permute-start.6) | collective-permute-done | bytes 61472 | tf_op jit(solution)/shard_map/ppermute | solution.py:30
  80.7 4.5 %collective-permute-done.7 = bf16[24,2048]{1,0:T(8,128)(2,1)S(1)} collective-permute-done((bf16[24,2048]{1,0:T(8,128)(2,1)S(1)}, bf16[24,2048]{1,0:T(8,128)(2,1)S(1)}, u32[]{:S(2)}, u32[]{:S(2)}) %collective-permute-start.7) | collective-permute-done | bytes 98336 | tf_op jit(solution)/shard_map/ppermute | solution.py:30
  85.4 1.9 %collective-permute-start.10 = (bf16[24,2048]{1,0:T(8,128)(2,1)S(1)}, bf16[24,2048]{1,0:T(8,128)(2,1)S(1)}, u32[]{:S(2)}, u32[]{:S(2)}) collective-permute-start(bf16[24,2048]{1,0:T(8,128)(2,1)S(1)} %multiply_convert_fusion), channel_id=1, source_target_pairs={{0,64},{192,128},{1,65},{193,129},{2,66},{194,130},{3,67},{195,131... | collective-permute-start | bytes 294920 | tf_op jit(solution)/shard_map/ppermute | solution.py:222
  89.2 4.9 %collective-permute-done.8 = bf16[24,2048]{1,0:T(8,128)(2,1)S(1)} collective-permute-done((bf16[24,2048]{1,0:T(8,128)(2,1)S(1)}, bf16[24,2048]{1,0:T(8,128)(2,1)S(1)}, u32[]{:S(2)}, u32[]{:S(2)}) %collective-permute-start.8) | collective-permute-done | bytes 98336 | tf_op jit(solution)/shard_map/ppermute | solution.py:224
  94.3 11.3 %all-gather = bf16[96,2048]{1,0:T(8,128)(2,1)} all-gather(bf16[24,2048]{1,0:T(8,128)(2,1)S(1)} %fusion.34), channel_id=2, replica_groups=mesh['guide'=2,'x_lo'=2,'y'=4,'z'=8,'core'=2] {'y'}, dimensions={0}, use_global_device_ids=true | all-gather | bytes 491520 | tf_op jit(solution)/shard_map/all_gather | solution.py:231
  105.6 51.6 %all-gather.4.cloned.1.call-done = bf16[4,192,2048]{2,1,0:T(8,128)(2,1)} async-done(((bf16[4,24,2048]{2,1,0:T(8,128)(2,1)}), bf16[4,192,2048]{2,1,0:T(8,128)(2,1)}) %all-gather.4.cloned.1.call-update) | async-done | bytes 3145744 | tf_op jit(solution)/shard_map/all_gather | solution.py:232
  158.1 3.2 %fusion.23 = f32[4,8,24,250]{3,2,1,0:T(8,128)S(1)} fusion(bf16[4,8,24,2048]{3,2,1,0:T(8,128)(2,1)} %bitcast.162, bf16[2048,250]{1,0:T(8,128)(2,1)} %param.16), kind=kOutput, calls=%fused_computation.32 | convolution fusion | flops 786432000 | bytes 4937728 | tf_op jit(solution)/shard_map/yzrd,dv->yzrv/dot_general | solution.py:235
  161.4 2.4 %collective-permute-done.11 = bf16[4,8,24,2048]{3,2,1,0:T(8,128)(2,1)} collective-permute-done((bf16[4,8,24,2048]{3,2,1,0:T(8,128)(2,1)}, bf16[4,8,24,2048]{3,2,1,0:T(8,128)(2,1)}, u32[]{:S(2)}, u32[]{:S(2)}) %collective-permute-start.11) | collective-permute-done | bytes 3145760 | tf_op jit(solution)/shard_map/ppermute | solution.py:234
  163.7 2.9 %select_bitcast_fusion.1 = (f32[4,8,1,24,250]{4,3,1,0,2:T(8,128)S(1)}, f32[4,8,1,24,250]{4,3,1,0,2:T(8,128)S(1)}) fusion(f32[4,8,24,250]{3,2,1,0:T(8,128)S(1)} %fusion.23, pred[]{:T(512)S(6)} %eq.128, bf16[4,8,24,2048]{3,2,1,0:T(8,128)(2,1)} %collective-permute-done.11, bf16[2048,250]{1,0:T(8,128)(2,1)S(1)} %copy-done.5), kind=kOutput, calls=%fused_computation.41 | convolution fusion | flops 786816000 | bytes 6473729 | tf_op jit(solution)/shard_map/yzrd,dv->yzrv/dot_general | solution.py:236
  166.8 1.4 copy.103
  (114 shorter events, 28.5 us)
Async XLA Ops:
  6.5 72.9 %copy-start = (bf16[640,2048]{1,0:T(8,128)(2,1)S(1)}, bf16[640,2048]{1,0:T(8,128)(2,1)}, u32[]{:S(2)}) copy-start(bf16[640,2048]{1,0:T(8,128)(2,1)} %param.14) | copy-start | bytes 7864324
  6.5 150.7 %all-gather.4.cloned.1.call-start = ((), (), s32[]{:S(2)}) async-start(), calls=%async_computation | async-start | bytes 3538944 | tf_op jit(solution)/shard_map/all_gather | solution.py:232
  9.4 20.4 %copy-start.3 = (bf16[1,24,2048]{2,1,0:T(8,128)(2,1)S(1)}, bf16[1,24,2048]{2,1,0:T(8,128)(2,1)}, u32[]{:S(2)}) copy-start(bf16[1,24,2048]{2,1,0:T(8,128)(2,1)} %param.11) | copy-start | bytes 294916
  9.4 20.5 %copy-start.14 = (f32[2048]{0:T(1024)S(1)}, f32[2048]{0:T(1024)}, u32[]{:S(2)}) copy-start(f32[2048]{0:T(1024)} %param.12) | copy-start | bytes 24580
  16.2 27.6 %collective-permute-start.2 = (bf16[2,64,640]{2,1,0:T(8,128)(2,1)}, bf16[2,64,640]{2,1,0:T(8,128)(2,1)}, u32[]{:S(2)}, u32[]{:S(2)}) collective-permute-start(bf16[2,64,640]{2,1,0:T(8,128)(2,1)} %bitcast.146), channel_id=1, source_target_pairs={{0,126},{1,127},{2,0},{3,1},{4,2},{5,3},{6,4},{7,5},{8,6},{9,7},{1... | collective-permute-start | bytes 491528 | tf_op jit(solution)/shard_map/ppermute | solution.py:36
  26.6 17.2 %collective-permute-start.3 = (bf16[2,64,640]{2,1,0:T(8,128)(2,1)}, bf16[2,64,640]{2,1,0:T(8,128)(2,1)}, u32[]{:S(2)}, u32[]{:S(2)}) collective-permute-start(bf16[2,64,640]{2,1,0:T(8,128)(2,1)} %bitcast.145), channel_id=1, source_target_pairs={{0,127},{1,0},{2,1},{3,2},{4,3},{5,4},{6,5},{7,6},{8,7},{9,8},{10,... | collective-permute-start | bytes 491528 | tf_op jit(solution)/shard_map/ppermute | solution.py:36
  28.3 15.5 %collective-permute-start.4 = (bf16[2,64,640]{2,1,0:T(8,128)(2,1)}, bf16[2,64,640]{2,1,0:T(8,128)(2,1)}, u32[]{:S(2)}, u32[]{:S(2)}) collective-permute-start(bf16[2,64,640]{2,1,0:T(8,128)(2,1)} %bitcast.144), channel_id=1, source_target_pairs={{0,1},{1,2},{2,3},{3,4},{4,5},{5,6},{6,7},{7,8},{8,9},{9,10},{10,1... | collective-permute-start | bytes 491528 | tf_op jit(solution)/shard_map/ppermute | solution.py:36
  29.8 14.1 %collective-permute-start.5 = (bf16[2,64,640]{2,1,0:T(8,128)(2,1)}, bf16[2,64,640]{2,1,0:T(8,128)(2,1)}, u32[]{:S(2)}, u32[]{:S(2)}) collective-permute-start(bf16[2,64,640]{2,1,0:T(8,128)(2,1)} %bitcast.143), channel_id=1, source_target_pairs={{0,2},{1,3},{2,4},{3,5},{4,6},{5,7},{6,8},{7,9},{8,10},{9,11},{10,... | collective-permute-start | bytes 491528 | tf_op jit(solution)/shard_map/ppermute | solution.py:36
  30.0 8.0 %collective-permute-start = (bf16[24,2048]{1,0:T(8,128)(2,1)S(1)}, bf16[24,2048]{1,0:T(8,128)(2,1)S(1)}, u32[]{:S(2)}, u32[]{:S(2)}) collective-permute-start(bf16[24,2048]{1,0:T(8,128)(2,1)S(1)} %fusion.37), channel_id=1, source_target_pairs={{0,128},{128,0},{1,129},{129,1},{2,130},{130,2},{3,131},{131,3},{4... | collective-permute-start | bytes 294920 | tf_op jit(solution)/shard_map/ppermute | solution.py:30
  42.4 7.3 %collective-permute-start.1 = (f32[24,1920]{1,0:T(8,128)}, f32[24,1920]{1,0:T(8,128)}, u32[]{:S(2)}, u32[]{:S(2)}) collective-permute-start(f32[24,1920]{1,0:T(8,128)} %select_bitcast_fusion.2), channel_id=1, source_target_pairs={{0,128},{128,0},{1,129},{129,1},{2,130},{130,2},{3,131},{131,3},{4... | collective-permute-start | bytes 552968 | tf_op jit(solution)/shard_map/ppermute | solution.py:30
  42.9 11.5 %copy-start.15 = (pred[5,5]{1,0:T(8,128)(4,1)}, pred[5,5]{1,0:T(8,128)(4,1)S(1)}, u32[]{:S(2)}) copy-start(pred[5,5]{1,0:T(8,128)(4,1)S(1)} %iota_compare_fusion.4) | copy-start | bytes 79
  43.8 12.2 %copy-start.6 = (pred[24,2944]{1,0:T(8,128)(4,1)S(1)}, pred[24,2944]{1,0:T(8,128)(4,1)}, u32[]{:S(2)}) copy-start(pred[24,2944]{1,0:T(8,128)(4,1)} %broadcast_compare_fusion) | copy-start | bytes 211972
  54.4 5.1 %copy-start.8 = (f32[24,5,1,4]{0,3,1,2:T(4,128)}, f32[24,5,1,4]{0,3,1,2:T(4,128)S(1)}, u32[]{:S(2)}) copy-start(f32[24,5,1,4]{0,3,1,2:T(4,128)S(1)} %copy.105) | copy-start | bytes 5764
  56.0 4.1 %copy-start.4 = (f32[24,2944]{1,0:T(8,128)S(1)}, f32[24,2944]{1,0:T(8,128)}, u32[]{:S(2)}) copy-start(f32[24,2944]{1,0:T(8,128)} %slice.94) | copy-start | bytes 847876
  70.0 4.1 %copy-start.9 = (f32[24,5,1,4]{0,3,1,2:T(4,128)S(1)}, f32[24,5,1,4]{0,3,1,2:T(4,128)}, u32[]{:S(2)}) copy-start(f32[24,5,1,4]{0,3,1,2:T(4,128)} %copy-done.8) | copy-start | bytes 5764
  70.1 4.1 %copy-start.12 = (f32[24,5,4]{0,2,1:T(4,128)S(1)}, f32[24,5,4]{0,2,1:T(4,128)}, u32[]{:S(2)}) copy-start(f32[24,5,4]{0,2,1:T(4,128)} %get-tuple-element.7) | copy-start | bytes 5764
  74.0 11.3 %copy-start.13 = (f32[2048]{0:T(1024)S(1)}, f32[2048]{0:T(1024)}, u32[]{:S(2)}) copy-start(f32[2048]{0:T(1024)} %param.15) | copy-start | bytes 24580
  74.6 4.9 %collective-permute-start.6 = (bf16[24,1280]{1,0:T(8,128)(2,1)S(1)}, bf16[24,1280]{1,0:T(8,128)(2,1)S(1)}, u32[]{:S(2)}, u32[]{:S(2)}) collective-permute-start(bf16[24,1280]{1,0:T(8,128)(2,1)S(1)} %convert_element_type.130), channel_id=1, source_target_pairs={{0,128},{128,0},{1,129},{129,1},{2,130},{130,2},{3,131},{131,3},{4... | collective-permute-start | bytes 184328 | tf_op jit(solution)/shard_map/ppermute | solution.py:30
  80.1 5.1 %collective-permute-start.7 = (bf16[24,2048]{1,0:T(8,128)(2,1)S(1)}, bf16[24,2048]{1,0:T(8,128)(2,1)S(1)}, u32[]{:S(2)}, u32[]{:S(2)}) collective-permute-start(bf16[24,2048]{1,0:T(8,128)(2,1)S(1)} %fusion.45), channel_id=1, source_target_pairs={{0,128},{128,0},{1,129},{129,1},{2,130},{130,2},{3,131},{131,3},{4... | collective-permute-start | bytes 294920 | tf_op jit(solution)/shard_map/ppermute | solution.py:30
  85.4 3.8 %collective-permute-start.10 = (bf16[24,2048]{1,0:T(8,128)(2,1)S(1)}, bf16[24,2048]{1,0:T(8,128)(2,1)S(1)}, u32[]{:S(2)}, u32[]{:S(2)}) collective-permute-start(bf16[24,2048]{1,0:T(8,128)(2,1)S(1)} %multiply_convert_fusion), channel_id=1, source_target_pairs={{0,64},{192,128},{1,65},{193,129},{2,66},{194,130},{3,67},{195,131... | collective-permute-start | bytes 294920 | tf_op jit(solution)/shard_map/ppermute | solution.py:222
  87.2 6.9 %collective-permute-start.8 = (bf16[24,2048]{1,0:T(8,128)(2,1)S(1)}, bf16[24,2048]{1,0:T(8,128)(2,1)S(1)}, u32[]{:S(2)}, u32[]{:S(2)}) collective-permute-start(bf16[24,2048]{1,0:T(8,128)(2,1)S(1)} %multiply_convert_fusion), channel_id=1, source_target_pairs={{128,0},{64,192},{129,1},{65,193},{130,2},{66,194},{131,3},{67,195... | collective-permute-start | bytes 294920 | tf_op jit(solution)/shard_map/ppermute | solution.py:224
  88.5 5.6 %collective-permute-start.9 = (bf16[24,2048]{1,0:T(8,128)(2,1)S(1)}, bf16[24,2048]{1,0:T(8,128)(2,1)S(1)}, u32[]{:S(2)}, u32[]{:S(2)}) collective-permute-start(bf16[24,2048]{1,0:T(8,128)(2,1)S(1)} %multiply_convert_fusion), channel_id=1, source_target_pairs={{128,64},{64,128},{129,65},{65,129},{130,66},{66,130},{131,67},{67... | collective-permute-start | bytes 294920 | tf_op jit(solution)/shard_map/ppermute | solution.py:223
  157.2 6.5 %collective-permute-start.11 = (bf16[4,8,24,2048]{3,2,1,0:T(8,128)(2,1)}, bf16[4,8,24,2048]{3,2,1,0:T(8,128)(2,1)}, u32[]{:S(2)}, u32[]{:S(2)}) collective-permute-start(bf16[4,8,24,2048]{3,2,1,0:T(8,128)(2,1)} %bitcast.161), channel_id=1, source_target_pairs={{0,1},{1,0},{2,3},{3,2},{4,5},{5,4},{6,7},{7,6},{8,9},{9,8},{10,11... | collective-permute-start | bytes 9437192 | tf_op jit(solution)/shard_map/ppermute | solution.py:234
  158.1 5.6 %copy-start.5 = (bf16[2048,250]{1,0:T(8,128)(2,1)S(1)}, bf16[2048,250]{1,0:T(8,128)(2,1)}, u32[]{:S(2)}) copy-start(bf16[2048,250]{1,0:T(8,128)(2,1)} %param.16) | copy-start | bytes 3072004
  (5 other events, 15.6 us)
Sparse Core Ops, SparseCore 0:
  105.7 51.4 all-gather.3

commit v11 on v7

--- a/solution.py
+++ b/solution.py
@@ -220,19 +220,30 @@
     cond = jnp.where(side == 0, same_group, other_group).astype(jnp.float32)
     uncond = jnp.where(side == 0, other_group, same_group).astype(jnp.float32)
     combined = (uncond + guidance * (cond - uncond)).astype(jnp.bfloat16)
-    gathered = lax.all_gather(combined, "y", axis=0, tiled=False)
+    y_index = lax.axis_index("y")
+    y_count = lax.axis_size("y")
+    by_distance = [combined] + [
+        shifted(combined, "y", distance) for distance in range(1, y_count)
+    ]
+    in_order = []
+    for position in range(y_count):
+        distance = jnp.remainder(position - y_index, y_count)
+        pick = by_distance[0]
+        for step in range(1, y_count):
+            pick = jnp.where(distance == y_count - step, by_distance[step], pick)
+        in_order.append(pick)
+    gathered = jnp.stack(in_order)
     gathered = lax.all_gather(gathered, "z", axis=1, tiled=False)
     core = lax.axis_index("core")
+    cores = lax.axis_size("core")
     twin = lax.ppermute(gathered, "core", [(0, 1), (1, 0)])
     mine_logits = jnp.einsum("yzrd,dv->yzrv", gathered, w_vocab, preferred_element_type=jnp.float32)
     twin_logits = jnp.einsum("yzrd,dv->yzrv", twin, w_vocab, preferred_element_type=jnp.float32)
-    logits = jnp.stack(
-        [
-            jnp.where(core == 0, mine_logits, twin_logits),
-            jnp.where(core == 0, twin_logits, mine_logits),
-        ],
-        axis=2,
-    )
+    logits = jnp.zeros(
+        mine_logits.shape[:2] + (cores,) + mine_logits.shape[2:], jnp.float32
+    )
+    logits = lax.dynamic_update_slice_in_dim(logits, mine_logits[:, :, None], core, 2)
+    logits = lax.dynamic_update_slice_in_dim(logits, twin_logits[:, :, None], 1 - core, 2)
     return logits.reshape(-1, logits.shape[-1])
 
 

time: 174 us -> 173 us (level)
  blocking collectives: 10.4 us -> 0 us
  waiting for transfers between devices: 66 us -> 73.4 us
  local copies, waits for them, and re-layouts: 26.2 us -> 28.5 us
    all_gather x1 -> x0, blocking collectives: 10.4 us -> none  [body(): gathered = lax.all_gather(combined, 'y', axis=0, tiled=False)]
    ppermute x4 -> x7, waiting for transfers between devices: 0.01 us -> 4.88 us  [shifted(): return lax.ppermute(value, axis, pairs)]
    ppermute x4 -> x7, starting transfers between devices: 9.02 us -> 13.1 us  [shifted(): return lax.ppermute(value, axis, pairs)]
    ppermute x4, starting transfers between devices: 8.18 us -> 4.21 us  [from_partner(): return lax.ppermute(block, axis, route)]
    ppermute x4, waiting for transfers between devices: 6.8 us -> 10.4 us  [from_partner(): return lax.ppermute(block, axis, route)]
    slice x1, local copies, waits for them, and re-layouts: 3.42 us -> 5.68 us  [dense_scores(): key_rows = flat[:, :half_width].reshape(count, KVH, HD)]
    unnamed x33 -> x29, local copies, waits for them, and re-layouts: 14.4 us -> 15.6 us
  transfers between devices with their start and end apart: 13 -> 16, of which waited for: 5 -> 9; matrix products, arithmetic and copies ran while one was open for 24% -> 20% of each run, Pallas kernels for 0% -> 0%
where the time goes in v11:
time: 173 us; the launch traced here: 172 us
  waiting for transfers between devices  73.4 us (42%)
  local copies, waits for them, and re-layouts  28.5 us (16%)
  matrix products  24.9 us (14%)
  starting transfers between devices  22 us (13%)
  between operations  13.8 us (8%)
  other arithmetic  9.46 us (5%)
    all_gather x1, waiting for transfers between devices, body(): gathered = lax.all_gather(gathered, 'z', axis=1, tiled=False)  51 us
    unnamed x29, local copies, waits for them, and re-layouts  15.6 us
    ppermute x7, starting transfers between devices, shifted(): return lax.ppermute(value, axis, pairs)  13.1 us
    ppermute x4, waiting for transfers between devices, from_partner(): return lax.ppermute(block, axis, route)  10.4 us
    slice x1, local copies, waits for them, and re-layouts, dense_scores(): key_rows = flat[:, :half_width].reshape(count, KVH, HD)  5.68 us
    dot_general x1, matrix products, body(): jnp.einsum('smp,pwc->smwc', page_hit, pool, preferred_element_type=jnp.fl...  5.05 us
    ppermute x7, waiting for transfers between devices, shifted(): return lax.ppermute(value, axis, pairs)  4.88 us
    ppermute x1, waiting for transfers between devices, body(): from_guide = lax.ppermute(final, pair, [(2, 0), (1, 3)])  4.88 us
  transfers between devices with their start and end apart: 16, of which 9 were waited for; matrix products, arithmetic and copies ran while one was open for 20% of the time, Pallas kernels for 0%

profile of v11, /device:TPU:1, one launch (start us, length us, event | category | flops | bytes accessed | tf_op | source)
XLA Modules:
  0.0 172.0 jit_solution(17864761783289324508)
XLA Ops:
  9.4 5.1 %fusion.18 = bf16[4,2,64,640]{3,0,2,1:T(4,128)(2,1)S(1)} fusion(bf16[46,64,640]{2,1,0:T(8,128)(2,1)} %bitcast.177, s32[4,2]{0,1:T(2,128)S(1)} %select_reduce_fusion), kind=kOutput, calls=%fused_computation.21 | convolution fusion | flops 30474608 | bytes 4423712 | tf_op jit(solution)/shard_map/smp,pwc->smwc/dot_general | solution.py:155
  16.1 9.8 %collective-permute-start.2 = (bf16[2,64,640]{2,1,0:T(8,128)(2,1)}, bf16[2,64,640]{2,1,0:T(8,128)(2,1)S(1)}, u32[]{:S(2)}, u32[]{:S(2)}) collective-permute-start(bf16[2,64,640]{2,1,0:T(8,128)(2,1)} %bitcast.175), channel_id=1, source_target_pairs={{0,126},{1,127},{2,0},{3,1},{4,2},{5,3},{6,4},{7,5},{8,6},{9,7},{1... | collective-permute-start | bytes 491528 | tf_op jit(solution)/shard_map/ppermute | solution.py:36
  30.0 2.5 %collective-permute-start = (bf16[24,2048]{1,0:T(8,128)(2,1)S(1)}, bf16[24,2048]{1,0:T(8,128)(2,1)}, u32[]{:S(2)}, u32[]{:S(2)}) collective-permute-start(bf16[24,2048]{1,0:T(8,128)(2,1)S(1)} %fusion.49), channel_id=1, source_target_pairs={{0,128},{128,0},{1,129},{129,1},{2,130},{130,2},{3,131},{131,3},{4... | collective-permute-start | bytes 294920 | tf_op jit(solution)/shard_map/ppermute | solution.py:30
  34.7 1.3 fusion.62
  37.3 5.7 %fusion.90 = (bf16[2944,320]{1,0:T(8,128)(2,1)}, bf16[2944,320]{1,0:T(8,128)(2,1)}) fusion(bf16[2944,640]{1,0:T(8,128)(2,1)} %bitcast.178), kind=kLoop, calls=%fused_computation.149 | loop fusion | bytes 7536640 | tf_op jit(solution)/shard_map/slice | solution.py:83
  45.0 4.1 %copy.112 = bf16[2944,320]{0,1:T(8,128)(2,1)} copy(bf16[2944,320]{1,0:T(8,128)(2,1)} %get-tuple-element.9) | data formatting | bytes 3768320
  49.0 4.1 %copy.114 = bf16[2944,320]{0,1:T(8,128)(2,1)} copy(bf16[2944,320]{1,0:T(8,128)(2,1)} %get-tuple-element.10) | data formatting | bytes 3768320
  53.1 2.9 %fusion.7 = f32[2,24,1920]{2,1,0:T(8,128)S(1)} fusion(bf16[1024,1920]{1,0:T(8,128)(2,1)} %param.13, s32[]{:T(128)S(6)} %select_n.243, bf16[1,24,2048]{2,1,0:T(8,128)(2,1)} %bitcast.1, bf16[1,24,2048]{2,1,0:T(8,128)(2,1)S(1)} %fusion.51, pred[]{:T(512)S(6)} %eq.143), kind=kOutput, calls=%fused_computation.11 | convolution fusion | flops 189186048 | bytes 4497413 | tf_op jit(solution)/shard_map/grd,df->grf/dot_general | solution.py:123
  59.4 1.9 %copy.113 = bf16[512,320]{0,1:T(8,128)(2,1)} copy(bf16[512,320]{1,0:T(8,128)(2,1)} %get-tuple-element.12) | data formatting | bytes 655360
  62.2 1.9 %collective-permute-done.1 = f32[24,1920]{1,0:T(8,128)} collective-permute-done((f32[24,1920]{1,0:T(8,128)}, f32[24,1920]{1,0:T(8,128)}, u32[]{:S(2)}, u32[]{:S(2)}) %collective-permute-start.1) | collective-permute-done | bytes 184352 | tf_op jit(solution)/shard_map/ppermute | solution.py:30
  65.9 1.3 fusion.93
  67.2 2.6 %bitcast_reduce_fusion = (f32[24,5,4]{0,2,1:T(4,128)S(1)}, f32[5,24,4,2944]{3,1,2,0:T(8,128)S(1)}) fusion(pred[24,2944]{1,0:T(8,128)(4,1)S(1)} %broadcast_compare_fusion, bf16[2944,5,64,1]{0,2,3,1:T(8,128)(2,1)} %bitcast.179, bf16[24,5,4,64]{3,2,1,0:T(4,128)(2,1)S(1)} %reshape.239), kind=kOutput, calls=%fused_computation.1 | convolution fusion | flops 185118240 | bytes 7670656 | tf_op jit(solution)/shard_map/rkgd,tkd->rkgt/dot_general | solution.py:85
  69.9 1.6 multiply_reduce_fusion
  71.9 4.0 %fusion.30 = f32[24,5,4,64]{3,0,2,1:T(8,128)S(1)} fusion(bf16[2944,5,64,1]{0,2,3,1:T(8,128)(2,1)S(1)} %bitcast.181, f32[5,24,4,2944]{3,1,2,0:T(8,128)S(1)} %get-tuple-element.27, f32[24,2944]{1,0:T(8,128)S(1)} %copy-done.4, f32[24,5,4]{0,2,1:T(4,128)S(1)} %get-tuple-element.8, pred[24,2944]{1,0:T(8,128)(4,1)S(1)} %broadcast_compare_fusion, ...), kind=kOutput, calls=%fused_computation.33 | convolution fusion | flops 1093816320 | bytes 8047360 | tf_op jit(solution)/shard_map/rkgt,tkd->rkgd/dot_general | solution.py:191
  77.5 3.9 %collective-permute-done.6 = bf16[24,1280]{1,0:T(8,128)(2,1)S(1)} collective-permute-done((bf16[24,1280]{1,0:T(8,128)(2,1)S(1)}, bf16[24,1280]{1,0:T(8,128)(2,1)S(1)}, u32[]{:S(2)}, u32[]{:S(2)}) %collective-permute-start.6) | collective-permute-done | bytes 61472 | tf_op jit(solution)/shard_map/ppermute | solution.py:30
  82.6 4.5 %collective-permute-done.7 = bf16[24,2048]{1,0:T(8,128)(2,1)S(1)} collective-permute-done((bf16[24,2048]{1,0:T(8,128)(2,1)S(1)}, bf16[24,2048]{1,0:T(8,128)(2,1)S(1)}, u32[]{:S(2)}, u32[]{:S(2)}) %collective-permute-start.7) | collective-permute-done | bytes 98336 | tf_op jit(solution)/shard_map/ppermute | solution.py:30
  87.4 1.8 %collective-permute-start.10 = (bf16[24,2048]{1,0:T(8,128)(2,1)S(1)}, bf16[24,2048]{1,0:T(8,128)(2,1)S(1)}, u32[]{:S(2)}, u32[]{:S(2)}) collective-permute-start(bf16[24,2048]{1,0:T(8,128)(2,1)S(1)} %multiply_convert_fusion), channel_id=1, source_target_pairs={{0,64},{192,128},{1,65},{193,129},{2,66},{194,130},{3,67},{195,131... | collective-permute-start | bytes 294920 | tf_op jit(solution)/shard_map/ppermute | solution.py:214
  91.2 4.9 %collective-permute-done.8 = bf16[24,2048]{1,0:T(8,128)(2,1)S(1)} collective-permute-done((bf16[24,2048]{1,0:T(8,128)(2,1)S(1)}, bf16[24,2048]{1,0:T(8,128)(2,1)S(1)}, u32[]{:S(2)}, u32[]{:S(2)}) %collective-permute-start.8) | collective-permute-done | bytes 98336 | tf_op jit(solution)/shard_map/ppermute | solution.py:216
  97.8 2.3 %collective-permute-done.11 = bf16[24,2048]{1,0:T(8,128)(2,1)S(1)} collective-permute-done((bf16[24,2048]{1,0:T(8,128)(2,1)S(1)}, bf16[24,2048]{1,0:T(8,128)(2,1)S(1)}, u32[]{:S(2)}, u32[]{:S(2)}) %collective-permute-start.11) | collective-permute-done | bytes 98336 | tf_op jit(solution)/shard_map/ppermute | solution.py:36
  100.1 1.6 collective-permute-done.12
  103.5 51.0 %all-gather.3.cloned.1.call-done = bf16[4,192,2048]{2,1,0:T(8,128)(2,1)} async-done(((bf16[4,24,2048]{2,1,0:T(8,128)(2,1)}), bf16[4,192,2048]{2,1,0:T(8,128)(2,1)}) %all-gather.3.cloned.1.call-update) | async-done | bytes 3145744 | tf_op jit(solution)/shard_map/all_gather | solution.py:236
  155.7 3.3 %fusion.24 = f32[4,8,2,24,250]{4,3,2,1,0:T(8,128)S(1)} fusion(f32[4,8,2,24,250]{4,3,2,1,0:T(8,128)S(1)} %broadcast_in_dim.84, s32[]{:T(128)S(6)} %select_n.294, bf16[4,8,24,2048]{3,2,1,0:T(8,128)(2,1)} %bitcast.189, bf16[2048,250]{1,0:T(8,128)(2,1)} %param.16), kind=kOutput, calls=%fused_computation.28 | convolution fusion | flops 786432000 | bytes 4956164 | tf_op jit(solution)/shard_map/yzrd,dv->yzrv/dot_general | solution.py:240
  158.9 2.2 %collective-permute-done.14 = bf16[4,8,24,2048]{3,2,1,0:T(8,128)(2,1)} collective-permute-done((bf16[4,8,24,2048]{3,2,1,0:T(8,128)(2,1)}, bf16[4,8,24,2048]{3,2,1,0:T(8,128)(2,1)}, u32[]{:S(2)}, u32[]{:S(2)}) %collective-permute-start.14) | collective-permute-done | bytes 3145760 | tf_op jit(solution)/shard_map/ppermute | solution.py:239
  161.1 2.9 %fusion.23 = f32[4,8,2,24,250]{4,3,2,1,0:T(8,128)S(1)} fusion(f32[4,8,2,24,250]{4,3,2,1,0:T(8,128)S(1)} %fusion.24, s32[]{:T(128)S(6)} %select_n.295, bf16[4,8,24,2048]{3,2,1,0:T(8,128)(2,1)} %collective-permute-done.14, bf16[2048,250]{1,0:T(8,128)(2,1)S(1)} %copy-done.9), kind=kOutput, calls=%fused_computation.26 | convolution fusion | flops 786432000 | bytes 4980740 | tf_op jit(solution)/shard_map/yzrd,dv->yzrv/dot_general | solution.py:241
  (103 shorter events, 31.1 us)
Async XLA Ops:
  6.5 74.9 %copy-start = (bf16[640,2048]{1,0:T(8,128)(2,1)S(1)}, bf16[640,2048]{1,0:T(8,128)(2,1)}, u32[]{:S(2)}) copy-start(bf16[640,2048]{1,0:T(8,128)(2,1)} %param.14) | copy-start | bytes 7864324
  6.5 148.0 %all-gather.3.cloned.1.call-start = ((), (), s32[]{:S(2)}) async-start(), calls=%async_computation | async-start | bytes 3538944 | tf_op jit(solution)/shard_map/all_gather | solution.py:236
  9.4 20.3 %copy-start.3 = (bf16[1,24,2048]{2,1,0:T(8,128)(2,1)S(1)}, bf16[1,24,2048]{2,1,0:T(8,128)(2,1)}, u32[]{:S(2)}) copy-start(bf16[1,24,2048]{2,1,0:T(8,128)(2,1)} %param.11) | copy-start | bytes 294916
  9.4 20.4 %copy-start.8 = (f32[2048]{0:T(1024)S(1)}, f32[2048]{0:T(1024)}, u32[]{:S(2)}) copy-start(f32[2048]{0:T(1024)} %param.12) | copy-start | bytes 24580
  16.1 41.2 %collective-permute-start.2 = (bf16[2,64,640]{2,1,0:T(8,128)(2,1)}, bf16[2,64,640]{2,1,0:T(8,128)(2,1)S(1)}, u32[]{:S(2)}, u32[]{:S(2)}) collective-permute-start(bf16[2,64,640]{2,1,0:T(8,128)(2,1)} %bitcast.175), channel_id=1, source_target_pairs={{0,126},{1,127},{2,0},{3,1},{4,2},{5,3},{6,4},{7,5},{8,6},{9,7},{1... | collective-permute-start | bytes 491528 | tf_op jit(solution)/shard_map/ppermute | solution.py:36
  26.6 30.7 %collective-permute-start.3 = (bf16[2,64,640]{2,1,0:T(8,128)(2,1)}, bf16[2,64,640]{2,1,0:T(8,128)(2,1)}, u32[]{:S(2)}, u32[]{:S(2)}) collective-permute-start(bf16[2,64,640]{2,1,0:T(8,128)(2,1)} %bitcast.174), channel_id=1, source_target_pairs={{0,127},{1,0},{2,1},{3,2},{4,3},{5,4},{6,5},{7,6},{8,7},{9,8},{10,... | collective-permute-start | bytes 491528 | tf_op jit(solution)/shard_map/ppermute | solution.py:36
  28.2 29.1 %collective-permute-start.4 = (bf16[2,64,640]{2,1,0:T(8,128)(2,1)}, bf16[2,64,640]{2,1,0:T(8,128)(2,1)}, u32[]{:S(2)}, u32[]{:S(2)}) collective-permute-start(bf16[2,64,640]{2,1,0:T(8,128)(2,1)} %bitcast.173), channel_id=1, source_target_pairs={{0,1},{1,2},{2,3},{3,4},{4,5},{5,6},{6,7},{7,8},{8,9},{9,10},{10,1... | collective-permute-start | bytes 491528 | tf_op jit(solution)/shard_map/ppermute | solution.py:36
  29.7 27.6 %collective-permute-start.5 = (bf16[2,64,640]{2,1,0:T(8,128)(2,1)}, bf16[2,64,640]{2,1,0:T(8,128)(2,1)}, u32[]{:S(2)}, u32[]{:S(2)}) collective-permute-start(bf16[2,64,640]{2,1,0:T(8,128)(2,1)} %bitcast.172), channel_id=1, source_target_pairs={{0,2},{1,3},{2,4},{3,5},{4,6},{5,7},{6,8},{7,9},{8,10},{9,11},{10,... | collective-permute-start | bytes 491528 | tf_op jit(solution)/shard_map/ppermute | solution.py:36
  30.0 23.2 %collective-permute-start = (bf16[24,2048]{1,0:T(8,128)(2,1)S(1)}, bf16[24,2048]{1,0:T(8,128)(2,1)}, u32[]{:S(2)}, u32[]{:S(2)}) collective-permute-start(bf16[24,2048]{1,0:T(8,128)(2,1)S(1)} %fusion.49), channel_id=1, source_target_pairs={{0,128},{128,0},{1,129},{129,1},{2,130},{130,2},{3,131},{131,3},{4... | collective-permute-start | bytes 294920 | tf_op jit(solution)/shard_map/ppermute | solution.py:30
  56.8 7.3 %collective-permute-start.1 = (f32[24,1920]{1,0:T(8,128)}, f32[24,1920]{1,0:T(8,128)}, u32[]{:S(2)}, u32[]{:S(2)}) collective-permute-start(f32[24,1920]{1,0:T(8,128)} %select_bitcast_fusion), channel_id=1, source_target_pairs={{0,128},{128,0},{1,129},{129,1},{2,130},{130,2},{3,131},{131,3},{4... | collective-permute-start | bytes 552968 | tf_op jit(solution)/shard_map/ppermute | solution.py:30
  67.2 2.7 %copy-start.4 = (f32[24,2944]{1,0:T(8,128)S(1)}, f32[24,2944]{1,0:T(8,128)}, u32[]{:S(2)}) copy-start(f32[24,2944]{1,0:T(8,128)} %slice.94) | copy-start | bytes 847876
  69.8 2.0 %copy-start.1 = (bf16[2944,320]{0,1:T(8,128)(2,1)S(1)}, bf16[2944,320]{0,1:T(8,128)(2,1)}, u32[]{:S(2)}) copy-start(bf16[2944,320]{0,1:T(8,128)(2,1)} %copy.114) | copy-start | bytes 5652484
  71.8 4.0 %copy-start.5 = (bf16[512,320]{0,1:T(8,128)(2,1)S(1)}, bf16[512,320]{0,1:T(8,128)(2,1)}, u32[]{:S(2)}) copy-start(bf16[512,320]{0,1:T(8,128)(2,1)} %copy.115) | copy-start | bytes 983044
  75.8 11.4 %copy-start.7 = (f32[2048]{0:T(1024)S(1)}, f32[2048]{0:T(1024)}, u32[]{:S(2)}) copy-start(f32[2048]{0:T(1024)} %param.15) | copy-start | bytes 24580
  76.8 4.7 %collective-permute-start.6 = (bf16[24,1280]{1,0:T(8,128)(2,1)S(1)}, bf16[24,1280]{1,0:T(8,128)(2,1)S(1)}, u32[]{:S(2)}, u32[]{:S(2)}) collective-permute-start(bf16[24,1280]{1,0:T(8,128)(2,1)S(1)} %convert_element_type.108), channel_id=1, source_target_pairs={{0,128},{128,0},{1,129},{129,1},{2,130},{130,2},{3,131},{131,3},{4... | collective-permute-start | bytes 184328 | tf_op jit(solution)/shard_map/ppermute | solution.py:30
  82.0 5.1 %collective-permute-start.7 = (bf16[24,2048]{1,0:T(8,128)(2,1)S(1)}, bf16[24,2048]{1,0:T(8,128)(2,1)S(1)}, u32[]{:S(2)}, u32[]{:S(2)}) collective-permute-start(bf16[24,2048]{1,0:T(8,128)(2,1)S(1)} %fusion.56), channel_id=1, source_target_pairs={{0,128},{128,0},{1,129},{129,1},{2,130},{130,2},{3,131},{131,3},{4... | collective-permute-start | bytes 294920 | tf_op jit(solution)/shard_map/ppermute | solution.py:30
  87.4 3.8 %collective-permute-start.10 = (bf16[24,2048]{1,0:T(8,128)(2,1)S(1)}, bf16[24,2048]{1,0:T(8,128)(2,1)S(1)}, u32[]{:S(2)}, u32[]{:S(2)}) collective-permute-start(bf16[24,2048]{1,0:T(8,128)(2,1)S(1)} %multiply_convert_fusion), channel_id=1, source_target_pairs={{0,64},{192,128},{1,65},{193,129},{2,66},{194,130},{3,67},{195,131... | collective-permute-start | bytes 294920 | tf_op jit(solution)/shard_map/ppermute | solution.py:214
  89.2 6.9 %collective-permute-start.8 = (bf16[24,2048]{1,0:T(8,128)(2,1)S(1)}, bf16[24,2048]{1,0:T(8,128)(2,1)S(1)}, u32[]{:S(2)}, u32[]{:S(2)}) collective-permute-start(bf16[24,2048]{1,0:T(8,128)(2,1)S(1)} %multiply_convert_fusion), channel_id=1, source_target_pairs={{128,0},{64,192},{129,1},{65,193},{130,2},{66,194},{131,3},{67,195... | collective-permute-start | bytes 294920 | tf_op jit(solution)/shard_map/ppermute | solution.py:216
  90.5 5.6 %collective-permute-start.9 = (bf16[24,2048]{1,0:T(8,128)(2,1)S(1)}, bf16[24,2048]{1,0:T(8,128)(2,1)S(1)}, u32[]{:S(2)}, u32[]{:S(2)}) collective-permute-start(bf16[24,2048]{1,0:T(8,128)(2,1)S(1)} %multiply_convert_fusion), channel_id=1, source_target_pairs={{128,64},{64,128},{129,65},{65,129},{130,66},{66,130},{131,67},{67... | collective-permute-start | bytes 294920 | tf_op jit(solution)/shard_map/ppermute | solution.py:215
  96.2 3.8 %collective-permute-start.11 = (bf16[24,2048]{1,0:T(8,128)(2,1)S(1)}, bf16[24,2048]{1,0:T(8,128)(2,1)S(1)}, u32[]{:S(2)}, u32[]{:S(2)}) collective-permute-start(bf16[24,2048]{1,0:T(8,128)(2,1)S(1)} %fusion.46), channel_id=1, source_target_pairs={{0,48},{16,0},{32,16},{48,32},{1,49},{17,1},{33,17},{49,33},{2,50}... | collective-permute-start | bytes 294920 | tf_op jit(solution)/shard_map/ppermute | solution.py:36
  96.5 5.1 %collective-permute-start.12 = (bf16[24,2048]{1,0:T(8,128)(2,1)S(1)}, bf16[24,2048]{1,0:T(8,128)(2,1)S(1)}, u32[]{:S(2)}, u32[]{:S(2)}) collective-permute-start(bf16[24,2048]{1,0:T(8,128)(2,1)S(1)} %fusion.46), channel_id=1, source_target_pairs={{0,32},{16,48},{32,0},{48,16},{1,33},{17,49},{33,1},{49,17},{2,34}... | collective-permute-start | bytes 294920 | tf_op jit(solution)/shard_map/ppermute | solution.py:36
  96.7 5.9 %collective-permute-start.13 = (bf16[24,2048]{1,0:T(8,128)(2,1)S(1)}, bf16[24,2048]{1,0:T(8,128)(2,1)S(1)}, u32[]{:S(2)}, u32[]{:S(2)}) collective-permute-start(bf16[24,2048]{1,0:T(8,128)(2,1)S(1)} %fusion.46), channel_id=1, source_target_pairs={{0,16},{16,32},{32,48},{48,0},{1,17},{17,33},{33,49},{49,1},{2,18}... | collective-permute-start | bytes 294920 | tf_op jit(solution)/shard_map/ppermute | solution.py:36
  154.6 6.5 %collective-permute-start.14 = (bf16[4,8,24,2048]{3,2,1,0:T(8,128)(2,1)}, bf16[4,8,24,2048]{3,2,1,0:T(8,128)(2,1)}, u32[]{:S(2)}, u32[]{:S(2)}) collective-permute-start(bf16[4,8,24,2048]{3,2,1,0:T(8,128)(2,1)} %bitcast.188), channel_id=1, source_target_pairs={{0,1},{1,0},{2,3},{3,2},{4,5},{5,4},{6,7},{7,6},{8,9},{9,8},{10,11... | collective-permute-start | bytes 9437192 | tf_op jit(solution)/shard_map/ppermute | solution.py:239
  155.5 5.6 %copy-start.9 = (bf16[2048,250]{1,0:T(8,128)(2,1)S(1)}, bf16[2048,250]{1,0:T(8,128)(2,1)}, u32[]{:S(2)}) copy-start(bf16[2048,250]{1,0:T(8,128)(2,1)} %param.16) | copy-start | bytes 3072004
  (2 other events, 2.8 us)
Sparse Core Ops, SparseCore 0:
  103.6 50.8 all-gather.2

commit v12 on v11

--- a/solution.py
+++ b/solution.py
@@ -155,6 +155,7 @@
     pages_sent = jnp.einsum(
         "smp,pwc->smwc", page_hit, pool, preferred_element_type=jnp.float32
     ).astype(jnp.bfloat16)
+    partner_normed, pages_sent = lax.optimization_barrier((partner_normed, pages_sent))
     arrivals = [shifted(pages_sent[number], REQ, offsets[number]) for number in range(slots)]
     arrived = jnp.concatenate(arrivals, axis=0)
     page_column = jnp.minimum(jnp.arange(MAXP, dtype=jnp.int32), MIGP - 1)

time: 173 us -> 172 us (level)
  starting transfers between devices: 22 us -> 26.7 us
  matrix products: 24.9 us -> 21.5 us
  waiting for transfers between devices: 73.4 us -> 70.2 us
  other arithmetic: 9.46 us -> 12.1 us
    ppermute x7, waiting for transfers between devices: 4.88 us -> 12.1 us  [shifted(): return lax.ppermute(value, axis, pairs)]
    all_gather x1, waiting for transfers between devices: 51 us -> 44.7 us  [body(): gathered = lax.all_gather(gathered, 'z', axis=1, tiled=False)]
    ppermute x4, starting transfers between devices: 4.21 us -> 8.97 us  [from_partner(): return lax.ppermute(block, axis, route)]
    ppermute x4, waiting for transfers between devices: 10.4 us -> 6.31 us  [from_partner(): return lax.ppermute(block, axis, route)]
    unnamed x29 -> x31, local copies, waits for them, and re-layouts: 15.6 us -> 12.9 us
    convert_element_type x2, other arithmetic: 0.18 us -> 2.62 us  [body(): normed = rms_scale(states_in, attn_gain).astype(jnp.bfloat16)]
    dot_general x1, matrix products: 5.05 us -> 2.96 us  [body(): jnp.einsum('smp,pwc->smwc', page_hit, pool, preferred_element_type=jnp.fl...]
  transfers between devices with their start and end apart: 16 -> 16, of which waited for: 9 -> 9; matrix products, arithmetic and copies ran while one was open for 20% -> 22% of each run, Pallas kernels for 0% -> 0%
where the time goes in v12:
time: 172 us; the launch traced here: 171 us
  waiting for transfers between devices  70.2 us (41%)
  local copies, waits for them, and re-layouts  27.1 us (16%)
  starting transfers between devices  26.7 us (16%)
  matrix products  21.5 us (12%)
  between operations  13.8 us (8%)
  other arithmetic  12.1 us (7%)
    all_gather x1, waiting for transfers between devices, body(): gathered = lax.all_gather(gathered, 'z', axis=1, tiled=False)  44.7 us
    unnamed x31, local copies, waits for them, and re-layouts  12.9 us
    ppermute x7, waiting for transfers between devices, shifted(): return lax.ppermute(value, axis, pairs)  12.1 us
    ppermute x7, starting transfers between devices, shifted(): return lax.ppermute(value, axis, pairs)  11.6 us
    ppermute x4, starting transfers between devices, from_partner(): return lax.ppermute(block, axis, route)  8.97 us
    ppermute x4, waiting for transfers between devices, from_partner(): return lax.ppermute(block, axis, route)  6.31 us
    slice x1, local copies, waits for them, and re-layouts, dense_scores(): key_rows = flat[:, :half_width].reshape(count, KVH, HD)  5.85 us
    ppermute x1, waiting for transfers between devices, body(): from_guide = lax.ppermute(final, pair, [(2, 0), (1, 3)])  4.88 us
  transfers between devices with their start and end apart: 16, of which 9 were waited for; matrix products, arithmetic and copies ran while one was open for 22% of the time, Pallas kernels for 0%

profile of v12, /device:TPU:1, one launch (start us, length us, event | category | flops | bytes accessed | tf_op | source)
XLA Modules:
  0.0 171.3 jit_solution(14472299928770310833)
XLA Ops:
  9.4 3.6 %collective-permute-start = (bf16[24,2048]{1,0:T(8,128)(2,1)}, bf16[24,2048]{1,0:T(8,128)(2,1)}, u32[]{:S(2)}, u32[]{:S(2)}) collective-permute-start(bf16[24,2048]{1,0:T(8,128)(2,1)} %fusion.49), channel_id=1, source_target_pairs={{0,128},{128,0},{1,129},{129,1},{2,130},{130,2},{3,131},{131,3},{4... | collective-permute-start | bytes 294920 | tf_op jit(solution)/shard_map/ppermute | solution.py:30
  21.2 5.8 %fusion.90 = (bf16[2944,320]{1,0:T(8,128)(2,1)}, bf16[2944,320]{1,0:T(8,128)(2,1)}) fusion(bf16[2944,640]{1,0:T(8,128)(2,1)} %bitcast.177), kind=kLoop, calls=%fused_computation.149 | loop fusion | bytes 7536640 | tf_op jit(solution)/shard_map/slice | solution.py:83
  27.3 3.0 %fusion.18 = bf16[4,2,64,640]{3,0,2,1:T(4,128)(2,1)S(1)} fusion(bf16[46,64,640]{2,1,0:T(8,128)(2,1)S(1)} %bitcast.178, s32[4,2]{0,1:T(2,128)S(1)} %select_reduce_fusion), kind=kOutput, calls=%fused_computation.21 | convolution fusion | flops 30474608 | bytes 4423712 | tf_op jit(solution)/shard_map/smp,pwc->smwc/dot_general | solution.py:155
  31.1 1.7 slice.94
  33.5 4.1 %copy.112 = bf16[2944,320]{0,1:T(8,128)(2,1)} copy(bf16[2944,320]{1,0:T(8,128)(2,1)} %get-tuple-element.11) | data formatting | bytes 3768320
  37.7 4.1 %copy.114 = bf16[2944,320]{0,1:T(8,128)(2,1)} copy(bf16[2944,320]{1,0:T(8,128)(2,1)} %get-tuple-element.12) | data formatting | bytes 3768320
  42.8 8.1 %collective-permute-start.2 = (bf16[2,64,640]{2,1,0:T(8,128)(2,1)S(1)}, bf16[2,64,640]{2,1,0:T(8,128)(2,1)S(1)}, u32[]{:S(2)}, u32[]{:S(2)}) collective-permute-start(bf16[2,64,640]{2,1,0:T(8,128)(2,1)S(1)} %bitcast.184), channel_id=1, source_target_pairs={{0,126},{1,127},{2,0},{3,1},{4,2},{5,3},{6,4},{7,5},{8,6},{9,7},{1... | collective-permute-start | bytes 491528 | tf_op jit(solution)/shard_map/ppermute | solution.py:36
  55.3 1.7 %collective-permute-start.1 = (f32[24,1920]{1,0:T(8,128)}, f32[24,1920]{1,0:T(8,128)}, u32[]{:S(2)}, u32[]{:S(2)}) collective-permute-start(f32[24,1920]{1,0:T(8,128)} %select_bitcast_fusion), channel_id=1, source_target_pairs={{0,128},{128,0},{1,129},{129,1},{2,130},{130,2},{3,131},{131,3},{4... | collective-permute-start | bytes 552968 | tf_op jit(solution)/shard_map/ppermute | solution.py:30
  57.0 7.2 %collective-permute-done.5 = bf16[2,64,640]{2,1,0:T(8,128)(2,1)S(1)} collective-permute-done((bf16[2,64,640]{2,1,0:T(8,128)(2,1)S(1)}, bf16[2,64,640]{2,1,0:T(8,128)(2,1)S(1)}, u32[]{:S(2)}, u32[]{:S(2)}) %collective-permute-start.5) | collective-permute-done | bytes 163872 | tf_op jit(solution)/shard_map/ppermute | solution.py:36
  65.2 1.9 %copy.113 = bf16[512,320]{0,1:T(8,128)(2,1)} copy(bf16[512,320]{1,0:T(8,128)(2,1)} %get-tuple-element.14) | data formatting | bytes 655360
  71.1 2.6 %bitcast_reduce_fusion = (f32[24,5,4]{0,2,1:T(4,128)S(1)}, f32[5,24,4,2944]{3,1,2,0:T(8,128)S(1)}) fusion(pred[24,2944]{1,0:T(8,128)(4,1)S(1)} %broadcast_compare_fusion, bf16[2944,5,64,1]{0,2,3,1:T(8,128)(2,1)} %bitcast.179, bf16[24,5,4,64]{3,2,1,0:T(4,128)(2,1)S(1)} %reshape.239), kind=kOutput, calls=%fused_computation.1 | convolution fusion | flops 185118240 | bytes 7670656 | tf_op jit(solution)/shard_map/rkgd,tkd->rkgt/dot_general | solution.py:85
  75.7 4.0 %fusion.30 = f32[24,5,4,64]{3,0,2,1:T(8,128)S(1)} fusion(bf16[2944,5,64,1]{0,2,3,1:T(8,128)(2,1)S(1)} %bitcast.181, f32[5,24,4,2944]{3,1,2,0:T(8,128)S(1)} %get-tuple-element.29, f32[24,2944]{1,0:T(8,128)S(1)} %copy-done.7, f32[24,5,4]{0,2,1:T(4,128)S(1)} %get-tuple-element.10, pred[24,2944]{1,0:T(8,128)(4,1)S(1)} %broadcast_compare_fusion, ...), kind=kOutput, calls=%fused_computation.33 | convolution fusion | flops 1093816320 | bytes 8047360 | tf_op jit(solution)/shard_map/rkgt,tkd->rkgd/dot_general | solution.py:192
  80.6 1.8 %collective-permute-start.6 = (bf16[24,1280]{1,0:T(8,128)(2,1)S(1)}, bf16[24,1280]{1,0:T(8,128)(2,1)S(1)}, u32[]{:S(2)}, u32[]{:S(2)}) collective-permute-start(bf16[24,1280]{1,0:T(8,128)(2,1)S(1)} %convert_element_type.108), channel_id=1, source_target_pairs={{0,128},{128,0},{1,129},{129,1},{2,130},{130,2},{3,131},{131,3},{4... | collective-permute-start | bytes 184328 | tf_op jit(solution)/shard_map/ppermute | solution.py:30
  82.6 3.1 %collective-permute-done.6 = bf16[24,1280]{1,0:T(8,128)(2,1)S(1)} collective-permute-done((bf16[24,1280]{1,0:T(8,128)(2,1)S(1)}, bf16[24,1280]{1,0:T(8,128)(2,1)S(1)}, u32[]{:S(2)}, u32[]{:S(2)}) %collective-permute-start.6) | collective-permute-done | bytes 61472 | tf_op jit(solution)/shard_map/ppermute | solution.py:30
  86.3 1.8 %collective-permute-start.7 = (bf16[24,2048]{1,0:T(8,128)(2,1)S(1)}, bf16[24,2048]{1,0:T(8,128)(2,1)S(1)}, u32[]{:S(2)}, u32[]{:S(2)}) collective-permute-start(bf16[24,2048]{1,0:T(8,128)(2,1)S(1)} %fusion.56), channel_id=1, source_target_pairs={{0,128},{128,0},{1,129},{129,1},{2,130},{130,2},{3,131},{131,3},{4... | collective-permute-start | bytes 294920 | tf_op jit(solution)/shard_map/ppermute | solution.py:30
  88.1 3.2 %collective-permute-done.7 = bf16[24,2048]{1,0:T(8,128)(2,1)S(1)} collective-permute-done((bf16[24,2048]{1,0:T(8,128)(2,1)S(1)}, bf16[24,2048]{1,0:T(8,128)(2,1)S(1)}, u32[]{:S(2)}, u32[]{:S(2)}) %collective-permute-start.7) | collective-permute-done | bytes 98336 | tf_op jit(solution)/shard_map/ppermute | solution.py:30
  91.6 3.2 %collective-permute-start.10 = (bf16[24,2048]{1,0:T(8,128)(2,1)S(1)}, bf16[24,2048]{1,0:T(8,128)(2,1)S(1)}, u32[]{:S(2)}, u32[]{:S(2)}) collective-permute-start(bf16[24,2048]{1,0:T(8,128)(2,1)S(1)} %multiply_convert_fusion), channel_id=1, source_target_pairs={{0,64},{192,128},{1,65},{193,129},{2,66},{194,130},{3,67},{195,131... | collective-permute-start | bytes 294920 | tf_op jit(solution)/shard_map/ppermute | solution.py:215
  96.8 4.9 %collective-permute-done.8 = bf16[24,2048]{1,0:T(8,128)(2,1)S(1)} collective-permute-done((bf16[24,2048]{1,0:T(8,128)(2,1)S(1)}, bf16[24,2048]{1,0:T(8,128)(2,1)S(1)}, u32[]{:S(2)}, u32[]{:S(2)}) %collective-permute-start.8) | collective-permute-done | bytes 98336 | tf_op jit(solution)/shard_map/ppermute | solution.py:217
  103.4 2.0 %collective-permute-done.11 = bf16[24,2048]{1,0:T(8,128)(2,1)S(1)} collective-permute-done((bf16[24,2048]{1,0:T(8,128)(2,1)S(1)}, bf16[24,2048]{1,0:T(8,128)(2,1)S(1)}, u32[]{:S(2)}, u32[]{:S(2)}) %collective-permute-start.11) | collective-permute-done | bytes 98336 | tf_op jit(solution)/shard_map/ppermute | solution.py:36
  105.4 1.9 %collective-permute-done.12 = bf16[24,2048]{1,0:T(8,128)(2,1)S(1)} collective-permute-done((bf16[24,2048]{1,0:T(8,128)(2,1)S(1)}, bf16[24,2048]{1,0:T(8,128)(2,1)S(1)}, u32[]{:S(2)}, u32[]{:S(2)}) %collective-permute-start.12) | collective-permute-done | bytes 98336 | tf_op jit(solution)/shard_map/ppermute | solution.py:36
  109.2 44.7 %all-gather.3.cloned.1.call-done = bf16[4,192,2048]{2,1,0:T(8,128)(2,1)} async-done(((bf16[4,24,2048]{2,1,0:T(8,128)(2,1)}), bf16[4,192,2048]{2,1,0:T(8,128)(2,1)}) %all-gather.3.cloned.1.call-update) | async-done | bytes 3145744 | tf_op jit(solution)/shard_map/all_gather | solution.py:237
  155.0 3.3 %fusion.24 = f32[4,8,2,24,250]{4,3,2,1,0:T(8,128)S(1)} fusion(f32[4,8,2,24,250]{4,3,2,1,0:T(8,128)S(1)} %broadcast_in_dim.84, s32[]{:T(128)S(6)} %select_n.294, bf16[4,8,24,2048]{3,2,1,0:T(8,128)(2,1)} %bitcast.193, bf16[2048,250]{1,0:T(8,128)(2,1)} %param.16), kind=kOutput, calls=%fused_computation.28 | convolution fusion | flops 786432000 | bytes 4956164 | tf_op jit(solution)/shard_map/yzrd,dv->yzrv/dot_general | solution.py:241
  158.2 2.2 %collective-permute-done.14 = bf16[4,8,24,2048]{3,2,1,0:T(8,128)(2,1)} collective-permute-done((bf16[4,8,24,2048]{3,2,1,0:T(8,128)(2,1)}, bf16[4,8,24,2048]{3,2,1,0:T(8,128)(2,1)}, u32[]{:S(2)}, u32[]{:S(2)}) %collective-permute-start.14) | collective-permute-done | bytes 3145760 | tf_op jit(solution)/shard_map/ppermute | solution.py:240
  160.4 2.9 %fusion.23 = f32[4,8,2,24,250]{4,3,2,1,0:T(8,128)S(1)} fusion(f32[4,8,2,24,250]{4,3,2,1,0:T(8,128)S(1)} %fusion.24, s32[]{:T(128)S(6)} %select_n.295, bf16[4,8,24,2048]{3,2,1,0:T(8,128)(2,1)} %collective-permute-done.14, bf16[2048,250]{1,0:T(8,128)(2,1)S(1)} %copy-done.10), kind=kOutput, calls=%fused_computation.26 | convolution fusion | flops 786432000 | bytes 4980740 | tf_op jit(solution)/shard_map/yzrd,dv->yzrv/dot_general | solution.py:242
  (105 shorter events, 34.8 us)
Async XLA Ops:
  6.5 79.2 %copy-start = (bf16[640,2048]{1,0:T(8,128)(2,1)S(1)}, bf16[640,2048]{1,0:T(8,128)(2,1)}, u32[]{:S(2)}) copy-start(bf16[640,2048]{1,0:T(8,128)(2,1)} %param.14) | copy-start | bytes 7864324
  6.5 147.3 %all-gather.3.cloned.1.call-start = ((), (), s32[]{:S(2)}) async-start(), calls=%async_computation | async-start | bytes 3538944 | tf_op jit(solution)/shard_map/all_gather | solution.py:237
  9.4 32.4 %collective-permute-start = (bf16[24,2048]{1,0:T(8,128)(2,1)}, bf16[24,2048]{1,0:T(8,128)(2,1)}, u32[]{:S(2)}, u32[]{:S(2)}) collective-permute-start(bf16[24,2048]{1,0:T(8,128)(2,1)} %fusion.49), channel_id=1, source_target_pairs={{0,128},{128,0},{1,129},{129,1},{2,130},{130,2},{3,131},{131,3},{4... | collective-permute-start | bytes 294920 | tf_op jit(solution)/shard_map/ppermute | solution.py:30
  21.2 5.9 %copy-start.3 = (f32[24,3456]{1,0:T(8,128)}, f32[24,3456]{1,0:T(8,128)S(1)}, u32[]{:S(2)}) copy-start(f32[24,3456]{1,0:T(8,128)S(1)} %reshape.241) | copy-start | bytes 995332
  21.2 6.0 %copy-start.1 = (bf16[1,46,64,640]{3,2,1,0:T(8,128)(2,1)S(1)}, bf16[1,46,64,640]{3,2,1,0:T(8,128)(2,1)}, u32[]{:S(2)}) copy-start(bf16[1,46,64,640]{3,2,1,0:T(8,128)(2,1)} %param.17) | copy-start | bytes 11304964
  41.7 11.2 %copy-start.2 = (bf16[1024,1920]{1,0:T(8,128)(2,1)S(1)}, bf16[1024,1920]{1,0:T(8,128)(2,1)}, u32[]{:S(2)}) copy-start(bf16[1024,1920]{1,0:T(8,128)(2,1)} %param.13) | copy-start | bytes 11796484
  42.8 14.3 %collective-permute-start.2 = (bf16[2,64,640]{2,1,0:T(8,128)(2,1)S(1)}, bf16[2,64,640]{2,1,0:T(8,128)(2,1)S(1)}, u32[]{:S(2)}, u32[]{:S(2)}) collective-permute-start(bf16[2,64,640]{2,1,0:T(8,128)(2,1)S(1)} %bitcast.184), channel_id=1, source_target_pairs={{0,126},{1,127},{2,0},{3,1},{4,2},{5,3},{6,4},{7,5},{8,6},{9,7},{1... | collective-permute-start | bytes 491528 | tf_op jit(solution)/shard_map/ppermute | solution.py:36
  50.9 6.1 %collective-permute-start.3 = (bf16[2,64,640]{2,1,0:T(8,128)(2,1)S(1)}, bf16[2,64,640]{2,1,0:T(8,128)(2,1)S(1)}, u32[]{:S(2)}, u32[]{:S(2)}) collective-permute-start(bf16[2,64,640]{2,1,0:T(8,128)(2,1)S(1)} %bitcast.185), channel_id=1, source_target_pairs={{0,127},{1,0},{2,1},{3,2},{4,3},{5,4},{6,5},{7,6},{8,7},{9,8},{10,... | collective-permute-start | bytes 491528 | tf_op jit(solution)/shard_map/ppermute | solution.py:36
  52.2 4.8 %collective-permute-start.4 = (bf16[2,64,640]{2,1,0:T(8,128)(2,1)S(1)}, bf16[2,64,640]{2,1,0:T(8,128)(2,1)S(1)}, u32[]{:S(2)}, u32[]{:S(2)}) collective-permute-start(bf16[2,64,640]{2,1,0:T(8,128)(2,1)S(1)} %bitcast.186), channel_id=1, source_target_pairs={{0,1},{1,2},{2,3},{3,4},{4,5},{5,6},{6,7},{7,8},{8,9},{9,10},{10,1... | collective-permute-start | bytes 491528 | tf_op jit(solution)/shard_map/ppermute | solution.py:36
  52.8 11.4 %collective-permute-start.5 = (bf16[2,64,640]{2,1,0:T(8,128)(2,1)S(1)}, bf16[2,64,640]{2,1,0:T(8,128)(2,1)S(1)}, u32[]{:S(2)}, u32[]{:S(2)}) collective-permute-start(bf16[2,64,640]{2,1,0:T(8,128)(2,1)S(1)} %bitcast.187), channel_id=1, source_target_pairs={{0,2},{1,3},{2,4},{3,5},{4,6},{5,7},{6,8},{7,9},{8,10},{9,11},{10,... | collective-permute-start | bytes 491528 | tf_op jit(solution)/shard_map/ppermute | solution.py:36
  55.3 12.7 %collective-permute-start.1 = (f32[24,1920]{1,0:T(8,128)}, f32[24,1920]{1,0:T(8,128)}, u32[]{:S(2)}, u32[]{:S(2)}) collective-permute-start(f32[24,1920]{1,0:T(8,128)} %select_bitcast_fusion), channel_id=1, source_target_pairs={{0,128},{128,0},{1,129},{129,1},{2,130},{130,2},{3,131},{131,3},{4... | collective-permute-start | bytes 552968 | tf_op jit(solution)/shard_map/ppermute | solution.py:30
  75.7 4.0 %copy-start.8 = (bf16[512,320]{0,1:T(8,128)(2,1)S(1)}, bf16[512,320]{0,1:T(8,128)(2,1)}, u32[]{:S(2)}) copy-start(bf16[512,320]{0,1:T(8,128)(2,1)} %copy.115) | copy-start | bytes 983044
  79.7 11.6 %copy-start.6 = (bf16[1,24,2048]{2,1,0:T(8,128)(2,1)S(1)}, bf16[1,24,2048]{2,1,0:T(8,128)(2,1)}, u32[]{:S(2)}) copy-start(bf16[1,24,2048]{2,1,0:T(8,128)(2,1)} %param.11) | copy-start | bytes 294916
  79.7 11.8 %copy-start.9 = (f32[2048]{0:T(1024)S(1)}, f32[2048]{0:T(1024)}, u32[]{:S(2)}) copy-start(f32[2048]{0:T(1024)} %param.15) | copy-start | bytes 24580
  80.6 5.0 %collective-permute-start.6 = (bf16[24,1280]{1,0:T(8,128)(2,1)S(1)}, bf16[24,1280]{1,0:T(8,128)(2,1)S(1)}, u32[]{:S(2)}, u32[]{:S(2)}) collective-permute-start(bf16[24,1280]{1,0:T(8,128)(2,1)S(1)} %convert_element_type.108), channel_id=1, source_target_pairs={{0,128},{128,0},{1,129},{129,1},{2,130},{130,2},{3,131},{131,3},{4... | collective-permute-start | bytes 184328 | tf_op jit(solution)/shard_map/ppermute | solution.py:30
  86.3 5.1 %collective-permute-start.7 = (bf16[24,2048]{1,0:T(8,128)(2,1)S(1)}, bf16[24,2048]{1,0:T(8,128)(2,1)S(1)}, u32[]{:S(2)}, u32[]{:S(2)}) collective-permute-start(bf16[24,2048]{1,0:T(8,128)(2,1)S(1)} %fusion.56), channel_id=1, source_target_pairs={{0,128},{128,0},{1,129},{129,1},{2,130},{130,2},{3,131},{131,3},{4... | collective-permute-start | bytes 294920 | tf_op jit(solution)/shard_map/ppermute | solution.py:30
  91.6 5.2 %collective-permute-start.10 = (bf16[24,2048]{1,0:T(8,128)(2,1)S(1)}, bf16[24,2048]{1,0:T(8,128)(2,1)S(1)}, u32[]{:S(2)}, u32[]{:S(2)}) collective-permute-start(bf16[24,2048]{1,0:T(8,128)(2,1)S(1)} %multiply_convert_fusion), channel_id=1, source_target_pairs={{0,64},{192,128},{1,65},{193,129},{2,66},{194,130},{3,67},{195,131... | collective-permute-start | bytes 294920 | tf_op jit(solution)/shard_map/ppermute | solution.py:215
  94.8 6.9 %collective-permute-start.8 = (bf16[24,2048]{1,0:T(8,128)(2,1)S(1)}, bf16[24,2048]{1,0:T(8,128)(2,1)S(1)}, u32[]{:S(2)}, u32[]{:S(2)}) collective-permute-start(bf16[24,2048]{1,0:T(8,128)(2,1)S(1)} %multiply_convert_fusion), channel_id=1, source_target_pairs={{128,0},{64,192},{129,1},{65,193},{130,2},{66,194},{131,3},{67,195... | collective-permute-start | bytes 294920 | tf_op jit(solution)/shard_map/ppermute | solution.py:217
  96.1 5.6 %collective-permute-start.9 = (bf16[24,2048]{1,0:T(8,128)(2,1)S(1)}, bf16[24,2048]{1,0:T(8,128)(2,1)S(1)}, u32[]{:S(2)}, u32[]{:S(2)}) collective-permute-start(bf16[24,2048]{1,0:T(8,128)(2,1)S(1)} %multiply_convert_fusion), channel_id=1, source_target_pairs={{128,64},{64,128},{129,65},{65,129},{130,66},{66,130},{131,67},{67... | collective-permute-start | bytes 294920 | tf_op jit(solution)/shard_map/ppermute | solution.py:216
  101.9 3.5 %collective-permute-start.11 = (bf16[24,2048]{1,0:T(8,128)(2,1)S(1)}, bf16[24,2048]{1,0:T(8,128)(2,1)S(1)}, u32[]{:S(2)}, u32[]{:S(2)}) collective-permute-start(bf16[24,2048]{1,0:T(8,128)(2,1)S(1)} %fusion.46), channel_id=1, source_target_pairs={{0,48},{16,0},{32,16},{48,32},{1,49},{17,1},{33,17},{49,33},{2,50}... | collective-permute-start | bytes 294920 | tf_op jit(solution)/shard_map/ppermute | solution.py:36
  101.9 5.3 %collective-permute-start.12 = (bf16[24,2048]{1,0:T(8,128)(2,1)S(1)}, bf16[24,2048]{1,0:T(8,128)(2,1)S(1)}, u32[]{:S(2)}, u32[]{:S(2)}) collective-permute-start(bf16[24,2048]{1,0:T(8,128)(2,1)S(1)} %fusion.46), channel_id=1, source_target_pairs={{0,32},{16,48},{32,0},{48,16},{1,33},{17,49},{33,1},{49,17},{2,34}... | collective-permute-start | bytes 294920 | tf_op jit(solution)/shard_map/ppermute | solution.py:36
  102.3 6.0 %collective-permute-start.13 = (bf16[24,2048]{1,0:T(8,128)(2,1)S(1)}, bf16[24,2048]{1,0:T(8,128)(2,1)S(1)}, u32[]{:S(2)}, u32[]{:S(2)}) collective-permute-start(bf16[24,2048]{1,0:T(8,128)(2,1)S(1)} %fusion.46), channel_id=1, source_target_pairs={{0,16},{16,32},{32,48},{48,0},{1,17},{17,33},{33,49},{49,1},{2,18}... | collective-permute-start | bytes 294920 | tf_op jit(solution)/shard_map/ppermute | solution.py:36
  153.9 6.5 %collective-permute-start.14 = (bf16[4,8,24,2048]{3,2,1,0:T(8,128)(2,1)}, bf16[4,8,24,2048]{3,2,1,0:T(8,128)(2,1)}, u32[]{:S(2)}, u32[]{:S(2)}) collective-permute-start(bf16[4,8,24,2048]{3,2,1,0:T(8,128)(2,1)} %bitcast.192), channel_id=1, source_target_pairs={{0,1},{1,0},{2,3},{3,2},{4,5},{5,4},{6,7},{7,6},{8,9},{9,8},{10,11... | collective-permute-start | bytes 9437192 | tf_op jit(solution)/shard_map/ppermute | solution.py:240
  154.8 5.6 %copy-start.10 = (bf16[2048,250]{1,0:T(8,128)(2,1)S(1)}, bf16[2048,250]{1,0:T(8,128)(2,1)}, u32[]{:S(2)}) copy-start(bf16[2048,250]{1,0:T(8,128)(2,1)} %param.16) | copy-start | bytes 3072004
  (3 other events, 5.8 us)
Sparse Core Ops, SparseCore 0:
  109.3 44.5 all-gather.2

commit v13 on v12

--- a/solution.py
+++ b/solution.py
@@ -207,17 +207,16 @@
     out_parts = jnp.einsum("grc,cd->grd", selected, w_out, preferred_element_type=jnp.float32)
     own_out = jnp.where(side == 0, out_parts[0], out_parts[1])
     other_out = jnp.where(side == 0, out_parts[1], out_parts[0]).astype(jnp.bfloat16)
-    state_after = states_in + (
-        own_out + from_partner(other_out, "guide", 0).astype(jnp.float32)
-    )
-    final = rms_scale(state_after, final_gain).astype(jnp.bfloat16)
+    payload = jnp.stack([states_in + own_out, other_out.astype(jnp.float32)])
     pair = ("guide", "x_lo")
-    from_side = lax.ppermute(final, pair, [(0, 1), (3, 2)])
-    from_diagonal = lax.ppermute(final, pair, [(2, 1), (1, 2)])
-    from_guide = lax.ppermute(final, pair, [(2, 0), (1, 3)])
+    from_side = lax.ppermute(payload, pair, [(0, 1), (3, 2)])
+    from_diagonal = lax.ppermute(payload, pair, [(2, 1), (1, 2)])
+    from_guide = lax.ppermute(payload, pair, [(2, 0), (1, 3)])
     home = lax.axis_index("x_lo") == side
-    same_group = jnp.where(home, final, from_side)
-    other_group = jnp.where(home, from_guide, from_diagonal)
+    same_source = jnp.where(home, payload, from_side)
+    other_source = jnp.where(home, from_guide, from_diagonal)
+    same_group = rms_scale(same_source[0] + other_source[1], final_gain).astype(jnp.bfloat16)
+    other_group = rms_scale(other_source[0] + same_source[1], final_gain).astype(jnp.bfloat16)
     cond = jnp.where(side == 0, same_group, other_group).astype(jnp.float32)
     uncond = jnp.where(side == 0, other_group, same_group).astype(jnp.float32)
     combined = (uncond + guidance * (cond - uncond)).astype(jnp.bfloat16)

time: 172 us -> 172 us (level)
    ppermute x3, waiting for transfers between devices: 4.88 us -> 10.8 us  [the longest x1 6.01 us: body(): from_guide = lax.ppermute(payload, pair, [(2, 0), (1, 3)])]
    ppermute x4 -> x3, waiting for transfers between devices: 6.31 us -> 3.21 us  [from_partner(): return lax.ppermute(block, axis, route)]
    ppermute x4 -> x3, starting transfers between devices: 8.97 us -> 7.12 us  [from_partner(): return lax.ppermute(block, axis, route)]
  transfers between devices with their start and end apart: 16 -> 15, of which waited for: 9 -> 9; matrix products, arithmetic and copies ran while one was open for 22% -> 22% of each run, Pallas kernels for 0% -> 0%
where the time goes in v13:
time: 172 us; the launch traced here: 171 us
  waiting for transfers between devices  71.4 us (42%)
  local copies, waits for them, and re-layouts  27 us (16%)
  starting transfers between devices  25.5 us (15%)
  matrix products  21.5 us (12%)
  between operations  13.8 us (8%)
  other arithmetic  12.1 us (7%)
    all_gather x1, waiting for transfers between devices, body(): gathered = lax.all_gather(gathered, 'z', axis=1, tiled=False)  43.3 us
    unnamed x31, local copies, waits for them, and re-layouts  12.9 us
    ppermute x7, waiting for transfers between devices, shifted(): return lax.ppermute(value, axis, pairs)  11.9 us
    ppermute x7, starting transfers between devices, shifted(): return lax.ppermute(value, axis, pairs)  11.6 us
    ppermute x3, starting transfers between devices, from_partner(): return lax.ppermute(block, axis, route)  7.12 us
    ppermute x1, waiting for transfers between devices, body(): from_guide = lax.ppermute(payload, pair, [(2, 0), (1, 3)])  6.01 us
    slice x1, local copies, waits for them, and re-layouts, dense_scores(): key_rows = flat[:, :half_width].reshape(count, KVH, HD)  5.82 us
    ppermute x1, waiting for transfers between devices, body(): from_side = lax.ppermute(payload, pair, [(0, 1), (3, 2)])  4.8 us
  transfers between devices with their start and end apart: 15, of which 9 were waited for; matrix products, arithmetic and copies ran while one was open for 22% of the time, Pallas kernels for 0%

profile of v13, /device:TPU:1, one launch (start us, length us, event | category | flops | bytes accessed | tf_op | source)
XLA Modules:
  0.0 171.3 jit_solution(6734174091363461468)
XLA Ops:
  9.3 3.6 %collective-permute-start = (bf16[24,2048]{1,0:T(8,128)(2,1)}, bf16[24,2048]{1,0:T(8,128)(2,1)}, u32[]{:S(2)}, u32[]{:S(2)}) collective-permute-start(bf16[24,2048]{1,0:T(8,128)(2,1)} %fusion.48), channel_id=1, source_target_pairs={{0,128},{128,0},{1,129},{129,1},{2,130},{130,2},{3,131},{131,3},{4... | collective-permute-start | bytes 294920 | tf_op jit(solution)/shard_map/ppermute | solution.py:30
  21.2 5.8 %fusion.90 = (bf16[2944,320]{1,0:T(8,128)(2,1)}, bf16[2944,320]{1,0:T(8,128)(2,1)}) fusion(bf16[2944,640]{1,0:T(8,128)(2,1)} %bitcast.179), kind=kLoop, calls=%fused_computation.158 | loop fusion | bytes 7536640 | tf_op jit(solution)/shard_map/slice | solution.py:83
  27.2 3.0 %fusion.18 = bf16[4,2,64,640]{3,0,2,1:T(4,128)(2,1)S(1)} fusion(bf16[46,64,640]{2,1,0:T(8,128)(2,1)S(1)} %bitcast.180, s32[4,2]{0,1:T(2,128)S(1)} %select_reduce_fusion), kind=kOutput, calls=%fused_computation.21 | convolution fusion | flops 30474608 | bytes 4423712 | tf_op jit(solution)/shard_map/smp,pwc->smwc/dot_general | solution.py:155
  31.0 1.7 slice.110
  33.5 4.1 %copy.112 = bf16[2944,320]{0,1:T(8,128)(2,1)} copy(bf16[2944,320]{1,0:T(8,128)(2,1)} %get-tuple-element.11) | data formatting | bytes 3768320
  37.6 4.1 %copy.114 = bf16[2944,320]{0,1:T(8,128)(2,1)} copy(bf16[2944,320]{1,0:T(8,128)(2,1)} %get-tuple-element.12) | data formatting | bytes 3768320
  42.7 8.1 %collective-permute-start.2 = (bf16[2,64,640]{2,1,0:T(8,128)(2,1)S(1)}, bf16[2,64,640]{2,1,0:T(8,128)(2,1)S(1)}, u32[]{:S(2)}, u32[]{:S(2)}) collective-permute-start(bf16[2,64,640]{2,1,0:T(8,128)(2,1)S(1)} %bitcast.186), channel_id=1, source_target_pairs={{0,126},{1,127},{2,0},{3,1},{4,2},{5,3},{6,4},{7,5},{8,6},{9,7},{1... | collective-permute-start | bytes 491528 | tf_op jit(solution)/shard_map/ppermute | solution.py:36
  52.9 1.7 fusion.7
  55.2 1.7 %collective-permute-start.1 = (f32[24,1920]{1,0:T(8,128)}, f32[24,1920]{1,0:T(8,128)}, u32[]{:S(2)}, u32[]{:S(2)}) collective-permute-start(f32[24,1920]{1,0:T(8,128)} %select_bitcast_fusion), channel_id=1, source_target_pairs={{0,128},{128,0},{1,129},{129,1},{2,130},{130,2},{3,131},{131,3},{4... | collective-permute-start | bytes 552968 | tf_op jit(solution)/shard_map/ppermute | solution.py:30
  57.0 7.2 %collective-permute-done.5 = bf16[2,64,640]{2,1,0:T(8,128)(2,1)S(1)} collective-permute-done((bf16[2,64,640]{2,1,0:T(8,128)(2,1)S(1)}, bf16[2,64,640]{2,1,0:T(8,128)(2,1)S(1)}, u32[]{:S(2)}, u32[]{:S(2)}) %collective-permute-start.5) | collective-permute-done | bytes 163872 | tf_op jit(solution)/shard_map/ppermute | solution.py:36
  65.2 1.9 %copy.113 = bf16[512,320]{0,1:T(8,128)(2,1)} copy(bf16[512,320]{1,0:T(8,128)(2,1)} %get-tuple-element.14) | data formatting | bytes 655360
  71.1 2.6 %bitcast_reduce_fusion = (f32[24,5,4]{0,2,1:T(4,128)S(1)}, f32[5,24,4,2944]{3,1,2,0:T(8,128)S(1)}) fusion(pred[24,2944]{1,0:T(8,128)(4,1)S(1)} %broadcast_compare_fusion, bf16[2944,5,64,1]{0,2,3,1:T(8,128)(2,1)} %bitcast.181, bf16[24,5,4,64]{3,2,1,0:T(4,128)(2,1)S(1)} %reshape.244), kind=kOutput, calls=%fused_computation.1 | convolution fusion | flops 185118240 | bytes 7670656 | tf_op jit(solution)/shard_map/rkgd,tkd->rkgt/dot_general | solution.py:85
  75.7 4.0 %fusion.30 = f32[24,5,4,64]{3,0,2,1:T(8,128)S(1)} fusion(bf16[2944,5,64,1]{0,2,3,1:T(8,128)(2,1)S(1)} %bitcast.183, f32[5,24,4,2944]{3,1,2,0:T(8,128)S(1)} %get-tuple-element.29, f32[24,2944]{1,0:T(8,128)S(1)} %copy-done.7, f32[24,5,4]{0,2,1:T(4,128)S(1)} %get-tuple-element.10, pred[24,2944]{1,0:T(8,128)(4,1)S(1)} %broadcast_compare_fusion, ...), kind=kOutput, calls=%fused_computation.33 | convolution fusion | flops 1093816320 | bytes 8047360 | tf_op jit(solution)/shard_map/rkgt,tkd->rkgd/dot_general | solution.py:192
  80.6 1.8 %collective-permute-start.6 = (bf16[24,1280]{1,0:T(8,128)(2,1)S(1)}, bf16[24,1280]{1,0:T(8,128)(2,1)S(1)}, u32[]{:S(2)}, u32[]{:S(2)}) collective-permute-start(bf16[24,1280]{1,0:T(8,128)(2,1)S(1)} %convert_element_type.111), channel_id=1, source_target_pairs={{0,128},{128,0},{1,129},{129,1},{2,130},{130,2},{3,131},{131,3},{4... | collective-permute-start | bytes 184328 | tf_op jit(solution)/shard_map/ppermute | solution.py:30
  82.5 3.2 %collective-permute-done.6 = bf16[24,1280]{1,0:T(8,128)(2,1)S(1)} collective-permute-done((bf16[24,1280]{1,0:T(8,128)(2,1)S(1)}, bf16[24,1280]{1,0:T(8,128)(2,1)S(1)}, u32[]{:S(2)}, u32[]{:S(2)}) %collective-permute-start.6) | collective-permute-done | bytes 61472 | tf_op jit(solution)/shard_map/ppermute | solution.py:30
  86.4 3.9 %collective-permute-start.9 = (f32[2,24,2048]{2,1,0:T(8,128)S(1)}, f32[2,24,2048]{2,1,0:T(8,128)}, u32[]{:S(2)}, u32[]{:S(2)}) collective-permute-start(f32[2,24,2048]{2,1,0:T(8,128)S(1)} %pad_maximum_fusion.1), channel_id=1, source_target_pairs={{0,64},{192,128},{1,65},{193,129},{2,66},{194,130},{3,67},{195,131... | collective-permute-start | bytes 1179656 | tf_op jit(solution)/shard_map/ppermute | solution.py:212
  92.3 4.8 %collective-permute-done.9 = f32[2,24,2048]{2,1,0:T(8,128)} collective-permute-done((f32[2,24,2048]{2,1,0:T(8,128)S(1)}, f32[2,24,2048]{2,1,0:T(8,128)}, u32[]{:S(2)}, u32[]{:S(2)}) %collective-permute-start.9) | collective-permute-done | bytes 393248 | tf_op jit(solution)/shard_map/ppermute | solution.py:212
  97.1 6.0 %collective-permute-done.7 = f32[2,24,2048]{2,1,0:T(8,128)S(1)} collective-permute-done((f32[2,24,2048]{2,1,0:T(8,128)S(1)}, f32[2,24,2048]{2,1,0:T(8,128)S(1)}, u32[]{:S(2)}, u32[]{:S(2)}) %collective-permute-start.7) | collective-permute-done | bytes 393248 | tf_op jit(solution)/shard_map/ppermute | solution.py:214
  105.0 2.0 %collective-permute-done.10 = bf16[24,2048]{1,0:T(8,128)(2,1)S(1)} collective-permute-done((bf16[24,2048]{1,0:T(8,128)(2,1)S(1)}, bf16[24,2048]{1,0:T(8,128)(2,1)S(1)}, u32[]{:S(2)}, u32[]{:S(2)}) %collective-permute-start.10) | collective-permute-done | bytes 98336 | tf_op jit(solution)/shard_map/ppermute | solution.py:36
  107.0 1.6 collective-permute-done.11
  110.6 43.3 %all-gather.3.cloned.1.call-done = bf16[4,192,2048]{2,1,0:T(8,128)(2,1)} async-done(((bf16[4,24,2048]{2,1,0:T(8,128)(2,1)}), bf16[4,192,2048]{2,1,0:T(8,128)(2,1)}) %all-gather.3.cloned.1.call-update) | async-done | bytes 3145744 | tf_op jit(solution)/shard_map/all_gather | solution.py:236
  155.0 3.3 %fusion.24 = f32[4,8,2,24,250]{4,3,2,1,0:T(8,128)S(1)} fusion(f32[4,8,2,24,250]{4,3,2,1,0:T(8,128)S(1)} %broadcast_in_dim.84, s32[]{:T(128)S(6)} %select_n.293, bf16[4,8,24,2048]{3,2,1,0:T(8,128)(2,1)} %bitcast.195, bf16[2048,250]{1,0:T(8,128)(2,1)} %param.16), kind=kOutput, calls=%fused_computation.28 | convolution fusion | flops 786432000 | bytes 4956164 | tf_op jit(solution)/shard_map/yzrd,dv->yzrv/dot_general | solution.py:240
  158.2 2.2 %collective-permute-done.13 = bf16[4,8,24,2048]{3,2,1,0:T(8,128)(2,1)} collective-permute-done((bf16[4,8,24,2048]{3,2,1,0:T(8,128)(2,1)}, bf16[4,8,24,2048]{3,2,1,0:T(8,128)(2,1)}, u32[]{:S(2)}, u32[]{:S(2)}) %collective-permute-start.13) | collective-permute-done | bytes 3145760 | tf_op jit(solution)/shard_map/ppermute | solution.py:239
  160.4 2.9 %fusion.23 = f32[4,8,2,24,250]{4,3,2,1,0:T(8,128)S(1)} fusion(f32[4,8,2,24,250]{4,3,2,1,0:T(8,128)S(1)} %fusion.24, s32[]{:T(128)S(6)} %select_n.294, bf16[4,8,24,2048]{3,2,1,0:T(8,128)(2,1)} %collective-permute-done.13, bf16[2048,250]{1,0:T(8,128)(2,1)S(1)} %copy-done.10), kind=kOutput, calls=%fused_computation.26 | convolution fusion | flops 786432000 | bytes 4980740 | tf_op jit(solution)/shard_map/yzrd,dv->yzrv/dot_general | solution.py:241
  (106 shorter events, 33.3 us)
Async XLA Ops:
  6.5 79.2 %copy-start = (bf16[640,2048]{1,0:T(8,128)(2,1)S(1)}, bf16[640,2048]{1,0:T(8,128)(2,1)}, u32[]{:S(2)}) copy-start(bf16[640,2048]{1,0:T(8,128)(2,1)} %param.14) | copy-start | bytes 7864324
  6.5 147.3 %all-gather.3.cloned.1.call-start = ((), (), s32[]{:S(2)}) async-start(), calls=%async_computation | async-start | bytes 3538944 | tf_op jit(solution)/shard_map/all_gather | solution.py:236
  9.3 32.3 %collective-permute-start = (bf16[24,2048]{1,0:T(8,128)(2,1)}, bf16[24,2048]{1,0:T(8,128)(2,1)}, u32[]{:S(2)}, u32[]{:S(2)}) collective-permute-start(bf16[24,2048]{1,0:T(8,128)(2,1)} %fusion.48), channel_id=1, source_target_pairs={{0,128},{128,0},{1,129},{129,1},{2,130},{130,2},{3,131},{131,3},{4... | collective-permute-start | bytes 294920 | tf_op jit(solution)/shard_map/ppermute | solution.py:30
  21.2 5.9 %copy-start.3 = (f32[24,3456]{1,0:T(8,128)}, f32[24,3456]{1,0:T(8,128)S(1)}, u32[]{:S(2)}) copy-start(f32[24,3456]{1,0:T(8,128)S(1)} %reshape.246) | copy-start | bytes 995332
  21.2 6.0 %copy-start.1 = (bf16[1,46,64,640]{3,2,1,0:T(8,128)(2,1)S(1)}, bf16[1,46,64,640]{3,2,1,0:T(8,128)(2,1)}, u32[]{:S(2)}) copy-start(bf16[1,46,64,640]{3,2,1,0:T(8,128)(2,1)} %param.17) | copy-start | bytes 11304964
  41.7 11.2 %copy-start.2 = (bf16[1024,1920]{1,0:T(8,128)(2,1)S(1)}, bf16[1024,1920]{1,0:T(8,128)(2,1)}, u32[]{:S(2)}) copy-start(bf16[1024,1920]{1,0:T(8,128)(2,1)} %param.13) | copy-start | bytes 11796484
  42.7 14.3 %collective-permute-start.2 = (bf16[2,64,640]{2,1,0:T(8,128)(2,1)S(1)}, bf16[2,64,640]{2,1,0:T(8,128)(2,1)S(1)}, u32[]{:S(2)}, u32[]{:S(2)}) collective-permute-start(bf16[2,64,640]{2,1,0:T(8,128)(2,1)S(1)} %bitcast.186), channel_id=1, source_target_pairs={{0,126},{1,127},{2,0},{3,1},{4,2},{5,3},{6,4},{7,5},{8,6},{9,7},{1... | collective-permute-start | bytes 491528 | tf_op jit(solution)/shard_map/ppermute | solution.py:36
  50.8 6.1 %collective-permute-start.3 = (bf16[2,64,640]{2,1,0:T(8,128)(2,1)S(1)}, bf16[2,64,640]{2,1,0:T(8,128)(2,1)S(1)}, u32[]{:S(2)}, u32[]{:S(2)}) collective-permute-start(bf16[2,64,640]{2,1,0:T(8,128)(2,1)S(1)} %bitcast.187), channel_id=1, source_target_pairs={{0,127},{1,0},{2,1},{3,2},{4,3},{5,4},{6,5},{7,6},{8,7},{9,8},{10,... | collective-permute-start | bytes 491528 | tf_op jit(solution)/shard_map/ppermute | solution.py:36
  52.2 4.8 %collective-permute-start.4 = (bf16[2,64,640]{2,1,0:T(8,128)(2,1)S(1)}, bf16[2,64,640]{2,1,0:T(8,128)(2,1)S(1)}, u32[]{:S(2)}, u32[]{:S(2)}) collective-permute-start(bf16[2,64,640]{2,1,0:T(8,128)(2,1)S(1)} %bitcast.188), channel_id=1, source_target_pairs={{0,1},{1,2},{2,3},{3,4},{4,5},{5,6},{6,7},{7,8},{8,9},{9,10},{10,1... | collective-permute-start | bytes 491528 | tf_op jit(solution)/shard_map/ppermute | solution.py:36
  52.8 11.4 %collective-permute-start.5 = (bf16[2,64,640]{2,1,0:T(8,128)(2,1)S(1)}, bf16[2,64,640]{2,1,0:T(8,128)(2,1)S(1)}, u32[]{:S(2)}, u32[]{:S(2)}) collective-permute-start(bf16[2,64,640]{2,1,0:T(8,128)(2,1)S(1)} %bitcast.189), channel_id=1, source_target_pairs={{0,2},{1,3},{2,4},{3,5},{4,6},{5,7},{6,8},{7,9},{8,10},{9,11},{10,... | collective-permute-start | bytes 491528 | tf_op jit(solution)/shard_map/ppermute | solution.py:36
  55.2 12.7 %collective-permute-start.1 = (f32[24,1920]{1,0:T(8,128)}, f32[24,1920]{1,0:T(8,128)}, u32[]{:S(2)}, u32[]{:S(2)}) collective-permute-start(f32[24,1920]{1,0:T(8,128)} %select_bitcast_fusion), channel_id=1, source_target_pairs={{0,128},{128,0},{1,129},{129,1},{2,130},{130,2},{3,131},{131,3},{4... | collective-permute-start | bytes 552968 | tf_op jit(solution)/shard_map/ppermute | solution.py:30
  71.0 2.6 %copy-start.7 = (f32[24,2944]{1,0:T(8,128)S(1)}, f32[24,2944]{1,0:T(8,128)}, u32[]{:S(2)}) copy-start(f32[24,2944]{1,0:T(8,128)} %slice.110) | copy-start | bytes 847876
  75.7 4.0 %copy-start.8 = (bf16[512,320]{0,1:T(8,128)(2,1)S(1)}, bf16[512,320]{0,1:T(8,128)(2,1)}, u32[]{:S(2)}) copy-start(bf16[512,320]{0,1:T(8,128)(2,1)} %copy.115) | copy-start | bytes 983044
  79.6 6.7 %copy-start.6 = (bf16[1,24,2048]{2,1,0:T(8,128)(2,1)S(1)}, bf16[1,24,2048]{2,1,0:T(8,128)(2,1)}, u32[]{:S(2)}) copy-start(bf16[1,24,2048]{2,1,0:T(8,128)(2,1)} %param.11) | copy-start | bytes 294916
  80.6 5.2 %collective-permute-start.6 = (bf16[24,1280]{1,0:T(8,128)(2,1)S(1)}, bf16[24,1280]{1,0:T(8,128)(2,1)S(1)}, u32[]{:S(2)}, u32[]{:S(2)}) collective-permute-start(bf16[24,1280]{1,0:T(8,128)(2,1)S(1)} %convert_element_type.111), channel_id=1, source_target_pairs={{0,128},{128,0},{1,129},{129,1},{2,130},{130,2},{3,131},{131,3},{4... | collective-permute-start | bytes 184328 | tf_op jit(solution)/shard_map/ppermute | solution.py:30
  85.7 17.6 %copy-start.9 = (f32[2048]{0:T(1024)S(1)}, f32[2048]{0:T(1024)}, u32[]{:S(2)}) copy-start(f32[2048]{0:T(1024)} %param.15) | copy-start | bytes 24580
  86.4 10.6 %collective-permute-start.9 = (f32[2,24,2048]{2,1,0:T(8,128)S(1)}, f32[2,24,2048]{2,1,0:T(8,128)}, u32[]{:S(2)}, u32[]{:S(2)}) collective-permute-start(f32[2,24,2048]{2,1,0:T(8,128)S(1)} %pad_maximum_fusion.1), channel_id=1, source_target_pairs={{0,64},{192,128},{1,65},{193,129},{2,66},{194,130},{3,67},{195,131... | collective-permute-start | bytes 1179656 | tf_op jit(solution)/shard_map/ppermute | solution.py:212
  90.3 12.8 %collective-permute-start.7 = (f32[2,24,2048]{2,1,0:T(8,128)S(1)}, f32[2,24,2048]{2,1,0:T(8,128)S(1)}, u32[]{:S(2)}, u32[]{:S(2)}) collective-permute-start(f32[2,24,2048]{2,1,0:T(8,128)S(1)} %pad_maximum_fusion.1), channel_id=1, source_target_pairs={{128,0},{64,192},{129,1},{65,193},{130,2},{66,194},{131,3},{67,195... | collective-permute-start | bytes 1179656 | tf_op jit(solution)/shard_map/ppermute | solution.py:214
  91.6 11.6 %collective-permute-start.8 = (f32[2,24,2048]{2,1,0:T(8,128)S(1)}, f32[2,24,2048]{2,1,0:T(8,128)S(1)}, u32[]{:S(2)}, u32[]{:S(2)}) collective-permute-start(f32[2,24,2048]{2,1,0:T(8,128)S(1)} %pad_maximum_fusion.1), channel_id=1, source_target_pairs={{128,64},{64,128},{129,65},{65,129},{130,66},{66,130},{131,67},{67... | collective-permute-start | bytes 1179656 | tf_op jit(solution)/shard_map/ppermute | solution.py:213
  103.5 3.5 %collective-permute-start.10 = (bf16[24,2048]{1,0:T(8,128)(2,1)S(1)}, bf16[24,2048]{1,0:T(8,128)(2,1)S(1)}, u32[]{:S(2)}, u32[]{:S(2)}) collective-permute-start(bf16[24,2048]{1,0:T(8,128)(2,1)S(1)} %fusion.45), channel_id=1, source_target_pairs={{0,48},{16,0},{32,16},{48,32},{1,49},{17,1},{33,17},{49,33},{2,50}... | collective-permute-start | bytes 294920 | tf_op jit(solution)/shard_map/ppermute | solution.py:36
  103.6 5.1 %collective-permute-start.11 = (bf16[24,2048]{1,0:T(8,128)(2,1)S(1)}, bf16[24,2048]{1,0:T(8,128)(2,1)S(1)}, u32[]{:S(2)}, u32[]{:S(2)}) collective-permute-start(bf16[24,2048]{1,0:T(8,128)(2,1)S(1)} %fusion.45), channel_id=1, source_target_pairs={{0,32},{16,48},{32,0},{48,16},{1,33},{17,49},{33,1},{49,17},{2,34}... | collective-permute-start | bytes 294920 | tf_op jit(solution)/shard_map/ppermute | solution.py:36
  103.7 6.0 %collective-permute-start.12 = (bf16[24,2048]{1,0:T(8,128)(2,1)S(1)}, bf16[24,2048]{1,0:T(8,128)(2,1)S(1)}, u32[]{:S(2)}, u32[]{:S(2)}) collective-permute-start(bf16[24,2048]{1,0:T(8,128)(2,1)S(1)} %fusion.45), channel_id=1, source_target_pairs={{0,16},{16,32},{32,48},{48,0},{1,17},{17,33},{33,49},{49,1},{2,18}... | collective-permute-start | bytes 294920 | tf_op jit(solution)/shard_map/ppermute | solution.py:36
  153.9 6.5 %collective-permute-start.13 = (bf16[4,8,24,2048]{3,2,1,0:T(8,128)(2,1)}, bf16[4,8,24,2048]{3,2,1,0:T(8,128)(2,1)}, u32[]{:S(2)}, u32[]{:S(2)}) collective-permute-start(bf16[4,8,24,2048]{3,2,1,0:T(8,128)(2,1)} %bitcast.194), channel_id=1, source_target_pairs={{0,1},{1,0},{2,3},{3,2},{4,5},{5,4},{6,7},{7,6},{8,9},{9,8},{10,11... | collective-permute-start | bytes 9437192 | tf_op jit(solution)/shard_map/ppermute | solution.py:239
  154.8 5.6 %copy-start.10 = (bf16[2048,250]{1,0:T(8,128)(2,1)S(1)}, bf16[2048,250]{1,0:T(8,128)(2,1)}, u32[]{:S(2)}) copy-start(bf16[2048,250]{1,0:T(8,128)(2,1)} %param.16) | copy-start | bytes 3072004
  (2 other events, 3.2 us)
Sparse Core Ops, SparseCore 0:
  110.7 43.1 all-gather.2

commit v14 on v13

--- a/solution.py
+++ b/solution.py
@@ -236,14 +236,22 @@
     gathered = lax.all_gather(gathered, "z", axis=1, tiled=False)
     core = lax.axis_index("core")
     cores = lax.axis_size("core")
-    twin = lax.ppermute(gathered, "core", [(0, 1), (1, 0)])
+    pieces = 2
+    piece_rows = gathered.shape[0] // pieces
+    twins = [
+        lax.ppermute(gathered[piece * piece_rows : (piece + 1) * piece_rows], "core", [(0, 1), (1, 0)])
+        for piece in range(pieces)
+    ]
     mine_logits = jnp.einsum("yzrd,dv->yzrv", gathered, w_vocab, preferred_element_type=jnp.float32)
-    twin_logits = jnp.einsum("yzrd,dv->yzrv", twin, w_vocab, preferred_element_type=jnp.float32)
     logits = jnp.zeros(
         mine_logits.shape[:2] + (cores,) + mine_logits.shape[2:], jnp.float32
     )
     logits = lax.dynamic_update_slice_in_dim(logits, mine_logits[:, :, None], core, 2)
-    logits = lax.dynamic_update_slice_in_dim(logits, twin_logits[:, :, None], 1 - core, 2)
+    for piece, twin in enumerate(twins):
+        twin_logits = jnp.einsum("yzrd,dv->yzrv", twin, w_vocab, preferred_element_type=jnp.float32)
+        logits = lax.dynamic_update_slice(
+            logits, twin_logits[:, :, None], (piece * piece_rows, 0, 1 - core, 0, 0)
+        )
     return logits.reshape(-1, logits.shape[-1])
 
 

time: 172 us -> 175 us (1.017)
  local copies, waits for them, and re-layouts: 27 us -> 31 us
  waiting for transfers between devices: 71.4 us -> 69.3 us
    slice x0 -> x1, local copies, waits for them, and re-layouts: none -> 3.98 us  [body(): gathered[piece * piece_rows:(piece + 1) * piece_rows]]
    ppermute x1 -> x2, waiting for transfers between devices: 2.18 us -> 0.15 us  [body(): lax.ppermute(gathered[piece * piece_rows:(piece + 1) * piece_rows], 'core...]
    dot_general x1 -> x2, matrix products: 2.87 us -> 3.99 us  [body(): jnp.einsum('yzrd,dv->yzrv', twin, w_vocab, preferred_element_type=jnp.flo...]
  transfers between devices with their start and end apart: 15 -> 16, of which waited for: 9 -> 9; matrix products, arithmetic and copies ran while one was open for 22% -> 23% of each run, Pallas kernels for 0% -> 0%
where the time goes in v14:
time: 175 us; the launch traced here: 174 us
  waiting for transfers between devices  69.3 us (40%)
  local copies, waits for them, and re-layouts  31 us (18%)
  starting transfers between devices  25.4 us (15%)
  matrix products  22.6 us (13%)
  between operations  13.9 us (8%)
  other arithmetic  12.1 us (7%)
    all_gather x1, waiting for transfers between devices, body(): gathered = lax.all_gather(gathered, 'z', axis=1, tiled=False)  43.4 us
    unnamed x31, local copies, waits for them, and re-layouts  12.9 us
    ppermute x7, waiting for transfers between devices, shifted(): return lax.ppermute(value, axis, pairs)  11.9 us
    ppermute x7, starting transfers between devices, shifted(): return lax.ppermute(value, axis, pairs)  11.6 us
    ppermute x3, starting transfers between devices, from_partner(): return lax.ppermute(block, axis, route)  7.12 us
    ppermute x1, waiting for transfers between devices, body(): from_guide = lax.ppermute(payload, pair, [(2, 0), (1, 3)])  6.01 us
    slice x1, local copies, waits for them, and re-layouts, dense_scores(): key_rows = flat[:, :half_width].reshape(count, KVH, HD)  5.83 us
    dot_general x2, matrix products, body(): jnp.einsum('rkgt,tkd->rkgd', rounded, values.astype(jnp.float32), precisi...  4.72 us
  transfers between devices with their start and end apart: 16, of which 9 were waited for; matrix products, arithmetic and copies ran while one was open for 23% of the time, Pallas kernels for 0%

profile of v14, /device:TPU:1, one launch (start us, length us, event | category | flops | bytes accessed | tf_op | source)
XLA Modules:
  0.0 174.3 jit_solution(24446286307539321)
XLA Ops:
  9.3 3.6 %collective-permute-start = (bf16[24,2048]{1,0:T(8,128)(2,1)}, bf16[24,2048]{1,0:T(8,128)(2,1)}, u32[]{:S(2)}, u32[]{:S(2)}) collective-permute-start(bf16[24,2048]{1,0:T(8,128)(2,1)} %fusion.50), channel_id=1, source_target_pairs={{0,128},{128,0},{1,129},{129,1},{2,130},{130,2},{3,131},{131,3},{4... | collective-permute-start | bytes 294920 | tf_op jit(solution)/shard_map/ppermute | solution.py:30
  21.3 5.8 %fusion.92 = (bf16[2944,320]{1,0:T(8,128)(2,1)}, bf16[2944,320]{1,0:T(8,128)(2,1)}) fusion(bf16[2944,640]{1,0:T(8,128)(2,1)} %bitcast.190), kind=kLoop, calls=%fused_computation.161 | loop fusion | bytes 7536640 | tf_op jit(solution)/shard_map/slice | solution.py:83
  27.3 3.0 %fusion.18 = bf16[4,2,64,640]{3,0,2,1:T(4,128)(2,1)S(1)} fusion(bf16[46,64,640]{2,1,0:T(8,128)(2,1)S(1)} %bitcast.191, s32[4,2]{0,1:T(2,128)S(1)} %select_reduce_fusion), kind=kOutput, calls=%fused_computation.21 | convolution fusion | flops 30474608 | bytes 4423712 | tf_op jit(solution)/shard_map/smp,pwc->smwc/dot_general | solution.py:155
  31.1 1.7 slice.120
  33.5 4.1 %copy.118 = bf16[2944,320]{0,1:T(8,128)(2,1)} copy(bf16[2944,320]{1,0:T(8,128)(2,1)} %get-tuple-element.11) | data formatting | bytes 3768320
  37.6 4.1 %copy.120 = bf16[2944,320]{0,1:T(8,128)(2,1)} copy(bf16[2944,320]{1,0:T(8,128)(2,1)} %get-tuple-element.12) | data formatting | bytes 3768320
  42.7 8.1 %collective-permute-start.2 = (bf16[2,64,640]{2,1,0:T(8,128)(2,1)S(1)}, bf16[2,64,640]{2,1,0:T(8,128)(2,1)S(1)}, u32[]{:S(2)}, u32[]{:S(2)}) collective-permute-start(bf16[2,64,640]{2,1,0:T(8,128)(2,1)S(1)} %bitcast.198), channel_id=1, source_target_pairs={{0,126},{1,127},{2,0},{3,1},{4,2},{5,3},{6,4},{7,5},{8,6},{9,7},{1... | collective-permute-start | bytes 491528 | tf_op jit(solution)/shard_map/ppermute | solution.py:36
  52.9 1.7 fusion.7
  55.2 1.7 collective-permute-start.1
  57.0 7.2 %collective-permute-done.5 = bf16[2,64,640]{2,1,0:T(8,128)(2,1)S(1)} collective-permute-done((bf16[2,64,640]{2,1,0:T(8,128)(2,1)S(1)}, bf16[2,64,640]{2,1,0:T(8,128)(2,1)S(1)}, u32[]{:S(2)}, u32[]{:S(2)}) %collective-permute-start.5) | collective-permute-done | bytes 163872 | tf_op jit(solution)/shard_map/ppermute | solution.py:36
  65.2 1.9 %copy.119 = bf16[512,320]{0,1:T(8,128)(2,1)} copy(bf16[512,320]{1,0:T(8,128)(2,1)} %get-tuple-element.16) | data formatting | bytes 655360
  71.1 2.6 %bitcast_reduce_fusion = (f32[24,5,4]{0,2,1:T(4,128)S(1)}, f32[5,24,4,2944]{3,1,2,0:T(8,128)S(1)}) fusion(pred[24,2944]{1,0:T(8,128)(4,1)S(1)} %broadcast_compare_fusion, bf16[2944,5,64,1]{0,2,3,1:T(8,128)(2,1)} %bitcast.192, bf16[24,5,4,64]{3,2,1,0:T(4,128)(2,1)S(1)} %reshape.244), kind=kOutput, calls=%fused_computation.1 | convolution fusion | flops 185118240 | bytes 7670656 | tf_op jit(solution)/shard_map/rkgd,tkd->rkgt/dot_general | solution.py:85
  75.7 4.0 %fusion.31 = f32[24,5,4,64]{3,0,2,1:T(8,128)S(1)} fusion(bf16[2944,5,64,1]{0,2,3,1:T(8,128)(2,1)S(1)} %bitcast.195, f32[5,24,4,2944]{3,1,2,0:T(8,128)S(1)} %get-tuple-element.31, f32[24,2944]{1,0:T(8,128)S(1)} %copy-done.7, f32[24,5,4]{0,2,1:T(4,128)S(1)} %get-tuple-element.10, pred[24,2944]{1,0:T(8,128)(4,1)S(1)} %broadcast_compare_fusion, ...), kind=kOutput, calls=%fused_computation.35 | convolution fusion | flops 1093816320 | bytes 8047360 | tf_op jit(solution)/shard_map/rkgt,tkd->rkgd/dot_general | solution.py:192
  80.6 1.8 %collective-permute-start.6 = (bf16[24,1280]{1,0:T(8,128)(2,1)S(1)}, bf16[24,1280]{1,0:T(8,128)(2,1)S(1)}, u32[]{:S(2)}, u32[]{:S(2)}) collective-permute-start(bf16[24,1280]{1,0:T(8,128)(2,1)S(1)} %convert_element_type.111), channel_id=1, source_target_pairs={{0,128},{128,0},{1,129},{129,1},{2,130},{130,2},{3,131},{131,3},{4... | collective-permute-start | bytes 184328 | tf_op jit(solution)/shard_map/ppermute | solution.py:30
  82.6 3.1 %collective-permute-done.6 = bf16[24,1280]{1,0:T(8,128)(2,1)S(1)} collective-permute-done((bf16[24,1280]{1,0:T(8,128)(2,1)S(1)}, bf16[24,1280]{1,0:T(8,128)(2,1)S(1)}, u32[]{:S(2)}, u32[]{:S(2)}) %collective-permute-start.6) | collective-permute-done | bytes 61472 | tf_op jit(solution)/shard_map/ppermute | solution.py:30
  86.3 3.8 %collective-permute-start.9 = (f32[2,24,2048]{2,1,0:T(8,128)S(1)}, f32[2,24,2048]{2,1,0:T(8,128)}, u32[]{:S(2)}, u32[]{:S(2)}) collective-permute-start(f32[2,24,2048]{2,1,0:T(8,128)S(1)} %pad_maximum_fusion.1), channel_id=1, source_target_pairs={{0,64},{192,128},{1,65},{193,129},{2,66},{194,130},{3,67},{195,131... | collective-permute-start | bytes 1179656 | tf_op jit(solution)/shard_map/ppermute | solution.py:212
  92.1 4.7 %collective-permute-done.9 = f32[2,24,2048]{2,1,0:T(8,128)} collective-permute-done((f32[2,24,2048]{2,1,0:T(8,128)S(1)}, f32[2,24,2048]{2,1,0:T(8,128)}, u32[]{:S(2)}, u32[]{:S(2)}) %collective-permute-start.9) | collective-permute-done | bytes 393248 | tf_op jit(solution)/shard_map/ppermute | solution.py:212
  96.9 6.0 %collective-permute-done.7 = f32[2,24,2048]{2,1,0:T(8,128)S(1)} collective-permute-done((f32[2,24,2048]{2,1,0:T(8,128)S(1)}, f32[2,24,2048]{2,1,0:T(8,128)S(1)}, u32[]{:S(2)}, u32[]{:S(2)}) %collective-permute-start.7) | collective-permute-done | bytes 393248 | tf_op jit(solution)/shard_map/ppermute | solution.py:214
  104.8 2.0 %collective-permute-done.10 = bf16[24,2048]{1,0:T(8,128)(2,1)S(1)} collective-permute-done((bf16[24,2048]{1,0:T(8,128)(2,1)S(1)}, bf16[24,2048]{1,0:T(8,128)(2,1)S(1)}, u32[]{:S(2)}, u32[]{:S(2)}) %collective-permute-start.10) | collective-permute-done | bytes 98336 | tf_op jit(solution)/shard_map/ppermute | solution.py:36
  110.4 43.4 %all-gather.3.cloned.1.call-done = bf16[4,192,2048]{2,1,0:T(8,128)(2,1)} async-done(((bf16[4,24,2048]{2,1,0:T(8,128)(2,1)}), bf16[4,192,2048]{2,1,0:T(8,128)(2,1)}) %all-gather.3.cloned.1.call-update) | async-done | bytes 3145744 | tf_op jit(solution)/shard_map/all_gather | solution.py:236
  153.8 4.0 %fusion.93 = (bf16[2,192,2048]{2,1,0:T(8,128)(2,1)}, bf16[2,192,2048]{2,1,0:T(8,128)(2,1)}) fusion(bf16[4,192,2048]{2,1,0:T(8,128)(2,1)} %all-gather.3.cloned.1.call-done), kind=kLoop, calls=%fused_computation.162 | loop fusion | bytes 6291456 | tf_op jit(solution)/shard_map/slice | solution.py:242
  158.9 3.2 %fusion.23 = f32[4,8,2,24,250]{4,3,2,1,0:T(8,128)S(1)} fusion(f32[4,8,2,24,250]{4,3,2,1,0:T(8,128)S(1)} %broadcast_in_dim.86, s32[]{:T(128)S(6)} %select_n.294, bf16[4,8,24,2048]{3,2,1,0:T(8,128)(2,1)} %bitcast.194, bf16[2048,250]{1,0:T(8,128)(2,1)} %param.16), kind=kOutput, calls=%fused_computation.26 | convolution fusion | flops 786432000 | bytes 4956164 | tf_op jit(solution)/shard_map/yzrd,dv->yzrv/dot_general | solution.py:245
  162.1 2.0 %fusion.25 = f32[4,8,2,24,250]{4,3,2,1,0:T(8,128)S(1)} fusion(f32[4,8,2,24,250]{4,3,2,1,0:T(8,128)S(1)} %fusion.23, s32[]{:T(128)S(6)} %select_n.295, bf16[2,8,24,2048]{3,2,1,0:T(8,128)(2,1)} %collective-permute-done.13, bf16[2048,250]{1,0:T(8,128)(2,1)S(1)} %copy-done.10), kind=kOutput, calls=%fused_computation.30 | convolution fusion | flops 393216000 | bytes 3014660 | tf_op jit(solution)/shard_map/yzrd,dv->yzrv/dot_general | solution.py:251
  164.3 2.0 %fusion.24 = f32[4,8,2,24,250]{4,3,2,1,0:T(8,128)S(1)} fusion(f32[4,8,2,24,250]{4,3,2,1,0:T(8,128)S(1)} %fusion.25, s32[]{:T(128)S(6)} %select_n.295, bf16[2,8,24,2048]{3,2,1,0:T(8,128)(2,1)} %collective-permute-done.14, bf16[2048,250]{1,0:T(8,128)(2,1)S(1)} %copy-done.10), kind=kOutput, calls=%fused_computation.28 | convolution fusion | flops 393216000 | bytes 3014660 | tf_op jit(solution)/shard_map/yzrd,dv->yzrv/dot_general | solution.py:251
  (110 shorter events, 35.1 us)
Async XLA Ops:
  6.5 79.1 %copy-start = (bf16[640,2048]{1,0:T(8,128)(2,1)S(1)}, bf16[640,2048]{1,0:T(8,128)(2,1)}, u32[]{:S(2)}) copy-start(bf16[640,2048]{1,0:T(8,128)(2,1)} %param.14) | copy-start | bytes 7864324
  6.5 147.2 %all-gather.3.cloned.1.call-start = ((), (), s32[]{:S(2)}) async-start(), calls=%async_computation | async-start | bytes 3538944 | tf_op jit(solution)/shard_map/all_gather | solution.py:236
  9.3 32.4 %collective-permute-start = (bf16[24,2048]{1,0:T(8,128)(2,1)}, bf16[24,2048]{1,0:T(8,128)(2,1)}, u32[]{:S(2)}, u32[]{:S(2)}) collective-permute-start(bf16[24,2048]{1,0:T(8,128)(2,1)} %fusion.50), channel_id=1, source_target_pairs={{0,128},{128,0},{1,129},{129,1},{2,130},{130,2},{3,131},{131,3},{4... | collective-permute-start | bytes 294920 | tf_op jit(solution)/shard_map/ppermute | solution.py:30
  19.3 7.8 %copy-start.3 = (f32[24,3456]{1,0:T(8,128)}, f32[24,3456]{1,0:T(8,128)S(1)}, u32[]{:S(2)}) copy-start(f32[24,3456]{1,0:T(8,128)S(1)} %reshape.246) | copy-start | bytes 995332
  21.3 6.0 %copy-start.1 = (bf16[1,46,64,640]{3,2,1,0:T(8,128)(2,1)S(1)}, bf16[1,46,64,640]{3,2,1,0:T(8,128)(2,1)}, u32[]{:S(2)}) copy-start(bf16[1,46,64,640]{3,2,1,0:T(8,128)(2,1)} %param.17) | copy-start | bytes 11304964
  41.7 11.2 %copy-start.2 = (bf16[1024,1920]{1,0:T(8,128)(2,1)S(1)}, bf16[1024,1920]{1,0:T(8,128)(2,1)}, u32[]{:S(2)}) copy-start(bf16[1024,1920]{1,0:T(8,128)(2,1)} %param.13) | copy-start | bytes 11796484
  42.7 14.3 %collective-permute-start.2 = (bf16[2,64,640]{2,1,0:T(8,128)(2,1)S(1)}, bf16[2,64,640]{2,1,0:T(8,128)(2,1)S(1)}, u32[]{:S(2)}, u32[]{:S(2)}) collective-permute-start(bf16[2,64,640]{2,1,0:T(8,128)(2,1)S(1)} %bitcast.198), channel_id=1, source_target_pairs={{0,126},{1,127},{2,0},{3,1},{4,2},{5,3},{6,4},{7,5},{8,6},{9,7},{1... | collective-permute-start | bytes 491528 | tf_op jit(solution)/shard_map/ppermute | solution.py:36
  50.8 6.1 %collective-permute-start.3 = (bf16[2,64,640]{2,1,0:T(8,128)(2,1)S(1)}, bf16[2,64,640]{2,1,0:T(8,128)(2,1)S(1)}, u32[]{:S(2)}, u32[]{:S(2)}) collective-permute-start(bf16[2,64,640]{2,1,0:T(8,128)(2,1)S(1)} %bitcast.199), channel_id=1, source_target_pairs={{0,127},{1,0},{2,1},{3,2},{4,3},{5,4},{6,5},{7,6},{8,7},{9,8},{10,... | collective-permute-start | bytes 491528 | tf_op jit(solution)/shard_map/ppermute | solution.py:36
  52.2 4.8 %collective-permute-start.4 = (bf16[2,64,640]{2,1,0:T(8,128)(2,1)S(1)}, bf16[2,64,640]{2,1,0:T(8,128)(2,1)S(1)}, u32[]{:S(2)}, u32[]{:S(2)}) collective-permute-start(bf16[2,64,640]{2,1,0:T(8,128)(2,1)S(1)} %bitcast.200), channel_id=1, source_target_pairs={{0,1},{1,2},{2,3},{3,4},{4,5},{5,6},{6,7},{7,8},{8,9},{9,10},{10,1... | collective-permute-start | bytes 491528 | tf_op jit(solution)/shard_map/ppermute | solution.py:36
  52.8 11.4 %collective-permute-start.5 = (bf16[2,64,640]{2,1,0:T(8,128)(2,1)S(1)}, bf16[2,64,640]{2,1,0:T(8,128)(2,1)S(1)}, u32[]{:S(2)}, u32[]{:S(2)}) collective-permute-start(bf16[2,64,640]{2,1,0:T(8,128)(2,1)S(1)} %bitcast.201), channel_id=1, source_target_pairs={{0,2},{1,3},{2,4},{3,5},{4,6},{5,7},{6,8},{7,9},{8,10},{9,11},{10,... | collective-permute-start | bytes 491528 | tf_op jit(solution)/shard_map/ppermute | solution.py:36
  55.2 12.7 %collective-permute-start.1 = (f32[24,1920]{1,0:T(8,128)}, f32[24,1920]{1,0:T(8,128)}, u32[]{:S(2)}, u32[]{:S(2)}) collective-permute-start(f32[24,1920]{1,0:T(8,128)} %select_bitcast_fusion), channel_id=1, source_target_pairs={{0,128},{128,0},{1,129},{129,1},{2,130},{130,2},{3,131},{131,3},{4... | collective-permute-start | bytes 552968 | tf_op jit(solution)/shard_map/ppermute | solution.py:30
  75.7 4.0 %copy-start.8 = (bf16[512,320]{0,1:T(8,128)(2,1)S(1)}, bf16[512,320]{0,1:T(8,128)(2,1)}, u32[]{:S(2)}) copy-start(bf16[512,320]{0,1:T(8,128)(2,1)} %copy.121) | copy-start | bytes 983044
  80.4 5.8 %copy-start.6 = (bf16[1,24,2048]{2,1,0:T(8,128)(2,1)S(1)}, bf16[1,24,2048]{2,1,0:T(8,128)(2,1)}, u32[]{:S(2)}) copy-start(bf16[1,24,2048]{2,1,0:T(8,128)(2,1)} %param.11) | copy-start | bytes 294916
  80.6 5.1 %collective-permute-start.6 = (bf16[24,1280]{1,0:T(8,128)(2,1)S(1)}, bf16[24,1280]{1,0:T(8,128)(2,1)S(1)}, u32[]{:S(2)}, u32[]{:S(2)}) collective-permute-start(bf16[24,1280]{1,0:T(8,128)(2,1)S(1)} %convert_element_type.111), channel_id=1, source_target_pairs={{0,128},{128,0},{1,129},{129,1},{2,130},{130,2},{3,131},{131,3},{4... | collective-permute-start | bytes 184328 | tf_op jit(solution)/shard_map/ppermute | solution.py:30
  86.2 16.9 %copy-start.9 = (f32[2048]{0:T(1024)S(1)}, f32[2048]{0:T(1024)}, u32[]{:S(2)}) copy-start(f32[2048]{0:T(1024)} %param.15) | copy-start | bytes 24580
  86.3 10.5 %collective-permute-start.9 = (f32[2,24,2048]{2,1,0:T(8,128)S(1)}, f32[2,24,2048]{2,1,0:T(8,128)}, u32[]{:S(2)}, u32[]{:S(2)}) collective-permute-start(f32[2,24,2048]{2,1,0:T(8,128)S(1)} %pad_maximum_fusion.1), channel_id=1, source_target_pairs={{0,64},{192,128},{1,65},{193,129},{2,66},{194,130},{3,67},{195,131... | collective-permute-start | bytes 1179656 | tf_op jit(solution)/shard_map/ppermute | solution.py:212
  90.2 12.7 %collective-permute-start.7 = (f32[2,24,2048]{2,1,0:T(8,128)S(1)}, f32[2,24,2048]{2,1,0:T(8,128)S(1)}, u32[]{:S(2)}, u32[]{:S(2)}) collective-permute-start(f32[2,24,2048]{2,1,0:T(8,128)S(1)} %pad_maximum_fusion.1), channel_id=1, source_target_pairs={{128,0},{64,192},{129,1},{65,193},{130,2},{66,194},{131,3},{67,195... | collective-permute-start | bytes 1179656 | tf_op jit(solution)/shard_map/ppermute | solution.py:214
  91.5 11.5 %collective-permute-start.8 = (f32[2,24,2048]{2,1,0:T(8,128)S(1)}, f32[2,24,2048]{2,1,0:T(8,128)S(1)}, u32[]{:S(2)}, u32[]{:S(2)}) collective-permute-start(f32[2,24,2048]{2,1,0:T(8,128)S(1)} %pad_maximum_fusion.1), channel_id=1, source_target_pairs={{128,64},{64,128},{129,65},{65,129},{130,66},{66,130},{131,67},{67... | collective-permute-start | bytes 1179656 | tf_op jit(solution)/shard_map/ppermute | solution.py:213
  103.3 3.5 %collective-permute-start.10 = (bf16[24,2048]{1,0:T(8,128)(2,1)S(1)}, bf16[24,2048]{1,0:T(8,128)(2,1)S(1)}, u32[]{:S(2)}, u32[]{:S(2)}) collective-permute-start(bf16[24,2048]{1,0:T(8,128)(2,1)S(1)} %fusion.47), channel_id=1, source_target_pairs={{0,48},{16,0},{32,16},{48,32},{1,49},{17,1},{33,17},{49,33},{2,50}... | collective-permute-start | bytes 294920 | tf_op jit(solution)/shard_map/ppermute | solution.py:36
  103.4 5.1 %collective-permute-start.11 = (bf16[24,2048]{1,0:T(8,128)(2,1)S(1)}, bf16[24,2048]{1,0:T(8,128)(2,1)S(1)}, u32[]{:S(2)}, u32[]{:S(2)}) collective-permute-start(bf16[24,2048]{1,0:T(8,128)(2,1)S(1)} %fusion.47), channel_id=1, source_target_pairs={{0,32},{16,48},{32,0},{48,16},{1,33},{17,49},{33,1},{49,17},{2,34}... | collective-permute-start | bytes 294920 | tf_op jit(solution)/shard_map/ppermute | solution.py:36
  103.5 6.0 %collective-permute-start.12 = (bf16[24,2048]{1,0:T(8,128)(2,1)S(1)}, bf16[24,2048]{1,0:T(8,128)(2,1)S(1)}, u32[]{:S(2)}, u32[]{:S(2)}) collective-permute-start(bf16[24,2048]{1,0:T(8,128)(2,1)S(1)} %fusion.47), channel_id=1, source_target_pairs={{0,16},{16,32},{32,48},{48,0},{1,17},{17,33},{33,49},{49,1},{2,18}... | collective-permute-start | bytes 294920 | tf_op jit(solution)/shard_map/ppermute | solution.py:36
  157.7 4.4 %collective-permute-start.13 = (bf16[2,8,24,2048]{3,2,1,0:T(8,128)(2,1)}, bf16[2,8,24,2048]{3,2,1,0:T(8,128)(2,1)}, u32[]{:S(2)}, u32[]{:S(2)}) collective-permute-start(bf16[2,8,24,2048]{3,2,1,0:T(8,128)(2,1)} %bitcast.47), channel_id=1, source_target_pairs={{0,1},{1,0},{2,3},{3,2},{4,5},{5,4},{6,7},{7,6},{8,9},{9,8},{10,11... | collective-permute-start | bytes 4718600 | tf_op jit(solution)/shard_map/ppermute | solution.py:242
  158.7 5.6 %collective-permute-start.14 = (bf16[2,8,24,2048]{3,2,1,0:T(8,128)(2,1)}, bf16[2,8,24,2048]{3,2,1,0:T(8,128)(2,1)}, u32[]{:S(2)}, u32[]{:S(2)}) collective-permute-start(bf16[2,8,24,2048]{3,2,1,0:T(8,128)(2,1)} %bitcast.51), channel_id=1, source_target_pairs={{0,1},{1,0},{2,3},{3,2},{4,5},{5,4},{6,7},{7,6},{8,9},{9,8},{10,11... | collective-permute-start | bytes 4718600 | tf_op jit(solution)/shard_map/ppermute | solution.py:242
  158.8 3.3 %copy-start.10 = (bf16[2048,250]{1,0:T(8,128)(2,1)S(1)}, bf16[2048,250]{1,0:T(8,128)(2,1)}, u32[]{:S(2)}) copy-start(bf16[2048,250]{1,0:T(8,128)(2,1)} %param.16) | copy-start | bytes 3072004
  (3 other events, 5.7 us)
Sparse Core Ops, SparseCore 0:
  110.5 43.2 all-gather.2

commit v15 on v13

--- a/solution.py
+++ b/solution.py
@@ -113,13 +113,16 @@
     offsets = [number - HOP if number < HOP else number - HOP + 1 for number in range(slots)]
     states_in = hidden_in[0].astype(jnp.float32)
     normed = rms_scale(states_in, attn_gain).astype(jnp.bfloat16)
-    partner_normed = from_partner(normed, "guide", 0)
-    both_normed = jnp.where(
-        side == 0, jnp.stack([normed, partner_normed]), jnp.stack([partner_normed, normed])
-    )
     inner_half = w_qkv.shape[0]
-    normed_part = lax.dynamic_slice_in_dim(both_normed, side * inner_half, inner_half, 2)
-    selected = normed_part
+    own_columns = lax.dynamic_slice_in_dim(normed, side * inner_half, inner_half, 1)
+    partner_normed = from_partner(
+        lax.dynamic_slice_in_dim(normed, (1 - side) * inner_half, inner_half, 1), "guide", 0
+    )
+    selected = jnp.where(
+        side == 0,
+        jnp.stack([own_columns, partner_normed]),
+        jnp.stack([partner_normed, own_columns]),
+    )
     qkv_parts = jnp.einsum("grd,df->grf", selected, w_qkv, preferred_element_type=jnp.float32)
     own_qkv = jnp.where(side == 0, qkv_parts[0], qkv_parts[1])
     other_qkv = jnp.where(side == 0, qkv_parts[1], qkv_parts[0])
@@ -197,13 +200,14 @@
             preferred_element_type=jnp.float32,
         )
     attended = (accs / sums[..., None]).reshape(local_rows, query_width).astype(jnp.bfloat16)
-    partner_attended = from_partner(attended, "guide", 0)
-    both_attended = jnp.where(
-        side == 0, jnp.stack([attended, partner_attended]), jnp.stack([partner_attended, attended])
-    )
     head_half = w_out.shape[0]
-    attended_part = lax.dynamic_slice_in_dim(both_attended, side * head_half, head_half, 2)
-    selected = attended_part
+    own_heads = lax.dynamic_slice_in_dim(attended, side * head_half, head_half, 1)
+    partner_heads = from_partner(
+        lax.dynamic_slice_in_dim(attended, (1 - side) * head_half, head_half, 1), "guide", 0
+    )
+    selected = jnp.where(
+        side == 0, jnp.stack([own_heads, partner_heads]), jnp.stack([partner_heads, own_heads])
+    )
     out_parts = jnp.einsum("grc,cd->grd", selected, w_out, preferred_element_type=jnp.float32)
     own_out = jnp.where(side == 0, out_parts[0], out_parts[1])
     other_out = jnp.where(side == 0, out_parts[1], out_parts[0]).astype(jnp.bfloat16)

time: 172 us -> 171 us (level)
    unnamed x31 -> x33, local copies, waits for them, and re-layouts: 12.9 us -> 12.9 us
where the time goes in v15:
time: 171 us; the launch traced here: 170 us
  waiting for transfers between devices  71.5 us (42%)
  local copies, waits for them, and re-layouts  27.6 us (16%)
  starting transfers between devices  25.5 us (15%)
  matrix products  20.6 us (12%)
  between operations  13.8 us (8%)
  other arithmetic  11.1 us (6%)
    all_gather x1, waiting for transfers between devices, body(): gathered = lax.all_gather(gathered, 'z', axis=1, tiled=False)  43.7 us
    unnamed x33, local copies, waits for them, and re-layouts  12.9 us
    ppermute x7, waiting for transfers between devices, shifted(): return lax.ppermute(value, axis, pairs)  12.7 us
    ppermute x7, starting transfers between devices, shifted(): return lax.ppermute(value, axis, pairs)  11.6 us
    ppermute x3, starting transfers between devices, from_partner(): return lax.ppermute(block, axis, route)  7.16 us
    ppermute x1, waiting for transfers between devices, body(): from_guide = lax.ppermute(payload, pair, [(2, 0), (1, 3)])  6.01 us
    slice x1, local copies, waits for them, and re-layouts, dense_scores(): key_rows = flat[:, :half_width].reshape(count, KVH, HD)  5.85 us
    dot_general x2, matrix products, body(): jnp.einsum('rkgt,tkd->rkgd', rounded, values.astype(jnp.float32), precisi...  4.7 us
  transfers between devices with their start and end apart: 15, of which 9 were waited for; matrix products, arithmetic and copies ran while one was open for 22% of the time, Pallas kernels for 0%

profile of v15, /device:TPU:1, one launch (start us, length us, event | category | flops | bytes accessed | tf_op | source)
XLA Modules:
  0.0 170.2 jit_solution(1356315703010627123)
XLA Ops:
  9.4 3.6 %collective-permute-start = (bf16[24,1024]{1,0:T(8,128)(2,1)}, bf16[24,1024]{1,0:T(8,128)(2,1)S(1)}, u32[]{:S(2)}, u32[]{:S(2)}) collective-permute-start(bf16[24,1024]{1,0:T(8,128)(2,1)} %get-tuple-element.24), channel_id=1, source_target_pairs={{0,128},{128,0},{1,129},{129,1},{2,130},{130,2},{3,131},{131,3},{4... | collective-permute-start | bytes 147464 | tf_op jit(solution)/shard_map/ppermute | solution.py:30
  20.3 5.8 %fusion.86 = (bf16[2944,320]{1,0:T(8,128)(2,1)}, bf16[2944,320]{1,0:T(8,128)(2,1)}) fusion(bf16[2944,640]{1,0:T(8,128)(2,1)} %bitcast.183), kind=kLoop, calls=%fused_computation.155 | loop fusion | bytes 7536640 | tf_op jit(solution)/shard_map/slice | solution.py:83
  26.3 3.0 %fusion.18 = bf16[4,2,64,640]{3,0,2,1:T(4,128)(2,1)S(1)} fusion(bf16[46,64,640]{2,1,0:T(8,128)(2,1)S(1)} %bitcast.184, s32[4,2]{0,1:T(2,128)S(1)} %select_reduce_fusion), kind=kOutput, calls=%fused_computation.21 | convolution fusion | flops 30474608 | bytes 4423712 | tf_op jit(solution)/shard_map/smp,pwc->smwc/dot_general | solution.py:158
  30.7 1.7 slice.110
  33.2 4.1 %copy.107 = bf16[2944,320]{0,1:T(8,128)(2,1)} copy(bf16[2944,320]{1,0:T(8,128)(2,1)} %get-tuple-element.11) | data formatting | bytes 3768320
  37.3 4.1 %copy.109 = bf16[2944,320]{0,1:T(8,128)(2,1)} copy(bf16[2944,320]{1,0:T(8,128)(2,1)} %get-tuple-element.12) | data formatting | bytes 3768320
  42.4 8.1 %collective-permute-start.2 = (bf16[2,64,640]{2,1,0:T(8,128)(2,1)S(1)}, bf16[2,64,640]{2,1,0:T(8,128)(2,1)S(1)}, u32[]{:S(2)}, u32[]{:S(2)}) collective-permute-start(bf16[2,64,640]{2,1,0:T(8,128)(2,1)S(1)} %bitcast.190), channel_id=1, source_target_pairs={{0,126},{1,127},{2,0},{3,1},{4,2},{5,3},{6,4},{7,5},{8,6},{9,7},{1... | collective-permute-start | bytes 491528 | tf_op jit(solution)/shard_map/ppermute | solution.py:36
  54.0 1.7 %collective-permute-start.1 = (f32[24,1920]{1,0:T(8,128)}, f32[24,1920]{1,0:T(8,128)}, u32[]{:S(2)}, u32[]{:S(2)}) collective-permute-start(f32[24,1920]{1,0:T(8,128)} %select_bitcast_fusion), channel_id=1, source_target_pairs={{0,128},{128,0},{1,129},{129,1},{2,130},{130,2},{3,131},{131,3},{4... | collective-permute-start | bytes 552968 | tf_op jit(solution)/shard_map/ppermute | solution.py:30
  55.8 8.1 %collective-permute-done.5 = bf16[2,64,640]{2,1,0:T(8,128)(2,1)S(1)} collective-permute-done((bf16[2,64,640]{2,1,0:T(8,128)(2,1)S(1)}, bf16[2,64,640]{2,1,0:T(8,128)(2,1)S(1)}, u32[]{:S(2)}, u32[]{:S(2)}) %collective-permute-start.5) | collective-permute-done | bytes 163872 | tf_op jit(solution)/shard_map/ppermute | solution.py:36
  64.8 1.9 %copy.108 = bf16[512,320]{0,1:T(8,128)(2,1)} copy(bf16[512,320]{1,0:T(8,128)(2,1)} %get-tuple-element.14) | data formatting | bytes 655360
  70.7 2.6 %bitcast_reduce_fusion = (f32[24,5,4]{0,2,1:T(4,128)S(1)}, f32[5,24,4,2944]{3,1,2,0:T(8,128)S(1)}) fusion(pred[24,2944]{1,0:T(8,128)(4,1)S(1)} %broadcast_compare_fusion, bf16[2944,5,64,1]{0,2,3,1:T(8,128)(2,1)} %bitcast.185, bf16[24,5,4,64]{3,2,1,0:T(4,128)(2,1)S(1)} %reshape.220), kind=kOutput, calls=%fused_computation.1 | convolution fusion | flops 185118240 | bytes 7670656 | tf_op jit(solution)/shard_map/rkgd,tkd->rkgt/dot_general | solution.py:85
  73.4 1.6 multiply_reduce_fusion
  75.4 4.0 %fusion.30 = f32[24,5,4,64]{3,0,2,1:T(8,128)S(1)} fusion(bf16[2944,5,64,1]{0,2,3,1:T(8,128)(2,1)S(1)} %bitcast.187, f32[5,24,4,2944]{3,1,2,0:T(8,128)S(1)} %get-tuple-element.33, f32[24,2944]{1,0:T(8,128)S(1)} %copy-done.6, f32[24,5,4]{0,2,1:T(4,128)S(1)} %get-tuple-element.10, pred[24,2944]{1,0:T(8,128)(4,1)S(1)} %broadcast_compare_fusion, ...), kind=kOutput, calls=%fused_computation.33 | convolution fusion | flops 1093816320 | bytes 8047360 | tf_op jit(solution)/shard_map/rkgt,tkd->rkgd/dot_general | solution.py:195
  80.3 1.9 %collective-permute-start.6 = (bf16[24,640]{1,0:T(8,128)(2,1)S(1)}, bf16[24,640]{1,0:T(8,128)(2,1)S(1)}, u32[]{:S(2)}, u32[]{:S(2)}) collective-permute-start(bf16[24,640]{1,0:T(8,128)(2,1)S(1)} %get-tuple-element.28), channel_id=1, source_target_pairs={{0,128},{128,0},{1,129},{129,1},{2,130},{130,2},{3,131},{131,3},{4... | collective-permute-start | bytes 92168 | tf_op jit(solution)/shard_map/ppermute | solution.py:30
  82.2 2.5 %collective-permute-done.6 = bf16[24,640]{1,0:T(8,128)(2,1)S(1)} collective-permute-done((bf16[24,640]{1,0:T(8,128)(2,1)S(1)}, bf16[24,640]{1,0:T(8,128)(2,1)S(1)}, u32[]{:S(2)}, u32[]{:S(2)}) %collective-permute-start.6) | collective-permute-done | bytes 30752 | tf_op jit(solution)/shard_map/ppermute | solution.py:30
  85.3 3.9 %collective-permute-start.9 = (f32[2,24,2048]{2,1,0:T(8,128)S(1)}, f32[2,24,2048]{2,1,0:T(8,128)}, u32[]{:S(2)}, u32[]{:S(2)}) collective-permute-start(f32[2,24,2048]{2,1,0:T(8,128)S(1)} %pad_maximum_fusion.1), channel_id=1, source_target_pairs={{0,64},{192,128},{1,65},{193,129},{2,66},{194,130},{3,67},{195,131... | collective-permute-start | bytes 1179656 | tf_op jit(solution)/shard_map/ppermute | solution.py:216
  91.1 4.4 %collective-permute-done.9 = f32[2,24,2048]{2,1,0:T(8,128)} collective-permute-done((f32[2,24,2048]{2,1,0:T(8,128)S(1)}, f32[2,24,2048]{2,1,0:T(8,128)}, u32[]{:S(2)}, u32[]{:S(2)}) %collective-permute-start.9) | collective-permute-done | bytes 393248 | tf_op jit(solution)/shard_map/ppermute | solution.py:216
  95.6 6.0 %collective-permute-done.7 = f32[2,24,2048]{2,1,0:T(8,128)S(1)} collective-permute-done((f32[2,24,2048]{2,1,0:T(8,128)S(1)}, f32[2,24,2048]{2,1,0:T(8,128)S(1)}, u32[]{:S(2)}, u32[]{:S(2)}) %collective-permute-start.7) | collective-permute-done | bytes 393248 | tf_op jit(solution)/shard_map/ppermute | solution.py:218
  103.5 2.0 %collective-permute-done.10 = bf16[24,2048]{1,0:T(8,128)(2,1)S(1)} collective-permute-done((bf16[24,2048]{1,0:T(8,128)(2,1)S(1)}, bf16[24,2048]{1,0:T(8,128)(2,1)S(1)}, u32[]{:S(2)}, u32[]{:S(2)}) %collective-permute-start.10) | collective-permute-done | bytes 98336 | tf_op jit(solution)/shard_map/ppermute | solution.py:36
  105.5 1.6 collective-permute-done.11
  109.0 43.7 %all-gather.3.cloned.1.call-done = bf16[4,192,2048]{2,1,0:T(8,128)(2,1)} async-done(((bf16[4,24,2048]{2,1,0:T(8,128)(2,1)}), bf16[4,192,2048]{2,1,0:T(8,128)(2,1)}) %all-gather.3.cloned.1.call-update) | async-done | bytes 3145744 | tf_op jit(solution)/shard_map/all_gather | solution.py:240
  153.9 3.3 %fusion.24 = f32[4,8,2,24,250]{4,3,2,1,0:T(8,128)S(1)} fusion(f32[4,8,2,24,250]{4,3,2,1,0:T(8,128)S(1)} %broadcast_in_dim.84, s32[]{:T(128)S(6)} %select_n.301, bf16[4,8,24,2048]{3,2,1,0:T(8,128)(2,1)} %bitcast.200, bf16[2048,250]{1,0:T(8,128)(2,1)} %param.16), kind=kOutput, calls=%fused_computation.28 | convolution fusion | flops 786432000 | bytes 4956164 | tf_op jit(solution)/shard_map/yzrd,dv->yzrv/dot_general | solution.py:244
  157.1 2.2 %collective-permute-done.13 = bf16[4,8,24,2048]{3,2,1,0:T(8,128)(2,1)} collective-permute-done((bf16[4,8,24,2048]{3,2,1,0:T(8,128)(2,1)}, bf16[4,8,24,2048]{3,2,1,0:T(8,128)(2,1)}, u32[]{:S(2)}, u32[]{:S(2)}) %collective-permute-start.13) | collective-permute-done | bytes 3145760 | tf_op jit(solution)/shard_map/ppermute | solution.py:243
  159.3 2.9 %fusion.23 = f32[4,8,2,24,250]{4,3,2,1,0:T(8,128)S(1)} fusion(f32[4,8,2,24,250]{4,3,2,1,0:T(8,128)S(1)} %fusion.24, s32[]{:T(128)S(6)} %select_n.302, bf16[4,8,24,2048]{3,2,1,0:T(8,128)(2,1)} %collective-permute-done.13, bf16[2048,250]{1,0:T(8,128)(2,1)S(1)} %copy-done.11), kind=kOutput, calls=%fused_computation.26 | convolution fusion | flops 786432000 | bytes 4980740 | tf_op jit(solution)/shard_map/yzrd,dv->yzrv/dot_general | solution.py:245
  (108 shorter events, 32.0 us)
Async XLA Ops:
  6.5 78.1 %copy-start = (bf16[640,2048]{1,0:T(8,128)(2,1)S(1)}, bf16[640,2048]{1,0:T(8,128)(2,1)}, u32[]{:S(2)}) copy-start(bf16[640,2048]{1,0:T(8,128)(2,1)} %param.14) | copy-start | bytes 7864324
  6.5 146.2 %all-gather.3.cloned.1.call-start = ((), (), s32[]{:S(2)}) async-start(), calls=%async_computation | async-start | bytes 3538944 | tf_op jit(solution)/shard_map/all_gather | solution.py:240
  9.4 32.0 %collective-permute-start = (bf16[24,1024]{1,0:T(8,128)(2,1)}, bf16[24,1024]{1,0:T(8,128)(2,1)S(1)}, u32[]{:S(2)}, u32[]{:S(2)}) collective-permute-start(bf16[24,1024]{1,0:T(8,128)(2,1)} %get-tuple-element.24), channel_id=1, source_target_pairs={{0,128},{128,0},{1,129},{129,1},{2,130},{130,2},{3,131},{131,3},{4... | collective-permute-start | bytes 147464 | tf_op jit(solution)/shard_map/ppermute | solution.py:30
  20.2 5.9 %copy-start.3 = (f32[24,3456]{1,0:T(8,128)}, f32[24,3456]{1,0:T(8,128)S(1)}, u32[]{:S(2)}) copy-start(f32[24,3456]{1,0:T(8,128)S(1)} %reshape.222) | copy-start | bytes 995332
  20.3 6.0 %copy-start.1 = (bf16[1,46,64,640]{3,2,1,0:T(8,128)(2,1)S(1)}, bf16[1,46,64,640]{3,2,1,0:T(8,128)(2,1)}, u32[]{:S(2)}) copy-start(bf16[1,46,64,640]{3,2,1,0:T(8,128)(2,1)} %param.17) | copy-start | bytes 11304964
  41.4 11.2 %copy-start.2 = (bf16[1024,1920]{1,0:T(8,128)(2,1)S(1)}, bf16[1024,1920]{1,0:T(8,128)(2,1)}, u32[]{:S(2)}) copy-start(bf16[1024,1920]{1,0:T(8,128)(2,1)} %param.13) | copy-start | bytes 11796484
  42.4 13.4 %collective-permute-start.2 = (bf16[2,64,640]{2,1,0:T(8,128)(2,1)S(1)}, bf16[2,64,640]{2,1,0:T(8,128)(2,1)S(1)}, u32[]{:S(2)}, u32[]{:S(2)}) collective-permute-start(bf16[2,64,640]{2,1,0:T(8,128)(2,1)S(1)} %bitcast.190), channel_id=1, source_target_pairs={{0,126},{1,127},{2,0},{3,1},{4,2},{5,3},{6,4},{7,5},{8,6},{9,7},{1... | collective-permute-start | bytes 491528 | tf_op jit(solution)/shard_map/ppermute | solution.py:36
  50.5 5.3 %collective-permute-start.3 = (bf16[2,64,640]{2,1,0:T(8,128)(2,1)S(1)}, bf16[2,64,640]{2,1,0:T(8,128)(2,1)S(1)}, u32[]{:S(2)}, u32[]{:S(2)}) collective-permute-start(bf16[2,64,640]{2,1,0:T(8,128)(2,1)S(1)} %bitcast.191), channel_id=1, source_target_pairs={{0,127},{1,0},{2,1},{3,2},{4,3},{5,4},{6,5},{7,6},{8,7},{9,8},{10,... | collective-permute-start | bytes 491528 | tf_op jit(solution)/shard_map/ppermute | solution.py:36
  51.9 3.9 %collective-permute-start.4 = (bf16[2,64,640]{2,1,0:T(8,128)(2,1)S(1)}, bf16[2,64,640]{2,1,0:T(8,128)(2,1)S(1)}, u32[]{:S(2)}, u32[]{:S(2)}) collective-permute-start(bf16[2,64,640]{2,1,0:T(8,128)(2,1)S(1)} %bitcast.192), channel_id=1, source_target_pairs={{0,1},{1,2},{2,3},{3,4},{4,5},{5,6},{6,7},{7,8},{8,9},{9,10},{10,1... | collective-permute-start | bytes 491528 | tf_op jit(solution)/shard_map/ppermute | solution.py:36
  52.4 11.4 %collective-permute-start.5 = (bf16[2,64,640]{2,1,0:T(8,128)(2,1)S(1)}, bf16[2,64,640]{2,1,0:T(8,128)(2,1)S(1)}, u32[]{:S(2)}, u32[]{:S(2)}) collective-permute-start(bf16[2,64,640]{2,1,0:T(8,128)(2,1)S(1)} %bitcast.193), channel_id=1, source_target_pairs={{0,2},{1,3},{2,4},{3,5},{4,6},{5,7},{6,8},{7,9},{8,10},{9,11},{10,... | collective-permute-start | bytes 491528 | tf_op jit(solution)/shard_map/ppermute | solution.py:36
  53.3 16.1 %copy-start.9 = (pred[24,512]{1,0:T(8,128)(4,1)S(1)}, pred[24,512]{1,0:T(8,128)(4,1)}, u32[]{:S(2)}) copy-start(pred[24,512]{1,0:T(8,128)(4,1)} %broadcast_compare_fusion.1) | copy-start | bytes 36868
  54.0 13.6 %collective-permute-start.1 = (f32[24,1920]{1,0:T(8,128)}, f32[24,1920]{1,0:T(8,128)}, u32[]{:S(2)}, u32[]{:S(2)}) collective-permute-start(f32[24,1920]{1,0:T(8,128)} %select_bitcast_fusion), channel_id=1, source_target_pairs={{0,128},{128,0},{1,129},{129,1},{2,130},{130,2},{3,131},{131,3},{4... | collective-permute-start | bytes 552968 | tf_op jit(solution)/shard_map/ppermute | solution.py:30
  75.3 4.0 %copy-start.8 = (bf16[512,320]{0,1:T(8,128)(2,1)S(1)}, bf16[512,320]{0,1:T(8,128)(2,1)}, u32[]{:S(2)}) copy-start(bf16[512,320]{0,1:T(8,128)(2,1)} %copy.110) | copy-start | bytes 983044
  79.3 5.9 %copy-start.7 = (bf16[1,24,2048]{2,1,0:T(8,128)(2,1)S(1)}, bf16[1,24,2048]{2,1,0:T(8,128)(2,1)}, u32[]{:S(2)}) copy-start(bf16[1,24,2048]{2,1,0:T(8,128)(2,1)} %param.11) | copy-start | bytes 294916
  80.3 4.3 %collective-permute-start.6 = (bf16[24,640]{1,0:T(8,128)(2,1)S(1)}, bf16[24,640]{1,0:T(8,128)(2,1)S(1)}, u32[]{:S(2)}, u32[]{:S(2)}) collective-permute-start(bf16[24,640]{1,0:T(8,128)(2,1)S(1)} %get-tuple-element.28), channel_id=1, source_target_pairs={{0,128},{128,0},{1,129},{129,1},{2,130},{130,2},{3,131},{131,3},{4... | collective-permute-start | bytes 92168 | tf_op jit(solution)/shard_map/ppermute | solution.py:30
  84.6 17.2 %copy-start.10 = (f32[2048]{0:T(1024)S(1)}, f32[2048]{0:T(1024)}, u32[]{:S(2)}) copy-start(f32[2048]{0:T(1024)} %param.15) | copy-start | bytes 24580
  85.3 10.2 %collective-permute-start.9 = (f32[2,24,2048]{2,1,0:T(8,128)S(1)}, f32[2,24,2048]{2,1,0:T(8,128)}, u32[]{:S(2)}, u32[]{:S(2)}) collective-permute-start(f32[2,24,2048]{2,1,0:T(8,128)S(1)} %pad_maximum_fusion.1), channel_id=1, source_target_pairs={{0,64},{192,128},{1,65},{193,129},{2,66},{194,130},{3,67},{195,131... | collective-permute-start | bytes 1179656 | tf_op jit(solution)/shard_map/ppermute | solution.py:216
  89.2 12.4 %collective-permute-start.7 = (f32[2,24,2048]{2,1,0:T(8,128)S(1)}, f32[2,24,2048]{2,1,0:T(8,128)S(1)}, u32[]{:S(2)}, u32[]{:S(2)}) collective-permute-start(f32[2,24,2048]{2,1,0:T(8,128)S(1)} %pad_maximum_fusion.1), channel_id=1, source_target_pairs={{128,0},{64,192},{129,1},{65,193},{130,2},{66,194},{131,3},{67,195... | collective-permute-start | bytes 1179656 | tf_op jit(solution)/shard_map/ppermute | solution.py:218
  90.5 11.1 %collective-permute-start.8 = (f32[2,24,2048]{2,1,0:T(8,128)S(1)}, f32[2,24,2048]{2,1,0:T(8,128)S(1)}, u32[]{:S(2)}, u32[]{:S(2)}) collective-permute-start(f32[2,24,2048]{2,1,0:T(8,128)S(1)} %pad_maximum_fusion.1), channel_id=1, source_target_pairs={{128,64},{64,128},{129,65},{65,129},{130,66},{66,130},{131,67},{67... | collective-permute-start | bytes 1179656 | tf_op jit(solution)/shard_map/ppermute | solution.py:217
  101.9 3.5 %collective-permute-start.10 = (bf16[24,2048]{1,0:T(8,128)(2,1)S(1)}, bf16[24,2048]{1,0:T(8,128)(2,1)S(1)}, u32[]{:S(2)}, u32[]{:S(2)}) collective-permute-start(bf16[24,2048]{1,0:T(8,128)(2,1)S(1)} %fusion.48), channel_id=1, source_target_pairs={{0,48},{16,0},{32,16},{48,32},{1,49},{17,1},{33,17},{49,33},{2,50}... | collective-permute-start | bytes 294920 | tf_op jit(solution)/shard_map/ppermute | solution.py:36
  102.0 5.1 %collective-permute-start.11 = (bf16[24,2048]{1,0:T(8,128)(2,1)S(1)}, bf16[24,2048]{1,0:T(8,128)(2,1)S(1)}, u32[]{:S(2)}, u32[]{:S(2)}) collective-permute-start(bf16[24,2048]{1,0:T(8,128)(2,1)S(1)} %fusion.48), channel_id=1, source_target_pairs={{0,32},{16,48},{32,0},{48,16},{1,33},{17,49},{33,1},{49,17},{2,34}... | collective-permute-start | bytes 294920 | tf_op jit(solution)/shard_map/ppermute | solution.py:36
  102.1 6.0 %collective-permute-start.12 = (bf16[24,2048]{1,0:T(8,128)(2,1)S(1)}, bf16[24,2048]{1,0:T(8,128)(2,1)S(1)}, u32[]{:S(2)}, u32[]{:S(2)}) collective-permute-start(bf16[24,2048]{1,0:T(8,128)(2,1)S(1)} %fusion.48), channel_id=1, source_target_pairs={{0,16},{16,32},{32,48},{48,0},{1,17},{17,33},{33,49},{49,1},{2,18}... | collective-permute-start | bytes 294920 | tf_op jit(solution)/shard_map/ppermute | solution.py:36
  152.8 6.5 %collective-permute-start.13 = (bf16[4,8,24,2048]{3,2,1,0:T(8,128)(2,1)}, bf16[4,8,24,2048]{3,2,1,0:T(8,128)(2,1)}, u32[]{:S(2)}, u32[]{:S(2)}) collective-permute-start(bf16[4,8,24,2048]{3,2,1,0:T(8,128)(2,1)} %bitcast.199), channel_id=1, source_target_pairs={{0,1},{1,0},{2,3},{3,2},{4,5},{5,4},{6,7},{7,6},{8,9},{9,8},{10,11... | collective-permute-start | bytes 9437192 | tf_op jit(solution)/shard_map/ppermute | solution.py:243
  153.7 5.6 %copy-start.11 = (bf16[2048,250]{1,0:T(8,128)(2,1)S(1)}, bf16[2048,250]{1,0:T(8,128)(2,1)}, u32[]{:S(2)}) copy-start(bf16[2048,250]{1,0:T(8,128)(2,1)} %param.16) | copy-start | bytes 3072004
  (3 other events, 5.8 us)
Sparse Core Ops, SparseCore 0:
  109.2 43.5 all-gather.2

commit v16 on v15

--- a/solution.py
+++ b/solution.py
@@ -211,16 +211,18 @@
     out_parts = jnp.einsum("grc,cd->grd", selected, w_out, preferred_element_type=jnp.float32)
     own_out = jnp.where(side == 0, out_parts[0], out_parts[1])
     other_out = jnp.where(side == 0, out_parts[1], out_parts[0]).astype(jnp.bfloat16)
-    payload = jnp.stack([states_in + own_out, other_out.astype(jnp.float32)])
+    state_part = states_in + own_out
     pair = ("guide", "x_lo")
-    from_side = lax.ppermute(payload, pair, [(0, 1), (3, 2)])
-    from_diagonal = lax.ppermute(payload, pair, [(2, 1), (1, 2)])
-    from_guide = lax.ppermute(payload, pair, [(2, 0), (1, 3)])
+    routes = ([(0, 1), (3, 2)], [(2, 1), (1, 2)], [(2, 0), (1, 3)])
+    side_state, diagonal_state, guide_state = [lax.ppermute(state_part, pair, r) for r in routes]
+    side_out, diagonal_out, guide_out = [lax.ppermute(other_out, pair, r) for r in routes]
     home = lax.axis_index("x_lo") == side
-    same_source = jnp.where(home, payload, from_side)
-    other_source = jnp.where(home, from_guide, from_diagonal)
-    same_group = rms_scale(same_source[0] + other_source[1], final_gain).astype(jnp.bfloat16)
-    other_group = rms_scale(other_source[0] + same_source[1], final_gain).astype(jnp.bfloat16)
+    same_state = jnp.where(home, state_part, side_state)
+    same_out = jnp.where(home, other_out, side_out).astype(jnp.float32)
+    other_state = jnp.where(home, guide_state, diagonal_state)
+    other_part = jnp.where(home, guide_out, diagonal_out).astype(jnp.float32)
+    same_group = rms_scale(same_state + other_part, final_gain).astype(jnp.bfloat16)
+    other_group = rms_scale(other_state + same_out, final_gain).astype(jnp.bfloat16)
     cond = jnp.where(side == 0, same_group, other_group).astype(jnp.float32)
     uncond = jnp.where(side == 0, other_group, same_group).astype(jnp.float32)
     combined = (uncond + guidance * (cond - uncond)).astype(jnp.bfloat16)

time: 171 us -> 173 us (1.012)
  starting transfers between devices: 25.5 us -> 32.2 us
  waiting for transfers between devices: 71.5 us -> 66.3 us
    ppermute x3 -> x6, starting transfers between devices: 5.83 us -> 12.5 us  [the longest x3 7.34 us: body(): lax.ppermute(other_out, pair, r)]
    ppermute x3 -> x6, waiting for transfers between devices: 10.4 us -> 4.25 us  [the longest x3 4.24 us: body(): lax.ppermute(other_out, pair, r)]
  transfers between devices with their start and end apart: 15 -> 18, of which waited for: 9 -> 9; matrix products, arithmetic and copies ran while one was open for 22% -> 22% of each run, Pallas kernels for 0% -> 0%
where the time goes in v16:
time: 173 us; the launch traced here: 172 us
  waiting for transfers between devices  66.3 us (38%)
  starting transfers between devices  32.2 us (19%)
  local copies, waits for them, and re-layouts  27.6 us (16%)
  matrix products  20.6 us (12%)
  between operations  13.9 us (8%)
  other arithmetic  11.8 us (7%)
    all_gather x1, waiting for transfers between devices, body(): gathered = lax.all_gather(gathered, 'z', axis=1, tiled=False)  44.6 us
    unnamed x33, local copies, waits for them, and re-layouts  12.9 us
    ppermute x7, waiting for transfers between devices, shifted(): return lax.ppermute(value, axis, pairs)  12.7 us
    ppermute x7, starting transfers between devices, shifted(): return lax.ppermute(value, axis, pairs)  11.6 us
    ppermute x3, starting transfers between devices, body(): lax.ppermute(other_out, pair, r)  7.34 us
    ppermute x3, starting transfers between devices, from_partner(): return lax.ppermute(block, axis, route)  7.17 us
    slice x1, local copies, waits for them, and re-layouts, dense_scores(): key_rows = flat[:, :half_width].reshape(count, KVH, HD)  5.85 us
    ppermute x3, starting transfers between devices, body(): lax.ppermute(state_part, pair, r)  5.12 us
  transfers between devices with their start and end apart: 18, of which 9 were waited for; matrix products, arithmetic and copies ran while one was open for 22% of the time, Pallas kernels for 0%

profile of v16, /device:TPU:1, one launch (start us, length us, event | category | flops | bytes accessed | tf_op | source)
XLA Modules:
  0.0 172.3 jit_solution(9552575490064026827)
XLA Ops:
  9.4 3.6 %collective-permute-start = (bf16[24,1024]{1,0:T(8,128)(2,1)}, bf16[24,1024]{1,0:T(8,128)(2,1)S(1)}, u32[]{:S(2)}, u32[]{:S(2)}) collective-permute-start(bf16[24,1024]{1,0:T(8,128)(2,1)} %get-tuple-element.26), channel_id=1, source_target_pairs={{0,128},{128,0},{1,129},{129,1},{2,130},{130,2},{3,131},{131,3},{4... | collective-permute-start | bytes 147464 | tf_op jit(solution)/shard_map/ppermute | solution.py:30
  20.3 5.8 %fusion.82 = (bf16[2944,320]{1,0:T(8,128)(2,1)}, bf16[2944,320]{1,0:T(8,128)(2,1)}) fusion(bf16[2944,640]{1,0:T(8,128)(2,1)} %bitcast.170), kind=kLoop, calls=%fused_computation.149 | loop fusion | bytes 7536640 | tf_op jit(solution)/shard_map/slice | solution.py:83
  26.3 3.0 %fusion.18 = bf16[4,2,64,640]{3,0,2,1:T(4,128)(2,1)S(1)} fusion(bf16[46,64,640]{2,1,0:T(8,128)(2,1)S(1)} %bitcast.171, s32[4,2]{0,1:T(2,128)S(1)} %select_reduce_fusion), kind=kOutput, calls=%fused_computation.21 | convolution fusion | flops 30474608 | bytes 4423712 | tf_op jit(solution)/shard_map/smp,pwc->smwc/dot_general | solution.py:158
  30.7 1.7 slice.94
  33.2 4.1 %copy.107 = bf16[2944,320]{0,1:T(8,128)(2,1)} copy(bf16[2944,320]{1,0:T(8,128)(2,1)} %get-tuple-element.13) | data formatting | bytes 3768320
  37.3 4.1 %copy.109 = bf16[2944,320]{0,1:T(8,128)(2,1)} copy(bf16[2944,320]{1,0:T(8,128)(2,1)} %get-tuple-element.14) | data formatting | bytes 3768320
  42.4 8.1 %collective-permute-start.2 = (bf16[2,64,640]{2,1,0:T(8,128)(2,1)S(1)}, bf16[2,64,640]{2,1,0:T(8,128)(2,1)S(1)}, u32[]{:S(2)}, u32[]{:S(2)}) collective-permute-start(bf16[2,64,640]{2,1,0:T(8,128)(2,1)S(1)} %bitcast.177), channel_id=1, source_target_pairs={{0,126},{1,127},{2,0},{3,1},{4,2},{5,3},{6,4},{7,5},{8,6},{9,7},{1... | collective-permute-start | bytes 491528 | tf_op jit(solution)/shard_map/ppermute | solution.py:36
  54.0 1.7 %collective-permute-start.1 = (f32[24,1920]{1,0:T(8,128)}, f32[24,1920]{1,0:T(8,128)}, u32[]{:S(2)}, u32[]{:S(2)}) collective-permute-start(f32[24,1920]{1,0:T(8,128)} %select_bitcast_fusion), channel_id=1, source_target_pairs={{0,128},{128,0},{1,129},{129,1},{2,130},{130,2},{3,131},{131,3},{4... | collective-permute-start | bytes 552968 | tf_op jit(solution)/shard_map/ppermute | solution.py:30
  55.8 8.1 %collective-permute-done.5 = bf16[2,64,640]{2,1,0:T(8,128)(2,1)S(1)} collective-permute-done((bf16[2,64,640]{2,1,0:T(8,128)(2,1)S(1)}, bf16[2,64,640]{2,1,0:T(8,128)(2,1)S(1)}, u32[]{:S(2)}, u32[]{:S(2)}) %collective-permute-start.5) | collective-permute-done | bytes 163872 | tf_op jit(solution)/shard_map/ppermute | solution.py:36
  64.9 1.9 %copy.108 = bf16[512,320]{0,1:T(8,128)(2,1)} copy(bf16[512,320]{1,0:T(8,128)(2,1)} %get-tuple-element.16) | data formatting | bytes 655360
  70.7 2.6 %bitcast_reduce_fusion = (f32[24,5,4]{0,2,1:T(4,128)S(1)}, f32[5,24,4,2944]{3,1,2,0:T(8,128)S(1)}) fusion(pred[24,2944]{1,0:T(8,128)(4,1)S(1)} %broadcast_compare_fusion, bf16[2944,5,64,1]{0,2,3,1:T(8,128)(2,1)} %bitcast.172, bf16[24,5,4,64]{3,2,1,0:T(4,128)(2,1)S(1)} %reshape.223), kind=kOutput, calls=%fused_computation.1 | convolution fusion | flops 185118240 | bytes 7670656 | tf_op jit(solution)/shard_map/rkgd,tkd->rkgt/dot_general | solution.py:85
  75.3 4.0 %fusion.30 = f32[24,5,4,64]{3,0,2,1:T(8,128)S(1)} fusion(bf16[2944,5,64,1]{0,2,3,1:T(8,128)(2,1)S(1)} %bitcast.174, f32[5,24,4,2944]{3,1,2,0:T(8,128)S(1)} %get-tuple-element.35, f32[24,2944]{1,0:T(8,128)S(1)} %copy-done.6, f32[24,5,4]{0,2,1:T(4,128)S(1)} %get-tuple-element.12, pred[24,2944]{1,0:T(8,128)(4,1)S(1)} %broadcast_compare_fusion, ...), kind=kOutput, calls=%fused_computation.33 | convolution fusion | flops 1093816320 | bytes 8047360 | tf_op jit(solution)/shard_map/rkgt,tkd->rkgd/dot_general | solution.py:195
  80.3 1.9 %collective-permute-start.6 = (bf16[24,640]{1,0:T(8,128)(2,1)S(1)}, bf16[24,640]{1,0:T(8,128)(2,1)S(1)}, u32[]{:S(2)}, u32[]{:S(2)}) collective-permute-start(bf16[24,640]{1,0:T(8,128)(2,1)S(1)} %get-tuple-element.30), channel_id=1, source_target_pairs={{0,128},{128,0},{1,129},{129,1},{2,130},{130,2},{3,131},{131,3},{4... | collective-permute-start | bytes 92168 | tf_op jit(solution)/shard_map/ppermute | solution.py:30
  82.2 2.5 %collective-permute-done.6 = bf16[24,640]{1,0:T(8,128)(2,1)S(1)} collective-permute-done((bf16[24,640]{1,0:T(8,128)(2,1)S(1)}, bf16[24,640]{1,0:T(8,128)(2,1)S(1)}, u32[]{:S(2)}, u32[]{:S(2)}) %collective-permute-start.6) | collective-permute-done | bytes 30752 | tf_op jit(solution)/shard_map/ppermute | solution.py:30
  85.2 3.2 %collective-permute-start.10 = (f32[24,2048]{1,0:T(8,128)S(1)}, f32[24,2048]{1,0:T(8,128)S(1)}, u32[]{:S(2)}, u32[]{:S(2)}) collective-permute-start(f32[24,2048]{1,0:T(8,128)S(1)} %convert_add_fusion), channel_id=1, source_target_pairs={{0,64},{192,128},{1,65},{193,129},{2,66},{194,130},{3,67},{195,131... | collective-permute-start | bytes 589832 | tf_op jit(solution)/shard_map/ppermute | solution.py:217
  93.6 2.5 %collective-permute-done.11 = bf16[24,2048]{1,0:T(8,128)(2,1)S(1)} collective-permute-done((bf16[24,2048]{1,0:T(8,128)(2,1)}, bf16[24,2048]{1,0:T(8,128)(2,1)S(1)}, u32[]{:S(2)}, u32[]{:S(2)}) %collective-permute-start.11) | collective-permute-done | bytes 98336 | tf_op jit(solution)/shard_map/ppermute | solution.py:218
  96.1 4.8 %collective-permute-start.9 = (bf16[24,2048]{1,0:T(8,128)(2,1)}, bf16[24,2048]{1,0:T(8,128)(2,1)S(1)}, u32[]{:S(2)}, u32[]{:S(2)}) collective-permute-start(bf16[24,2048]{1,0:T(8,128)(2,1)} %fusion.51), channel_id=1, source_target_pairs={{0,64},{192,128},{1,65},{193,129},{2,66},{194,130},{3,67},{195,131... | collective-permute-start | bytes 294920 | tf_op jit(solution)/shard_map/ppermute | solution.py:218
  101.1 1.7 %collective-permute-done.9 = bf16[24,2048]{1,0:T(8,128)(2,1)S(1)} collective-permute-done((bf16[24,2048]{1,0:T(8,128)(2,1)}, bf16[24,2048]{1,0:T(8,128)(2,1)S(1)}, u32[]{:S(2)}, u32[]{:S(2)}) %collective-permute-start.9) | collective-permute-done | bytes 98336 | tf_op jit(solution)/shard_map/ppermute | solution.py:218
  104.7 2.0 %collective-permute-done.13 = bf16[24,2048]{1,0:T(8,128)(2,1)S(1)} collective-permute-done((bf16[24,2048]{1,0:T(8,128)(2,1)S(1)}, bf16[24,2048]{1,0:T(8,128)(2,1)S(1)}, u32[]{:S(2)}, u32[]{:S(2)}) %collective-permute-start.13) | collective-permute-done | bytes 98336 | tf_op jit(solution)/shard_map/ppermute | solution.py:36
  106.7 1.6 collective-permute-done.14
  110.3 44.6 %all-gather.3.cloned.1.call-done = bf16[4,192,2048]{2,1,0:T(8,128)(2,1)} async-done(((bf16[4,24,2048]{2,1,0:T(8,128)(2,1)}), bf16[4,192,2048]{2,1,0:T(8,128)(2,1)}) %all-gather.3.cloned.1.call-update) | async-done | bytes 3145744 | tf_op jit(solution)/shard_map/all_gather | solution.py:242
  156.0 3.3 %fusion.24 = f32[4,8,2,24,250]{4,3,2,1,0:T(8,128)S(1)} fusion(f32[4,8,2,24,250]{4,3,2,1,0:T(8,128)S(1)} %broadcast_in_dim.84, s32[]{:T(128)S(6)} %select_n.312, bf16[4,8,24,2048]{3,2,1,0:T(8,128)(2,1)} %bitcast.187, bf16[2048,250]{1,0:T(8,128)(2,1)} %param.16), kind=kOutput, calls=%fused_computation.28 | convolution fusion | flops 786432000 | bytes 4956164 | tf_op jit(solution)/shard_map/yzrd,dv->yzrv/dot_general | solution.py:246
  159.3 2.2 %collective-permute-done.16 = bf16[4,8,24,2048]{3,2,1,0:T(8,128)(2,1)} collective-permute-done((bf16[4,8,24,2048]{3,2,1,0:T(8,128)(2,1)}, bf16[4,8,24,2048]{3,2,1,0:T(8,128)(2,1)}, u32[]{:S(2)}, u32[]{:S(2)}) %collective-permute-start.16) | collective-permute-done | bytes 3145760 | tf_op jit(solution)/shard_map/ppermute | solution.py:245
  161.4 2.9 %fusion.23 = f32[4,8,2,24,250]{4,3,2,1,0:T(8,128)S(1)} fusion(f32[4,8,2,24,250]{4,3,2,1,0:T(8,128)S(1)} %fusion.24, s32[]{:T(128)S(6)} %select_n.313, bf16[4,8,24,2048]{3,2,1,0:T(8,128)(2,1)} %collective-permute-done.16, bf16[2048,250]{1,0:T(8,128)(2,1)S(1)} %copy-done.11), kind=kOutput, calls=%fused_computation.26 | convolution fusion | flops 786432000 | bytes 4980740 | tf_op jit(solution)/shard_map/yzrd,dv->yzrv/dot_general | solution.py:247
  (113 shorter events, 36.8 us)
Async XLA Ops:
  6.5 78.1 %copy-start = (bf16[640,2048]{1,0:T(8,128)(2,1)S(1)}, bf16[640,2048]{1,0:T(8,128)(2,1)}, u32[]{:S(2)}) copy-start(bf16[640,2048]{1,0:T(8,128)(2,1)} %param.14) | copy-start | bytes 7864324
  6.5 148.4 %all-gather.3.cloned.1.call-start = ((), (), s32[]{:S(2)}) async-start(), calls=%async_computation | async-start | bytes 3538944 | tf_op jit(solution)/shard_map/all_gather | solution.py:242
  9.4 32.0 %collective-permute-start = (bf16[24,1024]{1,0:T(8,128)(2,1)}, bf16[24,1024]{1,0:T(8,128)(2,1)S(1)}, u32[]{:S(2)}, u32[]{:S(2)}) collective-permute-start(bf16[24,1024]{1,0:T(8,128)(2,1)} %get-tuple-element.26), channel_id=1, source_target_pairs={{0,128},{128,0},{1,129},{129,1},{2,130},{130,2},{3,131},{131,3},{4... | collective-permute-start | bytes 147464 | tf_op jit(solution)/shard_map/ppermute | solution.py:30
  20.2 5.9 %copy-start.3 = (f32[24,3456]{1,0:T(8,128)}, f32[24,3456]{1,0:T(8,128)S(1)}, u32[]{:S(2)}) copy-start(f32[24,3456]{1,0:T(8,128)S(1)} %reshape.225) | copy-start | bytes 995332
  20.3 6.0 %copy-start.1 = (bf16[1,46,64,640]{3,2,1,0:T(8,128)(2,1)S(1)}, bf16[1,46,64,640]{3,2,1,0:T(8,128)(2,1)}, u32[]{:S(2)}) copy-start(bf16[1,46,64,640]{3,2,1,0:T(8,128)(2,1)} %param.17) | copy-start | bytes 11304964
  41.4 11.2 %copy-start.2 = (bf16[1024,1920]{1,0:T(8,128)(2,1)S(1)}, bf16[1024,1920]{1,0:T(8,128)(2,1)}, u32[]{:S(2)}) copy-start(bf16[1024,1920]{1,0:T(8,128)(2,1)} %param.13) | copy-start | bytes 11796484
  42.4 13.4 %collective-permute-start.2 = (bf16[2,64,640]{2,1,0:T(8,128)(2,1)S(1)}, bf16[2,64,640]{2,1,0:T(8,128)(2,1)S(1)}, u32[]{:S(2)}, u32[]{:S(2)}) collective-permute-start(bf16[2,64,640]{2,1,0:T(8,128)(2,1)S(1)} %bitcast.177), channel_id=1, source_target_pairs={{0,126},{1,127},{2,0},{3,1},{4,2},{5,3},{6,4},{7,5},{8,6},{9,7},{1... | collective-permute-start | bytes 491528 | tf_op jit(solution)/shard_map/ppermute | solution.py:36
  50.5 5.3 %collective-permute-start.3 = (bf16[2,64,640]{2,1,0:T(8,128)(2,1)S(1)}, bf16[2,64,640]{2,1,0:T(8,128)(2,1)S(1)}, u32[]{:S(2)}, u32[]{:S(2)}) collective-permute-start(bf16[2,64,640]{2,1,0:T(8,128)(2,1)S(1)} %bitcast.178), channel_id=1, source_target_pairs={{0,127},{1,0},{2,1},{3,2},{4,3},{5,4},{6,5},{7,6},{8,7},{9,8},{10,... | collective-permute-start | bytes 491528 | tf_op jit(solution)/shard_map/ppermute | solution.py:36
  51.9 3.9 %collective-permute-start.4 = (bf16[2,64,640]{2,1,0:T(8,128)(2,1)S(1)}, bf16[2,64,640]{2,1,0:T(8,128)(2,1)S(1)}, u32[]{:S(2)}, u32[]{:S(2)}) collective-permute-start(bf16[2,64,640]{2,1,0:T(8,128)(2,1)S(1)} %bitcast.179), channel_id=1, source_target_pairs={{0,1},{1,2},{2,3},{3,4},{4,5},{5,6},{6,7},{7,8},{8,9},{9,10},{10,1... | collective-permute-start | bytes 491528 | tf_op jit(solution)/shard_map/ppermute | solution.py:36
  52.5 11.4 %collective-permute-start.5 = (bf16[2,64,640]{2,1,0:T(8,128)(2,1)S(1)}, bf16[2,64,640]{2,1,0:T(8,128)(2,1)S(1)}, u32[]{:S(2)}, u32[]{:S(2)}) collective-permute-start(bf16[2,64,640]{2,1,0:T(8,128)(2,1)S(1)} %bitcast.180), channel_id=1, source_target_pairs={{0,2},{1,3},{2,4},{3,5},{4,6},{5,7},{6,8},{7,9},{8,10},{9,11},{10,... | collective-permute-start | bytes 491528 | tf_op jit(solution)/shard_map/ppermute | solution.py:36
  53.3 16.1 %copy-start.9 = (pred[24,512]{1,0:T(8,128)(4,1)S(1)}, pred[24,512]{1,0:T(8,128)(4,1)}, u32[]{:S(2)}) copy-start(pred[24,512]{1,0:T(8,128)(4,1)} %broadcast_compare_fusion.1) | copy-start | bytes 36868
  54.0 13.6 %collective-permute-start.1 = (f32[24,1920]{1,0:T(8,128)}, f32[24,1920]{1,0:T(8,128)}, u32[]{:S(2)}, u32[]{:S(2)}) collective-permute-start(f32[24,1920]{1,0:T(8,128)} %select_bitcast_fusion), channel_id=1, source_target_pairs={{0,128},{128,0},{1,129},{129,1},{2,130},{130,2},{3,131},{131,3},{4... | collective-permute-start | bytes 552968 | tf_op jit(solution)/shard_map/ppermute | solution.py:30
  80.3 22.8 %copy-start.10 = (f32[2048]{0:T(1024)S(1)}, f32[2048]{0:T(1024)}, u32[]{:S(2)}) copy-start(f32[2048]{0:T(1024)} %param.15) | copy-start | bytes 24580
  80.3 4.3 %collective-permute-start.6 = (bf16[24,640]{1,0:T(8,128)(2,1)S(1)}, bf16[24,640]{1,0:T(8,128)(2,1)S(1)}, u32[]{:S(2)}, u32[]{:S(2)}) collective-permute-start(bf16[24,640]{1,0:T(8,128)(2,1)S(1)} %get-tuple-element.30), channel_id=1, source_target_pairs={{0,128},{128,0},{1,129},{129,1},{2,130},{130,2},{3,131},{131,3},{4... | collective-permute-start | bytes 92168 | tf_op jit(solution)/shard_map/ppermute | solution.py:30
  85.2 15.7 %collective-permute-start.10 = (f32[24,2048]{1,0:T(8,128)S(1)}, f32[24,2048]{1,0:T(8,128)S(1)}, u32[]{:S(2)}, u32[]{:S(2)}) collective-permute-start(f32[24,2048]{1,0:T(8,128)S(1)} %convert_add_fusion), channel_id=1, source_target_pairs={{0,64},{192,128},{1,65},{193,129},{2,66},{194,130},{3,67},{195,131... | collective-permute-start | bytes 589832 | tf_op jit(solution)/shard_map/ppermute | solution.py:217
  89.1 7.1 %collective-permute-start.11 = (bf16[24,2048]{1,0:T(8,128)(2,1)}, bf16[24,2048]{1,0:T(8,128)(2,1)S(1)}, u32[]{:S(2)}, u32[]{:S(2)}) collective-permute-start(bf16[24,2048]{1,0:T(8,128)(2,1)} %fusion.51), channel_id=1, source_target_pairs={{128,0},{64,192},{129,1},{65,193},{130,2},{66,194},{131,3},{67,195... | collective-permute-start | bytes 294920 | tf_op jit(solution)/shard_map/ppermute | solution.py:218
  90.4 10.6 %collective-permute-start.12 = (bf16[24,2048]{1,0:T(8,128)(2,1)}, bf16[24,2048]{1,0:T(8,128)(2,1)}, u32[]{:S(2)}, u32[]{:S(2)}) collective-permute-start(bf16[24,2048]{1,0:T(8,128)(2,1)} %fusion.51), channel_id=1, source_target_pairs={{128,64},{64,128},{129,65},{65,129},{130,66},{66,130},{131,67},{67... | collective-permute-start | bytes 294920 | tf_op jit(solution)/shard_map/ppermute | solution.py:218
  91.7 11.2 %collective-permute-start.7 = (f32[24,2048]{1,0:T(8,128)S(1)}, f32[24,2048]{1,0:T(8,128)S(1)}, u32[]{:S(2)}, u32[]{:S(2)}) collective-permute-start(f32[24,2048]{1,0:T(8,128)S(1)} %convert_add_fusion), channel_id=1, source_target_pairs={{128,0},{64,192},{129,1},{65,193},{130,2},{66,194},{131,3},{67,195... | collective-permute-start | bytes 589832 | tf_op jit(solution)/shard_map/ppermute | solution.py:217
  93.0 9.9 %collective-permute-start.8 = (f32[24,2048]{1,0:T(8,128)S(1)}, f32[24,2048]{1,0:T(8,128)S(1)}, u32[]{:S(2)}, u32[]{:S(2)}) collective-permute-start(f32[24,2048]{1,0:T(8,128)S(1)} %convert_add_fusion), channel_id=1, source_target_pairs={{128,64},{64,128},{129,65},{65,129},{130,66},{66,130},{131,67},{67... | collective-permute-start | bytes 589832 | tf_op jit(solution)/shard_map/ppermute | solution.py:217
  96.1 6.7 %collective-permute-start.9 = (bf16[24,2048]{1,0:T(8,128)(2,1)}, bf16[24,2048]{1,0:T(8,128)(2,1)S(1)}, u32[]{:S(2)}, u32[]{:S(2)}) collective-permute-start(bf16[24,2048]{1,0:T(8,128)(2,1)} %fusion.51), channel_id=1, source_target_pairs={{0,64},{192,128},{1,65},{193,129},{2,66},{194,130},{3,67},{195,131... | collective-permute-start | bytes 294920 | tf_op jit(solution)/shard_map/ppermute | solution.py:218
  103.2 3.5 %collective-permute-start.13 = (bf16[24,2048]{1,0:T(8,128)(2,1)S(1)}, bf16[24,2048]{1,0:T(8,128)(2,1)S(1)}, u32[]{:S(2)}, u32[]{:S(2)}) collective-permute-start(bf16[24,2048]{1,0:T(8,128)(2,1)S(1)} %fusion.43), channel_id=1, source_target_pairs={{0,48},{16,0},{32,16},{48,32},{1,49},{17,1},{33,17},{49,33},{2,50}... | collective-permute-start | bytes 294920 | tf_op jit(solution)/shard_map/ppermute | solution.py:36
  103.3 5.1 %collective-permute-start.14 = (bf16[24,2048]{1,0:T(8,128)(2,1)S(1)}, bf16[24,2048]{1,0:T(8,128)(2,1)S(1)}, u32[]{:S(2)}, u32[]{:S(2)}) collective-permute-start(bf16[24,2048]{1,0:T(8,128)(2,1)S(1)} %fusion.43), channel_id=1, source_target_pairs={{0,32},{16,48},{32,0},{48,16},{1,33},{17,49},{33,1},{49,17},{2,34}... | collective-permute-start | bytes 294920 | tf_op jit(solution)/shard_map/ppermute | solution.py:36
  103.4 6.0 %collective-permute-start.15 = (bf16[24,2048]{1,0:T(8,128)(2,1)S(1)}, bf16[24,2048]{1,0:T(8,128)(2,1)S(1)}, u32[]{:S(2)}, u32[]{:S(2)}) collective-permute-start(bf16[24,2048]{1,0:T(8,128)(2,1)S(1)} %fusion.43), channel_id=1, source_target_pairs={{0,16},{16,32},{32,48},{48,0},{1,17},{17,33},{33,49},{49,1},{2,18}... | collective-permute-start | bytes 294920 | tf_op jit(solution)/shard_map/ppermute | solution.py:36
  154.9 6.5 %collective-permute-start.16 = (bf16[4,8,24,2048]{3,2,1,0:T(8,128)(2,1)}, bf16[4,8,24,2048]{3,2,1,0:T(8,128)(2,1)}, u32[]{:S(2)}, u32[]{:S(2)}) collective-permute-start(bf16[4,8,24,2048]{3,2,1,0:T(8,128)(2,1)} %bitcast.186), channel_id=1, source_target_pairs={{0,1},{1,0},{2,3},{3,2},{4,5},{5,4},{6,7},{7,6},{8,9},{9,8},{10,11... | collective-permute-start | bytes 9437192 | tf_op jit(solution)/shard_map/ppermute | solution.py:245
  (6 other events, 21.3 us)
Sparse Core Ops, SparseCore 0:
  110.4 44.4 all-gather.2

commit v17 on v15

--- a/solution.py
+++ b/solution.py
@@ -237,12 +237,12 @@
             pick = jnp.where(distance == y_count - step, by_distance[step], pick)
         in_order.append(pick)
     gathered = jnp.stack(in_order)
-    gathered = lax.all_gather(gathered, "z", axis=1, tiled=False)
+    gathered = lax.all_gather(gathered, "z", axis=0, tiled=False)
     core = lax.axis_index("core")
     cores = lax.axis_size("core")
     twin = lax.ppermute(gathered, "core", [(0, 1), (1, 0)])
-    mine_logits = jnp.einsum("yzrd,dv->yzrv", gathered, w_vocab, preferred_element_type=jnp.float32)
-    twin_logits = jnp.einsum("yzrd,dv->yzrv", twin, w_vocab, preferred_element_type=jnp.float32)
+    mine_logits = jnp.einsum("zyrd,dv->yzrv", gathered, w_vocab, preferred_element_type=jnp.float32)
+    twin_logits = jnp.einsum("zyrd,dv->yzrv", twin, w_vocab, preferred_element_type=jnp.float32)
     logits = jnp.zeros(
         mine_logits.shape[:2] + (cores,) + mine_logits.shape[2:], jnp.float32
     )

time: 171 us -> 171 us (level)
  no operation moved by 1% of the time
where the time goes in v17:
time: 171 us; the launch traced here: 170 us
  waiting for transfers between devices  71.5 us (42%)
  local copies, waits for them, and re-layouts  27.8 us (16%)
  starting transfers between devices  25.5 us (15%)
  matrix products  20.7 us (12%)
  between operations  13.8 us (8%)
  other arithmetic  11.1 us (6%)
    all_gather x1, waiting for transfers between devices, body(): gathered = lax.all_gather(gathered, 'z', axis=0, tiled=False)  43.7 us
    unnamed x33, local copies, waits for them, and re-layouts  12.9 us
    ppermute x7, waiting for transfers between devices, shifted(): return lax.ppermute(value, axis, pairs)  12.7 us
    ppermute x7, starting transfers between devices, shifted(): return lax.ppermute(value, axis, pairs)  11.6 us
    ppermute x3, starting transfers between devices, from_partner(): return lax.ppermute(block, axis, route)  7.16 us
    ppermute x1, waiting for transfers between devices, body(): from_guide = lax.ppermute(payload, pair, [(2, 0), (1, 3)])  6.01 us
    slice x1, local copies, waits for them, and re-layouts, dense_scores(): key_rows = flat[:, :half_width].reshape(count, KVH, HD)  5.85 us
    dot_general x2, matrix products, body(): jnp.einsum('rkgt,tkd->rkgd', rounded, values.astype(jnp.float32), precisi...  4.7 us
  transfers between devices with their start and end apart: 15, of which 9 were waited for; matrix products, arithmetic and copies ran while one was open for 22% of the time, Pallas kernels for 0%

profile of v17, /device:TPU:1, one launch (start us, length us, event | category | flops | bytes accessed | tf_op | source)
XLA Modules:
  0.0 170.4 jit_solution(10631959079614520312)
XLA Ops:
  9.4 3.6 %collective-permute-start = (bf16[24,1024]{1,0:T(8,128)(2,1)}, bf16[24,1024]{1,0:T(8,128)(2,1)S(1)}, u32[]{:S(2)}, u32[]{:S(2)}) collective-permute-start(bf16[24,1024]{1,0:T(8,128)(2,1)} %get-tuple-element.24), channel_id=1, source_target_pairs={{0,128},{128,0},{1,129},{129,1},{2,130},{130,2},{3,131},{131,3},{4... | collective-permute-start | bytes 147464 | tf_op jit(solution)/shard_map/ppermute | solution.py:30
  20.3 5.8 %fusion.84 = (bf16[2944,320]{1,0:T(8,128)(2,1)}, bf16[2944,320]{1,0:T(8,128)(2,1)}) fusion(bf16[2944,640]{1,0:T(8,128)(2,1)} %bitcast.179), kind=kLoop, calls=%fused_computation.155 | loop fusion | bytes 7536640 | tf_op jit(solution)/shard_map/slice | solution.py:83
  26.3 3.0 %fusion.18 = bf16[4,2,64,640]{3,0,2,1:T(4,128)(2,1)S(1)} fusion(bf16[46,64,640]{2,1,0:T(8,128)(2,1)S(1)} %bitcast.180, s32[4,2]{0,1:T(2,128)S(1)} %select_reduce_fusion), kind=kOutput, calls=%fused_computation.21 | convolution fusion | flops 30474608 | bytes 4423712 | tf_op jit(solution)/shard_map/smp,pwc->smwc/dot_general | solution.py:158
  30.7 1.7 slice.110
  33.2 4.1 %copy.120 = bf16[2944,320]{0,1:T(8,128)(2,1)} copy(bf16[2944,320]{1,0:T(8,128)(2,1)} %get-tuple-element.11) | data formatting | bytes 3768320
  37.3 4.1 %copy.122 = bf16[2944,320]{0,1:T(8,128)(2,1)} copy(bf16[2944,320]{1,0:T(8,128)(2,1)} %get-tuple-element.12) | data formatting | bytes 3768320
  42.4 8.1 %collective-permute-start.2 = (bf16[2,64,640]{2,1,0:T(8,128)(2,1)S(1)}, bf16[2,64,640]{2,1,0:T(8,128)(2,1)S(1)}, u32[]{:S(2)}, u32[]{:S(2)}) collective-permute-start(bf16[2,64,640]{2,1,0:T(8,128)(2,1)S(1)} %bitcast.186), channel_id=1, source_target_pairs={{0,126},{1,127},{2,0},{3,1},{4,2},{5,3},{6,4},{7,5},{8,6},{9,7},{1... | collective-permute-start | bytes 491528 | tf_op jit(solution)/shard_map/ppermute | solution.py:36
  54.0 1.7 %collective-permute-start.1 = (f32[24,1920]{1,0:T(8,128)}, f32[24,1920]{1,0:T(8,128)}, u32[]{:S(2)}, u32[]{:S(2)}) collective-permute-start(f32[24,1920]{1,0:T(8,128)} %select_bitcast_fusion), channel_id=1, source_target_pairs={{0,128},{128,0},{1,129},{129,1},{2,130},{130,2},{3,131},{131,3},{4... | collective-permute-start | bytes 552968 | tf_op jit(solution)/shard_map/ppermute | solution.py:30
  55.8 8.1 %collective-permute-done.5 = bf16[2,64,640]{2,1,0:T(8,128)(2,1)S(1)} collective-permute-done((bf16[2,64,640]{2,1,0:T(8,128)(2,1)S(1)}, bf16[2,64,640]{2,1,0:T(8,128)(2,1)S(1)}, u32[]{:S(2)}, u32[]{:S(2)}) %collective-permute-start.5) | collective-permute-done | bytes 163872 | tf_op jit(solution)/shard_map/ppermute | solution.py:36
  64.8 1.9 %copy.121 = bf16[512,320]{0,1:T(8,128)(2,1)} copy(bf16[512,320]{1,0:T(8,128)(2,1)} %get-tuple-element.14) | data formatting | bytes 655360
  70.7 2.6 %bitcast_reduce_fusion = (f32[24,5,4]{0,2,1:T(4,128)S(1)}, f32[5,24,4,2944]{3,1,2,0:T(8,128)S(1)}) fusion(pred[24,2944]{1,0:T(8,128)(4,1)S(1)} %broadcast_compare_fusion, bf16[2944,5,64,1]{0,2,3,1:T(8,128)(2,1)} %bitcast.181, bf16[24,5,4,64]{3,2,1,0:T(4,128)(2,1)S(1)} %reshape.220), kind=kOutput, calls=%fused_computation.1 | convolution fusion | flops 185118240 | bytes 7670656 | tf_op jit(solution)/shard_map/rkgd,tkd->rkgt/dot_general | solution.py:85
  73.4 1.6 multiply_reduce_fusion
  75.4 4.0 %fusion.28 = f32[24,5,4,64]{3,0,2,1:T(8,128)S(1)} fusion(bf16[2944,5,64,1]{0,2,3,1:T(8,128)(2,1)S(1)} %bitcast.183, f32[5,24,4,2944]{3,1,2,0:T(8,128)S(1)} %get-tuple-element.33, f32[24,2944]{1,0:T(8,128)S(1)} %copy-done.6, f32[24,5,4]{0,2,1:T(4,128)S(1)} %get-tuple-element.10, pred[24,2944]{1,0:T(8,128)(4,1)S(1)} %broadcast_compare_fusion, ...), kind=kOutput, calls=%fused_computation.31 | convolution fusion | flops 1093816320 | bytes 8047360 | tf_op jit(solution)/shard_map/rkgt,tkd->rkgd/dot_general | solution.py:195
  80.3 1.9 %collective-permute-start.6 = (bf16[24,640]{1,0:T(8,128)(2,1)S(1)}, bf16[24,640]{1,0:T(8,128)(2,1)S(1)}, u32[]{:S(2)}, u32[]{:S(2)}) collective-permute-start(bf16[24,640]{1,0:T(8,128)(2,1)S(1)} %get-tuple-element.28), channel_id=1, source_target_pairs={{0,128},{128,0},{1,129},{129,1},{2,130},{130,2},{3,131},{131,3},{4... | collective-permute-start | bytes 92168 | tf_op jit(solution)/shard_map/ppermute | solution.py:30
  82.2 2.5 %collective-permute-done.6 = bf16[24,640]{1,0:T(8,128)(2,1)S(1)} collective-permute-done((bf16[24,640]{1,0:T(8,128)(2,1)S(1)}, bf16[24,640]{1,0:T(8,128)(2,1)S(1)}, u32[]{:S(2)}, u32[]{:S(2)}) %collective-permute-start.6) | collective-permute-done | bytes 30752 | tf_op jit(solution)/shard_map/ppermute | solution.py:30
  85.3 3.9 %collective-permute-start.9 = (f32[2,24,2048]{2,1,0:T(8,128)S(1)}, f32[2,24,2048]{2,1,0:T(8,128)}, u32[]{:S(2)}, u32[]{:S(2)}) collective-permute-start(f32[2,24,2048]{2,1,0:T(8,128)S(1)} %pad_maximum_fusion.1), channel_id=1, source_target_pairs={{0,64},{192,128},{1,65},{193,129},{2,66},{194,130},{3,67},{195,131... | collective-permute-start | bytes 1179656 | tf_op jit(solution)/shard_map/ppermute | solution.py:216
  91.1 4.4 %collective-permute-done.9 = f32[2,24,2048]{2,1,0:T(8,128)} collective-permute-done((f32[2,24,2048]{2,1,0:T(8,128)S(1)}, f32[2,24,2048]{2,1,0:T(8,128)}, u32[]{:S(2)}, u32[]{:S(2)}) %collective-permute-start.9) | collective-permute-done | bytes 393248 | tf_op jit(solution)/shard_map/ppermute | solution.py:216
  95.6 6.0 %collective-permute-done.7 = f32[2,24,2048]{2,1,0:T(8,128)S(1)} collective-permute-done((f32[2,24,2048]{2,1,0:T(8,128)S(1)}, f32[2,24,2048]{2,1,0:T(8,128)S(1)}, u32[]{:S(2)}, u32[]{:S(2)}) %collective-permute-start.7) | collective-permute-done | bytes 393248 | tf_op jit(solution)/shard_map/ppermute | solution.py:218
  103.5 2.0 %collective-permute-done.10 = bf16[24,2048]{1,0:T(8,128)(2,1)S(1)} collective-permute-done((bf16[24,2048]{1,0:T(8,128)(2,1)S(1)}, bf16[24,2048]{1,0:T(8,128)(2,1)S(1)}, u32[]{:S(2)}, u32[]{:S(2)}) %collective-permute-start.10) | collective-permute-done | bytes 98336 | tf_op jit(solution)/shard_map/ppermute | solution.py:36
  105.5 1.6 collective-permute-done.11
  109.0 43.7 %all-gather.3.cloned.1.call-done = bf16[32,24,2048]{2,1,0:T(8,128)(2,1)} async-done(((bf16[4,24,2048]{2,1,0:T(8,128)(2,1)}), bf16[32,24,2048]{2,1,0:T(8,128)(2,1)}) %all-gather.3.cloned.1.call-update) | async-done | bytes 3145744 | tf_op jit(solution)/shard_map/all_gather | solution.py:240
  153.7 3.2 %convolution_bitcast_fusion.1 = f32[4,8,1,24,250]{4,3,0,1,2:T(8,128)S(1)} fusion(bf16[8,4,24,2048]{3,2,1,0:T(8,128)(2,1)} %bitcast.196, bf16[2048,250]{1,0:T(8,128)(2,1)} %param.16), kind=kOutput, calls=%fused_computation.26 | convolution fusion | flops 786432000 | bytes 4937728 | tf_op jit(solution)/shard_map/zyrd,dv->yzrv/dot_general | solution.py:244
  157.2 2.1 %collective-permute-done.13 = bf16[8,4,24,2048]{3,2,1,0:T(8,128)(2,1)} collective-permute-done((bf16[8,4,24,2048]{3,2,1,0:T(8,128)(2,1)}, bf16[8,4,24,2048]{3,2,1,0:T(8,128)(2,1)}, u32[]{:S(2)}, u32[]{:S(2)}) %collective-permute-start.13) | collective-permute-done | bytes 3145760 | tf_op jit(solution)/shard_map/ppermute | solution.py:243
  159.3 3.0 %convolution_bitcast_fusion = f32[4,8,1,24,250]{4,3,0,1,2:T(8,128)S(1)} fusion(bf16[8,4,24,2048]{3,2,1,0:T(8,128)(2,1)} %collective-permute-done.13, bf16[2048,250]{1,0:T(8,128)(2,1)S(1)} %copy-done.11), kind=kOutput, calls=%fused_computation.25 | convolution fusion | flops 786432000 | bytes 4937728 | tf_op jit(solution)/shard_map/zyrd,dv->yzrv/dot_general | solution.py:245
  (110 shorter events, 32.2 us)
Async XLA Ops:
  6.5 78.1 %copy-start = (bf16[640,2048]{1,0:T(8,128)(2,1)S(1)}, bf16[640,2048]{1,0:T(8,128)(2,1)}, u32[]{:S(2)}) copy-start(bf16[640,2048]{1,0:T(8,128)(2,1)} %param.14) | copy-start | bytes 7864324
  6.5 146.2 %all-gather.3.cloned.1.call-start = ((), (), s32[]{:S(2)}) async-start(), calls=%async_computation | async-start | bytes 3538944 | tf_op jit(solution)/shard_map/all_gather | solution.py:240
  9.4 32.0 %collective-permute-start = (bf16[24,1024]{1,0:T(8,128)(2,1)}, bf16[24,1024]{1,0:T(8,128)(2,1)S(1)}, u32[]{:S(2)}, u32[]{:S(2)}) collective-permute-start(bf16[24,1024]{1,0:T(8,128)(2,1)} %get-tuple-element.24), channel_id=1, source_target_pairs={{0,128},{128,0},{1,129},{129,1},{2,130},{130,2},{3,131},{131,3},{4... | collective-permute-start | bytes 147464 | tf_op jit(solution)/shard_map/ppermute | solution.py:30
  20.2 5.9 %copy-start.3 = (f32[24,3456]{1,0:T(8,128)}, f32[24,3456]{1,0:T(8,128)S(1)}, u32[]{:S(2)}) copy-start(f32[24,3456]{1,0:T(8,128)S(1)} %reshape.222) | copy-start | bytes 995332
  20.3 6.0 %copy-start.1 = (bf16[1,46,64,640]{3,2,1,0:T(8,128)(2,1)S(1)}, bf16[1,46,64,640]{3,2,1,0:T(8,128)(2,1)}, u32[]{:S(2)}) copy-start(bf16[1,46,64,640]{3,2,1,0:T(8,128)(2,1)} %param.17) | copy-start | bytes 11304964
  41.4 11.2 %copy-start.2 = (bf16[1024,1920]{1,0:T(8,128)(2,1)S(1)}, bf16[1024,1920]{1,0:T(8,128)(2,1)}, u32[]{:S(2)}) copy-start(bf16[1024,1920]{1,0:T(8,128)(2,1)} %param.13) | copy-start | bytes 11796484
  42.4 13.4 %collective-permute-start.2 = (bf16[2,64,640]{2,1,0:T(8,128)(2,1)S(1)}, bf16[2,64,640]{2,1,0:T(8,128)(2,1)S(1)}, u32[]{:S(2)}, u32[]{:S(2)}) collective-permute-start(bf16[2,64,640]{2,1,0:T(8,128)(2,1)S(1)} %bitcast.186), channel_id=1, source_target_pairs={{0,126},{1,127},{2,0},{3,1},{4,2},{5,3},{6,4},{7,5},{8,6},{9,7},{1... | collective-permute-start | bytes 491528 | tf_op jit(solution)/shard_map/ppermute | solution.py:36
  50.5 5.3 %collective-permute-start.3 = (bf16[2,64,640]{2,1,0:T(8,128)(2,1)S(1)}, bf16[2,64,640]{2,1,0:T(8,128)(2,1)S(1)}, u32[]{:S(2)}, u32[]{:S(2)}) collective-permute-start(bf16[2,64,640]{2,1,0:T(8,128)(2,1)S(1)} %bitcast.187), channel_id=1, source_target_pairs={{0,127},{1,0},{2,1},{3,2},{4,3},{5,4},{6,5},{7,6},{8,7},{9,8},{10,... | collective-permute-start | bytes 491528 | tf_op jit(solution)/shard_map/ppermute | solution.py:36
  51.9 3.9 %collective-permute-start.4 = (bf16[2,64,640]{2,1,0:T(8,128)(2,1)S(1)}, bf16[2,64,640]{2,1,0:T(8,128)(2,1)S(1)}, u32[]{:S(2)}, u32[]{:S(2)}) collective-permute-start(bf16[2,64,640]{2,1,0:T(8,128)(2,1)S(1)} %bitcast.188), channel_id=1, source_target_pairs={{0,1},{1,2},{2,3},{3,4},{4,5},{5,6},{6,7},{7,8},{8,9},{9,10},{10,1... | collective-permute-start | bytes 491528 | tf_op jit(solution)/shard_map/ppermute | solution.py:36
  52.4 11.4 %collective-permute-start.5 = (bf16[2,64,640]{2,1,0:T(8,128)(2,1)S(1)}, bf16[2,64,640]{2,1,0:T(8,128)(2,1)S(1)}, u32[]{:S(2)}, u32[]{:S(2)}) collective-permute-start(bf16[2,64,640]{2,1,0:T(8,128)(2,1)S(1)} %bitcast.189), channel_id=1, source_target_pairs={{0,2},{1,3},{2,4},{3,5},{4,6},{5,7},{6,8},{7,9},{8,10},{9,11},{10,... | collective-permute-start | bytes 491528 | tf_op jit(solution)/shard_map/ppermute | solution.py:36
  53.3 16.1 %copy-start.9 = (pred[24,512]{1,0:T(8,128)(4,1)S(1)}, pred[24,512]{1,0:T(8,128)(4,1)}, u32[]{:S(2)}) copy-start(pred[24,512]{1,0:T(8,128)(4,1)} %broadcast_compare_fusion.1) | copy-start | bytes 36868
  54.0 13.6 %collective-permute-start.1 = (f32[24,1920]{1,0:T(8,128)}, f32[24,1920]{1,0:T(8,128)}, u32[]{:S(2)}, u32[]{:S(2)}) collective-permute-start(f32[24,1920]{1,0:T(8,128)} %select_bitcast_fusion), channel_id=1, source_target_pairs={{0,128},{128,0},{1,129},{129,1},{2,130},{130,2},{3,131},{131,3},{4... | collective-permute-start | bytes 552968 | tf_op jit(solution)/shard_map/ppermute | solution.py:30
  75.3 4.0 %copy-start.8 = (bf16[512,320]{0,1:T(8,128)(2,1)S(1)}, bf16[512,320]{0,1:T(8,128)(2,1)}, u32[]{:S(2)}) copy-start(bf16[512,320]{0,1:T(8,128)(2,1)} %copy.123) | copy-start | bytes 983044
  79.3 5.9 %copy-start.7 = (bf16[1,24,2048]{2,1,0:T(8,128)(2,1)S(1)}, bf16[1,24,2048]{2,1,0:T(8,128)(2,1)}, u32[]{:S(2)}) copy-start(bf16[1,24,2048]{2,1,0:T(8,128)(2,1)} %param.11) | copy-start | bytes 294916
  80.3 4.3 %collective-permute-start.6 = (bf16[24,640]{1,0:T(8,128)(2,1)S(1)}, bf16[24,640]{1,0:T(8,128)(2,1)S(1)}, u32[]{:S(2)}, u32[]{:S(2)}) collective-permute-start(bf16[24,640]{1,0:T(8,128)(2,1)S(1)} %get-tuple-element.28), channel_id=1, source_target_pairs={{0,128},{128,0},{1,129},{129,1},{2,130},{130,2},{3,131},{131,3},{4... | collective-permute-start | bytes 92168 | tf_op jit(solution)/shard_map/ppermute | solution.py:30
  84.6 17.2 %copy-start.10 = (f32[2048]{0:T(1024)S(1)}, f32[2048]{0:T(1024)}, u32[]{:S(2)}) copy-start(f32[2048]{0:T(1024)} %param.15) | copy-start | bytes 24580
  85.3 10.2 %collective-permute-start.9 = (f32[2,24,2048]{2,1,0:T(8,128)S(1)}, f32[2,24,2048]{2,1,0:T(8,128)}, u32[]{:S(2)}, u32[]{:S(2)}) collective-permute-start(f32[2,24,2048]{2,1,0:T(8,128)S(1)} %pad_maximum_fusion.1), channel_id=1, source_target_pairs={{0,64},{192,128},{1,65},{193,129},{2,66},{194,130},{3,67},{195,131... | collective-permute-start | bytes 1179656 | tf_op jit(solution)/shard_map/ppermute | solution.py:216
  89.2 12.4 %collective-permute-start.7 = (f32[2,24,2048]{2,1,0:T(8,128)S(1)}, f32[2,24,2048]{2,1,0:T(8,128)S(1)}, u32[]{:S(2)}, u32[]{:S(2)}) collective-permute-start(f32[2,24,2048]{2,1,0:T(8,128)S(1)} %pad_maximum_fusion.1), channel_id=1, source_target_pairs={{128,0},{64,192},{129,1},{65,193},{130,2},{66,194},{131,3},{67,195... | collective-permute-start | bytes 1179656 | tf_op jit(solution)/shard_map/ppermute | solution.py:218
  90.5 11.1 %collective-permute-start.8 = (f32[2,24,2048]{2,1,0:T(8,128)S(1)}, f32[2,24,2048]{2,1,0:T(8,128)S(1)}, u32[]{:S(2)}, u32[]{:S(2)}) collective-permute-start(f32[2,24,2048]{2,1,0:T(8,128)S(1)} %pad_maximum_fusion.1), channel_id=1, source_target_pairs={{128,64},{64,128},{129,65},{65,129},{130,66},{66,130},{131,67},{67... | collective-permute-start | bytes 1179656 | tf_op jit(solution)/shard_map/ppermute | solution.py:217
  101.9 3.5 %collective-permute-start.10 = (bf16[24,2048]{1,0:T(8,128)(2,1)S(1)}, bf16[24,2048]{1,0:T(8,128)(2,1)S(1)}, u32[]{:S(2)}, u32[]{:S(2)}) collective-permute-start(bf16[24,2048]{1,0:T(8,128)(2,1)S(1)} %fusion.46), channel_id=1, source_target_pairs={{0,48},{16,0},{32,16},{48,32},{1,49},{17,1},{33,17},{49,33},{2,50}... | collective-permute-start | bytes 294920 | tf_op jit(solution)/shard_map/ppermute | solution.py:36
  102.0 5.1 %collective-permute-start.11 = (bf16[24,2048]{1,0:T(8,128)(2,1)S(1)}, bf16[24,2048]{1,0:T(8,128)(2,1)S(1)}, u32[]{:S(2)}, u32[]{:S(2)}) collective-permute-start(bf16[24,2048]{1,0:T(8,128)(2,1)S(1)} %fusion.46), channel_id=1, source_target_pairs={{0,32},{16,48},{32,0},{48,16},{1,33},{17,49},{33,1},{49,17},{2,34}... | collective-permute-start | bytes 294920 | tf_op jit(solution)/shard_map/ppermute | solution.py:36
  102.1 6.0 %collective-permute-start.12 = (bf16[24,2048]{1,0:T(8,128)(2,1)S(1)}, bf16[24,2048]{1,0:T(8,128)(2,1)S(1)}, u32[]{:S(2)}, u32[]{:S(2)}) collective-permute-start(bf16[24,2048]{1,0:T(8,128)(2,1)S(1)} %fusion.46), channel_id=1, source_target_pairs={{0,16},{16,32},{32,48},{48,0},{1,17},{17,33},{33,49},{49,1},{2,18}... | collective-permute-start | bytes 294920 | tf_op jit(solution)/shard_map/ppermute | solution.py:36
  152.8 6.5 %collective-permute-start.13 = (bf16[8,4,24,2048]{3,2,1,0:T(8,128)(2,1)}, bf16[8,4,24,2048]{3,2,1,0:T(8,128)(2,1)}, u32[]{:S(2)}, u32[]{:S(2)}) collective-permute-start(bf16[8,4,24,2048]{3,2,1,0:T(8,128)(2,1)} %bitcast.195), channel_id=1, source_target_pairs={{0,1},{1,0},{2,3},{3,2},{4,5},{5,4},{6,7},{7,6},{8,9},{9,8},{10,11... | collective-permute-start | bytes 9437192 | tf_op jit(solution)/shard_map/ppermute | solution.py:243
  153.7 5.6 %copy-start.11 = (bf16[2048,250]{1,0:T(8,128)(2,1)S(1)}, bf16[2048,250]{1,0:T(8,128)(2,1)}, u32[]{:S(2)}) copy-start(bf16[2048,250]{1,0:T(8,128)(2,1)} %param.16) | copy-start | bytes 3072004
  (3 other events, 5.8 us)
Sparse Core Ops, SparseCore 0:
  109.2 43.5 all-gather.2
